TPU v7x, 32 devices: a whole 2x2x4 slice. The times are simulated.
32 devices in a mesh: segment: 4 (over z), rows: 8 (over y, x, core).
Axes of the slice: x: 2, y: 2, z: 4, core: 2. Of those that a mesh axis runs over, the one named last changes fastest.
Arguments:
- features: bfloat16 [4, 32, 24, 384], P(None, 'rows'), may hold values from -6 to 6
- gains: bfloat16 [4, 384], P('segment'), may hold values from 0.5 to 2
- kernels: bfloat16 [4, 3, 3, 3, 384, 384], P('segment'), may hold values from -0.0625 to 0.0625
Outputs:
- decoded: bfloat16 [4, 32, 24, 384], P('segment', 'rows')
All inputs are finite; a program needn't handle non-finite values.
Results may differ from a plain program's by a relative error of at most 0.014.
Values may be sent and summed in bfloat16 or wider, within the bound.
No kernel may reach another device: no remote copies, remote signals or barrier semaphores. Data moves between devices by JAX's collectives and lax.ppermute only.
A program may use at most 64 MiB of HBM per device.

v0:
```python
import jax
import jax.numpy as jnp
from jax import lax
from jax.sharding import PartitionSpec as P


def with_halo(array, sides, width):
    for axis, dim in sides:
        devices, length = (lax.axis_size(axis), array.shape[dim])
        up = [(i, (i + 1) % devices) for i in range(devices - 1)]
        down = [(j, i) for i, j in up]
        last = lax.slice_in_dim(array, length - width, length, axis=dim)
        first = lax.slice_in_dim(array, 0, width, axis=dim)
        before = lax.ppermute(last, axis, up)
        after = lax.ppermute(first, axis, down)
        array = jnp.concatenate([before, array, after], axis=dim)
    return array


def passed_along(value, axis, steps):
    count = lax.axis_size(axis)
    first, last = (max(0, -steps), min(count, count - steps))
    return lax.ppermute(value, axis, [(source, source + steps) for source in range(first, last)])


def activate(values_in, gain_row):
    widened = values_in.astype(jnp.float32)
    mean_square = jnp.mean(widened * widened, axis=-1, keepdims=True)
    return jax.nn.silu(
        widened * lax.rsqrt(mean_square + 1e-06) * gain_row.astype(jnp.float32)
    ).astype(jnp.bfloat16)


def causal_block(window, kernel, group_size):
    height = window.shape[1] - 2
    columns = window.shape[2]
    channels = window.shape[3]
    padded = jnp.pad(window, ((0, 0), (0, 0), (1, 1), (0, 0)))
    tap_list = []
    for time_off in range(3):
        for row_off in range(3):
            for col_off in range(3):
                tap_list.append(
                    padded[
                        time_off : time_off + group_size,
                        row_off : row_off + height,
                        col_off : col_off + columns,
                    ]
                )
    stacked = jnp.concatenate(tap_list, axis=-1).reshape(
        group_size * height * columns, 27 * channels
    )
    result = jnp.dot(
        stacked, kernel.reshape(27 * channels, channels), preferred_element_type=jnp.float32
    )
    return result.reshape(group_size, height, columns, channels)


def local(features, gains, kernels):
    segment_count = lax.axis_size("segment")
    segment_index = lax.axis_index("segment")
    frame_count, height, columns, channels = features.shape
    gain_row = gains[0]
    kernel = kernels[0]
    group_size = 1
    step_count = frame_count // group_size + segment_count - 1
    segment_even = segment_index % 2 == 0
    segment_first = segment_index == 0
    segment_last = segment_index == segment_count - 1

    def advance(step_index, carry):
        skip_in, current_in, frame_cache, collected = carry
        first_frame = jnp.minimum(step_index * group_size, frame_count - group_size)
        arriving = lax.dynamic_slice_in_dim(features, first_frame, group_size, 0)
        arriving = jnp.where(
            step_index * group_size < frame_count, arriving, jnp.zeros_like(arriving)
        )
        skip_now = jnp.where(segment_first, arriving, skip_in)
        current_now = jnp.where(segment_first, arriving, current_in)
        activated = activate(current_now, gain_row)
        framed = with_halo(activated, (("rows", 1),), 1)
        window = jnp.concatenate([frame_cache, framed], axis=0)
        convolved = causal_block(window, kernel, group_size)
        inner_out = convolved.astype(jnp.bfloat16)
        summed = (skip_now.astype(jnp.float32) + convolved).astype(jnp.bfloat16)
        skip_out = jnp.where(segment_even, current_now, summed)
        current_out = jnp.where(segment_even, inner_out, summed)
        out_index = (step_index - (segment_count - 1)) * group_size
        out_valid = jnp.logical_and(out_index >= 0, segment_last)
        placed = lax.dynamic_update_slice_in_dim(
            collected, current_out, jnp.clip(out_index, 0, frame_count - group_size), 0
        )
        collected = jnp.where(out_valid, placed, collected)
        skip_next, current_next = passed_along((skip_out, current_out), "segment", 1)
        return (skip_next, current_next, window[group_size:], collected)

    empty_block = jnp.zeros((group_size, height, columns, channels), jnp.bfloat16)
    empty_cache = jnp.zeros((2, height + 2, columns, channels), jnp.bfloat16)
    empty_out = jnp.zeros((frame_count, height, columns, channels), jnp.bfloat16)
    finished = lax.fori_loop(
        0, step_count, advance, (empty_block, empty_block, empty_cache, empty_out)
    )
    delivered = lax.psum_scatter(
        finished[3].astype(jnp.float32).astype(jnp.bfloat16),
        "segment",
        scatter_dimension=0,
        tiled=True,
    )
    return delivered


def solution(mesh):
    placed = (
        P(None, "rows", None, None),
        P("segment", None),
        P("segment", None, None, None, None, None),
    )
    return jax.shard_map(
        local,
        mesh=mesh,
        in_specs=placed,
        out_specs=P("segment", "rows", None, None),
        check_vma=False,
    )
```

profile of v0, /device:TPU:0, one launch (start us, length us, event | category | flops | bytes accessed | tf_op | source)
XLA Modules:
  0.0 199.7 jit_solution(8769279775974403768)
XLA Ops:
  7.3 156.3 %while.21 = (s32[]{:T(128)}, bf16[1,4,24,384]{3,2,1,0:T(8,128)(2,1)S(1)}, bf16[1,4,24,384]{3,2,1,0:T(8,128)(2,1)S(1)}, bf16[2,6,24,384]{3,2,1,0:T(8,128)(2,1)S(1...) while((s32[]{:T(128)}, ...), condition=%wide.region_2.3_spmd, body=%wide.region_0.2_spmd.sunk | while | flops 766310912 | bytes 53573320 | solution.py:100
  8.5 1.3 collective-permute-start
  9.8 3.0 %collective-permute-start.1 = (bf16[1,1,24,384]{3,2,1,0:T(8,128)(2,1)S(1)}, bf16[1,1,24,384]{3,2,1,0:T(8,128)(2,1)S(1)}, u32[]{:S(2)}, u32[]{:S(2)}) collective-permute-start(bf16[1,1,24,384]{3,2,1,0:T(8,128)(2,1)S(1)} %get-tuple-element.377), channel_id=1, source_target_pairs={{0,1},{1,2},{2,3},{3,4},{4,5},{5,6},{6,7},{8,9},{9,10},{10,11},{11... | collective-permute-start | bytes 55304 | tf_op jit(solution)/shard_map/while/body/eval_jaxpr/ppermute | solution.py:14
  14.7 2.4 %copy-done = bf16[1,3,3,3,384,384]{5,4,3,2,1,0:T(8,128)(2,1)S(1)} copy-done((bf16[1,3,3,3,384,384]{5,4,3,2,1,0:T(8,128)(2,1)S(1)}, bf16[1,3,3,3,384,384]{5,4,3,2,1,0:T(8,128)(2,1)}, u32[]{:S(2)}) %copy-start) | copy-done | bytes 7962648 | tf_op jit(solution)/shard_map/while
  17.0 1.4 fusion.83
  19.4 4.9 %collective-permute-start.2 = (bf16[1,4,24,384]{3,2,1,0:T(8,128)(2,1)S(1)}, bf16[1,4,24,384]{3,2,1,0:T(8,128)(2,1)S(1)}, u32[]{:S(2)}, u32[]{:S(2)}) collective-permute-start(bf16[1,4,24,384]{3,2,1,0:T(8,128)(2,1)S(1)} %get-tuple-element.378), channel_id=1, source_target_pairs={{0,8},{8,16},{16,24},{1,9},{9,17},{17,25},{2,10},{10,18},{18,26},{... | collective-permute-start | bytes 221192 | tf_op jit(solution)/shard_map/while/body/eval_jaxpr/ppermute | solution.py:23
  24.4 3.5 %collective-permute-start.3 = (bf16[1,4,24,384]{3,2,1,0:T(8,128)(2,1)S(1)}, bf16[1,4,24,384]{3,2,1,0:T(8,128)(2,1)S(1)}, u32[]{:S(2)}, u32[]{:S(2)}) collective-permute-start(bf16[1,4,24,384]{3,2,1,0:T(8,128)(2,1)S(1)} %get-tuple-element.379), channel_id=1, source_target_pairs={{0,8},{8,16},{16,24},{1,9},{9,17},{17,25},{2,10},{10,18},{18,26},{... | collective-permute-start | bytes 221192 | tf_op jit(solution)/shard_map/while/body/eval_jaxpr/ppermute | solution.py:23
  27.9 2.5 %collective-permute-done.3 = bf16[1,4,24,384]{3,2,1,0:T(8,128)(2,1)S(1)} collective-permute-done((bf16[1,4,24,384]{3,2,1,0:T(8,128)(2,1)S(1)}, bf16[1,4,24,384]{3,2,1,0:T(8,128)(2,1)S(1)}, u32[]{:S(2)}, u32[]{:S(2)}) %collective-permute-start.3) | collective-permute-done | bytes 73760 | tf_op jit(solution)/shard_map/while/body/eval_jaxpr/ppermute | solution.py:23
  31.6 1.3 collective-permute-start
  32.9 3.0 %collective-permute-start.1 = (bf16[1,1,24,384]{3,2,1,0:T(8,128)(2,1)S(1)}, bf16[1,1,24,384]{3,2,1,0:T(8,128)(2,1)S(1)}, u32[]{:S(2)}, u32[]{:S(2)}) collective-permute-start(bf16[1,1,24,384]{3,2,1,0:T(8,128)(2,1)S(1)} %get-tuple-element.377), channel_id=1, source_target_pairs={{0,1},{1,2},{2,3},{3,4},{4,5},{5,6},{6,7},{8,9},{9,10},{10,11},{11... | collective-permute-start | bytes 55304 | tf_op jit(solution)/shard_map/while/body/eval_jaxpr/ppermute | solution.py:14
  37.7 2.4 %copy-done = bf16[1,3,3,3,384,384]{5,4,3,2,1,0:T(8,128)(2,1)S(1)} copy-done((bf16[1,3,3,3,384,384]{5,4,3,2,1,0:T(8,128)(2,1)S(1)}, bf16[1,3,3,3,384,384]{5,4,3,2,1,0:T(8,128)(2,1)}, u32[]{:S(2)}) %copy-start) | copy-done | bytes 7962648 | tf_op jit(solution)/shard_map/while
  40.1 1.4 fusion.83
  42.5 4.4 %collective-permute-start.2 = (bf16[1,4,24,384]{3,2,1,0:T(8,128)(2,1)S(1)}, bf16[1,4,24,384]{3,2,1,0:T(8,128)(2,1)S(1)}, u32[]{:S(2)}, u32[]{:S(2)}) collective-permute-start(bf16[1,4,24,384]{3,2,1,0:T(8,128)(2,1)S(1)} %get-tuple-element.378), channel_id=1, source_target_pairs={{0,8},{8,16},{16,24},{1,9},{9,17},{17,25},{2,10},{10,18},{18,26},{... | collective-permute-start | bytes 221192 | tf_op jit(solution)/shard_map/while/body/eval_jaxpr/ppermute | solution.py:23
  46.9 3.5 %collective-permute-start.3 = (bf16[1,4,24,384]{3,2,1,0:T(8,128)(2,1)S(1)}, bf16[1,4,24,384]{3,2,1,0:T(8,128)(2,1)S(1)}, u32[]{:S(2)}, u32[]{:S(2)}) collective-permute-start(bf16[1,4,24,384]{3,2,1,0:T(8,128)(2,1)S(1)} %get-tuple-element.379), channel_id=1, source_target_pairs={{0,8},{8,16},{16,24},{1,9},{9,17},{17,25},{2,10},{10,18},{18,26},{... | collective-permute-start | bytes 221192 | tf_op jit(solution)/shard_map/while/body/eval_jaxpr/ppermute | solution.py:23
  50.4 1.9 collective-permute-done.3
  53.5 1.3 collective-permute-start
  54.8 3.7 %collective-permute-start.1 = (bf16[1,1,24,384]{3,2,1,0:T(8,128)(2,1)S(1)}, bf16[1,1,24,384]{3,2,1,0:T(8,128)(2,1)S(1)}, u32[]{:S(2)}, u32[]{:S(2)}) collective-permute-start(bf16[1,1,24,384]{3,2,1,0:T(8,128)(2,1)S(1)} %get-tuple-element.377), channel_id=1, source_target_pairs={{0,1},{1,2},{2,3},{3,4},{4,5},{5,6},{6,7},{8,9},{9,10},{10,11},{11... | collective-permute-start | bytes 55304 | tf_op jit(solution)/shard_map/while/body/eval_jaxpr/ppermute | solution.py:14
  60.4 2.4 %copy-done = bf16[1,3,3,3,384,384]{5,4,3,2,1,0:T(8,128)(2,1)S(1)} copy-done((bf16[1,3,3,3,384,384]{5,4,3,2,1,0:T(8,128)(2,1)S(1)}, bf16[1,3,3,3,384,384]{5,4,3,2,1,0:T(8,128)(2,1)}, u32[]{:S(2)}) %copy-start) | copy-done | bytes 7962648 | tf_op jit(solution)/shard_map/while
  62.7 1.4 fusion.83
  65.1 4.0 %collective-permute-start.2 = (bf16[1,4,24,384]{3,2,1,0:T(8,128)(2,1)S(1)}, bf16[1,4,24,384]{3,2,1,0:T(8,128)(2,1)S(1)}, u32[]{:S(2)}, u32[]{:S(2)}) collective-permute-start(bf16[1,4,24,384]{3,2,1,0:T(8,128)(2,1)S(1)} %get-tuple-element.378), channel_id=1, source_target_pairs={{0,8},{8,16},{16,24},{1,9},{9,17},{17,25},{2,10},{10,18},{18,26},{... | collective-permute-start | bytes 221192 | tf_op jit(solution)/shard_map/while/body/eval_jaxpr/ppermute | solution.py:23
  69.1 2.2 %collective-permute-start.3 = (bf16[1,4,24,384]{3,2,1,0:T(8,128)(2,1)S(1)}, bf16[1,4,24,384]{3,2,1,0:T(8,128)(2,1)S(1)}, u32[]{:S(2)}, u32[]{:S(2)}) collective-permute-start(bf16[1,4,24,384]{3,2,1,0:T(8,128)(2,1)S(1)} %get-tuple-element.379), channel_id=1, source_target_pairs={{0,8},{8,16},{16,24},{1,9},{9,17},{17,25},{2,10},{10,18},{18,26},{... | collective-permute-start | bytes 221192 | tf_op jit(solution)/shard_map/while/body/eval_jaxpr/ppermute | solution.py:23
  71.4 1.9 collective-permute-done.3
  74.4 1.3 collective-permute-start
  75.7 5.8 %collective-permute-start.1 = (bf16[1,1,24,384]{3,2,1,0:T(8,128)(2,1)S(1)}, bf16[1,1,24,384]{3,2,1,0:T(8,128)(2,1)S(1)}, u32[]{:S(2)}, u32[]{:S(2)}) collective-permute-start(bf16[1,1,24,384]{3,2,1,0:T(8,128)(2,1)S(1)} %get-tuple-element.377), channel_id=1, source_target_pairs={{0,1},{1,2},{2,3},{3,4},{4,5},{5,6},{6,7},{8,9},{9,10},{10,11},{11... | collective-permute-start | bytes 55304 | tf_op jit(solution)/shard_map/while/body/eval_jaxpr/ppermute | solution.py:14
  83.3 2.4 %copy-done = bf16[1,3,3,3,384,384]{5,4,3,2,1,0:T(8,128)(2,1)S(1)} copy-done((bf16[1,3,3,3,384,384]{5,4,3,2,1,0:T(8,128)(2,1)S(1)}, bf16[1,3,3,3,384,384]{5,4,3,2,1,0:T(8,128)(2,1)}, u32[]{:S(2)}) %copy-start) | copy-done | bytes 7962648 | tf_op jit(solution)/shard_map/while
  85.7 1.4 fusion.83
  88.1 4.0 %collective-permute-start.2 = (bf16[1,4,24,384]{3,2,1,0:T(8,128)(2,1)S(1)}, bf16[1,4,24,384]{3,2,1,0:T(8,128)(2,1)S(1)}, u32[]{:S(2)}, u32[]{:S(2)}) collective-permute-start(bf16[1,4,24,384]{3,2,1,0:T(8,128)(2,1)S(1)} %get-tuple-element.378), channel_id=1, source_target_pairs={{0,8},{8,16},{16,24},{1,9},{9,17},{17,25},{2,10},{10,18},{18,26},{... | collective-permute-start | bytes 221192 | tf_op jit(solution)/shard_map/while/body/eval_jaxpr/ppermute | solution.py:23
  92.1 2.2 %collective-permute-start.3 = (bf16[1,4,24,384]{3,2,1,0:T(8,128)(2,1)S(1)}, bf16[1,4,24,384]{3,2,1,0:T(8,128)(2,1)S(1)}, u32[]{:S(2)}, u32[]{:S(2)}) collective-permute-start(bf16[1,4,24,384]{3,2,1,0:T(8,128)(2,1)S(1)} %get-tuple-element.379), channel_id=1, source_target_pairs={{0,8},{8,16},{16,24},{1,9},{9,17},{17,25},{2,10},{10,18},{18,26},{... | collective-permute-start | bytes 221192 | tf_op jit(solution)/shard_map/while/body/eval_jaxpr/ppermute | solution.py:23
  94.3 1.9 collective-permute-done.3
  98.7 5.5 %collective-permute-start.1 = (bf16[1,1,24,384]{3,2,1,0:T(8,128)(2,1)S(1)}, bf16[1,1,24,384]{3,2,1,0:T(8,128)(2,1)S(1)}, u32[]{:S(2)}, u32[]{:S(2)}) collective-permute-start(bf16[1,1,24,384]{3,2,1,0:T(8,128)(2,1)S(1)} %get-tuple-element.377), channel_id=1, source_target_pairs={{0,1},{1,2},{2,3},{3,4},{4,5},{5,6},{6,7},{8,9},{9,10},{10,11},{11... | collective-permute-start | bytes 55304 | tf_op jit(solution)/shard_map/while/body/eval_jaxpr/ppermute | solution.py:14
  106.0 2.4 %copy-done = bf16[1,3,3,3,384,384]{5,4,3,2,1,0:T(8,128)(2,1)S(1)} copy-done((bf16[1,3,3,3,384,384]{5,4,3,2,1,0:T(8,128)(2,1)S(1)}, bf16[1,3,3,3,384,384]{5,4,3,2,1,0:T(8,128)(2,1)}, u32[]{:S(2)}) %copy-start) | copy-done | bytes 7962648 | tf_op jit(solution)/shard_map/while
  108.4 1.4 fusion.83
  110.8 4.0 %collective-permute-start.2 = (bf16[1,4,24,384]{3,2,1,0:T(8,128)(2,1)S(1)}, bf16[1,4,24,384]{3,2,1,0:T(8,128)(2,1)S(1)}, u32[]{:S(2)}, u32[]{:S(2)}) collective-permute-start(bf16[1,4,24,384]{3,2,1,0:T(8,128)(2,1)S(1)} %get-tuple-element.378), channel_id=1, source_target_pairs={{0,8},{8,16},{16,24},{1,9},{9,17},{17,25},{2,10},{10,18},{18,26},{... | collective-permute-start | bytes 221192 | tf_op jit(solution)/shard_map/while/body/eval_jaxpr/ppermute | solution.py:23
  114.8 2.2 %collective-permute-start.3 = (bf16[1,4,24,384]{3,2,1,0:T(8,128)(2,1)S(1)}, bf16[1,4,24,384]{3,2,1,0:T(8,128)(2,1)S(1)}, u32[]{:S(2)}, u32[]{:S(2)}) collective-permute-start(bf16[1,4,24,384]{3,2,1,0:T(8,128)(2,1)S(1)} %get-tuple-element.379), channel_id=1, source_target_pairs={{0,8},{8,16},{16,24},{1,9},{9,17},{17,25},{2,10},{10,18},{18,26},{... | collective-permute-start | bytes 221192 | tf_op jit(solution)/shard_map/while/body/eval_jaxpr/ppermute | solution.py:23
  117.0 2.3 %collective-permute-done.3 = bf16[1,4,24,384]{3,2,1,0:T(8,128)(2,1)S(1)} collective-permute-done((bf16[1,4,24,384]{3,2,1,0:T(8,128)(2,1)S(1)}, bf16[1,4,24,384]{3,2,1,0:T(8,128)(2,1)S(1)}, u32[]{:S(2)}, u32[]{:S(2)}) %collective-permute-start.3) | collective-permute-done | bytes 73760 | tf_op jit(solution)/shard_map/while/body/eval_jaxpr/ppermute | solution.py:23
  121.7 4.7 %collective-permute-start.1 = (bf16[1,1,24,384]{3,2,1,0:T(8,128)(2,1)S(1)}, bf16[1,1,24,384]{3,2,1,0:T(8,128)(2,1)S(1)}, u32[]{:S(2)}, u32[]{:S(2)}) collective-permute-start(bf16[1,1,24,384]{3,2,1,0:T(8,128)(2,1)S(1)} %get-tuple-element.377), channel_id=1, source_target_pairs={{0,1},{1,2},{2,3},{3,4},{4,5},{5,6},{6,7},{8,9},{9,10},{10,11},{11... | collective-permute-start | bytes 55304 | tf_op jit(solution)/shard_map/while/body/eval_jaxpr/ppermute | solution.py:14
  128.2 2.4 %copy-done = bf16[1,3,3,3,384,384]{5,4,3,2,1,0:T(8,128)(2,1)S(1)} copy-done((bf16[1,3,3,3,384,384]{5,4,3,2,1,0:T(8,128)(2,1)S(1)}, bf16[1,3,3,3,384,384]{5,4,3,2,1,0:T(8,128)(2,1)}, u32[]{:S(2)}) %copy-start) | copy-done | bytes 7962648 | tf_op jit(solution)/shard_map/while
  130.6 1.4 fusion.83
  133.0 4.0 %collective-permute-start.2 = (bf16[1,4,24,384]{3,2,1,0:T(8,128)(2,1)S(1)}, bf16[1,4,24,384]{3,2,1,0:T(8,128)(2,1)S(1)}, u32[]{:S(2)}, u32[]{:S(2)}) collective-permute-start(bf16[1,4,24,384]{3,2,1,0:T(8,128)(2,1)S(1)} %get-tuple-element.378), channel_id=1, source_target_pairs={{0,8},{8,16},{16,24},{1,9},{9,17},{17,25},{2,10},{10,18},{18,26},{... | collective-permute-start | bytes 221192 | tf_op jit(solution)/shard_map/while/body/eval_jaxpr/ppermute | solution.py:23
  137.0 2.2 %collective-permute-start.3 = (bf16[1,4,24,384]{3,2,1,0:T(8,128)(2,1)S(1)}, bf16[1,4,24,384]{3,2,1,0:T(8,128)(2,1)S(1)}, u32[]{:S(2)}, u32[]{:S(2)}) collective-permute-start(bf16[1,4,24,384]{3,2,1,0:T(8,128)(2,1)S(1)} %get-tuple-element.379), channel_id=1, source_target_pairs={{0,8},{8,16},{16,24},{1,9},{9,17},{17,25},{2,10},{10,18},{18,26},{... | collective-permute-start | bytes 221192 | tf_op jit(solution)/shard_map/while/body/eval_jaxpr/ppermute | solution.py:23
  139.2 1.9 collective-permute-done.3
  143.6 5.2 %collective-permute-start.1 = (bf16[1,1,24,384]{3,2,1,0:T(8,128)(2,1)S(1)}, bf16[1,1,24,384]{3,2,1,0:T(8,128)(2,1)S(1)}, u32[]{:S(2)}, u32[]{:S(2)}) collective-permute-start(bf16[1,1,24,384]{3,2,1,0:T(8,128)(2,1)S(1)} %get-tuple-element.377), channel_id=1, source_target_pairs={{0,1},{1,2},{2,3},{3,4},{4,5},{5,6},{6,7},{8,9},{9,10},{10,11},{11... | collective-permute-start | bytes 55304 | tf_op jit(solution)/shard_map/while/body/eval_jaxpr/ppermute | solution.py:14
  150.7 2.4 %copy-done = bf16[1,3,3,3,384,384]{5,4,3,2,1,0:T(8,128)(2,1)S(1)} copy-done((bf16[1,3,3,3,384,384]{5,4,3,2,1,0:T(8,128)(2,1)S(1)}, bf16[1,3,3,3,384,384]{5,4,3,2,1,0:T(8,128)(2,1)}, u32[]{:S(2)}) %copy-start) | copy-done | bytes 7962648 | tf_op jit(solution)/shard_map/while
  153.1 1.4 fusion.83
  155.5 4.0 %collective-permute-start.2 = (bf16[1,4,24,384]{3,2,1,0:T(8,128)(2,1)S(1)}, bf16[1,4,24,384]{3,2,1,0:T(8,128)(2,1)S(1)}, u32[]{:S(2)}, u32[]{:S(2)}) collective-permute-start(bf16[1,4,24,384]{3,2,1,0:T(8,128)(2,1)S(1)} %get-tuple-element.378), channel_id=1, source_target_pairs={{0,8},{8,16},{16,24},{1,9},{9,17},{17,25},{2,10},{10,18},{18,26},{... | collective-permute-start | bytes 221192 | tf_op jit(solution)/shard_map/while/body/eval_jaxpr/ppermute | solution.py:23
  159.4 2.2 %collective-permute-start.3 = (bf16[1,4,24,384]{3,2,1,0:T(8,128)(2,1)S(1)}, bf16[1,4,24,384]{3,2,1,0:T(8,128)(2,1)S(1)}, u32[]{:S(2)}, u32[]{:S(2)}) collective-permute-start(bf16[1,4,24,384]{3,2,1,0:T(8,128)(2,1)S(1)} %get-tuple-element.379), channel_id=1, source_target_pairs={{0,8},{8,16},{16,24},{1,9},{9,17},{17,25},{2,10},{10,18},{18,26},{... | collective-permute-start | bytes 221192 | tf_op jit(solution)/shard_map/while/body/eval_jaxpr/ppermute | solution.py:23
  161.7 1.9 collective-permute-done.3
  164.4 28.5 %reduce-scatter.2.cloned.1.call-done = bf16[1,4,24,384]{3,2,1,0:T(8,128)(2,1)} async-done(((bf16[4,4,24,384]{3,2,1,0:T(8,128)(2,1)}), bf16[1,4,24,384]{3,2,1,0:T(8,128)(2,1)}) %reduce-scatter.2.cloned.1.call-update) | async-done | bytes 73744 | tf_op jit(solution)/shard_map/reduce_scatter | solution.py:103
  (285 shorter events, 31.9 us)
Async XLA Ops:
  6.5 186.4 %reduce-scatter.2.cloned.1.call-start = ((), (), s32[]{:S(2)}) async-start(), calls=%async_computation.1 | async-start | bytes 368640 | tf_op jit(solution)/shard_map/reduce_scatter | solution.py:103
  8.5 4.4 %collective-permute-start = (bf16[1,1,24,384]{3,2,1,0:T(8,128)(2,1)S(1)}, bf16[1,1,24,384]{3,2,1,0:T(8,128)(2,1)S(1)}, u32[]{:S(2)}, u32[]{:S(2)}) collective-permute-start(bf16[1,1,24,384]{3,2,1,0:T(8,128)(2,1)S(1)} %get-tuple-element.376), channel_id=1, source_target_pairs={{1,0},{2,1},{3,2},{4,3},{5,4},{6,5},{7,6},{9,8},{10,9},{11,10},{12... | collective-permute-start | bytes 55304 | tf_op jit(solution)/shard_map/while/body/eval_jaxpr/ppermute | solution.py:15
  9.8 3.9 %collective-permute-start.1 = (bf16[1,1,24,384]{3,2,1,0:T(8,128)(2,1)S(1)}, bf16[1,1,24,384]{3,2,1,0:T(8,128)(2,1)S(1)}, u32[]{:S(2)}, u32[]{:S(2)}) collective-permute-start(bf16[1,1,24,384]{3,2,1,0:T(8,128)(2,1)S(1)} %get-tuple-element.377), channel_id=1, source_target_pairs={{0,1},{1,2},{2,3},{3,4},{4,5},{5,6},{6,7},{8,9},{9,10},{10,11},{11... | collective-permute-start | bytes 55304 | tf_op jit(solution)/shard_map/while/body/eval_jaxpr/ppermute | solution.py:14
  13.8 3.3 %copy-start = (bf16[1,3,3,3,384,384]{5,4,3,2,1,0:T(8,128)(2,1)S(1)}, bf16[1,3,3,3,384,384]{5,4,3,2,1,0:T(8,128)(2,1)}, u32[]{:S(2)}) copy-start(bf16[1,3,3,3,384,384]{5,4,3,2,1,0:T(8,128)(2,1)} %get-tuple-element.422) | copy-start | bytes 23887876 | tf_op jit(solution)/shard_map/while
  19.4 8.5 %collective-permute-start.2 = (bf16[1,4,24,384]{3,2,1,0:T(8,128)(2,1)S(1)}, bf16[1,4,24,384]{3,2,1,0:T(8,128)(2,1)S(1)}, u32[]{:S(2)}, u32[]{:S(2)}) collective-permute-start(bf16[1,4,24,384]{3,2,1,0:T(8,128)(2,1)S(1)} %get-tuple-element.378), channel_id=1, source_target_pairs={{0,8},{8,16},{16,24},{1,9},{9,17},{17,25},{2,10},{10,18},{18,26},{... | collective-permute-start | bytes 221192 | tf_op jit(solution)/shard_map/while/body/eval_jaxpr/ppermute | solution.py:23
  24.4 6.0 %collective-permute-start.3 = (bf16[1,4,24,384]{3,2,1,0:T(8,128)(2,1)S(1)}, bf16[1,4,24,384]{3,2,1,0:T(8,128)(2,1)S(1)}, u32[]{:S(2)}, u32[]{:S(2)}) collective-permute-start(bf16[1,4,24,384]{3,2,1,0:T(8,128)(2,1)S(1)} %get-tuple-element.379), channel_id=1, source_target_pairs={{0,8},{8,16},{16,24},{1,9},{9,17},{17,25},{2,10},{10,18},{18,26},{... | collective-permute-start | bytes 221192 | tf_op jit(solution)/shard_map/while/body/eval_jaxpr/ppermute | solution.py:23
  31.6 4.4 %collective-permute-start = (bf16[1,1,24,384]{3,2,1,0:T(8,128)(2,1)S(1)}, bf16[1,1,24,384]{3,2,1,0:T(8,128)(2,1)S(1)}, u32[]{:S(2)}, u32[]{:S(2)}) collective-permute-start(bf16[1,1,24,384]{3,2,1,0:T(8,128)(2,1)S(1)} %get-tuple-element.376), channel_id=1, source_target_pairs={{1,0},{2,1},{3,2},{4,3},{5,4},{6,5},{7,6},{9,8},{10,9},{11,10},{12... | collective-permute-start | bytes 55304 | tf_op jit(solution)/shard_map/while/body/eval_jaxpr/ppermute | solution.py:15
  32.9 3.9 %collective-permute-start.1 = (bf16[1,1,24,384]{3,2,1,0:T(8,128)(2,1)S(1)}, bf16[1,1,24,384]{3,2,1,0:T(8,128)(2,1)S(1)}, u32[]{:S(2)}, u32[]{:S(2)}) collective-permute-start(bf16[1,1,24,384]{3,2,1,0:T(8,128)(2,1)S(1)} %get-tuple-element.377), channel_id=1, source_target_pairs={{0,1},{1,2},{2,3},{3,4},{4,5},{5,6},{6,7},{8,9},{9,10},{10,11},{11... | collective-permute-start | bytes 55304 | tf_op jit(solution)/shard_map/while/body/eval_jaxpr/ppermute | solution.py:14
  36.8 3.3 %copy-start = (bf16[1,3,3,3,384,384]{5,4,3,2,1,0:T(8,128)(2,1)S(1)}, bf16[1,3,3,3,384,384]{5,4,3,2,1,0:T(8,128)(2,1)}, u32[]{:S(2)}) copy-start(bf16[1,3,3,3,384,384]{5,4,3,2,1,0:T(8,128)(2,1)} %get-tuple-element.422) | copy-start | bytes 23887876 | tf_op jit(solution)/shard_map/while
  42.5 7.9 %collective-permute-start.2 = (bf16[1,4,24,384]{3,2,1,0:T(8,128)(2,1)S(1)}, bf16[1,4,24,384]{3,2,1,0:T(8,128)(2,1)S(1)}, u32[]{:S(2)}, u32[]{:S(2)}) collective-permute-start(bf16[1,4,24,384]{3,2,1,0:T(8,128)(2,1)S(1)} %get-tuple-element.378), channel_id=1, source_target_pairs={{0,8},{8,16},{16,24},{1,9},{9,17},{17,25},{2,10},{10,18},{18,26},{... | collective-permute-start | bytes 221192 | tf_op jit(solution)/shard_map/while/body/eval_jaxpr/ppermute | solution.py:23
  46.9 5.5 %collective-permute-start.3 = (bf16[1,4,24,384]{3,2,1,0:T(8,128)(2,1)S(1)}, bf16[1,4,24,384]{3,2,1,0:T(8,128)(2,1)S(1)}, u32[]{:S(2)}, u32[]{:S(2)}) collective-permute-start(bf16[1,4,24,384]{3,2,1,0:T(8,128)(2,1)S(1)} %get-tuple-element.379), channel_id=1, source_target_pairs={{0,8},{8,16},{16,24},{1,9},{9,17},{17,25},{2,10},{10,18},{18,26},{... | collective-permute-start | bytes 221192 | tf_op jit(solution)/shard_map/while/body/eval_jaxpr/ppermute | solution.py:23
  53.5 5.0 %collective-permute-start = (bf16[1,1,24,384]{3,2,1,0:T(8,128)(2,1)S(1)}, bf16[1,1,24,384]{3,2,1,0:T(8,128)(2,1)S(1)}, u32[]{:S(2)}, u32[]{:S(2)}) collective-permute-start(bf16[1,1,24,384]{3,2,1,0:T(8,128)(2,1)S(1)} %get-tuple-element.376), channel_id=1, source_target_pairs={{1,0},{2,1},{3,2},{4,3},{5,4},{6,5},{7,6},{9,8},{10,9},{11,10},{12... | collective-permute-start | bytes 55304 | tf_op jit(solution)/shard_map/while/body/eval_jaxpr/ppermute | solution.py:15
  54.8 4.5 %collective-permute-start.1 = (bf16[1,1,24,384]{3,2,1,0:T(8,128)(2,1)S(1)}, bf16[1,1,24,384]{3,2,1,0:T(8,128)(2,1)S(1)}, u32[]{:S(2)}, u32[]{:S(2)}) collective-permute-start(bf16[1,1,24,384]{3,2,1,0:T(8,128)(2,1)S(1)} %get-tuple-element.377), channel_id=1, source_target_pairs={{0,1},{1,2},{2,3},{3,4},{4,5},{5,6},{6,7},{8,9},{9,10},{10,11},{11... | collective-permute-start | bytes 55304 | tf_op jit(solution)/shard_map/while/body/eval_jaxpr/ppermute | solution.py:14
  59.5 3.3 %copy-start = (bf16[1,3,3,3,384,384]{5,4,3,2,1,0:T(8,128)(2,1)S(1)}, bf16[1,3,3,3,384,384]{5,4,3,2,1,0:T(8,128)(2,1)}, u32[]{:S(2)}) copy-start(bf16[1,3,3,3,384,384]{5,4,3,2,1,0:T(8,128)(2,1)} %get-tuple-element.422) | copy-start | bytes 23887876 | tf_op jit(solution)/shard_map/while
  65.1 6.2 %collective-permute-start.2 = (bf16[1,4,24,384]{3,2,1,0:T(8,128)(2,1)S(1)}, bf16[1,4,24,384]{3,2,1,0:T(8,128)(2,1)S(1)}, u32[]{:S(2)}, u32[]{:S(2)}) collective-permute-start(bf16[1,4,24,384]{3,2,1,0:T(8,128)(2,1)S(1)} %get-tuple-element.378), channel_id=1, source_target_pairs={{0,8},{8,16},{16,24},{1,9},{9,17},{17,25},{2,10},{10,18},{18,26},{... | collective-permute-start | bytes 221192 | tf_op jit(solution)/shard_map/while/body/eval_jaxpr/ppermute | solution.py:23
  69.1 4.2 %collective-permute-start.3 = (bf16[1,4,24,384]{3,2,1,0:T(8,128)(2,1)S(1)}, bf16[1,4,24,384]{3,2,1,0:T(8,128)(2,1)S(1)}, u32[]{:S(2)}, u32[]{:S(2)}) collective-permute-start(bf16[1,4,24,384]{3,2,1,0:T(8,128)(2,1)S(1)} %get-tuple-element.379), channel_id=1, source_target_pairs={{0,8},{8,16},{16,24},{1,9},{9,17},{17,25},{2,10},{10,18},{18,26},{... | collective-permute-start | bytes 221192 | tf_op jit(solution)/shard_map/while/body/eval_jaxpr/ppermute | solution.py:23
  74.4 7.1 %collective-permute-start = (bf16[1,1,24,384]{3,2,1,0:T(8,128)(2,1)S(1)}, bf16[1,1,24,384]{3,2,1,0:T(8,128)(2,1)S(1)}, u32[]{:S(2)}, u32[]{:S(2)}) collective-permute-start(bf16[1,1,24,384]{3,2,1,0:T(8,128)(2,1)S(1)} %get-tuple-element.376), channel_id=1, source_target_pairs={{1,0},{2,1},{3,2},{4,3},{5,4},{6,5},{7,6},{9,8},{10,9},{11,10},{12... | collective-permute-start | bytes 55304 | tf_op jit(solution)/shard_map/while/body/eval_jaxpr/ppermute | solution.py:15
  75.7 6.6 %collective-permute-start.1 = (bf16[1,1,24,384]{3,2,1,0:T(8,128)(2,1)S(1)}, bf16[1,1,24,384]{3,2,1,0:T(8,128)(2,1)S(1)}, u32[]{:S(2)}, u32[]{:S(2)}) collective-permute-start(bf16[1,1,24,384]{3,2,1,0:T(8,128)(2,1)S(1)} %get-tuple-element.377), channel_id=1, source_target_pairs={{0,1},{1,2},{2,3},{3,4},{4,5},{5,6},{6,7},{8,9},{9,10},{10,11},{11... | collective-permute-start | bytes 55304 | tf_op jit(solution)/shard_map/while/body/eval_jaxpr/ppermute | solution.py:14
  82.4 3.3 %copy-start = (bf16[1,3,3,3,384,384]{5,4,3,2,1,0:T(8,128)(2,1)S(1)}, bf16[1,3,3,3,384,384]{5,4,3,2,1,0:T(8,128)(2,1)}, u32[]{:S(2)}) copy-start(bf16[1,3,3,3,384,384]{5,4,3,2,1,0:T(8,128)(2,1)} %get-tuple-element.422) | copy-start | bytes 23887876 | tf_op jit(solution)/shard_map/while
  88.1 6.2 %collective-permute-start.2 = (bf16[1,4,24,384]{3,2,1,0:T(8,128)(2,1)S(1)}, bf16[1,4,24,384]{3,2,1,0:T(8,128)(2,1)S(1)}, u32[]{:S(2)}, u32[]{:S(2)}) collective-permute-start(bf16[1,4,24,384]{3,2,1,0:T(8,128)(2,1)S(1)} %get-tuple-element.378), channel_id=1, source_target_pairs={{0,8},{8,16},{16,24},{1,9},{9,17},{17,25},{2,10},{10,18},{18,26},{... | collective-permute-start | bytes 221192 | tf_op jit(solution)/shard_map/while/body/eval_jaxpr/ppermute | solution.py:23
  92.1 4.2 %collective-permute-start.3 = (bf16[1,4,24,384]{3,2,1,0:T(8,128)(2,1)S(1)}, bf16[1,4,24,384]{3,2,1,0:T(8,128)(2,1)S(1)}, u32[]{:S(2)}, u32[]{:S(2)}) collective-permute-start(bf16[1,4,24,384]{3,2,1,0:T(8,128)(2,1)S(1)} %get-tuple-element.379), channel_id=1, source_target_pairs={{0,8},{8,16},{16,24},{1,9},{9,17},{17,25},{2,10},{10,18},{18,26},{... | collective-permute-start | bytes 221192 | tf_op jit(solution)/shard_map/while/body/eval_jaxpr/ppermute | solution.py:23
  97.4 6.8 %collective-permute-start = (bf16[1,1,24,384]{3,2,1,0:T(8,128)(2,1)S(1)}, bf16[1,1,24,384]{3,2,1,0:T(8,128)(2,1)S(1)}, u32[]{:S(2)}, u32[]{:S(2)}) collective-permute-start(bf16[1,1,24,384]{3,2,1,0:T(8,128)(2,1)S(1)} %get-tuple-element.376), channel_id=1, source_target_pairs={{1,0},{2,1},{3,2},{4,3},{5,4},{6,5},{7,6},{9,8},{10,9},{11,10},{12... | collective-permute-start | bytes 55304 | tf_op jit(solution)/shard_map/while/body/eval_jaxpr/ppermute | solution.py:15
  98.7 6.3 %collective-permute-start.1 = (bf16[1,1,24,384]{3,2,1,0:T(8,128)(2,1)S(1)}, bf16[1,1,24,384]{3,2,1,0:T(8,128)(2,1)S(1)}, u32[]{:S(2)}, u32[]{:S(2)}) collective-permute-start(bf16[1,1,24,384]{3,2,1,0:T(8,128)(2,1)S(1)} %get-tuple-element.377), channel_id=1, source_target_pairs={{0,1},{1,2},{2,3},{3,4},{4,5},{5,6},{6,7},{8,9},{9,10},{10,11},{11... | collective-permute-start | bytes 55304 | tf_op jit(solution)/shard_map/while/body/eval_jaxpr/ppermute | solution.py:14
  105.1 3.3 %copy-start = (bf16[1,3,3,3,384,384]{5,4,3,2,1,0:T(8,128)(2,1)S(1)}, bf16[1,3,3,3,384,384]{5,4,3,2,1,0:T(8,128)(2,1)}, u32[]{:S(2)}) copy-start(bf16[1,3,3,3,384,384]{5,4,3,2,1,0:T(8,128)(2,1)} %get-tuple-element.422) | copy-start | bytes 23887876 | tf_op jit(solution)/shard_map/while
  110.8 6.2 %collective-permute-start.2 = (bf16[1,4,24,384]{3,2,1,0:T(8,128)(2,1)S(1)}, bf16[1,4,24,384]{3,2,1,0:T(8,128)(2,1)S(1)}, u32[]{:S(2)}, u32[]{:S(2)}) collective-permute-start(bf16[1,4,24,384]{3,2,1,0:T(8,128)(2,1)S(1)} %get-tuple-element.378), channel_id=1, source_target_pairs={{0,8},{8,16},{16,24},{1,9},{9,17},{17,25},{2,10},{10,18},{18,26},{... | collective-permute-start | bytes 221192 | tf_op jit(solution)/shard_map/while/body/eval_jaxpr/ppermute | solution.py:23
  114.8 4.5 %collective-permute-start.3 = (bf16[1,4,24,384]{3,2,1,0:T(8,128)(2,1)S(1)}, bf16[1,4,24,384]{3,2,1,0:T(8,128)(2,1)S(1)}, u32[]{:S(2)}, u32[]{:S(2)}) collective-permute-start(bf16[1,4,24,384]{3,2,1,0:T(8,128)(2,1)S(1)} %get-tuple-element.379), channel_id=1, source_target_pairs={{0,8},{8,16},{16,24},{1,9},{9,17},{17,25},{2,10},{10,18},{18,26},{... | collective-permute-start | bytes 221192 | tf_op jit(solution)/shard_map/while/body/eval_jaxpr/ppermute | solution.py:23
  120.4 6.0 %collective-permute-start = (bf16[1,1,24,384]{3,2,1,0:T(8,128)(2,1)S(1)}, bf16[1,1,24,384]{3,2,1,0:T(8,128)(2,1)S(1)}, u32[]{:S(2)}, u32[]{:S(2)}) collective-permute-start(bf16[1,1,24,384]{3,2,1,0:T(8,128)(2,1)S(1)} %get-tuple-element.376), channel_id=1, source_target_pairs={{1,0},{2,1},{3,2},{4,3},{5,4},{6,5},{7,6},{9,8},{10,9},{11,10},{12... | collective-permute-start | bytes 55304 | tf_op jit(solution)/shard_map/while/body/eval_jaxpr/ppermute | solution.py:15
  121.7 5.5 %collective-permute-start.1 = (bf16[1,1,24,384]{3,2,1,0:T(8,128)(2,1)S(1)}, bf16[1,1,24,384]{3,2,1,0:T(8,128)(2,1)S(1)}, u32[]{:S(2)}, u32[]{:S(2)}) collective-permute-start(bf16[1,1,24,384]{3,2,1,0:T(8,128)(2,1)S(1)} %get-tuple-element.377), channel_id=1, source_target_pairs={{0,1},{1,2},{2,3},{3,4},{4,5},{5,6},{6,7},{8,9},{9,10},{10,11},{11... | collective-permute-start | bytes 55304 | tf_op jit(solution)/shard_map/while/body/eval_jaxpr/ppermute | solution.py:14
  127.3 3.3 %copy-start = (bf16[1,3,3,3,384,384]{5,4,3,2,1,0:T(8,128)(2,1)S(1)}, bf16[1,3,3,3,384,384]{5,4,3,2,1,0:T(8,128)(2,1)}, u32[]{:S(2)}) copy-start(bf16[1,3,3,3,384,384]{5,4,3,2,1,0:T(8,128)(2,1)} %get-tuple-element.422) | copy-start | bytes 23887876 | tf_op jit(solution)/shard_map/while
  133.0 6.2 %collective-permute-start.2 = (bf16[1,4,24,384]{3,2,1,0:T(8,128)(2,1)S(1)}, bf16[1,4,24,384]{3,2,1,0:T(8,128)(2,1)S(1)}, u32[]{:S(2)}, u32[]{:S(2)}) collective-permute-start(bf16[1,4,24,384]{3,2,1,0:T(8,128)(2,1)S(1)} %get-tuple-element.378), channel_id=1, source_target_pairs={{0,8},{8,16},{16,24},{1,9},{9,17},{17,25},{2,10},{10,18},{18,26},{... | collective-permute-start | bytes 221192 | tf_op jit(solution)/shard_map/while/body/eval_jaxpr/ppermute | solution.py:23
  137.0 4.2 %collective-permute-start.3 = (bf16[1,4,24,384]{3,2,1,0:T(8,128)(2,1)S(1)}, bf16[1,4,24,384]{3,2,1,0:T(8,128)(2,1)S(1)}, u32[]{:S(2)}, u32[]{:S(2)}) collective-permute-start(bf16[1,4,24,384]{3,2,1,0:T(8,128)(2,1)S(1)} %get-tuple-element.379), channel_id=1, source_target_pairs={{0,8},{8,16},{16,24},{1,9},{9,17},{17,25},{2,10},{10,18},{18,26},{... | collective-permute-start | bytes 221192 | tf_op jit(solution)/shard_map/while/body/eval_jaxpr/ppermute | solution.py:23
  142.3 6.6 %collective-permute-start = (bf16[1,1,24,384]{3,2,1,0:T(8,128)(2,1)S(1)}, bf16[1,1,24,384]{3,2,1,0:T(8,128)(2,1)S(1)}, u32[]{:S(2)}, u32[]{:S(2)}) collective-permute-start(bf16[1,1,24,384]{3,2,1,0:T(8,128)(2,1)S(1)} %get-tuple-element.376), channel_id=1, source_target_pairs={{1,0},{2,1},{3,2},{4,3},{5,4},{6,5},{7,6},{9,8},{10,9},{11,10},{12... | collective-permute-start | bytes 55304 | tf_op jit(solution)/shard_map/while/body/eval_jaxpr/ppermute | solution.py:15
  143.6 6.1 %collective-permute-start.1 = (bf16[1,1,24,384]{3,2,1,0:T(8,128)(2,1)S(1)}, bf16[1,1,24,384]{3,2,1,0:T(8,128)(2,1)S(1)}, u32[]{:S(2)}, u32[]{:S(2)}) collective-permute-start(bf16[1,1,24,384]{3,2,1,0:T(8,128)(2,1)S(1)} %get-tuple-element.377), channel_id=1, source_target_pairs={{0,1},{1,2},{2,3},{3,4},{4,5},{5,6},{6,7},{8,9},{9,10},{10,11},{11... | collective-permute-start | bytes 55304 | tf_op jit(solution)/shard_map/while/body/eval_jaxpr/ppermute | solution.py:14
  149.8 3.3 %copy-start = (bf16[1,3,3,3,384,384]{5,4,3,2,1,0:T(8,128)(2,1)S(1)}, bf16[1,3,3,3,384,384]{5,4,3,2,1,0:T(8,128)(2,1)}, u32[]{:S(2)}) copy-start(bf16[1,3,3,3,384,384]{5,4,3,2,1,0:T(8,128)(2,1)} %get-tuple-element.422) | copy-start | bytes 23887876 | tf_op jit(solution)/shard_map/while
  155.5 6.2 %collective-permute-start.2 = (bf16[1,4,24,384]{3,2,1,0:T(8,128)(2,1)S(1)}, bf16[1,4,24,384]{3,2,1,0:T(8,128)(2,1)S(1)}, u32[]{:S(2)}, u32[]{:S(2)}) collective-permute-start(bf16[1,4,24,384]{3,2,1,0:T(8,128)(2,1)S(1)} %get-tuple-element.378), channel_id=1, source_target_pairs={{0,8},{8,16},{16,24},{1,9},{9,17},{17,25},{2,10},{10,18},{18,26},{... | collective-permute-start | bytes 221192 | tf_op jit(solution)/shard_map/while/body/eval_jaxpr/ppermute | solution.py:23
  159.4 4.2 %collective-permute-start.3 = (bf16[1,4,24,384]{3,2,1,0:T(8,128)(2,1)S(1)}, bf16[1,4,24,384]{3,2,1,0:T(8,128)(2,1)S(1)}, u32[]{:S(2)}, u32[]{:S(2)}) collective-permute-start(bf16[1,4,24,384]{3,2,1,0:T(8,128)(2,1)S(1)} %get-tuple-element.379), channel_id=1, source_target_pairs={{0,8},{8,16},{16,24},{1,9},{9,17},{17,25},{2,10},{10,18},{18,26},{... | collective-permute-start | bytes 221192 | tf_op jit(solution)/shard_map/while/body/eval_jaxpr/ppermute | solution.py:23
  163.6 0.7 copy-start.1
Sparse Core Ops, SparseCore 0:
  164.5 28.3 reduce-scatter.1
where the time goes:
time: 201 us; the launch traced here: 200 us
  starting transfers between devices  87.2 us (43%)
  waiting for transfers between devices  48.6 us (24%)
  local copies, waits for them, and re-layouts  22.1 us (11%)
  other arithmetic  16.9 us (8%)
  between operations  13.4 us (7%)
  matrix products  9.87 us (5%)
    ppermute x14, starting transfers between devices, passed_along(): lax.ppermute(value, axis, [(source, source + steps) for source in range(f...  47.2 us
    ppermute x7, starting transfers between devices, with_halo(): before = lax.ppermute(last, axis, up)  30.9 us
    reduce_scatter x1, waiting for transfers between devices, local(): lax.psum_scatter(finished[3].astype(jnp.float32).astype(jnp.bfloat16), 's...  28.5 us
    while x175, local copies, waits for them, and re-layouts  20.9 us
    ppermute x14, waiting for transfers between devices, passed_along(): lax.ppermute(value, axis, [(source, source + steps) for source in range(f...  14.4 us
    dot_general x7, matrix products, causal_block(): jnp.dot(stacked, kernel.reshape(27 * channels, channels), preferred_eleme...  9.87 us
    ppermute x7, starting transfers between devices, with_halo(): after = lax.ppermute(first, axis, down)  9.04 us
    reduce_sum x7, other arithmetic, activate(): mean_square = jnp.mean(widened * widened, axis=-1, keepdims=True)  6.96 us
  transfers between devices with their start and end apart: 29, of which 15 were waited for; matrix products, arithmetic and copies ran while one was open for 0% of the time, Pallas kernels for 0%

commit v1 on v0

v1 whole, which is shorter than its diff:
```python
import jax
import jax.numpy as jnp
from jax import lax
from jax.sharding import PartitionSpec as P

BOTH = ("segment", "rows")


def activate(values_in, gain_row):
    widened = values_in.astype(jnp.float32)
    mean_square = jnp.mean(widened * widened, axis=-1, keepdims=True)
    return jax.nn.silu(
        widened * lax.rsqrt(mean_square + 1e-06) * gain_row.astype(jnp.float32)
    ).astype(jnp.bfloat16)


def causal_conv(window, kernel):
    result = lax.conv_general_dilated(
        window[None],
        kernel,
        window_strides=(1, 1, 1),
        padding=((2, 0), (0, 0), (1, 1)),
        dimension_numbers=("NDHWC", "DHWIO", "NDHWC"),
        preferred_element_type=jnp.float32,
    )
    return result[0]


def send(value, pairs):
    return lax.ppermute(value, BOTH, pairs)


def stage_send(value, stage, row_count):
    base, nxt = stage * row_count, (stage + 1) * row_count
    height = value.shape[1]
    body = send(value, [(base + r, nxt + r) for r in range(row_count)])
    top = send(
        value[:, height - 1 :],
        [(base + r, nxt + r + 1) for r in range(row_count - 1)],
    )
    bottom = send(value[:, :1], [(base + r, nxt + r - 1) for r in range(1, row_count)])
    return body, top, bottom


def local(features, gains, kernels):
    segment_count = lax.axis_size("segment")
    row_count = lax.axis_size("rows")
    segment_index = lax.axis_index("segment")
    frame_count, height, columns, channels = features.shape
    gain_row = gains[0]
    kernel = kernels[0]

    up = [(i, i + 1) for i in range(row_count - 1)]
    down = [(i + 1, i) for i in range(row_count - 1)]
    top = lax.ppermute(features[:, height - 1 :], "rows", up)
    bottom = lax.ppermute(features[:, :1], "rows", down)
    current = features
    skip = features

    for stage in range(segment_count):
        window = jnp.concatenate([top, current, bottom], axis=1)
        convolved = causal_conv(activate(window, gain_row), kernel)
        if stage % 2 == 0:
            produced = convolved.astype(jnp.bfloat16)
            next_skip = current
        else:
            produced = (skip.astype(jnp.float32) + convolved).astype(jnp.bfloat16)
            next_skip = None
        if stage == segment_count - 1:
            decoded = produced
            break
        current, top, bottom = stage_send(produced, stage, row_count)
        if next_skip is not None:
            base, nxt = stage * row_count, (stage + 1) * row_count
            skip = send(next_skip, [(base + r, nxt + r) for r in range(row_count)])

    group = frame_count // segment_count
    last = (segment_count - 1) * row_count
    delivered = decoded[(segment_count - 1) * group :]
    for target in range(segment_count - 1):
        piece = send(
            decoded[target * group : (target + 1) * group],
            [(last + r, target * row_count + r) for r in range(row_count)],
        )
        delivered = jnp.where(segment_index == target, piece, delivered)
    return delivered


def solution(mesh):
    placed = (
        P(None, "rows", None, None),
        P("segment", None),
        P("segment", None, None, None, None, None),
    )
    return jax.shard_map(
        local,
        mesh=mesh,
        in_specs=placed,
        out_specs=P("segment", "rows", None, None),
        check_vma=False,
    )
```

time: 201 us -> 119 us (0.59)
  the two profiles are of different devices: /device:TPU:0 before, /device:TPU:1 now
where the time goes in v1:
time: 119 us; the launch traced here: 118 us
  waiting for transfers between devices  44.7 us (38%)
  matrix products  36.9 us (31%)
  starting transfers between devices  21.1 us (18%)
  local copies, waits for them, and re-layouts  7.88 us (7%)
  other arithmetic  7.32 us (6%)
    ppermute x14, waiting for transfers between devices, send(): return lax.ppermute(value, BOTH, pairs)  42.8 us
    conv_general_dilated x4, matrix products, causal_conv(): lax.conv_general_dilated(window[None], kernel, window_strides=(1, 1, 1),...  36.9 us
    ppermute x14, starting transfers between devices, send(): return lax.ppermute(value, BOTH, pairs)  14.6 us
    ppermute x1, starting transfers between devices, local(): top = lax.ppermute(features[:, height - 1:], 'rows', up)  4.51 us
    convert_element_type x4, other arithmetic, activate(): return jax.nn.silu(widened * lax.rsqrt(mean_square + 1e-06) * gain_row.as...  3.13 us
    reduce_sum x4, other arithmetic, activate(): mean_square = jnp.mean(widened * widened, axis=-1, keepdims=True)  3.05 us
  transfers between devices with their start and end apart: 16, of which 4 were waited for; matrix products, arithmetic and copies ran while one was open for 24% of the time, Pallas kernels for 0%

profile of v1, /device:TPU:1, one launch (start us, length us, event | category | flops | bytes accessed | tf_op | source)
XLA Modules:
  0.0 118.5 jit_solution(2389808665768410708)
XLA Ops:
  0.0 0.9 slice_bitcast_fusion.5
  0.9 4.5 %collective-permute-start.1 = (bf16[4,1,24,384]{3,2,0,1:T(8,128)(2,1)S(1)}, bf16[4,1,24,384]{3,2,0,1:T(8,128)(2,1)S(1)}, u32[]{:S(2)}, u32[]{:S(2)}) collective-permute-start(bf16[4,1,24,384]{3,2,0,1:T(8,128)(2,1)S(1)} %get-tuple-element.16), channel_id=1, source_target_pairs={{0,1},{1,2},{2,3},{3,4},{4,5},{5,6},{6,7},{8,9},{9,10},{10,11},{11... | collective-permute-start | bytes 221192 | tf_op jit(solution)/shard_map/ppermute | solution.py:55
  5.5 1.9 %collective-permute-start.2 = (bf16[4,1,24,384]{3,2,0,1:T(8,128)(2,1)S(1)}, bf16[4,1,24,384]{3,2,0,1:T(8,128)(2,1)S(1)}, u32[]{:S(2)}, u32[]{:S(2)}) collective-permute-start(bf16[4,1,24,384]{3,2,0,1:T(8,128)(2,1)S(1)} %get-tuple-element.17), channel_id=1, source_target_pairs={{1,0},{2,1},{3,2},{4,3},{5,4},{6,5},{7,6},{9,8},{10,9},{11,10},{12... | collective-permute-start | bytes 221192 | tf_op jit(solution)/shard_map/ppermute | solution.py:56
  7.4 1.1 copy.193
  8.5 0.7 convert_reduce_fusion
  9.2 2.0 %collective-permute-done.2 = bf16[4,1,24,384]{3,2,0,1:T(8,128)(2,1)S(1)} collective-permute-done((bf16[4,1,24,384]{3,2,0,1:T(8,128)(2,1)S(1)}, bf16[4,1,24,384]{3,2,0,1:T(8,128)(2,1)S(1)}, u32[]{:S(2)}, u32[]{:S(2)}) %collective-permute-start.2) | collective-permute-done | bytes 73760 | tf_op jit(solution)/shard_map/ppermute | solution.py:56
  11.1 1.1 multiply_reduce_fusion.3
  12.6 0.8 fusion.54
  13.5 0.2 copy.154
  13.8 0.4 copy-done
  14.2 7.9 %fusion.27 = bf16[4,4,8,4,384]{4,2,3,1,0:T(8,128)(2,1)S(1)} fusion(bf16[1,3,3,3,384,384]{5,4,3,2,1,0:T(8,128)(2,1)} %param.5, bf16[4,6,1,7,2,384]{5,3,4,1,0,2:T(8,128)(2,1)S(1)} %slice.56, bf16[4,6,1,8,4,384]{5,3,4,1,0,2:T(8,128)(2,1)S(1)} %copy.154, pred[8,4]{0,1:T(4,128)(4,1)S(1)} %copy-done), kind=kOutput, calls=%fused_computation.18 | convolution fusion | flops 3060695040 | bytes 9203744 | tf_op jit(solution)/shard_map/conv_general_dilated | solution.py:18
  22.1 0.2 copy.155
  22.4 3.2 %collective-permute-start.4 = (bf16[4,4,24,384]{3,1,2,0:T(4,128)(2,1)S(1)}, bf16[4,4,24,384]{3,1,2,0:T(4,128)(2,1)S(1)}, u32[]{:S(2)}, u32[]{:S(2)}) collective-permute-start(bf16[4,4,24,384]{3,1,2,0:T(4,128)(2,1)S(1)} %slice_bitcast_fusion.3), channel_id=1, source_target_pairs={{0,8},{1,9},{2,10},{3,11},{4,12},{5,13},{6,14},{7,15}} | collective-permute-start | bytes 884744 | tf_op jit(solution)/shard_map/ppermute | solution.py:30
  25.7 0.2 fusion.84
  25.9 1.3 %collective-permute-start.3 = (bf16[4,1,24,384]{3,1,2,0:T(2,128)(2,1)S(1)}, bf16[4,1,24,384]{3,1,2,0:T(2,128)(2,1)S(1)}, u32[]{:S(2)}, u32[]{:S(2)}) collective-permute-start(bf16[4,1,24,384]{3,1,2,0:T(2,128)(2,1)S(1)} %get-tuple-element.14), channel_id=1, source_target_pairs={{0,9},{1,10},{2,11},{3,12},{4,13},{5,14},{6,15}} | collective-permute-start | bytes 221192 | tf_op jit(solution)/shard_map/ppermute | solution.py:30
  27.2 1.3 %collective-permute-start.5 = (bf16[4,1,24,384]{3,1,2,0:T(2,128)(2,1)S(1)}, bf16[4,1,24,384]{3,1,2,0:T(2,128)(2,1)S(1)}, u32[]{:S(2)}, u32[]{:S(2)}) collective-permute-start(bf16[4,1,24,384]{3,1,2,0:T(2,128)(2,1)S(1)} %get-tuple-element.15), channel_id=1, source_target_pairs={{1,8},{2,9},{3,10},{4,11},{5,12},{6,13},{7,14}} | collective-permute-start | bytes 221192 | tf_op jit(solution)/shard_map/ppermute | solution.py:30
  28.5 1.3 %collective-permute-start = (bf16[4,4,24,384]{3,1,2,0:T(4,128)(2,1)S(1)}, bf16[4,4,24,384]{3,1,2,0:T(4,128)(2,1)S(1)}, u32[]{:S(2)}, u32[]{:S(2)}) collective-permute-start(bf16[4,4,24,384]{3,1,2,0:T(4,128)(2,1)S(1)} %copy.193), channel_id=1, source_target_pairs={{0,8},{1,9},{2,10},{3,11},{4,12},{5,13},{6,14},{7,15}} | collective-permute-start | bytes 884744 | tf_op jit(solution)/shard_map/ppermute | solution.py:30
  29.8 5.9 %collective-permute-done.3 = bf16[4,1,24,384]{3,1,2,0:T(2,128)(2,1)S(1)} collective-permute-done((bf16[4,1,24,384]{3,1,2,0:T(2,128)(2,1)S(1)}, bf16[4,1,24,384]{3,1,2,0:T(2,128)(2,1)S(1)}, u32[]{:S(2)}, u32[]{:S(2)}) %collective-permute-start.3) | collective-permute-done | bytes 73760 | tf_op jit(solution)/shard_map/ppermute | solution.py:30
  35.7 2.6 %collective-permute-done.5 = bf16[4,1,24,384]{3,1,2,0:T(2,128)(2,1)S(1)} collective-permute-done((bf16[4,1,24,384]{3,1,2,0:T(2,128)(2,1)S(1)}, bf16[4,1,24,384]{3,1,2,0:T(2,128)(2,1)S(1)}, u32[]{:S(2)}, u32[]{:S(2)}) %collective-permute-start.5) | collective-permute-done | bytes 73760 | tf_op jit(solution)/shard_map/ppermute | solution.py:30
  38.3 0.6 multiply_reduce_fusion.2
  39.2 0.8 fusion.55
  40.1 0.2 copy.162
  40.4 10.6 %fusion.15 = f32[4,4,8,4,384]{4,2,3,1,0:T(8,128)S(1)} fusion(bf16[1,3,3,3,384,384]{5,4,3,2,1,0:T(8,128)(2,1)} %param.5, bf16[4,6,1,7,2,384]{5,3,4,1,0,2:T(8,128)(2,1)S(1)} %slice.60, bf16[4,6,1,8,4,384]{5,3,4,1,0,2:T(8,128)(2,1)S(1)} %copy.162, pred[8,4]{0,1:T(4,128)(4,1)S(1)} %copy-done), kind=kOutput, calls=%fused_computation.14 | convolution fusion | flops 3060498432 | bytes 9596960 | tf_op jit(solution)/shard_map/conv_general_dilated | solution.py:18
  50.9 0.5 copy.163
  51.6 0.7 collective-permute-start.6
  52.3 0.2 fusion.82
  52.5 0.7 collective-permute-start.8
  53.2 0.9 collective-permute-start.9
  54.1 0.6 multiply_reduce_fusion.1
  55.0 0.8 fusion.56
  55.9 0.2 copy.170
  56.2 7.9 %fusion.24 = bf16[4,4,8,4,384]{4,2,3,1,0:T(8,128)(2,1)S(1)} fusion(bf16[1,3,3,3,384,384]{5,4,3,2,1,0:T(8,128)(2,1)} %param.5, bf16[4,6,1,7,2,384]{5,3,4,1,0,2:T(8,128)(2,1)S(1)} %slice.64, bf16[4,6,1,8,4,384]{5,3,4,1,0,2:T(8,128)(2,1)S(1)} %copy.170, pred[8,4]{0,1:T(4,128)(4,1)S(1)} %copy-done), kind=kOutput, calls=%fused_computation.17 | convolution fusion | flops 3060695040 | bytes 9203744 | tf_op jit(solution)/shard_map/conv_general_dilated | solution.py:18
  64.1 0.2 copy.171
  64.4 0.7 collective-permute-start.11
  65.1 0.2 fusion.81
  65.3 0.7 collective-permute-start.10
  66.0 0.7 collective-permute-start.12
  66.7 0.7 collective-permute-start.7
  67.4 0.6 multiply_reduce_fusion
  68.3 0.8 fusion.57
  69.2 0.2 copy.178
  69.5 10.6 %fusion.21 = f32[4,4,8,4,384]{4,2,3,1,0:T(8,128)S(1)} fusion(bf16[1,3,3,3,384,384]{5,4,3,2,1,0:T(8,128)(2,1)} %param.5, bf16[4,6,1,7,2,384]{5,3,4,1,0,2:T(8,128)(2,1)S(1)} %slice.68, bf16[4,6,1,8,4,384]{5,3,4,1,0,2:T(8,128)(2,1)S(1)} %copy.178, pred[8,4]{0,1:T(4,128)(4,1)S(1)} %copy-done), kind=kOutput, calls=%fused_computation.16 | convolution fusion | flops 3060498432 | bytes 9596960 | tf_op jit(solution)/shard_map/conv_general_dilated | solution.py:18
  80.0 0.5 copy.179
  80.8 0.7 collective-permute-start.13
  81.5 0.7 collective-permute-start.14
  82.1 1.3 %collective-permute-start.15 = (bf16[1,4,24,384]{3,1,2,0:T(4,128)(2,1)S(1)}, bf16[1,4,24,384]{3,1,2,0:T(4,128)(2,1)S(1)}, u32[]{:S(2)}, u32[]{:S(2)}) collective-permute-start(bf16[1,4,24,384]{3,1,2,0:T(4,128)(2,1)S(1)} %get-tuple-element.5), channel_id=1, source_target_pairs={{24,0},{25,1},{26,2},{27,3},{28,4},{29,5},{30,6},{31,7}} | collective-permute-start | bytes 221192 | tf_op jit(solution)/shard_map/ppermute | solution.py:30
  83.5 34.2 %collective-permute-done.15 = bf16[1,4,24,384]{3,1,2,0:T(4,128)(2,1)S(1)} collective-permute-done((bf16[1,4,24,384]{3,1,2,0:T(4,128)(2,1)S(1)}, bf16[1,4,24,384]{3,1,2,0:T(4,128)(2,1)S(1)}, u32[]{:S(2)}, u32[]{:S(2)}) %collective-permute-start.15) | collective-permute-done | bytes 73760 | tf_op jit(solution)/shard_map/ppermute | solution.py:30
  117.8 0.6 copy.180
  (40 shorter events, 2.5 us)
Async XLA Ops:
  0.9 8.2 %collective-permute-start.1 = (bf16[4,1,24,384]{3,2,0,1:T(8,128)(2,1)S(1)}, bf16[4,1,24,384]{3,2,0,1:T(8,128)(2,1)S(1)}, u32[]{:S(2)}, u32[]{:S(2)}) collective-permute-start(bf16[4,1,24,384]{3,2,0,1:T(8,128)(2,1)S(1)} %get-tuple-element.16), channel_id=1, source_target_pairs={{0,1},{1,2},{2,3},{3,4},{4,5},{5,6},{6,7},{8,9},{9,10},{10,11},{11... | collective-permute-start | bytes 221192 | tf_op jit(solution)/shard_map/ppermute | solution.py:55
  5.5 5.7 %collective-permute-start.2 = (bf16[4,1,24,384]{3,2,0,1:T(8,128)(2,1)S(1)}, bf16[4,1,24,384]{3,2,0,1:T(8,128)(2,1)S(1)}, u32[]{:S(2)}, u32[]{:S(2)}) collective-permute-start(bf16[4,1,24,384]{3,2,0,1:T(8,128)(2,1)S(1)} %get-tuple-element.17), channel_id=1, source_target_pairs={{1,0},{2,1},{3,2},{4,3},{5,4},{6,5},{7,6},{9,8},{10,9},{11,10},{12... | collective-permute-start | bytes 221192 | tf_op jit(solution)/shard_map/ppermute | solution.py:56
  13.5 0.7 copy-start
  22.4 15.9 %collective-permute-start.4 = (bf16[4,4,24,384]{3,1,2,0:T(4,128)(2,1)S(1)}, bf16[4,4,24,384]{3,1,2,0:T(4,128)(2,1)S(1)}, u32[]{:S(2)}, u32[]{:S(2)}) collective-permute-start(bf16[4,4,24,384]{3,1,2,0:T(4,128)(2,1)S(1)} %slice_bitcast_fusion.3), channel_id=1, source_target_pairs={{0,8},{1,9},{2,10},{3,11},{4,12},{5,13},{6,14},{7,15}} | collective-permute-start | bytes 884744 | tf_op jit(solution)/shard_map/ppermute | solution.py:30
  25.9 9.8 %collective-permute-start.3 = (bf16[4,1,24,384]{3,1,2,0:T(2,128)(2,1)S(1)}, bf16[4,1,24,384]{3,1,2,0:T(2,128)(2,1)S(1)}, u32[]{:S(2)}, u32[]{:S(2)}) collective-permute-start(bf16[4,1,24,384]{3,1,2,0:T(2,128)(2,1)S(1)} %get-tuple-element.14), channel_id=1, source_target_pairs={{0,9},{1,10},{2,11},{3,12},{4,13},{5,14},{6,15}} | collective-permute-start | bytes 221192 | tf_op jit(solution)/shard_map/ppermute | solution.py:30
  27.2 11.1 %collective-permute-start.5 = (bf16[4,1,24,384]{3,1,2,0:T(2,128)(2,1)S(1)}, bf16[4,1,24,384]{3,1,2,0:T(2,128)(2,1)S(1)}, u32[]{:S(2)}, u32[]{:S(2)}) collective-permute-start(bf16[4,1,24,384]{3,1,2,0:T(2,128)(2,1)S(1)} %get-tuple-element.15), channel_id=1, source_target_pairs={{1,8},{2,9},{3,10},{4,11},{5,12},{6,13},{7,14}} | collective-permute-start | bytes 221192 | tf_op jit(solution)/shard_map/ppermute | solution.py:30
  28.5 23.0 %collective-permute-start = (bf16[4,4,24,384]{3,1,2,0:T(4,128)(2,1)S(1)}, bf16[4,4,24,384]{3,1,2,0:T(4,128)(2,1)S(1)}, u32[]{:S(2)}, u32[]{:S(2)}) collective-permute-start(bf16[4,4,24,384]{3,1,2,0:T(4,128)(2,1)S(1)} %copy.193), channel_id=1, source_target_pairs={{0,8},{1,9},{2,10},{3,11},{4,12},{5,13},{6,14},{7,15}} | collective-permute-start | bytes 884744 | tf_op jit(solution)/shard_map/ppermute | solution.py:30
  51.6 2.5 %collective-permute-start.6 = (bf16[4,4,24,384]{3,1,2,0:T(4,128)(2,1)S(1)}, bf16[4,4,24,384]{3,1,2,0:T(4,128)(2,1)S(1)}, u32[]{:S(2)}, u32[]{:S(2)}) collective-permute-start(bf16[4,4,24,384]{3,1,2,0:T(4,128)(2,1)S(1)} %fusion.61), channel_id=1, source_target_pairs={{8,16},{9,17},{10,18},{11,19},{12,20},{13,21},{14,22},{15,23}} | collective-permute-start | bytes 884744 | tf_op jit(solution)/shard_map/ppermute | solution.py:30
  52.5 1.5 %collective-permute-start.8 = (bf16[4,1,24,384]{3,1,2,0:T(2,128)(2,1)S(1)}, bf16[4,1,24,384]{3,1,2,0:T(2,128)(2,1)S(1)}, u32[]{:S(2)}, u32[]{:S(2)}) collective-permute-start(bf16[4,1,24,384]{3,1,2,0:T(2,128)(2,1)S(1)} %get-tuple-element.10), channel_id=1, source_target_pairs={{8,17},{9,18},{10,19},{11,20},{12,21},{13,22},{14,23}} | collective-permute-start | bytes 221192 | tf_op jit(solution)/shard_map/ppermute | solution.py:30
  53.2 0.9 collective-permute-start.9
  64.4 3.0 %collective-permute-start.11 = (bf16[4,4,24,384]{3,1,2,0:T(4,128)(2,1)S(1)}, bf16[4,4,24,384]{3,1,2,0:T(4,128)(2,1)S(1)}, u32[]{:S(2)}, u32[]{:S(2)}) collective-permute-start(bf16[4,4,24,384]{3,1,2,0:T(4,128)(2,1)S(1)} %slice_bitcast_fusion.2), channel_id=1, source_target_pairs={{16,24},{17,25},{18,26},{19,27},{20,28},{21,29},{22,30},{23,31}} | collective-permute-start | bytes 884744 | tf_op jit(solution)/shard_map/ppermute | solution.py:30
  65.3 2.0 %collective-permute-start.10 = (bf16[4,1,24,384]{3,1,2,0:T(2,128)(2,1)S(1)}, bf16[4,1,24,384]{3,1,2,0:T(2,128)(2,1)S(1)}, u32[]{:S(2)}, u32[]{:S(2)}) collective-permute-start(bf16[4,1,24,384]{3,1,2,0:T(2,128)(2,1)S(1)} %get-tuple-element.8), channel_id=1, source_target_pairs={{16,25},{17,26},{18,27},{19,28},{20,29},{21,30},{22,31}} | collective-permute-start | bytes 221192 | tf_op jit(solution)/shard_map/ppermute | solution.py:30
  66.0 1.4 %collective-permute-start.12 = (bf16[4,1,24,384]{3,1,2,0:T(2,128)(2,1)S(1)}, bf16[4,1,24,384]{3,1,2,0:T(2,128)(2,1)S(1)}, u32[]{:S(2)}, u32[]{:S(2)}) collective-permute-start(bf16[4,1,24,384]{3,1,2,0:T(2,128)(2,1)S(1)} %get-tuple-element.9), channel_id=1, source_target_pairs={{17,24},{18,25},{19,26},{20,27},{21,28},{22,29},{23,30}} | collective-permute-start | bytes 221192 | tf_op jit(solution)/shard_map/ppermute | solution.py:30
  66.7 13.9 %collective-permute-start.7 = (bf16[4,4,24,384]{3,1,2,0:T(4,128)(2,1)S(1)}, bf16[4,4,24,384]{3,1,2,0:T(4,128)(2,1)S(1)}, u32[]{:S(2)}, u32[]{:S(2)}) collective-permute-start(bf16[4,4,24,384]{3,1,2,0:T(4,128)(2,1)S(1)} %collective-permute-done.6), channel_id=1, source_target_pairs={{16,24},{17,25},{18,26},{19,27},{20,28},{21,29},{22,30},{23,31}} | collective-permute-start | bytes 884744 | tf_op jit(solution)/shard_map/ppermute | solution.py:30
  80.8 2.7 %collective-permute-start.13 = (bf16[1,4,24,384]{3,1,2,0:T(4,128)(2,1)S(1)}, bf16[1,4,24,384]{3,1,2,0:T(4,128)(2,1)S(1)}, u32[]{:S(2)}, u32[]{:S(2)}) collective-permute-start(bf16[1,4,24,384]{3,1,2,0:T(4,128)(2,1)S(1)} %get-tuple-element.7), channel_id=1, source_target_pairs={{24,16},{25,17},{26,18},{27,19},{28,20},{29,21},{30,22},{31,23}} | collective-permute-start | bytes 221192 | tf_op jit(solution)/shard_map/ppermute | solution.py:30
  81.5 2.0 %collective-permute-start.14 = (bf16[1,4,24,384]{3,1,2,0:T(4,128)(2,1)S(1)}, bf16[1,4,24,384]{3,1,2,0:T(4,128)(2,1)S(1)}, u32[]{:S(2)}, u32[]{:S(2)}) collective-permute-start(bf16[1,4,24,384]{3,1,2,0:T(4,128)(2,1)S(1)} %get-tuple-element.6), channel_id=1, source_target_pairs={{24,8},{25,9},{26,10},{27,11},{28,12},{29,13},{30,14},{31,15}} | collective-permute-start | bytes 221192 | tf_op jit(solution)/shard_map/ppermute | solution.py:30
  82.1 35.6 %collective-permute-start.15 = (bf16[1,4,24,384]{3,1,2,0:T(4,128)(2,1)S(1)}, bf16[1,4,24,384]{3,1,2,0:T(4,128)(2,1)S(1)}, u32[]{:S(2)}, u32[]{:S(2)}) collective-permute-start(bf16[1,4,24,384]{3,1,2,0:T(4,128)(2,1)S(1)} %get-tuple-element.5), channel_id=1, source_target_pairs={{24,0},{25,1},{26,2},{27,3},{28,4},{29,5},{30,6},{31,7}} | collective-permute-start | bytes 221192 | tf_op jit(solution)/shard_map/ppermute | solution.py:30

commit v2 on v1

--- a/solution.py
+++ b/solution.py
@@ -59,13 +59,19 @@
 
     for stage in range(segment_count):
         window = jnp.concatenate([top, current, bottom], axis=1)
-        convolved = causal_conv(activate(window, gain_row), kernel)
-        if stage % 2 == 0:
-            produced = convolved.astype(jnp.bfloat16)
-            next_skip = current
-        else:
-            produced = (skip.astype(jnp.float32) + convolved).astype(jnp.bfloat16)
-            next_skip = None
+        odd = stage % 2 == 1
+
+        def compute(window, skip, odd=odd):
+            convolved = causal_conv(activate(window, gain_row), kernel)
+            if odd:
+                convolved = skip.astype(jnp.float32) + convolved
+            return convolved.astype(jnp.bfloat16)
+
+        def idle(window, skip):
+            return jnp.zeros(skip.shape, jnp.bfloat16)
+
+        produced = lax.cond(segment_index == stage, compute, idle, window, skip)
+        next_skip = None if odd else current
         if stage == segment_count - 1:
             decoded = produced
             break

time: 119 us -> 116 us (0.975)
  waiting for transfers between devices: 44.7 us -> 78.5 us
  matrix products: 36.9 us -> 7.92 us
  local copies, waits for them, and re-layouts: 7.88 us -> 3.96 us
  other arithmetic: 7.32 us -> 3.78 us
    ppermute x14, waiting for transfers between devices: 42.8 us -> 78.5 us  [send(): return lax.ppermute(value, BOTH, pairs)]
    conv_general_dilated x4 -> x1, matrix products: 36.9 us -> 7.92 us  [causal_conv(): lax.conv_general_dilated(window[None], kernel, window_strides=(1, 1, 1),...]
    convert_element_type x6 -> x0, other arithmetic: 3.44 us -> none  [the longest x4 3.13 us: activate(): return jax.nn.silu(widened * lax.rsqrt(mean_square + 1e-06) * gain_row.as...]
    reduce_sum x4 -> x1, other arithmetic: 3.05 us -> 0.3 us  [activate(): mean_square = jnp.mean(widened * widened, axis=-1, keepdims=True)]
    ppermute x1, waiting for transfers between devices: 1.96 us -> 0.01 us  [local(): bottom = lax.ppermute(features[:, :1], 'rows', down)]
    conv_general_dilated x10 -> x2, local copies, waits for them, and re-layouts: 2.12 us -> 0.19 us  [causal_conv(): lax.conv_general_dilated(window[None], kernel, window_strides=(1, 1, 1),...]
    concatenate x0 -> x4, other arithmetic: none -> 1.5 us  [local(): window = jnp.concatenate([top, current, bottom], axis=1)]
  transfers between devices with their start and end apart: 16 -> 16, of which waited for: 4 -> 3; matrix products, arithmetic and copies ran while one was open for 24% -> 11% of each run, Pallas kernels for 0% -> 0%
where the time goes in v2:
time: 116 us
  waiting for transfers between devices  78.5 us (68%)
  starting transfers between devices  20.9 us (18%)
  matrix products  7.92 us (7%)
  local copies, waits for them, and re-layouts  3.96 us (3%)
  other arithmetic  3.78 us (3%)
    ppermute x14, waiting for transfers between devices, send(): return lax.ppermute(value, BOTH, pairs)  78.5 us
    ppermute x14, starting transfers between devices, send(): return lax.ppermute(value, BOTH, pairs)  14.4 us
    conv_general_dilated x1, matrix products, causal_conv(): lax.conv_general_dilated(window[None], kernel, window_strides=(1, 1, 1),...  7.92 us
    ppermute x1, starting transfers between devices, local(): top = lax.ppermute(features[:, height - 1:], 'rows', up)  4.51 us
  transfers between devices with their start and end apart: 16, of which 3 were waited for; matrix products, arithmetic and copies ran while one was open for 11% of the time, Pallas kernels for 0%

profile of v2, /device:TPU:1, one launch (start us, length us, event | category | flops | bytes accessed | tf_op | source)
XLA Modules:
  0.0 115.7 jit_solution(3352452658527466000)
XLA Ops:
  0.0 1.1 copy.17
  1.1 0.1 fusion.84
  1.2 4.5 %collective-permute-start.1 = (bf16[4,1,24,384]{3,0,2,1:T(4,128)(2,1)S(1)}, bf16[4,1,24,384]{3,0,2,1:T(4,128)(2,1)S(1)}, u32[]{:S(2)}, u32[]{:S(2)}) collective-permute-start(bf16[4,1,24,384]{3,0,2,1:T(4,128)(2,1)S(1)} %get-tuple-element.72), channel_id=1, source_target_pairs={{0,1},{1,2},{2,3},{3,4},{4,5},{5,6},{6,7},{8,9},{9,10},{10,11},{11... | collective-permute-start | bytes 221192 | tf_op jit(solution)/shard_map/ppermute | solution.py:55
  5.7 1.9 %collective-permute-start.2 = (bf16[4,1,24,384]{3,0,2,1:T(4,128)(2,1)S(1)}, bf16[4,1,24,384]{3,0,2,1:T(4,128)(2,1)S(1)}, u32[]{:S(2)}, u32[]{:S(2)}) collective-permute-start(bf16[4,1,24,384]{3,0,2,1:T(4,128)(2,1)S(1)} %get-tuple-element.73), channel_id=1, source_target_pairs={{1,0},{2,1},{3,2},{4,3},{5,4},{6,5},{7,6},{9,8},{10,9},{11,10},{12... | collective-permute-start | bytes 221192 | tf_op jit(solution)/shard_map/ppermute | solution.py:56
  7.6 1.1 copy.16
  8.7 3.2 %collective-permute-start = (bf16[4,4,24,384]{3,1,2,0:T(4,128)(2,1)S(1)}, bf16[4,4,24,384]{3,1,2,0:T(4,128)(2,1)S(1)}, u32[]{:S(2)}, u32[]{:S(2)}) collective-permute-start(bf16[4,4,24,384]{3,1,2,0:T(4,128)(2,1)S(1)} %copy.16), channel_id=1, source_target_pairs={{0,8},{1,9},{2,10},{3,11},{4,12},{5,13},{6,14},{7,15}} | collective-permute-start | bytes 884744 | tf_op jit(solution)/shard_map/ppermute | solution.py:30
  11.9 0.7 reduce
  12.7 0.3 pad_maximum_fusion.1
  13.0 9.7 %conditional.4 = (bf16[4,4,24,384]{3,1,2,0:T(4,128)(2,1)S(1)}) conditional(s32[]{:T(128)} %convert_element_type.74, () %tuple.31, (bf16[4,6,24,384]{3,0,2,1:T(4,128)(2,1)S(1)}, bf16[384]{0:T(512)(128)(2,1)S(1)}, bf16[3,3,3,384,384]{4,3,2,1,0:T(8,128)(2,1)}) %tuple.53), branch_computations={%region_0.0_spmd, %region_1.3_spmd} | conditional | flops 3063129088 | bytes 14648262 | solution.py:73
  13.0 0.3 fusion.2
  13.4 0.6 fusion.14
  14.0 0.2 pad
  14.2 0.1 copy.5
  14.3 0.1 slice.56
  14.4 7.9 %fusion.1 = bf16[4,4,8,4,384]{4,2,3,1,0:T(8,128)(2,1)S(1)} fusion(bf16[3,3,3,384,384]{4,3,2,1,0:T(8,128)(2,1)} %get-tuple-element.46, bf16[4,6,1,7,2,384]{5,3,4,1,0,2:T(8,128)(2,1)S(1)} %slice.56, bf16[4,6,1,8,4,384]{5,3,4,1,0,2:T(8,128)(2,1)S(1)} %copy.5, pred[8,4]{0,1:T(4,128)(4,1)S(1)} %copy-done), kind=kOutput, calls=%fused_computation.3 | convolution fusion | flops 3060695040 | bytes 9203744 | tf_op jit(solution)/shard_map/cond/branch_1_fun/conv_general_dilated | solution.py:18
  22.3 0.2 copy.6
  22.6 0.1 slice_bitcast_fusion
  22.7 0.2 copy.20
  22.8 1.3 %collective-permute-start.4 = (bf16[4,4,24,384]{3,0,2,1:T(4,128)(2,1)S(1)}, bf16[4,4,24,384]{3,0,2,1:T(4,128)(2,1)S(1)}, u32[]{:S(2)}, u32[]{:S(2)}) collective-permute-start(bf16[4,4,24,384]{3,0,2,1:T(4,128)(2,1)S(1)} %copy.20), channel_id=1, source_target_pairs={{0,8},{1,9},{2,10},{3,11},{4,12},{5,13},{6,14},{7,15}} | collective-permute-start | bytes 884744 | tf_op jit(solution)/shard_map/ppermute | solution.py:30
  24.1 0.1 fusion.83
  24.2 1.3 %collective-permute-start.3 = (bf16[4,1,24,384]{3,0,2,1:T(4,128)(2,1)S(1)}, bf16[4,1,24,384]{3,0,2,1:T(4,128)(2,1)S(1)}, u32[]{:S(2)}, u32[]{:S(2)}) collective-permute-start(bf16[4,1,24,384]{3,0,2,1:T(4,128)(2,1)S(1)} %get-tuple-element.70), channel_id=1, source_target_pairs={{0,9},{1,10},{2,11},{3,12},{4,13},{5,14},{6,15}} | collective-permute-start | bytes 221192 | tf_op jit(solution)/shard_map/ppermute | solution.py:30
  25.5 1.3 %collective-permute-start.5 = (bf16[4,1,24,384]{3,0,2,1:T(4,128)(2,1)S(1)}, bf16[4,1,24,384]{3,0,2,1:T(4,128)(2,1)S(1)}, u32[]{:S(2)}, u32[]{:S(2)}) collective-permute-start(bf16[4,1,24,384]{3,0,2,1:T(4,128)(2,1)S(1)} %get-tuple-element.71), channel_id=1, source_target_pairs={{1,8},{2,9},{3,10},{4,11},{5,12},{6,13},{7,14}} | collective-permute-start | bytes 221192 | tf_op jit(solution)/shard_map/ppermute | solution.py:30
  26.8 4.3 %collective-permute-done.3 = bf16[4,1,24,384]{3,0,2,1:T(4,128)(2,1)S(1)} collective-permute-done((bf16[4,1,24,384]{3,0,2,1:T(4,128)(2,1)S(1)}, bf16[4,1,24,384]{3,0,2,1:T(4,128)(2,1)S(1)}, u32[]{:S(2)}, u32[]{:S(2)}) %collective-permute-start.3) | collective-permute-done | bytes 73760 | tf_op jit(solution)/shard_map/ppermute | solution.py:30
  31.1 0.8 collective-permute-done.5
  31.9 0.3 pad_maximum_fusion.2
  32.2 0.1 conditional.5
  32.2 0.1 broadcast.80
  32.3 0.7 collective-permute-start.6
  33.0 0.2 fusion.82
  33.2 0.7 collective-permute-start.8
  33.9 0.7 collective-permute-start.9
  34.6 0.5 pad_maximum_fusion
  35.1 0.3 conditional.6
  35.1 0.1 broadcast.83
  35.4 0.2 copy.24
  35.6 0.7 collective-permute-start.11
  36.3 0.7 collective-permute-start.7
  37.0 0.7 collective-permute-start.10
  37.7 0.7 collective-permute-start.12
  38.4 0.3 pad_maximum_fusion.3
  38.7 0.1 conditional.7
  38.8 0.1 broadcast.86
  38.9 0.1 fusion.80
  39.0 0.7 collective-permute-start.13
  39.7 0.7 collective-permute-start.14
  40.4 1.3 %collective-permute-start.15 = (bf16[1,4,24,384]{3,2,1,0:T(8,128)(2,1)S(1)}, bf16[1,4,24,384]{3,2,1,0:T(8,128)(2,1)S(1)}, u32[]{:S(2)}, u32[]{:S(2)}) collective-permute-start(bf16[1,4,24,384]{3,2,1,0:T(8,128)(2,1)S(1)} %copy.33), channel_id=1, source_target_pairs={{24,0},{25,1},{26,2},{27,3},{28,4},{29,5},{30,6},{31,7}} | collective-permute-start | bytes 221192 | tf_op jit(solution)/shard_map/ppermute | solution.py:30
  41.7 73.4 %collective-permute-done.15 = bf16[1,4,24,384]{3,2,1,0:T(8,128)(2,1)S(1)} collective-permute-done((bf16[1,4,24,384]{3,2,1,0:T(8,128)(2,1)S(1)}, bf16[1,4,24,384]{3,2,1,0:T(8,128)(2,1)S(1)}, u32[]{:S(2)}, u32[]{:S(2)}) %collective-permute-start.15) | collective-permute-done | bytes 73760 | tf_op jit(solution)/shard_map/ppermute | solution.py:30
  115.1 0.7 fusion.79
  (21 shorter events, 0.2 us)
Async XLA Ops:
  1.2 11.5 %collective-permute-start.1 = (bf16[4,1,24,384]{3,0,2,1:T(4,128)(2,1)S(1)}, bf16[4,1,24,384]{3,0,2,1:T(4,128)(2,1)S(1)}, u32[]{:S(2)}, u32[]{:S(2)}) collective-permute-start(bf16[4,1,24,384]{3,0,2,1:T(4,128)(2,1)S(1)} %get-tuple-element.72), channel_id=1, source_target_pairs={{0,1},{1,2},{2,3},{3,4},{4,5},{5,6},{6,7},{8,9},{9,10},{10,11},{11... | collective-permute-start | bytes 221192 | tf_op jit(solution)/shard_map/ppermute | solution.py:55
  5.7 7.0 %collective-permute-start.2 = (bf16[4,1,24,384]{3,0,2,1:T(4,128)(2,1)S(1)}, bf16[4,1,24,384]{3,0,2,1:T(4,128)(2,1)S(1)}, u32[]{:S(2)}, u32[]{:S(2)}) collective-permute-start(bf16[4,1,24,384]{3,0,2,1:T(4,128)(2,1)S(1)} %get-tuple-element.73), channel_id=1, source_target_pairs={{1,0},{2,1},{3,2},{4,3},{5,4},{6,5},{7,6},{9,8},{10,9},{11,10},{12... | collective-permute-start | bytes 221192 | tf_op jit(solution)/shard_map/ppermute | solution.py:56
  8.7 23.5 %collective-permute-start = (bf16[4,4,24,384]{3,1,2,0:T(4,128)(2,1)S(1)}, bf16[4,4,24,384]{3,1,2,0:T(4,128)(2,1)S(1)}, u32[]{:S(2)}, u32[]{:S(2)}) collective-permute-start(bf16[4,4,24,384]{3,1,2,0:T(4,128)(2,1)S(1)} %copy.16), channel_id=1, source_target_pairs={{0,8},{1,9},{2,10},{3,11},{4,12},{5,13},{6,14},{7,15}} | collective-permute-start | bytes 884744 | tf_op jit(solution)/shard_map/ppermute | solution.py:30
  13.4 1.0 copy-start
  22.8 9.0 %collective-permute-start.4 = (bf16[4,4,24,384]{3,0,2,1:T(4,128)(2,1)S(1)}, bf16[4,4,24,384]{3,0,2,1:T(4,128)(2,1)S(1)}, u32[]{:S(2)}, u32[]{:S(2)}) collective-permute-start(bf16[4,4,24,384]{3,0,2,1:T(4,128)(2,1)S(1)} %copy.20), channel_id=1, source_target_pairs={{0,8},{1,9},{2,10},{3,11},{4,12},{5,13},{6,14},{7,15}} | collective-permute-start | bytes 884744 | tf_op jit(solution)/shard_map/ppermute | solution.py:30
  24.2 6.9 %collective-permute-start.3 = (bf16[4,1,24,384]{3,0,2,1:T(4,128)(2,1)S(1)}, bf16[4,1,24,384]{3,0,2,1:T(4,128)(2,1)S(1)}, u32[]{:S(2)}, u32[]{:S(2)}) collective-permute-start(bf16[4,1,24,384]{3,0,2,1:T(4,128)(2,1)S(1)} %get-tuple-element.70), channel_id=1, source_target_pairs={{0,9},{1,10},{2,11},{3,12},{4,13},{5,14},{6,15}} | collective-permute-start | bytes 221192 | tf_op jit(solution)/shard_map/ppermute | solution.py:30
  25.5 6.4 %collective-permute-start.5 = (bf16[4,1,24,384]{3,0,2,1:T(4,128)(2,1)S(1)}, bf16[4,1,24,384]{3,0,2,1:T(4,128)(2,1)S(1)}, u32[]{:S(2)}, u32[]{:S(2)}) collective-permute-start(bf16[4,1,24,384]{3,0,2,1:T(4,128)(2,1)S(1)} %get-tuple-element.71), channel_id=1, source_target_pairs={{1,8},{2,9},{3,10},{4,11},{5,12},{6,13},{7,14}} | collective-permute-start | bytes 221192 | tf_op jit(solution)/shard_map/ppermute | solution.py:30
  32.3 2.3 %collective-permute-start.6 = (bf16[4,4,24,384]{3,1,2,0:T(4,128)(2,1)S(1)}, bf16[4,4,24,384]{3,1,2,0:T(4,128)(2,1)S(1)}, u32[]{:S(2)}, u32[]{:S(2)}) collective-permute-start(bf16[4,4,24,384]{3,1,2,0:T(4,128)(2,1)S(1)} %get-tuple-element.75), channel_id=1, source_target_pairs={{8,16},{9,17},{10,18},{11,19},{12,20},{13,21},{14,22},{15,23}} | collective-permute-start | bytes 884744 | tf_op jit(solution)/shard_map/ppermute | solution.py:30
  33.2 1.4 %collective-permute-start.8 = (bf16[4,1,24,384]{3,1,2,0:T(2,128)(2,1)S(1)}, bf16[4,1,24,384]{3,1,2,0:T(2,128)(2,1)S(1)}, u32[]{:S(2)}, u32[]{:S(2)}) collective-permute-start(bf16[4,1,24,384]{3,1,2,0:T(2,128)(2,1)S(1)} %get-tuple-element.68), channel_id=1, source_target_pairs={{8,17},{9,18},{10,19},{11,20},{12,21},{13,22},{14,23}} | collective-permute-start | bytes 221192 | tf_op jit(solution)/shard_map/ppermute | solution.py:30
  33.9 0.7 collective-permute-start.9
  35.6 2.8 %collective-permute-start.11 = (bf16[4,4,24,384]{3,0,2,1:T(4,128)(2,1)S(1)}, bf16[4,4,24,384]{3,0,2,1:T(4,128)(2,1)S(1)}, u32[]{:S(2)}, u32[]{:S(2)}) collective-permute-start(bf16[4,4,24,384]{3,0,2,1:T(4,128)(2,1)S(1)} %copy.24), channel_id=1, source_target_pairs={{16,24},{17,25},{18,26},{19,27},{20,28},{21,29},{22,30},{23,31}} | collective-permute-start | bytes 884744 | tf_op jit(solution)/shard_map/ppermute | solution.py:30
  36.3 2.5 %collective-permute-start.7 = (bf16[4,4,24,384]{3,1,2,0:T(4,128)(2,1)S(1)}, bf16[4,4,24,384]{3,1,2,0:T(4,128)(2,1)S(1)}, u32[]{:S(2)}, u32[]{:S(2)}) collective-permute-start(bf16[4,4,24,384]{3,1,2,0:T(4,128)(2,1)S(1)} %collective-permute-done.6), channel_id=1, source_target_pairs={{16,24},{17,25},{18,26},{19,27},{20,28},{21,29},{22,30},{23,31}} | collective-permute-start | bytes 884744 | tf_op jit(solution)/shard_map/ppermute | solution.py:30
  37.0 1.4 %collective-permute-start.10 = (bf16[4,1,24,384]{3,0,2,1:T(4,128)(2,1)S(1)}, bf16[4,1,24,384]{3,0,2,1:T(4,128)(2,1)S(1)}, u32[]{:S(2)}, u32[]{:S(2)}) collective-permute-start(bf16[4,1,24,384]{3,0,2,1:T(4,128)(2,1)S(1)} %get-tuple-element.66), channel_id=1, source_target_pairs={{16,25},{17,26},{18,27},{19,28},{20,29},{21,30},{22,31}} | collective-permute-start | bytes 221192 | tf_op jit(solution)/shard_map/ppermute | solution.py:30
  37.7 0.7 collective-permute-start.12
  39.0 2.7 %collective-permute-start.13 = (bf16[1,4,24,384]{3,2,1,0:T(8,128)(2,1)S(1)}, bf16[1,4,24,384]{3,2,1,0:T(8,128)(2,1)S(1)}, u32[]{:S(2)}, u32[]{:S(2)}) collective-permute-start(bf16[1,4,24,384]{3,2,1,0:T(8,128)(2,1)S(1)} %copy.31), channel_id=1, source_target_pairs={{24,16},{25,17},{26,18},{27,19},{28,20},{29,21},{30,22},{31,23}} | collective-permute-start | bytes 221192 | tf_op jit(solution)/shard_map/ppermute | solution.py:30
  39.7 2.0 %collective-permute-start.14 = (bf16[1,4,24,384]{3,2,1,0:T(8,128)(2,1)S(1)}, bf16[1,4,24,384]{3,2,1,0:T(8,128)(2,1)S(1)}, u32[]{:S(2)}, u32[]{:S(2)}) collective-permute-start(bf16[1,4,24,384]{3,2,1,0:T(8,128)(2,1)S(1)} %copy.32), channel_id=1, source_target_pairs={{24,8},{25,9},{26,10},{27,11},{28,12},{29,13},{30,14},{31,15}} | collective-permute-start | bytes 221192 | tf_op jit(solution)/shard_map/ppermute | solution.py:30
  40.4 74.7 %collective-permute-start.15 = (bf16[1,4,24,384]{3,2,1,0:T(8,128)(2,1)S(1)}, bf16[1,4,24,384]{3,2,1,0:T(8,128)(2,1)S(1)}, u32[]{:S(2)}, u32[]{:S(2)}) collective-permute-start(bf16[1,4,24,384]{3,2,1,0:T(8,128)(2,1)S(1)} %copy.33), channel_id=1, source_target_pairs={{24,0},{25,1},{26,2},{27,3},{28,4},{29,5},{30,6},{31,7}} | collective-permute-start | bytes 221192 | tf_op jit(solution)/shard_map/ppermute | solution.py:30

commit v3 on v2

--- a/solution.py
+++ b/solution.py
@@ -47,8 +47,12 @@
     row_count = lax.axis_size("rows")
     segment_index = lax.axis_index("segment")
     frame_count, height, columns, channels = features.shape
+    group = frame_count // segment_count
     gain_row = gains[0]
     kernel = kernels[0]
+
+    def straight(source, target):
+        return [(source * row_count + r, target * row_count + r) for r in range(row_count)]
 
     up = [(i, i + 1) for i in range(row_count - 1)]
     down = [(i + 1, i) for i in range(row_count - 1)]
@@ -56,40 +60,51 @@
     bottom = lax.ppermute(features[:, :1], "rows", down)
     current = features
     skip = features
+    last_stage = segment_count - 1
 
     for stage in range(segment_count):
         window = jnp.concatenate([top, current, bottom], axis=1)
         odd = stage % 2 == 1
+        final = stage == last_stage
 
-        def compute(window, skip, odd=odd):
+        def compute(window, skip, odd=odd, final=final):
             convolved = causal_conv(activate(window, gain_row), kernel)
+            if final:
+                return convolved
             if odd:
                 convolved = skip.astype(jnp.float32) + convolved
             return convolved.astype(jnp.bfloat16)
 
-        def idle(window, skip):
-            return jnp.zeros(skip.shape, jnp.bfloat16)
+        def idle(window, skip, final=final):
+            return jnp.zeros(skip.shape, jnp.float32 if final else jnp.bfloat16)
 
         produced = lax.cond(segment_index == stage, compute, idle, window, skip)
-        next_skip = None if odd else current
-        if stage == segment_count - 1:
-            decoded = produced
+        if final:
             break
+        if stage == last_stage - 1:
+            owned = current[stage * group : (stage + 1) * group]
+            for target in range(segment_count):
+                chunk = current[target * group : (target + 1) * group]
+                if stage == 0:
+                    owned = jnp.where(segment_index == target, chunk, owned)
+                elif target != stage:
+                    piece = send(chunk, straight(stage, target))
+                    owned = jnp.where(segment_index == target, piece, owned)
+        next_skip = current if (not odd and stage > 0 and stage != last_stage - 1) else None
         current, top, bottom = stage_send(produced, stage, row_count)
         if next_skip is not None:
-            base, nxt = stage * row_count, (stage + 1) * row_count
-            skip = send(next_skip, [(base + r, nxt + r) for r in range(row_count)])
+            skip = send(next_skip, straight(stage, stage + 1))
+        elif not odd:
+            skip = features
 
-    group = frame_count // segment_count
-    last = (segment_count - 1) * row_count
-    delivered = decoded[(segment_count - 1) * group :]
-    for target in range(segment_count - 1):
+    branch = produced[last_stage * group :]
+    for target in range(last_stage):
         piece = send(
-            decoded[target * group : (target + 1) * group],
-            [(last + r, target * row_count + r) for r in range(row_count)],
+            produced[target * group : (target + 1) * group].astype(jnp.bfloat16),
+            straight(last_stage, target),
         )
-        delivered = jnp.where(segment_index == target, piece, delivered)
-    return delivered
+        branch = jnp.where(segment_index == target, piece.astype(jnp.float32), branch)
+    return (owned.astype(jnp.float32) + branch).astype(jnp.bfloat16)
 
 
 def solution(mesh):

time: 116 us -> 107 us (0.922)
  waiting for transfers between devices: 78.5 us -> 70.5 us
  starting transfers between devices: 20.9 us -> 19.6 us
    ppermute x14 -> x15, waiting for transfers between devices: 78.5 us -> 67.4 us  [send(): return lax.ppermute(value, BOTH, pairs)]
    ppermute x1, waiting for transfers between devices: 0.01 us -> 3.03 us  [local(): bottom = lax.ppermute(features[:, :1], 'rows', down)]
    ppermute x14 -> x15, starting transfers between devices: 14.4 us -> 13.2 us  [send(): return lax.ppermute(value, BOTH, pairs)]
  transfers between devices with their start and end apart: 16 -> 17, of which waited for: 3 -> 5; matrix products, arithmetic and copies ran while one was open for 11% -> 3% of each run, Pallas kernels for 0% -> 0%
where the time goes in v3:
time: 107 us
  waiting for transfers between devices  70.5 us (66%)
  starting transfers between devices  19.6 us (18%)
  matrix products  7.92 us (7%)
  other arithmetic  4.51 us (4%)
  local copies, waits for them, and re-layouts  3.44 us (3%)
    ppermute x15, waiting for transfers between devices, send(): return lax.ppermute(value, BOTH, pairs)  67.4 us
    ppermute x15, starting transfers between devices, send(): return lax.ppermute(value, BOTH, pairs)  13.2 us
    conv_general_dilated x1, matrix products, causal_conv(): lax.conv_general_dilated(window[None], kernel, window_strides=(1, 1, 1),...  7.92 us
    ppermute x1, starting transfers between devices, local(): top = lax.ppermute(features[:, height - 1:], 'rows', up)  4.51 us
    ppermute x1, waiting for transfers between devices, local(): bottom = lax.ppermute(features[:, :1], 'rows', down)  3.03 us
  transfers between devices with their start and end apart: 17, of which 5 were waited for; matrix products, arithmetic and copies ran while one was open for 3% of the time, Pallas kernels for 0%

profile of v3, /device:TPU:1, one launch (start us, length us, event | category | flops | bytes accessed | tf_op | source)
XLA Modules:
  0.0 106.6 jit_solution(14728538127915180568)
XLA Ops:
  0.0 1.1 %copy.16 = bf16[4,4,24,384]{3,0,2,1:T(4,128)(2,1)S(1)} copy(bf16[4,4,24,384]{3,2,1,0:T(8,128)(2,1)} %param.11) | data formatting | bytes 589824 | tf_op args[0]
  1.1 0.1 fusion.83
  1.2 4.5 %collective-permute-start = (bf16[4,1,24,384]{3,0,2,1:T(4,128)(2,1)S(1)}, bf16[4,1,24,384]{3,0,2,1:T(4,128)(2,1)S(1)}, u32[]{:S(2)}, u32[]{:S(2)}) collective-permute-start(bf16[4,1,24,384]{3,0,2,1:T(4,128)(2,1)S(1)} %get-tuple-element.77), channel_id=1, source_target_pairs={{0,1},{1,2},{2,3},{3,4},{4,5},{5,6},{6,7},{8,9},{9,10},{10,11},{11... | collective-permute-start | bytes 221192 | tf_op jit(solution)/shard_map/ppermute | solution.py:59
  5.7 1.9 %collective-permute-start.1 = (bf16[4,1,24,384]{3,0,2,1:T(4,128)(2,1)S(1)}, bf16[4,1,24,384]{3,0,2,1:T(4,128)(2,1)S(1)}, u32[]{:S(2)}, u32[]{:S(2)}) collective-permute-start(bf16[4,1,24,384]{3,0,2,1:T(4,128)(2,1)S(1)} %get-tuple-element.78), channel_id=1, source_target_pairs={{1,0},{2,1},{3,2},{4,3},{5,4},{6,5},{7,6},{9,8},{10,9},{11,10},{12... | collective-permute-start | bytes 221192 | tf_op jit(solution)/shard_map/ppermute | solution.py:60
  7.6 0.7 reduce
  8.3 3.0 %collective-permute-done.1 = bf16[4,1,24,384]{3,0,2,1:T(4,128)(2,1)S(1)} collective-permute-done((bf16[4,1,24,384]{3,0,2,1:T(4,128)(2,1)S(1)}, bf16[4,1,24,384]{3,0,2,1:T(4,128)(2,1)S(1)}, u32[]{:S(2)}, u32[]{:S(2)}) %collective-permute-start.1) | collective-permute-done | bytes 73760 | tf_op jit(solution)/shard_map/ppermute | solution.py:60
  11.4 0.3 pad_maximum_fusion
  11.7 9.7 %conditional.4 = (bf16[4,4,24,384]{3,1,2,0:T(4,128)(2,1)S(1)}) conditional(s32[]{:T(128)} %convert_element_type.85, () %tuple.30, (bf16[4,6,24,384]{3,0,2,1:T(4,128)(2,1)S(1)}, bf16[384]{0:T(512)(128)(2,1)S(1)}, bf16[3,3,3,384,384]{4,3,2,1,0:T(8,128)(2,1)}) %tuple.58), branch_computations={%region_0.0_spmd, %region_1.3_spmd} | conditional | flops 3063129088 | bytes 14648262 | solution.py:81
  11.7 0.3 fusion.2
  12.1 0.6 fusion.14
  12.7 0.2 pad
  12.9 0.1 copy.5
  13.0 0.1 slice.77
  13.1 7.9 %fusion.1 = bf16[4,4,8,4,384]{4,2,3,1,0:T(8,128)(2,1)S(1)} fusion(bf16[3,3,3,384,384]{4,3,2,1,0:T(8,128)(2,1)} %get-tuple-element.44, bf16[4,6,1,7,2,384]{5,3,4,1,0,2:T(8,128)(2,1)S(1)} %slice.77, bf16[4,6,1,8,4,384]{5,3,4,1,0,2:T(8,128)(2,1)S(1)} %copy.5, pred[8,4]{0,1:T(4,128)(4,1)S(1)} %copy-done.1), kind=kOutput, calls=%fused_computation.3 | convolution fusion | flops 3060695040 | bytes 9203744 | tf_op jit(solution)/shard_map/cond/branch_1_fun/conv_general_dilated | solution.py:18
  21.0 0.2 copy.6
  21.3 0.1 slice_bitcast_fusion
  21.4 0.2 copy.19
  21.5 1.3 %collective-permute-start.3 = (bf16[4,4,24,384]{3,0,2,1:T(4,128)(2,1)S(1)}, bf16[4,4,24,384]{3,0,2,1:T(4,128)(2,1)S(1)}, u32[]{:S(2)}, u32[]{:S(2)}) collective-permute-start(bf16[4,4,24,384]{3,0,2,1:T(4,128)(2,1)S(1)} %copy.19), channel_id=1, source_target_pairs={{0,8},{1,9},{2,10},{3,11},{4,12},{5,13},{6,14},{7,15}} | collective-permute-start | bytes 884744 | tf_op jit(solution)/shard_map/ppermute | solution.py:30
  22.9 1.3 %collective-permute-start.2 = (bf16[4,1,24,384]{3,0,2,1:T(4,128)(2,1)S(1)}, bf16[4,1,24,384]{3,0,2,1:T(4,128)(2,1)S(1)}, u32[]{:S(2)}, u32[]{:S(2)}) collective-permute-start(bf16[4,1,24,384]{3,0,2,1:T(4,128)(2,1)S(1)} %get-tuple-element.75), channel_id=1, source_target_pairs={{0,9},{1,10},{2,11},{3,12},{4,13},{5,14},{6,15}} | collective-permute-start | bytes 221192 | tf_op jit(solution)/shard_map/ppermute | solution.py:30
  24.2 1.3 %collective-permute-start.4 = (bf16[4,1,24,384]{3,0,2,1:T(4,128)(2,1)S(1)}, bf16[4,1,24,384]{3,0,2,1:T(4,128)(2,1)S(1)}, u32[]{:S(2)}, u32[]{:S(2)}) collective-permute-start(bf16[4,1,24,384]{3,0,2,1:T(4,128)(2,1)S(1)} %get-tuple-element.76), channel_id=1, source_target_pairs={{1,8},{2,9},{3,10},{4,11},{5,12},{6,13},{7,14}} | collective-permute-start | bytes 221192 | tf_op jit(solution)/shard_map/ppermute | solution.py:30
  25.5 3.4 %collective-permute-done.2 = bf16[4,1,24,384]{3,0,2,1:T(4,128)(2,1)S(1)} collective-permute-done((bf16[4,1,24,384]{3,0,2,1:T(4,128)(2,1)S(1)}, bf16[4,1,24,384]{3,0,2,1:T(4,128)(2,1)S(1)}, u32[]{:S(2)}, u32[]{:S(2)}) %collective-permute-start.2) | collective-permute-done | bytes 73760 | tf_op jit(solution)/shard_map/ppermute | solution.py:30
  28.9 0.8 collective-permute-done.4
  29.7 0.3 pad_maximum_fusion.1
  30.0 0.1 conditional.5
  30.1 0.1 broadcast.80
  30.2 0.7 collective-permute-start.5
  30.9 0.7 collective-permute-start.10
  31.6 0.7 collective-permute-start.9
  32.3 0.1 pad_maximum_fusion.2
  32.4 0.3 conditional.6
  32.4 0.1 broadcast.83
  32.7 0.2 copy.27
  32.8 0.7 collective-permute-start.12
  33.6 0.7 collective-permute-start.11
  34.2 0.7 collective-permute-start.13
  35.0 0.7 collective-permute-start.6
  35.6 0.7 collective-permute-start.7
  36.3 1.3 %collective-permute-start.8 = (bf16[1,4,24,384]{3,2,1,0:T(8,128)(2,1)S(1)}, bf16[1,4,24,384]{3,2,1,0:T(8,128)(2,1)S(1)}, u32[]{:S(2)}, u32[]{:S(2)}) collective-permute-start(bf16[1,4,24,384]{3,2,1,0:T(8,128)(2,1)S(1)} %get-tuple-element.65), channel_id=1, source_target_pairs={{16,0},{17,1},{18,2},{19,3},{20,4},{21,5},{22,6},{23,7}} | collective-permute-start | bytes 221192 | tf_op jit(solution)/shard_map/ppermute | solution.py:30
  37.6 0.3 pad_maximum_fusion.3
  38.0 0.9 conditional.7
  38.0 0.9 broadcast.86.clone
  38.9 1.1 %convert.5 = bf16[4,4,24,384]{3,2,1,0:T(8,128)(2,1)S(1)} convert(f32[4,4,24,384]{3,2,1,0:T(8,128)} %get-tuple-element.63) | non-fusion elementwise | flops 147456 | bytes 884736 | tf_op jit(solution)/shard_map/convert.2
  40.0 0.7 collective-permute-start.14
  40.7 0.7 collective-permute-start.15
  41.4 1.3 %collective-permute-start.16 = (bf16[1,4,24,384]{3,2,1,0:T(8,128)(2,1)S(1)}, bf16[1,4,24,384]{3,2,1,0:T(8,128)(2,1)S(1)}, u32[]{:S(2)}, u32[]{:S(2)}) collective-permute-start(bf16[1,4,24,384]{3,2,1,0:T(8,128)(2,1)S(1)} %get-tuple-element.69), channel_id=1, source_target_pairs={{24,0},{25,1},{26,2},{27,3},{28,4},{29,5},{30,6},{31,7}} | collective-permute-start | bytes 221192 | tf_op jit(solution)/shard_map/ppermute | solution.py:30
  42.7 38.6 %collective-permute-done.8 = bf16[1,4,24,384]{3,2,1,0:T(8,128)(2,1)S(1)} collective-permute-done((bf16[1,4,24,384]{3,2,1,0:T(8,128)(2,1)S(1)}, bf16[1,4,24,384]{3,2,1,0:T(8,128)(2,1)S(1)}, u32[]{:S(2)}, u32[]{:S(2)}) %collective-permute-start.8) | collective-permute-done | bytes 73760 | tf_op jit(solution)/shard_map/ppermute | solution.py:30
  81.3 24.7 %collective-permute-done.16 = bf16[1,4,24,384]{3,2,1,0:T(8,128)(2,1)S(1)} collective-permute-done((bf16[1,4,24,384]{3,2,1,0:T(8,128)(2,1)S(1)}, bf16[1,4,24,384]{3,2,1,0:T(8,128)(2,1)S(1)}, u32[]{:S(2)}, u32[]{:S(2)}) %collective-permute-start.16) | collective-permute-done | bytes 73760 | tf_op jit(solution)/shard_map/ppermute | solution.py:30
  105.9 0.7 add_convert_fusion
  (25 shorter events, 0.3 us)
Async XLA Ops:
  1.2 7.2 %collective-permute-start = (bf16[4,1,24,384]{3,0,2,1:T(4,128)(2,1)S(1)}, bf16[4,1,24,384]{3,0,2,1:T(4,128)(2,1)S(1)}, u32[]{:S(2)}, u32[]{:S(2)}) collective-permute-start(bf16[4,1,24,384]{3,0,2,1:T(4,128)(2,1)S(1)} %get-tuple-element.77), channel_id=1, source_target_pairs={{0,1},{1,2},{2,3},{3,4},{4,5},{5,6},{6,7},{8,9},{9,10},{10,11},{11... | collective-permute-start | bytes 221192 | tf_op jit(solution)/shard_map/ppermute | solution.py:59
  5.7 5.7 %collective-permute-start.1 = (bf16[4,1,24,384]{3,0,2,1:T(4,128)(2,1)S(1)}, bf16[4,1,24,384]{3,0,2,1:T(4,128)(2,1)S(1)}, u32[]{:S(2)}, u32[]{:S(2)}) collective-permute-start(bf16[4,1,24,384]{3,0,2,1:T(4,128)(2,1)S(1)} %get-tuple-element.78), channel_id=1, source_target_pairs={{1,0},{2,1},{3,2},{4,3},{5,4},{6,5},{7,6},{9,8},{10,9},{11,10},{12... | collective-permute-start | bytes 221192 | tf_op jit(solution)/shard_map/ppermute | solution.py:60
  12.1 1.0 copy-start.1
  21.4 8.7 %copy-start = (bf16[4,4,24,384]{3,2,1,0:T(8,128)(2,1)S(1)}, bf16[4,4,24,384]{3,2,1,0:T(8,128)(2,1)}, u32[]{:S(2)}) copy-start(bf16[4,4,24,384]{3,2,1,0:T(8,128)(2,1)} %param.11) | copy-start | bytes 884740
  21.5 8.2 %collective-permute-start.3 = (bf16[4,4,24,384]{3,0,2,1:T(4,128)(2,1)S(1)}, bf16[4,4,24,384]{3,0,2,1:T(4,128)(2,1)S(1)}, u32[]{:S(2)}, u32[]{:S(2)}) collective-permute-start(bf16[4,4,24,384]{3,0,2,1:T(4,128)(2,1)S(1)} %copy.19), channel_id=1, source_target_pairs={{0,8},{1,9},{2,10},{3,11},{4,12},{5,13},{6,14},{7,15}} | collective-permute-start | bytes 884744 | tf_op jit(solution)/shard_map/ppermute | solution.py:30
  22.9 6.0 %collective-permute-start.2 = (bf16[4,1,24,384]{3,0,2,1:T(4,128)(2,1)S(1)}, bf16[4,1,24,384]{3,0,2,1:T(4,128)(2,1)S(1)}, u32[]{:S(2)}, u32[]{:S(2)}) collective-permute-start(bf16[4,1,24,384]{3,0,2,1:T(4,128)(2,1)S(1)} %get-tuple-element.75), channel_id=1, source_target_pairs={{0,9},{1,10},{2,11},{3,12},{4,13},{5,14},{6,15}} | collective-permute-start | bytes 221192 | tf_op jit(solution)/shard_map/ppermute | solution.py:30
  24.2 5.5 %collective-permute-start.4 = (bf16[4,1,24,384]{3,0,2,1:T(4,128)(2,1)S(1)}, bf16[4,1,24,384]{3,0,2,1:T(4,128)(2,1)S(1)}, u32[]{:S(2)}, u32[]{:S(2)}) collective-permute-start(bf16[4,1,24,384]{3,0,2,1:T(4,128)(2,1)S(1)} %get-tuple-element.76), channel_id=1, source_target_pairs={{1,8},{2,9},{3,10},{4,11},{5,12},{6,13},{7,14}} | collective-permute-start | bytes 221192 | tf_op jit(solution)/shard_map/ppermute | solution.py:30
  30.2 2.1 %collective-permute-start.5 = (bf16[4,4,24,384]{3,2,1,0:T(8,128)(2,1)S(1)}, bf16[4,4,24,384]{3,2,1,0:T(8,128)(2,1)S(1)}, u32[]{:S(2)}, u32[]{:S(2)}) collective-permute-start(bf16[4,4,24,384]{3,2,1,0:T(8,128)(2,1)S(1)} %copy.23), channel_id=1, source_target_pairs={{8,16},{9,17},{10,18},{11,19},{12,20},{13,21},{14,22},{15,23}} | collective-permute-start | bytes 884744 | tf_op jit(solution)/shard_map/ppermute | solution.py:30
  30.9 1.4 %collective-permute-start.10 = (bf16[4,1,24,384]{3,2,1,0:T(8,128)(2,1)S(1)}, bf16[4,1,24,384]{3,2,1,0:T(8,128)(2,1)S(1)}, u32[]{:S(2)}, u32[]{:S(2)}) collective-permute-start(bf16[4,1,24,384]{3,2,1,0:T(8,128)(2,1)S(1)} %get-tuple-element.74), channel_id=1, source_target_pairs={{9,16},{10,17},{11,18},{12,19},{13,20},{14,21},{15,22}} | collective-permute-start | bytes 221192 | tf_op jit(solution)/shard_map/ppermute | solution.py:30
  31.6 0.7 collective-permute-start.9
  32.8 4.8 %collective-permute-start.12 = (bf16[4,4,24,384]{3,0,2,1:T(4,128)(2,1)S(1)}, bf16[4,4,24,384]{3,0,2,1:T(4,128)(2,1)S(1)}, u32[]{:S(2)}, u32[]{:S(2)}) collective-permute-start(bf16[4,4,24,384]{3,0,2,1:T(4,128)(2,1)S(1)} %copy.27), channel_id=1, source_target_pairs={{16,24},{17,25},{18,26},{19,27},{20,28},{21,29},{22,30},{23,31}} | collective-permute-start | bytes 884744 | tf_op jit(solution)/shard_map/ppermute | solution.py:30
  33.6 2.7 %collective-permute-start.11 = (bf16[4,1,24,384]{3,0,2,1:T(4,128)(2,1)S(1)}, bf16[4,1,24,384]{3,0,2,1:T(4,128)(2,1)S(1)}, u32[]{:S(2)}, u32[]{:S(2)}) collective-permute-start(bf16[4,1,24,384]{3,0,2,1:T(4,128)(2,1)S(1)} %get-tuple-element.71), channel_id=1, source_target_pairs={{16,25},{17,26},{18,27},{19,28},{20,29},{21,30},{22,31}} | collective-permute-start | bytes 221192 | tf_op jit(solution)/shard_map/ppermute | solution.py:30
  34.2 3.4 %collective-permute-start.13 = (bf16[4,1,24,384]{3,0,2,1:T(4,128)(2,1)S(1)}, bf16[4,1,24,384]{3,0,2,1:T(4,128)(2,1)S(1)}, u32[]{:S(2)}, u32[]{:S(2)}) collective-permute-start(bf16[4,1,24,384]{3,0,2,1:T(4,128)(2,1)S(1)} %get-tuple-element.72), channel_id=1, source_target_pairs={{17,24},{18,25},{19,26},{20,27},{21,28},{22,29},{23,30}} | collective-permute-start | bytes 221192 | tf_op jit(solution)/shard_map/ppermute | solution.py:30
  35.0 6.4 %collective-permute-start.6 = (bf16[1,4,24,384]{3,2,1,0:T(8,128)(2,1)S(1)}, bf16[1,4,24,384]{3,2,1,0:T(8,128)(2,1)S(1)}, u32[]{:S(2)}, u32[]{:S(2)}) collective-permute-start(bf16[1,4,24,384]{3,2,1,0:T(8,128)(2,1)S(1)} %get-tuple-element.67), channel_id=1, source_target_pairs={{16,24},{17,25},{18,26},{19,27},{20,28},{21,29},{22,30},{23,31}} | collective-permute-start | bytes 221192 | tf_op jit(solution)/shard_map/ppermute | solution.py:30
  35.6 7.0 %collective-permute-start.7 = (bf16[1,4,24,384]{3,2,1,0:T(8,128)(2,1)S(1)}, bf16[1,4,24,384]{3,2,1,0:T(8,128)(2,1)S(1)}, u32[]{:S(2)}, u32[]{:S(2)}) collective-permute-start(bf16[1,4,24,384]{3,2,1,0:T(8,128)(2,1)S(1)} %get-tuple-element.66), channel_id=1, source_target_pairs={{16,8},{17,9},{18,10},{19,11},{20,12},{21,13},{22,14},{23,15}} | collective-permute-start | bytes 221192 | tf_op jit(solution)/shard_map/ppermute | solution.py:30
  36.3 44.9 %collective-permute-start.8 = (bf16[1,4,24,384]{3,2,1,0:T(8,128)(2,1)S(1)}, bf16[1,4,24,384]{3,2,1,0:T(8,128)(2,1)S(1)}, u32[]{:S(2)}, u32[]{:S(2)}) collective-permute-start(bf16[1,4,24,384]{3,2,1,0:T(8,128)(2,1)S(1)} %get-tuple-element.65), channel_id=1, source_target_pairs={{16,0},{17,1},{18,2},{19,3},{20,4},{21,5},{22,6},{23,7}} | collective-permute-start | bytes 221192 | tf_op jit(solution)/shard_map/ppermute | solution.py:30
  40.0 41.2 %collective-permute-start.14 = (bf16[1,4,24,384]{3,2,1,0:T(8,128)(2,1)S(1)}, bf16[1,4,24,384]{3,2,1,0:T(8,128)(2,1)S(1)}, u32[]{:S(2)}, u32[]{:S(2)}) collective-permute-start(bf16[1,4,24,384]{3,2,1,0:T(8,128)(2,1)S(1)} %get-tuple-element.68), channel_id=1, source_target_pairs={{24,16},{25,17},{26,18},{27,19},{28,20},{29,21},{30,22},{31,23}} | collective-permute-start | bytes 221192 | tf_op jit(solution)/shard_map/ppermute | solution.py:30
  40.7 40.6 %collective-permute-start.15 = (bf16[1,4,24,384]{3,2,1,0:T(8,128)(2,1)S(1)}, bf16[1,4,24,384]{3,2,1,0:T(8,128)(2,1)S(1)}, u32[]{:S(2)}, u32[]{:S(2)}) collective-permute-start(bf16[1,4,24,384]{3,2,1,0:T(8,128)(2,1)S(1)} %get-tuple-element.70), channel_id=1, source_target_pairs={{24,8},{25,9},{26,10},{27,11},{28,12},{29,13},{30,14},{31,15}} | collective-permute-start | bytes 221192 | tf_op jit(solution)/shard_map/ppermute | solution.py:30
  41.4 64.6 %collective-permute-start.16 = (bf16[1,4,24,384]{3,2,1,0:T(8,128)(2,1)S(1)}, bf16[1,4,24,384]{3,2,1,0:T(8,128)(2,1)S(1)}, u32[]{:S(2)}, u32[]{:S(2)}) collective-permute-start(bf16[1,4,24,384]{3,2,1,0:T(8,128)(2,1)S(1)} %get-tuple-element.69), channel_id=1, source_target_pairs={{24,0},{25,1},{26,2},{27,3},{28,4},{29,5},{30,6},{31,7}} | collective-permute-start | bytes 221192 | tf_op jit(solution)/shard_map/ppermute | solution.py:30

commit v4 on v3

--- a/solution.py
+++ b/solution.py
@@ -68,15 +68,13 @@
         final = stage == last_stage
 
         def compute(window, skip, odd=odd, final=final):
-            convolved = causal_conv(activate(window, gain_row), kernel)
-            if final:
-                return convolved
-            if odd:
-                convolved = skip.astype(jnp.float32) + convolved
-            return convolved.astype(jnp.bfloat16)
+            convolved = causal_conv(activate(window, gain_row), kernel).astype(jnp.bfloat16)
+            if odd and not final:
+                convolved = (skip.astype(jnp.float32) + convolved).astype(jnp.bfloat16)
+            return convolved
 
-        def idle(window, skip, final=final):
-            return jnp.zeros(skip.shape, jnp.float32 if final else jnp.bfloat16)
+        def idle(window, skip):
+            return jnp.zeros(skip.shape, jnp.bfloat16)
 
         produced = lax.cond(segment_index == stage, compute, idle, window, skip)
         if final:
@@ -99,12 +97,10 @@
 
     branch = produced[last_stage * group :]
     for target in range(last_stage):
-        piece = send(
-            produced[target * group : (target + 1) * group].astype(jnp.bfloat16),
-            straight(last_stage, target),
-        )
-        branch = jnp.where(segment_index == target, piece.astype(jnp.float32), branch)
-    return (owned.astype(jnp.float32) + branch).astype(jnp.bfloat16)
+        chunk = produced[target * group : (target + 1) * group]
+        piece = send(chunk, straight(last_stage, target))
+        branch = jnp.where(segment_index == target, piece, branch)
+    return (owned.astype(jnp.float32) + branch.astype(jnp.float32)).astype(jnp.bfloat16)
 
 
 def solution(mesh):

time: 107 us -> 98.4 us (0.920)
  waiting for transfers between devices: 70.5 us -> 63.6 us
  other arithmetic: 4.51 us -> 3.38 us
    ppermute x15, waiting for transfers between devices: 67.4 us -> 60.6 us  [send(): return lax.ppermute(value, BOTH, pairs)]
    another operation x1 -> x0, other arithmetic: 1.1 us -> none
  transfers between devices with their start and end apart: 17 -> 17, of which waited for: 5 -> 5; matrix products, arithmetic and copies ran while one was open for 3% -> 1% of each run, Pallas kernels for 0% -> 0%
where the time goes in v4:
time: 98.4 us; the launch traced here: 98 us
  waiting for transfers between devices  63.6 us (65%)
  starting transfers between devices  19.6 us (20%)
  matrix products  7.91 us (8%)
  other arithmetic  3.38 us (3%)
  local copies, waits for them, and re-layouts  2.76 us (3%)
    ppermute x15, waiting for transfers between devices, send(): return lax.ppermute(value, BOTH, pairs)  60.6 us
    ppermute x15, starting transfers between devices, send(): return lax.ppermute(value, BOTH, pairs)  13.2 us
    conv_general_dilated x1, matrix products, causal_conv(): lax.conv_general_dilated(window[None], kernel, window_strides=(1, 1, 1),...  7.91 us
    ppermute x1, starting transfers between devices, local(): top = lax.ppermute(features[:, height - 1:], 'rows', up)  4.51 us
    ppermute x1, waiting for transfers between devices, local(): bottom = lax.ppermute(features[:, :1], 'rows', down)  3.03 us
  transfers between devices with their start and end apart: 17, of which 5 were waited for; matrix products, arithmetic and copies ran while one was open for 1% of the time, Pallas kernels for 0%

profile of v4, /device:TPU:1, one launch (start us, length us, event | category | flops | bytes accessed | tf_op | source)
XLA Modules:
  0.0 98.0 jit_solution(17967316694470730897)
XLA Ops:
  0.0 1.1 %copy.16 = bf16[4,4,24,384]{3,0,2,1:T(4,128)(2,1)S(1)} copy(bf16[4,4,24,384]{3,2,1,0:T(8,128)(2,1)} %param.11) | data formatting | bytes 589824 | tf_op args[0]
  1.1 0.1 fusion.86
  1.2 4.5 %collective-permute-start = (bf16[4,1,24,384]{3,0,2,1:T(4,128)(2,1)S(1)}, bf16[4,1,24,384]{3,0,2,1:T(4,128)(2,1)S(1)}, u32[]{:S(2)}, u32[]{:S(2)}) collective-permute-start(bf16[4,1,24,384]{3,0,2,1:T(4,128)(2,1)S(1)} %get-tuple-element.76), channel_id=1, source_target_pairs={{0,1},{1,2},{2,3},{3,4},{4,5},{5,6},{6,7},{8,9},{9,10},{10,11},{11... | collective-permute-start | bytes 221192 | tf_op jit(solution)/shard_map/ppermute | solution.py:59
  5.7 1.9 %collective-permute-start.1 = (bf16[4,1,24,384]{3,0,2,1:T(4,128)(2,1)S(1)}, bf16[4,1,24,384]{3,0,2,1:T(4,128)(2,1)S(1)}, u32[]{:S(2)}, u32[]{:S(2)}) collective-permute-start(bf16[4,1,24,384]{3,0,2,1:T(4,128)(2,1)S(1)} %get-tuple-element.77), channel_id=1, source_target_pairs={{1,0},{2,1},{3,2},{4,3},{5,4},{6,5},{7,6},{9,8},{10,9},{11,10},{12... | collective-permute-start | bytes 221192 | tf_op jit(solution)/shard_map/ppermute | solution.py:60
  7.6 0.7 reduce
  8.3 3.0 %collective-permute-done.1 = bf16[4,1,24,384]{3,0,2,1:T(4,128)(2,1)S(1)} collective-permute-done((bf16[4,1,24,384]{3,0,2,1:T(4,128)(2,1)S(1)}, bf16[4,1,24,384]{3,0,2,1:T(4,128)(2,1)S(1)}, u32[]{:S(2)}, u32[]{:S(2)}) %collective-permute-start.1) | collective-permute-done | bytes 73760 | tf_op jit(solution)/shard_map/ppermute | solution.py:60
  11.4 0.3 pad_maximum_fusion
  11.7 9.6 %conditional.4 = (bf16[4,4,24,384]{3,1,2,0:T(4,128)(2,1)S(1)}) conditional(s32[]{:T(128)} %convert_element_type.92, () %tuple.30, (bf16[4,6,24,384]{3,0,2,1:T(4,128)(2,1)S(1)}, bf16[384]{0:T(512)(128)(2,1)S(1)}, bf16[3,3,3,384,384]{4,3,2,1,0:T(8,128)(2,1)}) %tuple.57), branch_computations={%region_0.0_spmd, %region_1.3_spmd} | conditional | flops 3063129088 | bytes 14648262 | solution.py:79
  11.7 0.3 fusion.2
  12.1 0.6 fusion.14
  12.7 0.2 pad
  12.9 0.1 copy.5
  13.0 0.1 slice.72
  13.1 7.9 %fusion.1 = bf16[4,4,8,4,384]{4,2,3,1,0:T(8,128)(2,1)S(1)} fusion(bf16[3,3,3,384,384]{4,3,2,1,0:T(8,128)(2,1)} %get-tuple-element.44, bf16[4,6,1,7,2,384]{5,3,4,1,0,2:T(8,128)(2,1)S(1)} %slice.72, bf16[4,6,1,8,4,384]{5,3,4,1,0,2:T(8,128)(2,1)S(1)} %copy.5, pred[8,4]{0,1:T(4,128)(4,1)S(1)} %copy-done.1), kind=kOutput, calls=%fused_computation.3 | convolution fusion | flops 3060695040 | bytes 9203744 | tf_op jit(solution)/shard_map/cond/branch_1_fun/conv_general_dilated | solution.py:18
  21.0 0.2 copy.6
  21.2 0.1 slice_bitcast_fusion
  21.4 0.2 copy.19
  21.5 1.3 %collective-permute-start.3 = (bf16[4,4,24,384]{3,0,2,1:T(4,128)(2,1)S(1)}, bf16[4,4,24,384]{3,0,2,1:T(4,128)(2,1)S(1)}, u32[]{:S(2)}, u32[]{:S(2)}) collective-permute-start(bf16[4,4,24,384]{3,0,2,1:T(4,128)(2,1)S(1)} %copy.19), channel_id=1, source_target_pairs={{0,8},{1,9},{2,10},{3,11},{4,12},{5,13},{6,14},{7,15}} | collective-permute-start | bytes 884744 | tf_op jit(solution)/shard_map/ppermute | solution.py:30
  22.9 1.3 %collective-permute-start.2 = (bf16[4,1,24,384]{3,0,2,1:T(4,128)(2,1)S(1)}, bf16[4,1,24,384]{3,0,2,1:T(4,128)(2,1)S(1)}, u32[]{:S(2)}, u32[]{:S(2)}) collective-permute-start(bf16[4,1,24,384]{3,0,2,1:T(4,128)(2,1)S(1)} %get-tuple-element.74), channel_id=1, source_target_pairs={{0,9},{1,10},{2,11},{3,12},{4,13},{5,14},{6,15}} | collective-permute-start | bytes 221192 | tf_op jit(solution)/shard_map/ppermute | solution.py:30
  24.2 1.3 %collective-permute-start.4 = (bf16[4,1,24,384]{3,0,2,1:T(4,128)(2,1)S(1)}, bf16[4,1,24,384]{3,0,2,1:T(4,128)(2,1)S(1)}, u32[]{:S(2)}, u32[]{:S(2)}) collective-permute-start(bf16[4,1,24,384]{3,0,2,1:T(4,128)(2,1)S(1)} %get-tuple-element.75), channel_id=1, source_target_pairs={{1,8},{2,9},{3,10},{4,11},{5,12},{6,13},{7,14}} | collective-permute-start | bytes 221192 | tf_op jit(solution)/shard_map/ppermute | solution.py:30
  25.5 3.4 %collective-permute-done.2 = bf16[4,1,24,384]{3,0,2,1:T(4,128)(2,1)S(1)} collective-permute-done((bf16[4,1,24,384]{3,0,2,1:T(4,128)(2,1)S(1)}, bf16[4,1,24,384]{3,0,2,1:T(4,128)(2,1)S(1)}, u32[]{:S(2)}, u32[]{:S(2)}) %collective-permute-start.2) | collective-permute-done | bytes 73760 | tf_op jit(solution)/shard_map/ppermute | solution.py:30
  28.9 0.8 collective-permute-done.4
  29.7 0.3 pad_maximum_fusion.1
  30.0 0.1 conditional.5
  30.1 0.1 broadcast.80
  30.2 0.7 collective-permute-start.5
  30.9 0.7 collective-permute-start.10
  31.6 0.7 collective-permute-start.9
  32.3 0.1 pad_maximum_fusion.2
  32.4 0.3 conditional.6
  32.4 0.1 broadcast.83
  32.7 0.2 copy.27
  32.8 0.7 collective-permute-start.12
  33.6 0.7 collective-permute-start.11
  34.2 0.7 collective-permute-start.13
  34.9 0.7 collective-permute-start.6
  35.6 0.7 collective-permute-start.7
  36.3 1.3 %collective-permute-start.8 = (bf16[1,4,24,384]{3,2,1,0:T(8,128)(2,1)S(1)}, bf16[1,4,24,384]{3,2,1,0:T(8,128)(2,1)S(1)}, u32[]{:S(2)}, u32[]{:S(2)}) collective-permute-start(bf16[1,4,24,384]{3,2,1,0:T(8,128)(2,1)S(1)} %get-tuple-element.71), channel_id=1, source_target_pairs={{16,0},{17,1},{18,2},{19,3},{20,4},{21,5},{22,6},{23,7}} | collective-permute-start | bytes 221192 | tf_op jit(solution)/shard_map/ppermute | solution.py:30
  37.6 0.3 pad_maximum_fusion.3
  38.0 0.1 conditional.7
  38.0 0.1 broadcast.86
  38.1 0.1 fusion.81
  38.2 0.7 collective-permute-start.14
  38.9 0.7 collective-permute-start.15
  39.6 1.3 %collective-permute-start.16 = (bf16[1,4,24,384]{3,2,1,0:T(8,128)(2,1)S(1)}, bf16[1,4,24,384]{3,2,1,0:T(8,128)(2,1)S(1)}, u32[]{:S(2)}, u32[]{:S(2)}) collective-permute-start(bf16[1,4,24,384]{3,2,1,0:T(8,128)(2,1)S(1)} %copy.36), channel_id=1, source_target_pairs={{24,0},{25,1},{26,2},{27,3},{28,4},{29,5},{30,6},{31,7}} | collective-permute-start | bytes 221192 | tf_op jit(solution)/shard_map/ppermute | solution.py:30
  40.9 37.4 %collective-permute-done.8 = bf16[1,4,24,384]{3,2,1,0:T(8,128)(2,1)S(1)} collective-permute-done((bf16[1,4,24,384]{3,2,1,0:T(8,128)(2,1)S(1)}, bf16[1,4,24,384]{3,2,1,0:T(8,128)(2,1)S(1)}, u32[]{:S(2)}, u32[]{:S(2)}) %collective-permute-start.8) | collective-permute-done | bytes 73760 | tf_op jit(solution)/shard_map/ppermute | solution.py:30
  78.3 19.0 %collective-permute-done.16 = bf16[1,4,24,384]{3,2,1,0:T(8,128)(2,1)S(1)} collective-permute-done((bf16[1,4,24,384]{3,2,1,0:T(8,128)(2,1)S(1)}, bf16[1,4,24,384]{3,2,1,0:T(8,128)(2,1)S(1)}, u32[]{:S(2)}, u32[]{:S(2)}) %collective-permute-start.16) | collective-permute-done | bytes 73760 | tf_op jit(solution)/shard_map/ppermute | solution.py:30
  97.3 0.7 add_convert_fusion
  (26 shorter events, 0.3 us)
Async XLA Ops:
  1.2 7.2 %collective-permute-start = (bf16[4,1,24,384]{3,0,2,1:T(4,128)(2,1)S(1)}, bf16[4,1,24,384]{3,0,2,1:T(4,128)(2,1)S(1)}, u32[]{:S(2)}, u32[]{:S(2)}) collective-permute-start(bf16[4,1,24,384]{3,0,2,1:T(4,128)(2,1)S(1)} %get-tuple-element.76), channel_id=1, source_target_pairs={{0,1},{1,2},{2,3},{3,4},{4,5},{5,6},{6,7},{8,9},{9,10},{10,11},{11... | collective-permute-start | bytes 221192 | tf_op jit(solution)/shard_map/ppermute | solution.py:59
  5.7 5.7 %collective-permute-start.1 = (bf16[4,1,24,384]{3,0,2,1:T(4,128)(2,1)S(1)}, bf16[4,1,24,384]{3,0,2,1:T(4,128)(2,1)S(1)}, u32[]{:S(2)}, u32[]{:S(2)}) collective-permute-start(bf16[4,1,24,384]{3,0,2,1:T(4,128)(2,1)S(1)} %get-tuple-element.77), channel_id=1, source_target_pairs={{1,0},{2,1},{3,2},{4,3},{5,4},{6,5},{7,6},{9,8},{10,9},{11,10},{12... | collective-permute-start | bytes 221192 | tf_op jit(solution)/shard_map/ppermute | solution.py:60
  12.1 1.0 %copy-start.1 = (pred[8,4]{0,1:T(4,128)(4,1)S(1)}, pred[8,4]{0,1:T(4,128)(4,1)}, u32[]{:S(2)}) copy-start(pred[8,4]{0,1:T(4,128)(4,1)} %constant.80) | copy-start | bytes 100 | tf_op jit(solution)/shard_map/cond
  21.4 8.7 %copy-start = (bf16[4,4,24,384]{3,2,1,0:T(8,128)(2,1)S(1)}, bf16[4,4,24,384]{3,2,1,0:T(8,128)(2,1)}, u32[]{:S(2)}) copy-start(bf16[4,4,24,384]{3,2,1,0:T(8,128)(2,1)} %param.11) | copy-start | bytes 884740
  21.5 8.2 %collective-permute-start.3 = (bf16[4,4,24,384]{3,0,2,1:T(4,128)(2,1)S(1)}, bf16[4,4,24,384]{3,0,2,1:T(4,128)(2,1)S(1)}, u32[]{:S(2)}, u32[]{:S(2)}) collective-permute-start(bf16[4,4,24,384]{3,0,2,1:T(4,128)(2,1)S(1)} %copy.19), channel_id=1, source_target_pairs={{0,8},{1,9},{2,10},{3,11},{4,12},{5,13},{6,14},{7,15}} | collective-permute-start | bytes 884744 | tf_op jit(solution)/shard_map/ppermute | solution.py:30
  22.9 6.0 %collective-permute-start.2 = (bf16[4,1,24,384]{3,0,2,1:T(4,128)(2,1)S(1)}, bf16[4,1,24,384]{3,0,2,1:T(4,128)(2,1)S(1)}, u32[]{:S(2)}, u32[]{:S(2)}) collective-permute-start(bf16[4,1,24,384]{3,0,2,1:T(4,128)(2,1)S(1)} %get-tuple-element.74), channel_id=1, source_target_pairs={{0,9},{1,10},{2,11},{3,12},{4,13},{5,14},{6,15}} | collective-permute-start | bytes 221192 | tf_op jit(solution)/shard_map/ppermute | solution.py:30
  24.2 5.5 %collective-permute-start.4 = (bf16[4,1,24,384]{3,0,2,1:T(4,128)(2,1)S(1)}, bf16[4,1,24,384]{3,0,2,1:T(4,128)(2,1)S(1)}, u32[]{:S(2)}, u32[]{:S(2)}) collective-permute-start(bf16[4,1,24,384]{3,0,2,1:T(4,128)(2,1)S(1)} %get-tuple-element.75), channel_id=1, source_target_pairs={{1,8},{2,9},{3,10},{4,11},{5,12},{6,13},{7,14}} | collective-permute-start | bytes 221192 | tf_op jit(solution)/shard_map/ppermute | solution.py:30
  30.2 2.1 %collective-permute-start.5 = (bf16[4,4,24,384]{3,2,1,0:T(8,128)(2,1)S(1)}, bf16[4,4,24,384]{3,2,1,0:T(8,128)(2,1)S(1)}, u32[]{:S(2)}, u32[]{:S(2)}) collective-permute-start(bf16[4,4,24,384]{3,2,1,0:T(8,128)(2,1)S(1)} %copy.23), channel_id=1, source_target_pairs={{8,16},{9,17},{10,18},{11,19},{12,20},{13,21},{14,22},{15,23}} | collective-permute-start | bytes 884744 | tf_op jit(solution)/shard_map/ppermute | solution.py:30
  30.9 1.4 %collective-permute-start.10 = (bf16[4,1,24,384]{3,2,1,0:T(8,128)(2,1)S(1)}, bf16[4,1,24,384]{3,2,1,0:T(8,128)(2,1)S(1)}, u32[]{:S(2)}, u32[]{:S(2)}) collective-permute-start(bf16[4,1,24,384]{3,2,1,0:T(8,128)(2,1)S(1)} %get-tuple-element.70), channel_id=1, source_target_pairs={{9,16},{10,17},{11,18},{12,19},{13,20},{14,21},{15,22}} | collective-permute-start | bytes 221192 | tf_op jit(solution)/shard_map/ppermute | solution.py:30
  31.6 0.7 collective-permute-start.9
  32.8 4.8 %collective-permute-start.12 = (bf16[4,4,24,384]{3,0,2,1:T(4,128)(2,1)S(1)}, bf16[4,4,24,384]{3,0,2,1:T(4,128)(2,1)S(1)}, u32[]{:S(2)}, u32[]{:S(2)}) collective-permute-start(bf16[4,4,24,384]{3,0,2,1:T(4,128)(2,1)S(1)} %copy.27), channel_id=1, source_target_pairs={{16,24},{17,25},{18,26},{19,27},{20,28},{21,29},{22,30},{23,31}} | collective-permute-start | bytes 884744 | tf_op jit(solution)/shard_map/ppermute | solution.py:30
  33.6 2.7 %collective-permute-start.11 = (bf16[4,1,24,384]{3,0,2,1:T(4,128)(2,1)S(1)}, bf16[4,1,24,384]{3,0,2,1:T(4,128)(2,1)S(1)}, u32[]{:S(2)}, u32[]{:S(2)}) collective-permute-start(bf16[4,1,24,384]{3,0,2,1:T(4,128)(2,1)S(1)} %get-tuple-element.67), channel_id=1, source_target_pairs={{16,25},{17,26},{18,27},{19,28},{20,29},{21,30},{22,31}} | collective-permute-start | bytes 221192 | tf_op jit(solution)/shard_map/ppermute | solution.py:30
  34.2 3.4 %collective-permute-start.13 = (bf16[4,1,24,384]{3,0,2,1:T(4,128)(2,1)S(1)}, bf16[4,1,24,384]{3,0,2,1:T(4,128)(2,1)S(1)}, u32[]{:S(2)}, u32[]{:S(2)}) collective-permute-start(bf16[4,1,24,384]{3,0,2,1:T(4,128)(2,1)S(1)} %get-tuple-element.68), channel_id=1, source_target_pairs={{17,24},{18,25},{19,26},{20,27},{21,28},{22,29},{23,30}} | collective-permute-start | bytes 221192 | tf_op jit(solution)/shard_map/ppermute | solution.py:30
  34.9 4.7 %collective-permute-start.6 = (bf16[1,4,24,384]{3,2,1,0:T(8,128)(2,1)S(1)}, bf16[1,4,24,384]{3,2,1,0:T(8,128)(2,1)S(1)}, u32[]{:S(2)}, u32[]{:S(2)}) collective-permute-start(bf16[1,4,24,384]{3,2,1,0:T(8,128)(2,1)S(1)} %get-tuple-element.73), channel_id=1, source_target_pairs={{16,24},{17,25},{18,26},{19,27},{20,28},{21,29},{22,30},{23,31}} | collective-permute-start | bytes 221192 | tf_op jit(solution)/shard_map/ppermute | solution.py:30
  35.6 5.3 %collective-permute-start.7 = (bf16[1,4,24,384]{3,2,1,0:T(8,128)(2,1)S(1)}, bf16[1,4,24,384]{3,2,1,0:T(8,128)(2,1)S(1)}, u32[]{:S(2)}, u32[]{:S(2)}) collective-permute-start(bf16[1,4,24,384]{3,2,1,0:T(8,128)(2,1)S(1)} %get-tuple-element.72), channel_id=1, source_target_pairs={{16,8},{17,9},{18,10},{19,11},{20,12},{21,13},{22,14},{23,15}} | collective-permute-start | bytes 221192 | tf_op jit(solution)/shard_map/ppermute | solution.py:30
  36.3 42.0 %collective-permute-start.8 = (bf16[1,4,24,384]{3,2,1,0:T(8,128)(2,1)S(1)}, bf16[1,4,24,384]{3,2,1,0:T(8,128)(2,1)S(1)}, u32[]{:S(2)}, u32[]{:S(2)}) collective-permute-start(bf16[1,4,24,384]{3,2,1,0:T(8,128)(2,1)S(1)} %get-tuple-element.71), channel_id=1, source_target_pairs={{16,0},{17,1},{18,2},{19,3},{20,4},{21,5},{22,6},{23,7}} | collective-permute-start | bytes 221192 | tf_op jit(solution)/shard_map/ppermute | solution.py:30
  38.2 40.1 %collective-permute-start.14 = (bf16[1,4,24,384]{3,2,1,0:T(8,128)(2,1)S(1)}, bf16[1,4,24,384]{3,2,1,0:T(8,128)(2,1)S(1)}, u32[]{:S(2)}, u32[]{:S(2)}) collective-permute-start(bf16[1,4,24,384]{3,2,1,0:T(8,128)(2,1)S(1)} %copy.34), channel_id=1, source_target_pairs={{24,16},{25,17},{26,18},{27,19},{28,20},{29,21},{30,22},{31,23}} | collective-permute-start | bytes 221192 | tf_op jit(solution)/shard_map/ppermute | solution.py:30
  38.9 39.4 %collective-permute-start.15 = (bf16[1,4,24,384]{3,2,1,0:T(8,128)(2,1)S(1)}, bf16[1,4,24,384]{3,2,1,0:T(8,128)(2,1)S(1)}, u32[]{:S(2)}, u32[]{:S(2)}) collective-permute-start(bf16[1,4,24,384]{3,2,1,0:T(8,128)(2,1)S(1)} %copy.35), channel_id=1, source_target_pairs={{24,8},{25,9},{26,10},{27,11},{28,12},{29,13},{30,14},{31,15}} | collective-permute-start | bytes 221192 | tf_op jit(solution)/shard_map/ppermute | solution.py:30
  39.6 57.7 %collective-permute-start.16 = (bf16[1,4,24,384]{3,2,1,0:T(8,128)(2,1)S(1)}, bf16[1,4,24,384]{3,2,1,0:T(8,128)(2,1)S(1)}, u32[]{:S(2)}, u32[]{:S(2)}) collective-permute-start(bf16[1,4,24,384]{3,2,1,0:T(8,128)(2,1)S(1)} %copy.36), channel_id=1, source_target_pairs={{24,0},{25,1},{26,2},{27,3},{28,4},{29,5},{30,6},{31,7}} | collective-permute-start | bytes 221192 | tf_op jit(solution)/shard_map/ppermute | solution.py:30

commit v5 on v1

v5 whole, which is shorter than its diff:
```python
import jax
import jax.numpy as jnp
from jax import lax
from jax.sharding import PartitionSpec as P

BOTH = ("segment", "rows")


def activate(values_in, gain_row):
    widened = values_in.astype(jnp.float32)
    mean_square = jnp.mean(widened * widened, axis=-1, keepdims=True)
    return jax.nn.silu(
        widened * lax.rsqrt(mean_square + 1e-06) * gain_row.astype(jnp.float32)
    ).astype(jnp.bfloat16)


def causal_conv(window, kernel):
    result = lax.conv_general_dilated(
        window[None],
        kernel,
        window_strides=(1, 1, 1),
        padding=((2, 0), (0, 0), (1, 1)),
        dimension_numbers=("NDHWC", "DHWIO", "NDHWC"),
        preferred_element_type=jnp.float32,
    )
    return result[0]


def send(value, pairs):
    return lax.ppermute(value, BOTH, pairs)


def local(features, gains, kernels):
    segment_count = lax.axis_size("segment")
    row_count = lax.axis_size("rows")
    segment_index = lax.axis_index("segment")
    frame_count, height, columns, channels = features.shape
    size = 2 if frame_count % 2 == 0 else 1
    groups = frame_count // size
    owned_frames = frame_count // segment_count
    last = segment_count - 1
    gain_row = gains[0]
    kernel = kernels[0]

    def straight(source, target):
        return [(source * row_count + r, target * row_count + r) for r in range(row_count)]

    senders = range(segment_count - 1)
    body_pairs = [p for k in senders for p in straight(k, k + 1)]
    top_pairs = [
        (k * row_count + r, (k + 1) * row_count + r + 1)
        for k in senders
        for r in range(row_count - 1)
    ]
    bottom_pairs = [
        (k * row_count + r, (k + 1) * row_count + r - 1)
        for k in senders
        for r in range(1, row_count)
    ]
    skip_pairs = [p for k in range(2, segment_count - 2, 2) for p in straight(k, k + 1)]

    up = [(i, i + 1) for i in range(row_count - 1)]
    down = [(i + 1, i) for i in range(row_count - 1)]
    features_top = lax.ppermute(features[:, height - 1 :], "rows", up)
    features_bottom = lax.ppermute(features[:, :1], "rows", down)

    body_in = jnp.zeros((size, height, columns, channels), jnp.bfloat16)
    top_in = jnp.zeros((size, 1, columns, channels), jnp.bfloat16)
    bottom_in = top_in
    skip_in = body_in
    cache = jnp.zeros((2, height + 2, columns, channels), jnp.bfloat16)
    decoded = jnp.zeros(features.shape, jnp.bfloat16)
    block_input = jnp.zeros(features.shape, jnp.bfloat16)
    first_stage = segment_index == 0
    adds_skip = jnp.logical_and(segment_index % 2 == 1, segment_index != last)

    wavefronts = segment_count + groups - 1
    for wave in range(wavefronts):
        group = wave - segment_index
        valid = jnp.logical_and(group >= 0, group < groups)
        start = jnp.clip(group, 0, groups - 1) * size
        local_body = lax.dynamic_slice_in_dim(features, start, size, 0)
        body = jnp.where(first_stage, local_body, body_in)
        top = jnp.where(
            first_stage, lax.dynamic_slice_in_dim(features_top, start, size, 0), top_in
        )
        bottom = jnp.where(
            first_stage, lax.dynamic_slice_in_dim(features_bottom, start, size, 0), bottom_in
        )
        window = activate(jnp.concatenate([top, body, bottom], axis=1), gain_row)
        full = jnp.concatenate([cache, window], axis=0)
        convolved = lax.conv_general_dilated(
            full[None],
            kernel,
            window_strides=(1, 1, 1),
            padding=((0, 0), (0, 0), (1, 1)),
            dimension_numbers=("NDHWC", "DHWIO", "NDHWC"),
            preferred_element_type=jnp.float32,
        )[0].astype(jnp.bfloat16)
        skip = jnp.where(segment_index == 1, local_body, skip_in)
        summed = (skip.astype(jnp.float32) + convolved.astype(jnp.float32)).astype(
            jnp.bfloat16
        )
        produced = jnp.where(adds_skip, summed, convolved)
        cache = jnp.where(valid, full[size:], cache)
        decoded = jnp.where(
            jnp.logical_and(valid, segment_index == last),
            lax.dynamic_update_slice_in_dim(decoded, produced, start, 0),
            decoded,
        )
        block_input = jnp.where(
            jnp.logical_and(valid, segment_index == last - 1),
            lax.dynamic_update_slice_in_dim(block_input, body, start, 0),
            block_input,
        )
        if wave < wavefronts - 1:
            body_in = send(produced, body_pairs)
            top_in = send(produced[:, height - 1 :], top_pairs)
            bottom_in = send(produced[:, :1], bottom_pairs)
            if skip_pairs:
                skip_in = send(body, skip_pairs)

    def frames_of(array, target):
        return array[target * owned_frames : (target + 1) * owned_frames]

    held_input = frames_of(block_input, last - 1)
    held_branch = frames_of(decoded, last)
    for target in range(segment_count):
        if target != last - 1:
            piece = send(frames_of(block_input, target), straight(last - 1, target))
            held_input = jnp.where(segment_index == target, piece, held_input)
        if target != last:
            piece = send(frames_of(decoded, target), straight(last, target))
            held_branch = jnp.where(segment_index == target, piece, held_branch)
    return (held_input.astype(jnp.float32) + held_branch.astype(jnp.float32)).astype(
        jnp.bfloat16
    )


def solution(mesh):
    placed = (
        P(None, "rows", None, None),
        P("segment", None),
        P("segment", None, None, None, None, None),
    )
    return jax.shard_map(
        local,
        mesh=mesh,
        in_specs=placed,
        out_specs=P("segment", "rows", None, None),
        check_vma=False,
    )
```

time: 119 us -> 115 us (0.966)
  the two profiles are of different devices: /device:TPU:1 before, /device:TPU:0 now
where the time goes in v5:
time: 115 us; the launch traced here: 114 us
  starting transfers between devices  48.5 us (42%)
  matrix products  31.1 us (27%)
  waiting for transfers between devices  23 us (20%)
  other arithmetic  5.75 us (5%)
  local copies, waits for them, and re-layouts  4.81 us (4%)
    ppermute x18, starting transfers between devices, send(): return lax.ppermute(value, BOTH, pairs)  44.2 us
    conv_general_dilated x5, matrix products, local(): lax.conv_general_dilated(full[None], kernel, window_strides=(1, 1, 1), pa...  31.1 us
    ppermute x18, waiting for transfers between devices, send(): return lax.ppermute(value, BOTH, pairs)  23 us
    ppermute x1, starting transfers between devices, local(): features_top = lax.ppermute(features[:, height - 1:], 'rows', up)  3.03 us
  transfers between devices with their start and end apart: 20, of which 6 were waited for; matrix products, arithmetic and copies ran while one was open for 2% of the time, Pallas kernels for 0%

profile of v5, /device:TPU:0, one launch (start us, length us, event | category | flops | bytes accessed | tf_op | source)
XLA Modules:
  0.0 114.2 jit_solution(17156698279564953791)
XLA Ops:
  0.0 0.9 fusion.154
  0.9 1.3 %collective-permute-start.1 = (bf16[4,1,24,384]{3,2,1,0:T(8,128)(2,1)S(1)}, bf16[4,1,24,384]{3,2,1,0:T(8,128)(2,1)S(1)}, u32[]{:S(2)}, u32[]{:S(2)}) collective-permute-start(bf16[4,1,24,384]{3,2,1,0:T(8,128)(2,1)S(1)} %get-tuple-element.36), channel_id=1, source_target_pairs={{1,0},{2,1},{3,2},{4,3},{5,4},{6,5},{7,6},{9,8},{10,9},{11,10},{12... | collective-permute-start | bytes 221192 | tf_op jit(solution)/shard_map/ppermute | solution.py:65
  2.2 3.0 %collective-permute-start = (bf16[4,1,24,384]{3,2,1,0:T(8,128)(2,1)S(1)}, bf16[4,1,24,384]{3,2,1,0:T(8,128)(2,1)S(1)}, u32[]{:S(2)}, u32[]{:S(2)}) collective-permute-start(bf16[4,1,24,384]{3,2,1,0:T(8,128)(2,1)S(1)} %get-tuple-element.35), channel_id=1, source_target_pairs={{0,1},{1,2},{2,3},{3,4},{4,5},{5,6},{6,7},{8,9},{9,10},{10,11},{11... | collective-permute-start | bytes 221192 | tf_op jit(solution)/shard_map/ppermute | solution.py:64
  5.4 1.0 select_dynamic-update-slice_fusion.8
  6.3 0.7 convert_reduce_fusion
  7.2 0.2 fusion.82
  7.5 0.2 copy.62
  7.7 0.2 pad.1.clone
  8.2 6.3 %fusion.42 = bf16[2,4,8,4,384]{4,2,3,1,0:T(8,128)(2,1)S(1)} fusion(bf16[1,3,3,3,384,384]{5,4,3,2,1,0:T(8,128)(2,1)} %param.5, bf16[4,6,1,7,2,384]{5,3,4,1,0,2:T(8,128)(2,1)S(1)} %slice.82, bf16[4,6,1,8,4,384]{5,3,4,1,0,2:T(8,128)(2,1)S(1)} %copy.34, pred[8,4]{0,1:T(4,128)(4,1)S(1)} %copy-done.1), kind=kOutput, calls=%fused_computation.25 | convolution fusion | flops 2041282560 | bytes 9007136 | tf_op jit(solution)/shard_map/conv_general_dilated | solution.py:92
  14.8 5.6 %collective-permute-start.3 = (bf16[2,1,24,384]{3,2,1,0:T(8,128)(2,1)S(1)}, bf16[2,1,24,384]{3,2,1,0:T(8,128)(2,1)S(1)}, u32[]{:S(2)}, u32[]{:S(2)}) collective-permute-start(bf16[2,1,24,384]{3,2,1,0:T(8,128)(2,1)S(1)} %get-tuple-element.43), channel_id=1, source_target_pairs={{0,9},{1,10},{2,11},{3,12},{4,13},{5,14},{6,15},{8,17},{9,18},{10,... | collective-permute-start | bytes 110600 | tf_op jit(solution)/shard_map/ppermute | solution.py:30
  20.4 3.5 %collective-permute-start.2 = (bf16[2,4,24,384]{3,2,1,0:T(8,128)(2,1)S(1)}, bf16[2,4,24,384]{3,2,1,0:T(8,128)(2,1)S(1)}, u32[]{:S(2)}, u32[]{:S(2)}) collective-permute-start(bf16[2,4,24,384]{3,2,1,0:T(8,128)(2,1)S(1)} %get-tuple-element.28), channel_id=1, source_target_pairs={{0,8},{1,9},{2,10},{3,11},{4,12},{5,13},{6,14},{7,15},{8,16},{9,17... | collective-permute-start | bytes 442376 | tf_op jit(solution)/shard_map/ppermute | solution.py:30
  23.9 0.7 collective-permute-start.4
  24.7 2.7 %collective-permute-done.2 = bf16[2,4,24,384]{3,2,1,0:T(8,128)(2,1)S(1)} collective-permute-done((bf16[2,4,24,384]{3,2,1,0:T(8,128)(2,1)S(1)}, bf16[2,4,24,384]{3,2,1,0:T(8,128)(2,1)S(1)}, u32[]{:S(2)}, u32[]{:S(2)}) %collective-permute-start.2) | collective-permute-done | bytes 147488 | tf_op jit(solution)/shard_map/ppermute | solution.py:30
  27.6 0.4 broadcast_select_fusion.2
  28.0 0.2 copy.63
  28.2 0.2 pad.3.clone
  28.6 6.2 %fusion.39 = bf16[2,4,8,4,384]{4,2,3,1,0:T(8,128)(2,1)S(1)} fusion(bf16[1,3,3,3,384,384]{5,4,3,2,1,0:T(8,128)(2,1)} %param.5, bf16[4,6,1,7,2,384]{5,3,4,1,0,2:T(8,128)(2,1)S(1)} %slice.86, bf16[4,6,1,8,4,384]{5,3,4,1,0,2:T(8,128)(2,1)S(1)} %copy.39, pred[8,4]{0,1:T(4,128)(4,1)S(1)} %copy-done.1), kind=kOutput, calls=%fused_computation.24 | convolution fusion | flops 2041282560 | bytes 9007136 | tf_op jit(solution)/shard_map/conv_general_dilated | solution.py:92
  35.2 7.4 %collective-permute-start.6 = (bf16[2,1,24,384]{3,2,1,0:T(8,128)(2,1)S(1)}, bf16[2,1,24,384]{3,2,1,0:T(8,128)(2,1)S(1)}, u32[]{:S(2)}, u32[]{:S(2)}) collective-permute-start(bf16[2,1,24,384]{3,2,1,0:T(8,128)(2,1)S(1)} %get-tuple-element.41), channel_id=1, source_target_pairs={{0,9},{1,10},{2,11},{3,12},{4,13},{5,14},{6,15},{8,17},{9,18},{10,... | collective-permute-start | bytes 110600 | tf_op jit(solution)/shard_map/ppermute | solution.py:30
  42.6 2.6 %collective-permute-start.5 = (bf16[2,4,24,384]{3,2,1,0:T(8,128)(2,1)S(1)}, bf16[2,4,24,384]{3,2,1,0:T(8,128)(2,1)S(1)}, u32[]{:S(2)}, u32[]{:S(2)}) collective-permute-start(bf16[2,4,24,384]{3,2,1,0:T(8,128)(2,1)S(1)} %get-tuple-element.26), channel_id=1, source_target_pairs={{0,8},{1,9},{2,10},{3,11},{4,12},{5,13},{6,14},{7,15},{8,16},{9,17... | collective-permute-start | bytes 442376 | tf_op jit(solution)/shard_map/ppermute | solution.py:30
  45.2 0.8 collective-permute-start.7
  46.1 2.7 %collective-permute-done.5 = bf16[2,4,24,384]{3,2,1,0:T(8,128)(2,1)S(1)} collective-permute-done((bf16[2,4,24,384]{3,2,1,0:T(8,128)(2,1)S(1)}, bf16[2,4,24,384]{3,2,1,0:T(8,128)(2,1)S(1)}, u32[]{:S(2)}, u32[]{:S(2)}) %collective-permute-start.5) | collective-permute-done | bytes 147488 | tf_op jit(solution)/shard_map/ppermute | solution.py:30
  49.0 0.2 fusion.98
  49.3 0.2 copy.64
  49.5 0.2 pad.5.clone
  49.9 6.2 %fusion.36 = bf16[2,4,8,4,384]{4,2,3,1,0:T(8,128)(2,1)S(1)} fusion(bf16[1,3,3,3,384,384]{5,4,3,2,1,0:T(8,128)(2,1)} %param.5, bf16[4,6,1,7,2,384]{5,3,4,1,0,2:T(8,128)(2,1)S(1)} %slice.90, bf16[4,6,1,8,4,384]{5,3,4,1,0,2:T(8,128)(2,1)S(1)} %copy.44, pred[8,4]{0,1:T(4,128)(4,1)S(1)} %copy-done.1), kind=kOutput, calls=%fused_computation.23 | convolution fusion | flops 2041282560 | bytes 9007136 | tf_op jit(solution)/shard_map/conv_general_dilated | solution.py:92
  56.4 7.6 %collective-permute-start.9 = (bf16[2,1,24,384]{3,2,1,0:T(8,128)(2,1)S(1)}, bf16[2,1,24,384]{3,2,1,0:T(8,128)(2,1)S(1)}, u32[]{:S(2)}, u32[]{:S(2)}) collective-permute-start(bf16[2,1,24,384]{3,2,1,0:T(8,128)(2,1)S(1)} %get-tuple-element.39), channel_id=1, source_target_pairs={{0,9},{1,10},{2,11},{3,12},{4,13},{5,14},{6,15},{8,17},{9,18},{10,... | collective-permute-start | bytes 110600 | tf_op jit(solution)/shard_map/ppermute | solution.py:30
  64.1 2.2 %collective-permute-start.8 = (bf16[2,4,24,384]{3,2,1,0:T(8,128)(2,1)S(1)}, bf16[2,4,24,384]{3,2,1,0:T(8,128)(2,1)S(1)}, u32[]{:S(2)}, u32[]{:S(2)}) collective-permute-start(bf16[2,4,24,384]{3,2,1,0:T(8,128)(2,1)S(1)} %get-tuple-element.21), channel_id=1, source_target_pairs={{0,8},{1,9},{2,10},{3,11},{4,12},{5,13},{6,14},{7,15},{8,16},{9,17... | collective-permute-start | bytes 442376 | tf_op jit(solution)/shard_map/ppermute | solution.py:30
  66.3 0.7 collective-permute-start.10
  67.0 3.2 %collective-permute-done.8 = bf16[2,4,24,384]{3,2,1,0:T(8,128)(2,1)S(1)} collective-permute-done((bf16[2,4,24,384]{3,2,1,0:T(8,128)(2,1)S(1)}, bf16[2,4,24,384]{3,2,1,0:T(8,128)(2,1)S(1)}, u32[]{:S(2)}, u32[]{:S(2)}) %collective-permute-start.8) | collective-permute-done | bytes 147488 | tf_op jit(solution)/shard_map/ppermute | solution.py:30
  70.4 0.4 broadcast_select_fusion
  71.1 0.2 pad.7.clone
  71.5 6.2 %fusion.33 = bf16[2,4,8,4,384]{4,2,3,1,0:T(8,128)(2,1)S(1)} fusion(bf16[1,3,3,3,384,384]{5,4,3,2,1,0:T(8,128)(2,1)} %param.5, bf16[4,6,1,7,2,384]{5,3,4,1,0,2:T(8,128)(2,1)S(1)} %slice.94, bf16[4,6,1,8,4,384]{5,3,4,1,0,2:T(8,128)(2,1)S(1)} %copy.49, pred[8,4]{0,1:T(4,128)(4,1)S(1)} %copy-done.1), kind=kOutput, calls=%fused_computation.22 | convolution fusion | flops 2041282560 | bytes 9007136 | tf_op jit(solution)/shard_map/conv_general_dilated | solution.py:92
  78.0 4.8 %collective-permute-start.15 = (bf16[2,1,24,384]{3,2,1,0:T(8,128)(2,1)S(1)}, bf16[2,1,24,384]{3,2,1,0:T(8,128)(2,1)S(1)}, u32[]{:S(2)}, u32[]{:S(2)}) collective-permute-start(bf16[2,1,24,384]{3,2,1,0:T(8,128)(2,1)S(1)} %get-tuple-element.37), channel_id=1, source_target_pairs={{0,9},{1,10},{2,11},{3,12},{4,13},{5,14},{6,15},{8,17},{9,18},{10,... | collective-permute-start | bytes 110600 | tf_op jit(solution)/shard_map/ppermute | solution.py:30
  82.9 2.2 %collective-permute-start.11 = (bf16[2,4,24,384]{3,2,1,0:T(8,128)(2,1)S(1)}, bf16[2,4,24,384]{3,2,1,0:T(8,128)(2,1)S(1)}, u32[]{:S(2)}, u32[]{:S(2)}) collective-permute-start(bf16[2,4,24,384]{3,2,1,0:T(8,128)(2,1)S(1)} %get-tuple-element.19), channel_id=1, source_target_pairs={{0,8},{1,9},{2,10},{3,11},{4,12},{5,13},{6,14},{7,15},{8,16},{9,17... | collective-permute-start | bytes 442376 | tf_op jit(solution)/shard_map/ppermute | solution.py:30
  85.1 0.9 collective-permute-start.16
  86.1 3.0 %collective-permute-done.11 = bf16[2,4,24,384]{3,2,1,0:T(8,128)(2,1)S(1)} collective-permute-done((bf16[2,4,24,384]{3,2,1,0:T(8,128)(2,1)S(1)}, bf16[2,4,24,384]{3,2,1,0:T(8,128)(2,1)S(1)}, u32[]{:S(2)}, u32[]{:S(2)}) %collective-permute-start.11) | collective-permute-done | bytes 147488 | tf_op jit(solution)/shard_map/ppermute | solution.py:30
  89.3 0.2 fusion.114
  89.7 0.2 pad.9.clone
  90.1 6.2 %fusion.30 = bf16[2,4,8,4,384]{4,2,3,1,0:T(8,128)(2,1)S(1)} fusion(bf16[1,3,3,3,384,384]{5,4,3,2,1,0:T(8,128)(2,1)} %param.5, bf16[4,6,1,7,2,384]{5,3,4,1,0,2:T(8,128)(2,1)S(1)} %slice.102, bf16[4,6,1,8,4,384]{5,3,4,1,0,2:T(8,128)(2,1)S(1)} %copy.54, pred[8,4]{0,1:T(4,128)(4,1)S(1)} %copy-done.1), kind=kOutput, calls=%fused_computation.21 | convolution fusion | flops 2041282560 | bytes 9007136 | tf_op jit(solution)/shard_map/conv_general_dilated | solution.py:92
  96.7 0.7 collective-permute-start.17
  97.3 0.7 collective-permute-start.18
  98.0 1.3 %collective-permute-start.19 = (bf16[1,4,24,384]{3,2,1,0:T(8,128)(2,1)S(1)}, bf16[1,4,24,384]{3,2,1,0:T(8,128)(2,1)S(1)}, u32[]{:S(2)}, u32[]{:S(2)}) collective-permute-start(bf16[1,4,24,384]{3,2,1,0:T(8,128)(2,1)S(1)} %get-tuple-element.32), channel_id=1, source_target_pairs={{24,0},{25,1},{26,2},{27,3},{28,4},{29,5},{30,6},{31,7}} | collective-permute-start | bytes 221192 | tf_op jit(solution)/shard_map/ppermute | solution.py:30
  99.4 0.7 collective-permute-start.12
  100.0 0.7 collective-permute-start.13
  100.7 1.3 %collective-permute-start.14 = (bf16[1,4,24,384]{3,2,1,0:T(8,128)(2,1)S(1)}, bf16[1,4,24,384]{3,2,1,0:T(8,128)(2,1)S(1)}, u32[]{:S(2)}, u32[]{:S(2)}) collective-permute-start(bf16[1,4,24,384]{3,2,1,0:T(8,128)(2,1)S(1)} %get-tuple-element.29), channel_id=1, source_target_pairs={{16,0},{17,1},{18,2},{19,3},{20,4},{21,5},{22,6},{23,7}} | collective-permute-start | bytes 221192 | tf_op jit(solution)/shard_map/ppermute | solution.py:30
  102.0 6.6 %collective-permute-done.19 = bf16[1,4,24,384]{3,2,1,0:T(8,128)(2,1)S(1)} collective-permute-done((bf16[1,4,24,384]{3,2,1,0:T(8,128)(2,1)S(1)}, bf16[1,4,24,384]{3,2,1,0:T(8,128)(2,1)S(1)}, u32[]{:S(2)}, u32[]{:S(2)}) %collective-permute-start.19) | collective-permute-done | bytes 73760 | tf_op jit(solution)/shard_map/ppermute | solution.py:30
  108.7 4.8 %collective-permute-done.14 = bf16[1,4,24,384]{3,2,1,0:T(8,128)(2,1)S(1)} collective-permute-done((bf16[1,4,24,384]{3,2,1,0:T(8,128)(2,1)S(1)}, bf16[1,4,24,384]{3,2,1,0:T(8,128)(2,1)S(1)}, u32[]{:S(2)}, u32[]{:S(2)}) %collective-permute-start.14) | collective-permute-done | bytes 73760 | tf_op jit(solution)/shard_map/ppermute | solution.py:30
  113.5 0.7 add_convert_fusion.5
  (82 shorter events, 4.4 us)
Async XLA Ops:
  0.9 6.1 %collective-permute-start.1 = (bf16[4,1,24,384]{3,2,1,0:T(8,128)(2,1)S(1)}, bf16[4,1,24,384]{3,2,1,0:T(8,128)(2,1)S(1)}, u32[]{:S(2)}, u32[]{:S(2)}) collective-permute-start(bf16[4,1,24,384]{3,2,1,0:T(8,128)(2,1)S(1)} %get-tuple-element.36), channel_id=1, source_target_pairs={{1,0},{2,1},{3,2},{4,3},{5,4},{6,5},{7,6},{9,8},{10,9},{11,10},{12... | collective-permute-start | bytes 221192 | tf_op jit(solution)/shard_map/ppermute | solution.py:65
  2.2 4.8 %collective-permute-start = (bf16[4,1,24,384]{3,2,1,0:T(8,128)(2,1)S(1)}, bf16[4,1,24,384]{3,2,1,0:T(8,128)(2,1)S(1)}, u32[]{:S(2)}, u32[]{:S(2)}) collective-permute-start(bf16[4,1,24,384]{3,2,1,0:T(8,128)(2,1)S(1)} %get-tuple-element.35), channel_id=1, source_target_pairs={{0,1},{1,2},{2,3},{3,4},{4,5},{5,6},{6,7},{8,9},{9,10},{10,11},{11... | collective-permute-start | bytes 221192 | tf_op jit(solution)/shard_map/ppermute | solution.py:64
  7.5 0.7 copy-start.1
  8.2 6.5 %copy-start = (bf16[4,4,24,384]{3,2,1,0:T(8,128)(2,1)S(1)}, bf16[4,4,24,384]{3,2,1,0:T(8,128)(2,1)}, u32[]{:S(2)}) copy-start(bf16[4,4,24,384]{3,2,1,0:T(8,128)(2,1)} %param.3) | copy-start | bytes 884740
  14.8 9.8 %collective-permute-start.3 = (bf16[2,1,24,384]{3,2,1,0:T(8,128)(2,1)S(1)}, bf16[2,1,24,384]{3,2,1,0:T(8,128)(2,1)S(1)}, u32[]{:S(2)}, u32[]{:S(2)}) collective-permute-start(bf16[2,1,24,384]{3,2,1,0:T(8,128)(2,1)S(1)} %get-tuple-element.43), channel_id=1, source_target_pairs={{0,9},{1,10},{2,11},{3,12},{4,13},{5,14},{6,15},{8,17},{9,18},{10,... | collective-permute-start | bytes 110600 | tf_op jit(solution)/shard_map/ppermute | solution.py:30
  20.4 6.9 %collective-permute-start.2 = (bf16[2,4,24,384]{3,2,1,0:T(8,128)(2,1)S(1)}, bf16[2,4,24,384]{3,2,1,0:T(8,128)(2,1)S(1)}, u32[]{:S(2)}, u32[]{:S(2)}) collective-permute-start(bf16[2,4,24,384]{3,2,1,0:T(8,128)(2,1)S(1)} %get-tuple-element.28), channel_id=1, source_target_pairs={{0,8},{1,9},{2,10},{3,11},{4,12},{5,13},{6,14},{7,15},{8,16},{9,17... | collective-permute-start | bytes 442376 | tf_op jit(solution)/shard_map/ppermute | solution.py:30
  23.9 0.7 collective-permute-start.4
  35.2 10.8 %collective-permute-start.6 = (bf16[2,1,24,384]{3,2,1,0:T(8,128)(2,1)S(1)}, bf16[2,1,24,384]{3,2,1,0:T(8,128)(2,1)S(1)}, u32[]{:S(2)}, u32[]{:S(2)}) collective-permute-start(bf16[2,1,24,384]{3,2,1,0:T(8,128)(2,1)S(1)} %get-tuple-element.41), channel_id=1, source_target_pairs={{0,9},{1,10},{2,11},{3,12},{4,13},{5,14},{6,15},{8,17},{9,18},{10,... | collective-permute-start | bytes 110600 | tf_op jit(solution)/shard_map/ppermute | solution.py:30
  42.6 6.2 %collective-permute-start.5 = (bf16[2,4,24,384]{3,2,1,0:T(8,128)(2,1)S(1)}, bf16[2,4,24,384]{3,2,1,0:T(8,128)(2,1)S(1)}, u32[]{:S(2)}, u32[]{:S(2)}) collective-permute-start(bf16[2,4,24,384]{3,2,1,0:T(8,128)(2,1)S(1)} %get-tuple-element.26), channel_id=1, source_target_pairs={{0,8},{1,9},{2,10},{3,11},{4,12},{5,13},{6,14},{7,15},{8,16},{9,17... | collective-permute-start | bytes 442376 | tf_op jit(solution)/shard_map/ppermute | solution.py:30
  45.2 0.9 collective-permute-start.7
  56.4 10.5 %collective-permute-start.9 = (bf16[2,1,24,384]{3,2,1,0:T(8,128)(2,1)S(1)}, bf16[2,1,24,384]{3,2,1,0:T(8,128)(2,1)S(1)}, u32[]{:S(2)}, u32[]{:S(2)}) collective-permute-start(bf16[2,1,24,384]{3,2,1,0:T(8,128)(2,1)S(1)} %get-tuple-element.39), channel_id=1, source_target_pairs={{0,9},{1,10},{2,11},{3,12},{4,13},{5,14},{6,15},{8,17},{9,18},{10,... | collective-permute-start | bytes 110600 | tf_op jit(solution)/shard_map/ppermute | solution.py:30
  64.1 6.1 %collective-permute-start.8 = (bf16[2,4,24,384]{3,2,1,0:T(8,128)(2,1)S(1)}, bf16[2,4,24,384]{3,2,1,0:T(8,128)(2,1)S(1)}, u32[]{:S(2)}, u32[]{:S(2)}) collective-permute-start(bf16[2,4,24,384]{3,2,1,0:T(8,128)(2,1)S(1)} %get-tuple-element.21), channel_id=1, source_target_pairs={{0,8},{1,9},{2,10},{3,11},{4,12},{5,13},{6,14},{7,15},{8,16},{9,17... | collective-permute-start | bytes 442376 | tf_op jit(solution)/shard_map/ppermute | solution.py:30
  66.3 0.7 collective-permute-start.10
  78.0 8.0 %collective-permute-start.15 = (bf16[2,1,24,384]{3,2,1,0:T(8,128)(2,1)S(1)}, bf16[2,1,24,384]{3,2,1,0:T(8,128)(2,1)S(1)}, u32[]{:S(2)}, u32[]{:S(2)}) collective-permute-start(bf16[2,1,24,384]{3,2,1,0:T(8,128)(2,1)S(1)} %get-tuple-element.37), channel_id=1, source_target_pairs={{0,9},{1,10},{2,11},{3,12},{4,13},{5,14},{6,15},{8,17},{9,18},{10,... | collective-permute-start | bytes 110600 | tf_op jit(solution)/shard_map/ppermute | solution.py:30
  82.9 6.1 %collective-permute-start.11 = (bf16[2,4,24,384]{3,2,1,0:T(8,128)(2,1)S(1)}, bf16[2,4,24,384]{3,2,1,0:T(8,128)(2,1)S(1)}, u32[]{:S(2)}, u32[]{:S(2)}) collective-permute-start(bf16[2,4,24,384]{3,2,1,0:T(8,128)(2,1)S(1)} %get-tuple-element.19), channel_id=1, source_target_pairs={{0,8},{1,9},{2,10},{3,11},{4,12},{5,13},{6,14},{7,15},{8,16},{9,17... | collective-permute-start | bytes 442376 | tf_op jit(solution)/shard_map/ppermute | solution.py:30
  85.1 0.9 collective-permute-start.16
  96.7 4.0 %collective-permute-start.17 = (bf16[1,4,24,384]{3,2,1,0:T(8,128)(2,1)S(1)}, bf16[1,4,24,384]{3,2,1,0:T(8,128)(2,1)S(1)}, u32[]{:S(2)}, u32[]{:S(2)}) collective-permute-start(bf16[1,4,24,384]{3,2,1,0:T(8,128)(2,1)S(1)} %get-tuple-element.34), channel_id=1, source_target_pairs={{24,16},{25,17},{26,18},{27,19},{28,20},{29,21},{30,22},{31,23}} | collective-permute-start | bytes 221192 | tf_op jit(solution)/shard_map/ppermute | solution.py:30
  97.3 4.7 %collective-permute-start.18 = (bf16[1,4,24,384]{3,2,1,0:T(8,128)(2,1)S(1)}, bf16[1,4,24,384]{3,2,1,0:T(8,128)(2,1)S(1)}, u32[]{:S(2)}, u32[]{:S(2)}) collective-permute-start(bf16[1,4,24,384]{3,2,1,0:T(8,128)(2,1)S(1)} %get-tuple-element.33), channel_id=1, source_target_pairs={{24,8},{25,9},{26,10},{27,11},{28,12},{29,13},{30,14},{31,15}} | collective-permute-start | bytes 221192 | tf_op jit(solution)/shard_map/ppermute | solution.py:30
  98.0 10.6 %collective-permute-start.19 = (bf16[1,4,24,384]{3,2,1,0:T(8,128)(2,1)S(1)}, bf16[1,4,24,384]{3,2,1,0:T(8,128)(2,1)S(1)}, u32[]{:S(2)}, u32[]{:S(2)}) collective-permute-start(bf16[1,4,24,384]{3,2,1,0:T(8,128)(2,1)S(1)} %get-tuple-element.32), channel_id=1, source_target_pairs={{24,0},{25,1},{26,2},{27,3},{28,4},{29,5},{30,6},{31,7}} | collective-permute-start | bytes 221192 | tf_op jit(solution)/shard_map/ppermute | solution.py:30
  99.4 9.3 %collective-permute-start.12 = (bf16[1,4,24,384]{3,2,1,0:T(8,128)(2,1)S(1)}, bf16[1,4,24,384]{3,2,1,0:T(8,128)(2,1)S(1)}, u32[]{:S(2)}, u32[]{:S(2)}) collective-permute-start(bf16[1,4,24,384]{3,2,1,0:T(8,128)(2,1)S(1)} %get-tuple-element.31), channel_id=1, source_target_pairs={{16,24},{17,25},{18,26},{19,27},{20,28},{21,29},{22,30},{23,31}} | collective-permute-start | bytes 221192 | tf_op jit(solution)/shard_map/ppermute | solution.py:30
  100.0 8.6 %collective-permute-start.13 = (bf16[1,4,24,384]{3,2,1,0:T(8,128)(2,1)S(1)}, bf16[1,4,24,384]{3,2,1,0:T(8,128)(2,1)S(1)}, u32[]{:S(2)}, u32[]{:S(2)}) collective-permute-start(bf16[1,4,24,384]{3,2,1,0:T(8,128)(2,1)S(1)} %get-tuple-element.30), channel_id=1, source_target_pairs={{16,8},{17,9},{18,10},{19,11},{20,12},{21,13},{22,14},{23,15}} | collective-permute-start | bytes 221192 | tf_op jit(solution)/shard_map/ppermute | solution.py:30
  100.7 12.8 %collective-permute-start.14 = (bf16[1,4,24,384]{3,2,1,0:T(8,128)(2,1)S(1)}, bf16[1,4,24,384]{3,2,1,0:T(8,128)(2,1)S(1)}, u32[]{:S(2)}, u32[]{:S(2)}) collective-permute-start(bf16[1,4,24,384]{3,2,1,0:T(8,128)(2,1)S(1)} %get-tuple-element.29), channel_id=1, source_target_pairs={{16,0},{17,1},{18,2},{19,3},{20,4},{21,5},{22,6},{23,7}} | collective-permute-start | bytes 221192 | tf_op jit(solution)/shard_map/ppermute | solution.py:30

commit v6 on v4

--- a/solution.py
+++ b/solution.py
@@ -14,12 +14,12 @@
     ).astype(jnp.bfloat16)
 
 
-def causal_conv(window, kernel):
+def causal_conv(window, kernel, before=2):
     result = lax.conv_general_dilated(
         window[None],
         kernel,
         window_strides=(1, 1, 1),
-        padding=((2, 0), (0, 0), (1, 1)),
+        padding=((before, 0), (0, 0), (1, 1)),
         dimension_numbers=("NDHWC", "DHWIO", "NDHWC"),
         preferred_element_type=jnp.float32,
     )
@@ -76,9 +76,25 @@
         def idle(window, skip):
             return jnp.zeros(skip.shape, jnp.bfloat16)
 
+        if final:
+            activated = jnp.pad(activate(window, gain_row), ((2, 0), (0, 0), (0, 0), (0, 0)))
+            split = (segment_count // 2) * group
+            branch = None
+            for low, high in ((0, split), (split, frame_count)):
+                part = causal_conv(activated[low : high + 2], kernel, 0).astype(jnp.bfloat16)
+                for target in range(low // group, high // group):
+                    chunk = part[target * group - low : (target + 1) * group - low]
+                    if target == last_stage:
+                        branch = chunk if branch is None else jnp.where(
+                            segment_index == target, chunk, branch
+                        )
+                    else:
+                        piece = send(chunk, straight(last_stage, target))
+                        branch = piece if branch is None else jnp.where(
+                            segment_index == target, piece, branch
+                        )
+            break
         produced = lax.cond(segment_index == stage, compute, idle, window, skip)
-        if final:
-            break
         if stage == last_stage - 1:
             owned = current[stage * group : (stage + 1) * group]
             for target in range(segment_count):
@@ -95,11 +111,6 @@
         elif not odd:
             skip = features
 
-    branch = produced[last_stage * group :]
-    for target in range(last_stage):
-        chunk = produced[target * group : (target + 1) * group]
-        piece = send(chunk, straight(last_stage, target))
-        branch = jnp.where(segment_index == target, piece, branch)
     return (owned.astype(jnp.float32) + branch.astype(jnp.float32)).astype(jnp.bfloat16)
 
 

time: 98.4 us -> 95.6 us (0.972)
  the two profiles are of different devices: /device:TPU:1 before, /device:TPU:17 now
where the time goes in v6:
time: 95.6 us; the launch traced here: 95.2 us
  waiting for transfers between devices  48.1 us (50%)
  starting transfers between devices  22.5 us (24%)
  matrix products  13.9 us (15%)
  other arithmetic  5.27 us (6%)
  local copies, waits for them, and re-layouts  4.51 us (5%)
    ppermute x15, waiting for transfers between devices, send(): return lax.ppermute(value, BOTH, pairs)  45.1 us
    ppermute x15, starting transfers between devices, send(): return lax.ppermute(value, BOTH, pairs)  16.9 us
    conv_general_dilated x3, matrix products, causal_conv(): lax.conv_general_dilated(window[None], kernel, window_strides=(1, 1, 1),...  13.9 us
    ppermute x1, starting transfers between devices, local(): top = lax.ppermute(features[:, height - 1:], 'rows', up)  3.68 us
    ppermute x1, waiting for transfers between devices, local(): bottom = lax.ppermute(features[:, :1], 'rows', down)  3.03 us
    ppermute x1, starting transfers between devices, local(): bottom = lax.ppermute(features[:, :1], 'rows', down)  1.92 us
  transfers between devices with their start and end apart: 17, of which 4 were waited for; matrix products, arithmetic and copies ran while one was open for 12% of the time, Pallas kernels for 0%

profile of v6, /device:TPU:17, one launch (start us, length us, event | category | flops | bytes accessed | tf_op | source)
XLA Modules:
  0.0 95.2 jit_solution(18229018957303299790)
XLA Ops:
  0.0 1.1 %copy.79 = bf16[4,4,24,384]{3,0,2,1:T(4,128)(2,1)S(1)} copy(bf16[4,4,24,384]{3,2,1,0:T(8,128)(2,1)} %param.9) | data formatting | bytes 589824 | tf_op args[0]
  1.2 3.7 %collective-permute-start = (bf16[4,1,24,384]{3,0,2,1:T(4,128)(2,1)S(1)}, bf16[4,1,24,384]{3,0,2,1:T(4,128)(2,1)S(1)}, u32[]{:S(2)}, u32[]{:S(2)}) collective-permute-start(bf16[4,1,24,384]{3,0,2,1:T(4,128)(2,1)S(1)} %get-tuple-element.74), channel_id=1, source_target_pairs={{0,1},{1,2},{2,3},{3,4},{4,5},{5,6},{6,7},{8,9},{9,10},{10,11},{11... | collective-permute-start | bytes 221192 | tf_op jit(solution)/shard_map/ppermute | solution.py:59
  4.9 1.9 %collective-permute-start.1 = (bf16[4,1,24,384]{3,0,2,1:T(4,128)(2,1)S(1)}, bf16[4,1,24,384]{3,0,2,1:T(4,128)(2,1)S(1)}, u32[]{:S(2)}, u32[]{:S(2)}) collective-permute-start(bf16[4,1,24,384]{3,0,2,1:T(4,128)(2,1)S(1)} %get-tuple-element.75), channel_id=1, source_target_pairs={{1,0},{2,1},{3,2},{4,3},{5,4},{6,5},{7,6},{9,8},{10,9},{11,10},{12... | collective-permute-start | bytes 221192 | tf_op jit(solution)/shard_map/ppermute | solution.py:60
  6.8 0.7 reduce
  7.5 3.0 %collective-permute-done.1 = bf16[4,1,24,384]{3,0,2,1:T(4,128)(2,1)S(1)} collective-permute-done((bf16[4,1,24,384]{3,0,2,1:T(4,128)(2,1)S(1)}, bf16[4,1,24,384]{3,0,2,1:T(4,128)(2,1)S(1)}, u32[]{:S(2)}, u32[]{:S(2)}) %collective-permute-start.1) | collective-permute-done | bytes 73760 | tf_op jit(solution)/shard_map/ppermute | solution.py:60
  10.5 0.3 pad_maximum_fusion.1
  11.0 0.2 copy.82
  11.2 0.7 collective-permute-start.3
  11.9 0.7 collective-permute-start.2
  12.6 0.7 collective-permute-start.4
  13.3 0.3 pad_maximum_fusion.2
  13.8 1.3 %collective-permute-start.5 = (bf16[4,4,24,384]{3,2,1,0:T(8,128)(2,1)S(1)}, bf16[4,4,24,384]{3,2,1,0:T(8,128)(2,1)S(1)}, u32[]{:S(2)}, u32[]{:S(2)}) collective-permute-start(bf16[4,4,24,384]{3,2,1,0:T(8,128)(2,1)S(1)} %copy.86), channel_id=1, source_target_pairs={{8,16},{9,17},{10,18},{11,19},{12,20},{13,21},{14,22},{15,23}} | collective-permute-start | bytes 884744 | tf_op jit(solution)/shard_map/ppermute | solution.py:30
  15.1 1.3 %collective-permute-start.10 = (bf16[4,1,24,384]{3,2,1,0:T(8,128)(2,1)S(1)}, bf16[4,1,24,384]{3,2,1,0:T(8,128)(2,1)S(1)}, u32[]{:S(2)}, u32[]{:S(2)}) collective-permute-start(bf16[4,1,24,384]{3,2,1,0:T(8,128)(2,1)S(1)} %get-tuple-element.68), channel_id=1, source_target_pairs={{9,16},{10,17},{11,18},{12,19},{13,20},{14,21},{15,22}} | collective-permute-start | bytes 221192 | tf_op jit(solution)/shard_map/ppermute | solution.py:30
  16.4 1.3 %collective-permute-start.9 = (bf16[4,1,24,384]{3,2,1,0:T(8,128)(2,1)S(1)}, bf16[4,1,24,384]{3,2,1,0:T(8,128)(2,1)S(1)}, u32[]{:S(2)}, u32[]{:S(2)}) collective-permute-start(bf16[4,1,24,384]{3,2,1,0:T(8,128)(2,1)S(1)} %get-tuple-element.67), channel_id=1, source_target_pairs={{8,17},{9,18},{10,19},{11,20},{12,21},{13,22},{14,23}} | collective-permute-start | bytes 221192 | tf_op jit(solution)/shard_map/ppermute | solution.py:30
  17.7 35.2 %collective-permute-done.10 = bf16[4,1,24,384]{3,2,1,0:T(8,128)(2,1)S(1)} collective-permute-done((bf16[4,1,24,384]{3,2,1,0:T(8,128)(2,1)S(1)}, bf16[4,1,24,384]{3,2,1,0:T(8,128)(2,1)S(1)}, u32[]{:S(2)}, u32[]{:S(2)}) %collective-permute-start.10) | collective-permute-done | bytes 73760 | tf_op jit(solution)/shard_map/ppermute | solution.py:30
  53.0 9.8 %conditional.5 = (bf16[4,4,24,384]{3,1,2,0:T(4,128)(2,1)S(1)}) conditional(s32[]{:T(128)} %convert_element_type.117, () %tuple.27, (bf16[4,6,24,384]{3,2,1,0:T(8,128)(2,1)S(1)}, bf16[384]{0:T(512)(128)(2,1)S(1)}, bf16[3,3,3,384,384]{4,3,2,1,0:T(8,128)(2,1)}) %tuple.52), branch_computations={%region_6.7_spmd, %region_7.9_spmd} | conditional | flops 3063129088 | bytes 14648262 | solution.py:97
  53.2 0.3 fusion.41
  53.6 0.6 fusion.53
  54.2 0.2 pad.9
  54.4 0.1 copy.77
  54.6 7.9 %fusion.40 = bf16[4,4,8,4,384]{4,2,3,1,0:T(8,128)(2,1)S(1)} fusion(bf16[3,3,3,384,384]{4,3,2,1,0:T(8,128)(2,1)} %get-tuple-element.43, bf16[4,6,1,7,2,384]{5,3,4,1,0,2:T(8,128)(2,1)S(1)} %slice.105, bf16[4,6,1,8,4,384]{5,3,4,1,0,2:T(8,128)(2,1)S(1)} %copy.77, pred[8,4]{0,1:T(4,128)(4,1)S(1)} %copy-done.5), kind=kOutput, calls=%fused_computation.55 | convolution fusion | flops 3060695040 | bytes 9203744 | tf_op jit(solution)/shard_map/cond/branch_1_fun/conv_general_dilated | solution.py:18
  62.5 0.2 copy.78
  62.8 1.3 %collective-permute-start.12 = (bf16[4,4,24,384]{3,1,2,0:T(4,128)(2,1)S(1)}, bf16[4,4,24,384]{3,1,2,0:T(4,128)(2,1)S(1)}, u32[]{:S(2)}, u32[]{:S(2)}) collective-permute-start(bf16[4,4,24,384]{3,1,2,0:T(4,128)(2,1)S(1)} %get-tuple-element.82), channel_id=1, source_target_pairs={{16,24},{17,25},{18,26},{19,27},{20,28},{21,29},{22,30},{23,31}} | collective-permute-start | bytes 884744 | tf_op jit(solution)/shard_map/ppermute | solution.py:30
  64.1 0.2 fusion.97
  64.4 1.3 %collective-permute-start.11 = (bf16[4,1,24,384]{3,2,0,1:T(8,128)(2,1)S(1)}, bf16[4,1,24,384]{3,2,0,1:T(8,128)(2,1)S(1)}, u32[]{:S(2)}, u32[]{:S(2)}) collective-permute-start(bf16[4,1,24,384]{3,2,0,1:T(8,128)(2,1)S(1)} %copy.114), channel_id=1, source_target_pairs={{16,25},{17,26},{18,27},{19,28},{20,29},{21,30},{22,31}} | collective-permute-start | bytes 221192 | tf_op jit(solution)/shard_map/ppermute | solution.py:30
  65.7 1.6 %collective-permute-start.13 = (bf16[4,1,24,384]{3,2,0,1:T(8,128)(2,1)S(1)}, bf16[4,1,24,384]{3,2,0,1:T(8,128)(2,1)S(1)}, u32[]{:S(2)}, u32[]{:S(2)}) collective-permute-start(bf16[4,1,24,384]{3,2,0,1:T(8,128)(2,1)S(1)} %copy.115), channel_id=1, source_target_pairs={{17,24},{18,25},{19,26},{20,27},{21,28},{22,29},{23,30}} | collective-permute-start | bytes 221192 | tf_op jit(solution)/shard_map/ppermute | solution.py:30
  67.3 1.4 %collective-permute-start.6 = (bf16[1,4,24,384]{3,2,1,0:T(8,128)(2,1)S(1)}, bf16[1,4,24,384]{3,2,1,0:T(8,128)(2,1)S(1)}, u32[]{:S(2)}, u32[]{:S(2)}) collective-permute-start(bf16[1,4,24,384]{3,2,1,0:T(8,128)(2,1)S(1)} %get-tuple-element.71), channel_id=1, source_target_pairs={{16,24},{17,25},{18,26},{19,27},{20,28},{21,29},{22,30},{23,31}} | collective-permute-start | bytes 221192 | tf_op jit(solution)/shard_map/ppermute | solution.py:30
  68.7 1.3 %collective-permute-start.7 = (bf16[1,4,24,384]{3,2,1,0:T(8,128)(2,1)S(1)}, bf16[1,4,24,384]{3,2,1,0:T(8,128)(2,1)S(1)}, u32[]{:S(2)}, u32[]{:S(2)}) collective-permute-start(bf16[1,4,24,384]{3,2,1,0:T(8,128)(2,1)S(1)} %get-tuple-element.70), channel_id=1, source_target_pairs={{16,8},{17,9},{18,10},{19,11},{20,12},{21,13},{22,14},{23,15}} | collective-permute-start | bytes 221192 | tf_op jit(solution)/shard_map/ppermute | solution.py:30
  70.0 1.9 %collective-permute-done.11 = bf16[4,1,24,384]{3,2,0,1:T(8,128)(2,1)S(1)} collective-permute-done((bf16[4,1,24,384]{3,2,0,1:T(8,128)(2,1)S(1)}, bf16[4,1,24,384]{3,2,0,1:T(8,128)(2,1)S(1)}, u32[]{:S(2)}, u32[]{:S(2)}) %collective-permute-start.11) | collective-permute-done | bytes 73760 | tf_op jit(solution)/shard_map/ppermute | solution.py:30
  72.0 1.3 %collective-permute-start.8 = (bf16[1,4,24,384]{3,2,1,0:T(8,128)(2,1)S(1)}, bf16[1,4,24,384]{3,2,1,0:T(8,128)(2,1)S(1)}, u32[]{:S(2)}, u32[]{:S(2)}) collective-permute-start(bf16[1,4,24,384]{3,2,1,0:T(8,128)(2,1)S(1)} %get-tuple-element.69), channel_id=1, source_target_pairs={{16,0},{17,1},{18,2},{19,3},{20,4},{21,5},{22,6},{23,7}} | collective-permute-start | bytes 221192 | tf_op jit(solution)/shard_map/ppermute | solution.py:30
  73.3 0.1 copy.92
  73.4 0.1 copy.93
  73.6 0.1 copy.95
  73.8 0.6 fusion.60
  74.5 0.8 fusion.67
  75.3 0.1 pad.13
  75.4 0.2 copy.105
  75.7 0.2 copy-done.2
  76.0 3.0 %fusion.69 = bf16[2,4,8,4,384]{4,2,3,1,0:T(8,128)(2,1)S(1)} fusion(bf16[4,6,1,7,2,384]{5,3,4,1,0,2:T(8,128)(2,1)S(1)} %slice.124, bf16[4,6,1,8,4,384]{5,3,4,1,0,2:T(8,128)(2,1)S(1)} %copy.105, pred[8,4]{0,1:T(4,128)(4,1)S(1)} %copy-done.2, bf16[1,3,3,3,384,384]{5,4,3,2,1,0:T(8,128)(2,1)S(1)} %copy-done.1), kind=kOutput, calls=%fused_computation.94 | convolution fusion | flops 2041282560 | bytes 9007136 | tf_op jit(solution)/shard_map/conv_general_dilated | solution.py:18
  79.1 0.7 collective-permute-start.15
  79.9 0.9 collective-permute-start.16
  80.8 0.8 fusion.83
  81.6 0.1 pad.11
  81.7 0.2 copy.98
  82.0 3.0 %fusion.68 = bf16[2,4,8,4,384]{4,2,3,1,0:T(8,128)(2,1)S(1)} fusion(bf16[4,6,1,7,2,384]{5,3,4,1,0,2:T(8,128)(2,1)S(1)} %slice.119, bf16[4,6,1,8,4,384]{5,3,4,1,0,2:T(8,128)(2,1)S(1)} %copy.98, pred[8,4]{0,1:T(4,128)(4,1)S(1)} %copy-done.2, bf16[1,3,3,3,384,384]{5,4,3,2,1,0:T(8,128)(2,1)S(1)} %copy-done.1), kind=kOutput, calls=%fused_computation.93 | convolution fusion | flops 2041282560 | bytes 9007136 | tf_op jit(solution)/shard_map/conv_general_dilated | solution.py:18
  85.2 1.3 %collective-permute-start.14 = (bf16[1,4,24,384]{3,2,1,0:T(8,128)(2,1)S(1)}, bf16[1,4,24,384]{3,2,1,0:T(8,128)(2,1)S(1)}, u32[]{:S(2)}, u32[]{:S(2)}) collective-permute-start(bf16[1,4,24,384]{3,2,1,0:T(8,128)(2,1)S(1)} %bitcast.89), channel_id=1, source_target_pairs={{24,16},{25,17},{26,18},{27,19},{28,20},{29,21},{30,22},{31,23}} | collective-permute-start | bytes 221192 | tf_op jit(solution)/shard_map/ppermute | solution.py:30
  86.6 7.9 %collective-permute-done.14 = bf16[1,4,24,384]{3,2,1,0:T(8,128)(2,1)S(1)} collective-permute-done((bf16[1,4,24,384]{3,2,1,0:T(8,128)(2,1)S(1)}, bf16[1,4,24,384]{3,2,1,0:T(8,128)(2,1)S(1)}, u32[]{:S(2)}, u32[]{:S(2)}) %collective-permute-start.14) | collective-permute-done | bytes 73760 | tf_op jit(solution)/shard_map/ppermute | solution.py:30
  94.5 0.7 add_convert_fusion
  (55 shorter events, 1.7 us)
Async XLA Ops:
  1.2 6.3 %collective-permute-start = (bf16[4,1,24,384]{3,0,2,1:T(4,128)(2,1)S(1)}, bf16[4,1,24,384]{3,0,2,1:T(4,128)(2,1)S(1)}, u32[]{:S(2)}, u32[]{:S(2)}) collective-permute-start(bf16[4,1,24,384]{3,0,2,1:T(4,128)(2,1)S(1)} %get-tuple-element.74), channel_id=1, source_target_pairs={{0,1},{1,2},{2,3},{3,4},{4,5},{5,6},{6,7},{8,9},{9,10},{10,11},{11... | collective-permute-start | bytes 221192 | tf_op jit(solution)/shard_map/ppermute | solution.py:59
  4.9 5.7 %collective-permute-start.1 = (bf16[4,1,24,384]{3,0,2,1:T(4,128)(2,1)S(1)}, bf16[4,1,24,384]{3,0,2,1:T(4,128)(2,1)S(1)}, u32[]{:S(2)}, u32[]{:S(2)}) collective-permute-start(bf16[4,1,24,384]{3,0,2,1:T(4,128)(2,1)S(1)} %get-tuple-element.75), channel_id=1, source_target_pairs={{1,0},{2,1},{3,2},{4,3},{5,4},{6,5},{7,6},{9,8},{10,9},{11,10},{12... | collective-permute-start | bytes 221192 | tf_op jit(solution)/shard_map/ppermute | solution.py:60
  11.0 2.6 %copy-start = (bf16[4,4,24,384]{3,2,1,0:T(8,128)(2,1)S(1)}, bf16[4,4,24,384]{3,2,1,0:T(8,128)(2,1)}, u32[]{:S(2)}) copy-start(bf16[4,4,24,384]{3,2,1,0:T(8,128)(2,1)} %param.9) | copy-start | bytes 884740
  11.2 2.1 %collective-permute-start.3 = (bf16[4,4,24,384]{3,0,2,1:T(4,128)(2,1)S(1)}, bf16[4,4,24,384]{3,0,2,1:T(4,128)(2,1)S(1)}, u32[]{:S(2)}, u32[]{:S(2)}) collective-permute-start(bf16[4,4,24,384]{3,0,2,1:T(4,128)(2,1)S(1)} %copy.82), channel_id=1, source_target_pairs={{0,8},{1,9},{2,10},{3,11},{4,12},{5,13},{6,14},{7,15}} | collective-permute-start | bytes 884744 | tf_op jit(solution)/shard_map/ppermute | solution.py:30
  11.9 1.4 %collective-permute-start.2 = (bf16[4,1,24,384]{3,0,2,1:T(4,128)(2,1)S(1)}, bf16[4,1,24,384]{3,0,2,1:T(4,128)(2,1)S(1)}, u32[]{:S(2)}, u32[]{:S(2)}) collective-permute-start(bf16[4,1,24,384]{3,0,2,1:T(4,128)(2,1)S(1)} %get-tuple-element.72), channel_id=1, source_target_pairs={{0,9},{1,10},{2,11},{3,12},{4,13},{5,14},{6,15}} | collective-permute-start | bytes 221192 | tf_op jit(solution)/shard_map/ppermute | solution.py:30
  12.6 0.7 collective-permute-start.4
  13.8 39.1 %collective-permute-start.5 = (bf16[4,4,24,384]{3,2,1,0:T(8,128)(2,1)S(1)}, bf16[4,4,24,384]{3,2,1,0:T(8,128)(2,1)S(1)}, u32[]{:S(2)}, u32[]{:S(2)}) collective-permute-start(bf16[4,4,24,384]{3,2,1,0:T(8,128)(2,1)S(1)} %copy.86), channel_id=1, source_target_pairs={{8,16},{9,17},{10,18},{11,19},{12,20},{13,21},{14,22},{15,23}} | collective-permute-start | bytes 884744 | tf_op jit(solution)/shard_map/ppermute | solution.py:30
  15.1 37.8 %collective-permute-start.10 = (bf16[4,1,24,384]{3,2,1,0:T(8,128)(2,1)S(1)}, bf16[4,1,24,384]{3,2,1,0:T(8,128)(2,1)S(1)}, u32[]{:S(2)}, u32[]{:S(2)}) collective-permute-start(bf16[4,1,24,384]{3,2,1,0:T(8,128)(2,1)S(1)} %get-tuple-element.68), channel_id=1, source_target_pairs={{9,16},{10,17},{11,18},{12,19},{13,20},{14,21},{15,22}} | collective-permute-start | bytes 221192 | tf_op jit(solution)/shard_map/ppermute | solution.py:30
  16.4 36.5 %collective-permute-start.9 = (bf16[4,1,24,384]{3,2,1,0:T(8,128)(2,1)S(1)}, bf16[4,1,24,384]{3,2,1,0:T(8,128)(2,1)S(1)}, u32[]{:S(2)}, u32[]{:S(2)}) collective-permute-start(bf16[4,1,24,384]{3,2,1,0:T(8,128)(2,1)S(1)} %get-tuple-element.67), channel_id=1, source_target_pairs={{8,17},{9,18},{10,19},{11,20},{12,21},{13,22},{14,23}} | collective-permute-start | bytes 221192 | tf_op jit(solution)/shard_map/ppermute | solution.py:30
  53.5 1.0 %copy-start.5 = (pred[8,4]{0,1:T(4,128)(4,1)S(1)}, pred[8,4]{0,1:T(4,128)(4,1)}, u32[]{:S(2)}) copy-start(pred[8,4]{0,1:T(4,128)(4,1)} %constant.85) | copy-start | bytes 100 | tf_op jit(solution)/shard_map/cond
  62.8 10.9 %collective-permute-start.12 = (bf16[4,4,24,384]{3,1,2,0:T(4,128)(2,1)S(1)}, bf16[4,4,24,384]{3,1,2,0:T(4,128)(2,1)S(1)}, u32[]{:S(2)}, u32[]{:S(2)}) collective-permute-start(bf16[4,4,24,384]{3,1,2,0:T(4,128)(2,1)S(1)} %get-tuple-element.82), channel_id=1, source_target_pairs={{16,24},{17,25},{18,26},{19,27},{20,28},{21,29},{22,30},{23,31}} | collective-permute-start | bytes 884744 | tf_op jit(solution)/shard_map/ppermute | solution.py:30
  64.4 7.6 %collective-permute-start.11 = (bf16[4,1,24,384]{3,2,0,1:T(8,128)(2,1)S(1)}, bf16[4,1,24,384]{3,2,0,1:T(8,128)(2,1)S(1)}, u32[]{:S(2)}, u32[]{:S(2)}) collective-permute-start(bf16[4,1,24,384]{3,2,0,1:T(8,128)(2,1)S(1)} %copy.114), channel_id=1, source_target_pairs={{16,25},{17,26},{18,27},{19,28},{20,29},{21,30},{22,31}} | collective-permute-start | bytes 221192 | tf_op jit(solution)/shard_map/ppermute | solution.py:30
  65.7 10.1 %copy-start.1 = (bf16[1,3,3,3,384,384]{5,4,3,2,1,0:T(8,128)(2,1)S(1)}, bf16[1,3,3,3,384,384]{5,4,3,2,1,0:T(8,128)(2,1)}, u32[]{:S(2)}) copy-start(bf16[1,3,3,3,384,384]{5,4,3,2,1,0:T(8,128)(2,1)} %param.11) | copy-start | bytes 23887876
  65.7 7.7 %collective-permute-start.13 = (bf16[4,1,24,384]{3,2,0,1:T(8,128)(2,1)S(1)}, bf16[4,1,24,384]{3,2,0,1:T(8,128)(2,1)S(1)}, u32[]{:S(2)}, u32[]{:S(2)}) collective-permute-start(bf16[4,1,24,384]{3,2,0,1:T(8,128)(2,1)S(1)} %copy.115), channel_id=1, source_target_pairs={{17,24},{18,25},{19,26},{20,27},{21,28},{22,29},{23,30}} | collective-permute-start | bytes 221192 | tf_op jit(solution)/shard_map/ppermute | solution.py:30
  67.3 17.9 %collective-permute-start.6 = (bf16[1,4,24,384]{3,2,1,0:T(8,128)(2,1)S(1)}, bf16[1,4,24,384]{3,2,1,0:T(8,128)(2,1)S(1)}, u32[]{:S(2)}, u32[]{:S(2)}) collective-permute-start(bf16[1,4,24,384]{3,2,1,0:T(8,128)(2,1)S(1)} %get-tuple-element.71), channel_id=1, source_target_pairs={{16,24},{17,25},{18,26},{19,27},{20,28},{21,29},{22,30},{23,31}} | collective-permute-start | bytes 221192 | tf_op jit(solution)/shard_map/ppermute | solution.py:30
  68.7 17.8 %collective-permute-start.7 = (bf16[1,4,24,384]{3,2,1,0:T(8,128)(2,1)S(1)}, bf16[1,4,24,384]{3,2,1,0:T(8,128)(2,1)S(1)}, u32[]{:S(2)}, u32[]{:S(2)}) collective-permute-start(bf16[1,4,24,384]{3,2,1,0:T(8,128)(2,1)S(1)} %get-tuple-element.70), channel_id=1, source_target_pairs={{16,8},{17,9},{18,10},{19,11},{20,12},{21,13},{22,14},{23,15}} | collective-permute-start | bytes 221192 | tf_op jit(solution)/shard_map/ppermute | solution.py:30
  72.0 14.6 %collective-permute-start.8 = (bf16[1,4,24,384]{3,2,1,0:T(8,128)(2,1)S(1)}, bf16[1,4,24,384]{3,2,1,0:T(8,128)(2,1)S(1)}, u32[]{:S(2)}, u32[]{:S(2)}) collective-permute-start(bf16[1,4,24,384]{3,2,1,0:T(8,128)(2,1)S(1)} %get-tuple-element.69), channel_id=1, source_target_pairs={{16,0},{17,1},{18,2},{19,3},{20,4},{21,5},{22,6},{23,7}} | collective-permute-start | bytes 221192 | tf_op jit(solution)/shard_map/ppermute | solution.py:30
  75.3 0.7 copy-start.2
  79.1 7.5 %collective-permute-start.15 = (bf16[1,4,24,384]{3,2,1,0:T(8,128)(2,1)S(1)}, bf16[1,4,24,384]{3,2,1,0:T(8,128)(2,1)S(1)}, u32[]{:S(2)}, u32[]{:S(2)}) collective-permute-start(bf16[1,4,24,384]{3,2,1,0:T(8,128)(2,1)S(1)} %bitcast.87), channel_id=1, source_target_pairs={{24,8},{25,9},{26,10},{27,11},{28,12},{29,13},{30,14},{31,15}} | collective-permute-start | bytes 221192 | tf_op jit(solution)/shard_map/ppermute | solution.py:30
  79.9 6.7 %collective-permute-start.16 = (bf16[1,4,24,384]{3,2,1,0:T(8,128)(2,1)S(1)}, bf16[1,4,24,384]{3,2,1,0:T(8,128)(2,1)S(1)}, u32[]{:S(2)}, u32[]{:S(2)}) collective-permute-start(bf16[1,4,24,384]{3,2,1,0:T(8,128)(2,1)S(1)} %bitcast.88), channel_id=1, source_target_pairs={{24,0},{25,1},{26,2},{27,3},{28,4},{29,5},{30,6},{31,7}} | collective-permute-start | bytes 221192 | tf_op jit(solution)/shard_map/ppermute | solution.py:30
  85.2 9.4 %collective-permute-start.14 = (bf16[1,4,24,384]{3,2,1,0:T(8,128)(2,1)S(1)}, bf16[1,4,24,384]{3,2,1,0:T(8,128)(2,1)S(1)}, u32[]{:S(2)}, u32[]{:S(2)}) collective-permute-start(bf16[1,4,24,384]{3,2,1,0:T(8,128)(2,1)S(1)} %bitcast.89), channel_id=1, source_target_pairs={{24,16},{25,17},{26,18},{27,19},{28,20},{29,21},{30,22},{31,23}} | collective-permute-start | bytes 221192 | tf_op jit(solution)/shard_map/ppermute | solution.py:30

commit v7 on v6

--- a/solution.py
+++ b/solution.py
@@ -15,15 +15,18 @@
 
 
 def causal_conv(window, kernel, before=2):
-    result = lax.conv_general_dilated(
-        window[None],
+    return batched_conv(window[None], kernel, before)[0]
+
+
+def batched_conv(windows, kernel, before=2):
+    return lax.conv_general_dilated(
+        windows,
         kernel,
         window_strides=(1, 1, 1),
         padding=((before, 0), (0, 0), (1, 1)),
         dimension_numbers=("NDHWC", "DHWIO", "NDHWC"),
         preferred_element_type=jnp.float32,
     )
-    return result[0]
 
 
 def send(value, pairs):
@@ -94,7 +97,19 @@
                             segment_index == target, piece, branch
                         )
             break
-        produced = lax.cond(segment_index == stage, compute, idle, window, skip)
+        if stage == 0 and height >= 3:
+            inner = activate(features, gain_row)
+            middle = causal_conv(inner, kernel)
+            edges = jnp.stack(
+                [
+                    jnp.concatenate([activate(top, gain_row), inner[:, :2]], axis=1),
+                    jnp.concatenate([inner[:, height - 2 :], activate(bottom, gain_row)], axis=1),
+                ]
+            )
+            rims = batched_conv(edges, kernel)
+            produced = jnp.concatenate([rims[0], middle, rims[1]], axis=1).astype(jnp.bfloat16)
+        else:
+            produced = lax.cond(segment_index == stage, compute, idle, window, skip)
         if stage == last_stage - 1:
             owned = current[stage * group : (stage + 1) * group]
             for target in range(segment_count):

time: 95.6 us -> 104 us (1.088)
  matrix products: 13.9 us -> 26.2 us
  waiting for transfers between devices: 48.1 us -> 37.8 us
  other arithmetic: 5.27 us -> 8.64 us
  local copies, waits for them, and re-layouts: 4.51 us -> 6.62 us
    conv_general_dilated x3 -> x5, matrix products: 13.9 us -> 26.2 us  [batched_conv(): lax.conv_general_dilated(windows, kernel, window_strides=(1, 1, 1), paddi...]
    ppermute x15, waiting for transfers between devices: 45.1 us -> 37.8 us  [send(): return lax.ppermute(value, BOTH, pairs)]
    ppermute x1, waiting for transfers between devices: 3.03 us -> 0.01 us  [local(): bottom = lax.ppermute(features[:, :1], 'rows', down)]
    convert_element_type x2 -> x4, other arithmetic: 1.56 us -> 2.94 us  [activate(): return jax.nn.silu(widened * lax.rsqrt(mean_square + 1e-06) * gain_row.as...]
    reduce_sum x2 -> x5, other arithmetic: 0.95 us -> 2.24 us  [activate(): mean_square = jnp.mean(widened * widened, axis=-1, keepdims=True)]
  transfers between devices with their start and end apart: 17 -> 17, of which waited for: 4 -> 3; matrix products, arithmetic and copies ran while one was open for 12% -> 20% of each run, Pallas kernels for 0% -> 0%
where the time goes in v7:
time: 104 us; the launch traced here: 103 us
  waiting for transfers between devices  37.8 us (36%)
  matrix products  26.2 us (25%)
  starting transfers between devices  22.5 us (22%)
  other arithmetic  8.64 us (8%)
  local copies, waits for them, and re-layouts  6.62 us (6%)
    ppermute x15, waiting for transfers between devices, send(): return lax.ppermute(value, BOTH, pairs)  37.8 us
    conv_general_dilated x5, matrix products, batched_conv(): lax.conv_general_dilated(windows, kernel, window_strides=(1, 1, 1), paddi...  26.2 us
    ppermute x15, starting transfers between devices, send(): return lax.ppermute(value, BOTH, pairs)  16.9 us
    ppermute x1, starting transfers between devices, local(): top = lax.ppermute(features[:, height - 1:], 'rows', up)  3.02 us
    convert_element_type x4, other arithmetic, activate(): return jax.nn.silu(widened * lax.rsqrt(mean_square + 1e-06) * gain_row.as...  2.94 us
    ppermute x1, starting transfers between devices, local(): bottom = lax.ppermute(features[:, :1], 'rows', down)  2.58 us
    reduce_sum x5, other arithmetic, activate(): mean_square = jnp.mean(widened * widened, axis=-1, keepdims=True)  2.24 us
  transfers between devices with their start and end apart: 17, of which 3 were waited for; matrix products, arithmetic and copies ran while one was open for 20% of the time, Pallas kernels for 0%

profile of v7, /device:TPU:17, one launch (start us, length us, event | category | flops | bytes accessed | tf_op | source)
XLA Modules:
  0.0 102.8 jit_solution(2337605141371645799)
XLA Ops:
  0.0 1.0 fusion.131
  1.0 2.6 %collective-permute-start.1 = (bf16[4,1,24,384]{3,2,1,0:T(8,128)(2,1)S(1)}, bf16[4,1,24,384]{3,2,1,0:T(8,128)(2,1)S(1)}, u32[]{:S(2)}, u32[]{:S(2)}) collective-permute-start(bf16[4,1,24,384]{3,2,1,0:T(8,128)(2,1)S(1)} %get-tuple-element.61), channel_id=1, source_target_pairs={{1,0},{2,1},{3,2},{4,3},{5,4},{6,5},{7,6},{9,8},{10,9},{11,10},{12... | collective-permute-start | bytes 221192 | tf_op jit(solution)/shard_map/ppermute | solution.py:63
  3.6 3.0 %collective-permute-start = (bf16[4,1,24,384]{3,2,1,0:T(8,128)(2,1)S(1)}, bf16[4,1,24,384]{3,2,1,0:T(8,128)(2,1)S(1)}, u32[]{:S(2)}, u32[]{:S(2)}) collective-permute-start(bf16[4,1,24,384]{3,2,1,0:T(8,128)(2,1)S(1)} %get-tuple-element.60), channel_id=1, source_target_pairs={{0,1},{1,2},{2,3},{3,4},{4,5},{5,6},{6,7},{8,9},{9,10},{10,11},{11... | collective-permute-start | bytes 221192 | tf_op jit(solution)/shard_map/ppermute | solution.py:62
  6.6 1.1 %fusion.73 = f32[4,4,24]{2,1,0:T(4,128)S(1)} fusion(bf16[4,4,24,384]{3,2,1,0:T(8,128)(2,1)} %param.7), kind=kLoop, calls=%fused_computation.96 | loop fusion | flops 441984 | bytes 296448 | tf_op jit(solution)/shard_map/reduce_sum | solution.py:11
  7.7 0.7 reduce.2
  8.4 1.2 %fusion.80 = bf16[4,4,24,384]{3,2,1,0:T(8,128)(2,1)S(1)} fusion(bf16[4,4,24,384]{3,2,1,0:T(8,128)(2,1)} %param.7, f32[384]{0:T(512)S(1)} %convert_element_type.118, f32[4,4,24]{2,1,0:T(4,128)S(1)} %add_rsqrt_fusion.3), kind=kLoop, calls=%fused_computation.103 | loop fusion | flops 1179648 | bytes 592896 | tf_op jit(solution)/shard_map/convert_element_type | solution.py:14
  9.7 0.2 fusion.137
  10.4 0.2 copy-done.2
  10.6 6.2 %fusion.54 = bf16[4,2,8,4,384]{4,2,3,1,0:T(8,128)(2,1)S(1)} fusion(bf16[4,4,1,7,2,384]{5,3,4,1,0,2:T(8,128)(2,1)S(1)} %slice.125, bf16[4,4,1,8,4,384]{5,3,4,1,0,2:T(8,128)(2,1)S(1)} %copy.91, pred[8,4]{0,1:T(4,128)(4,1)S(1)} %copy-done.2, bf16[1,3,3,3,384,384]{5,4,3,2,1,0:T(8,128)(2,1)} %param.9), kind=kOutput, calls=%fused_computation.77 | convolution fusion | flops 1530789888 | bytes 8724512 | tf_op jit(solution)/shard_map/conv_general_dilated | solution.py:22
  18.1 0.5 copy-done.3
  18.6 6.2 %fusion.53 = bf16[4,1,16,4,384]{4,2,3,1,0:T(8,128)(2,1)S(1)} fusion(bf16[4,3,2,7,2,384]{5,3,2,4,1,0:T(8,128)(2,1)S(1)} %slice.121, bf16[4,3,2,8,4,384]{5,3,2,4,1,0:T(8,128)(2,1)S(1)} %copy.87, pred[16,4]{0,1:T(4,128)(4,1)S(1)} %copy-done.3, bf16[1,3,3,3,384,384]{5,4,3,2,1,0:T(8,128)(2,1)} %param.9), kind=kOutput, calls=%fused_computation.76 | convolution fusion | flops 1531674624 | bytes 9007168 | tf_op jit(solution)/shard_map/conv_general_dilated | solution.py:22
  25.4 0.5 pad_maximum_fusion.3
  25.9 0.7 collective-permute-start.3
  26.5 0.7 collective-permute-start.2
  27.2 0.7 collective-permute-start.4
  28.2 0.5 pad_maximum_fusion
  28.7 0.3 conditional.2
  29.0 1.3 %collective-permute-start.5 = (bf16[4,4,24,384]{3,2,1,0:T(8,128)(2,1)S(1)}, bf16[4,4,24,384]{3,2,1,0:T(8,128)(2,1)S(1)}, u32[]{:S(2)}, u32[]{:S(2)}) collective-permute-start(bf16[4,4,24,384]{3,2,1,0:T(8,128)(2,1)S(1)} %copy.99), channel_id=1, source_target_pairs={{8,16},{9,17},{10,18},{11,19},{12,20},{13,21},{14,22},{15,23}} | collective-permute-start | bytes 884744 | tf_op jit(solution)/shard_map/ppermute | solution.py:33
  30.3 1.3 %collective-permute-start.10 = (bf16[4,1,24,384]{3,2,1,0:T(8,128)(2,1)S(1)}, bf16[4,1,24,384]{3,2,1,0:T(8,128)(2,1)S(1)}, u32[]{:S(2)}, u32[]{:S(2)}) collective-permute-start(bf16[4,1,24,384]{3,2,1,0:T(8,128)(2,1)S(1)} %get-tuple-element.56), channel_id=1, source_target_pairs={{9,16},{10,17},{11,18},{12,19},{13,20},{14,21},{15,22}} | collective-permute-start | bytes 221192 | tf_op jit(solution)/shard_map/ppermute | solution.py:33
  31.6 1.3 %collective-permute-start.9 = (bf16[4,1,24,384]{3,2,1,0:T(8,128)(2,1)S(1)}, bf16[4,1,24,384]{3,2,1,0:T(8,128)(2,1)S(1)}, u32[]{:S(2)}, u32[]{:S(2)}) collective-permute-start(bf16[4,1,24,384]{3,2,1,0:T(8,128)(2,1)S(1)} %get-tuple-element.55), channel_id=1, source_target_pairs={{8,17},{9,18},{10,19},{11,20},{12,21},{13,22},{14,23}} | collective-permute-start | bytes 221192 | tf_op jit(solution)/shard_map/ppermute | solution.py:33
  32.9 29.7 %collective-permute-done.10 = bf16[4,1,24,384]{3,2,1,0:T(8,128)(2,1)S(1)} collective-permute-done((bf16[4,1,24,384]{3,2,1,0:T(8,128)(2,1)S(1)}, bf16[4,1,24,384]{3,2,1,0:T(8,128)(2,1)S(1)}, u32[]{:S(2)}, u32[]{:S(2)}) %collective-permute-start.10) | collective-permute-done | bytes 73760 | tf_op jit(solution)/shard_map/ppermute | solution.py:33
  62.7 9.9 %conditional.3 = (bf16[4,4,24,384]{3,1,2,0:T(4,128)(2,1)S(1)}) conditional(s32[]{:T(128)} %convert_element_type.125, () %tuple.19, (bf16[4,6,24,384]{3,2,1,0:T(8,128)(2,1)S(1)}, bf16[384]{0:T(512)(128)(2,1)S(1)}, bf16[3,3,3,384,384]{4,3,2,1,0:T(8,128)(2,1)}) %tuple.44), branch_computations={%region_6.7_spmd, %region_7.9_spmd} | conditional | flops 3063129088 | bytes 14648262 | solution.py:112
  62.7 0.3 fusion.22
  63.0 0.6 fusion.34
  63.7 0.2 pad.7
  64.1 0.2 copy-done.5
  64.3 7.9 %fusion.21 = bf16[4,4,8,4,384]{4,2,3,1,0:T(8,128)(2,1)S(1)} fusion(bf16[3,3,3,384,384]{4,3,2,1,0:T(8,128)(2,1)} %get-tuple-element.31, bf16[4,6,1,7,2,384]{5,3,4,1,0,2:T(8,128)(2,1)S(1)} %slice.117, bf16[4,6,1,8,4,384]{5,3,4,1,0,2:T(8,128)(2,1)S(1)} %copy.84, pred[8,4]{0,1:T(4,128)(4,1)S(1)} %copy-done.5), kind=kOutput, calls=%fused_computation.30 | convolution fusion | flops 3060695040 | bytes 9203744 | tf_op jit(solution)/shard_map/cond/branch_1_fun/conv_general_dilated | solution.py:22
  72.2 0.2 copy.85
  72.6 1.3 %collective-permute-start.12 = (bf16[4,4,24,384]{3,1,2,0:T(4,128)(2,1)S(1)}, bf16[4,4,24,384]{3,1,2,0:T(4,128)(2,1)S(1)}, u32[]{:S(2)}, u32[]{:S(2)}) collective-permute-start(bf16[4,4,24,384]{3,1,2,0:T(4,128)(2,1)S(1)} %get-tuple-element.75), channel_id=1, source_target_pairs={{16,24},{17,25},{18,26},{19,27},{20,28},{21,29},{22,30},{23,31}} | collective-permute-start | bytes 884744 | tf_op jit(solution)/shard_map/ppermute | solution.py:33
  73.9 0.2 fusion.128
  74.1 1.3 %collective-permute-start.11 = (bf16[4,1,24,384]{3,2,0,1:T(8,128)(2,1)S(1)}, bf16[4,1,24,384]{3,2,0,1:T(8,128)(2,1)S(1)}, u32[]{:S(2)}, u32[]{:S(2)}) collective-permute-start(bf16[4,1,24,384]{3,2,0,1:T(8,128)(2,1)S(1)} %copy.127), channel_id=1, source_target_pairs={{16,25},{17,26},{18,27},{19,28},{20,29},{21,30},{22,31}} | collective-permute-start | bytes 221192 | tf_op jit(solution)/shard_map/ppermute | solution.py:33
  75.4 1.6 %collective-permute-start.13 = (bf16[4,1,24,384]{3,2,0,1:T(8,128)(2,1)S(1)}, bf16[4,1,24,384]{3,2,0,1:T(8,128)(2,1)S(1)}, u32[]{:S(2)}, u32[]{:S(2)}) collective-permute-start(bf16[4,1,24,384]{3,2,0,1:T(8,128)(2,1)S(1)} %copy.128), channel_id=1, source_target_pairs={{17,24},{18,25},{19,26},{20,27},{21,28},{22,29},{23,30}} | collective-permute-start | bytes 221192 | tf_op jit(solution)/shard_map/ppermute | solution.py:33
  77.0 1.4 %collective-permute-start.6 = (bf16[1,4,24,384]{3,2,1,0:T(8,128)(2,1)S(1)}, bf16[1,4,24,384]{3,2,1,0:T(8,128)(2,1)S(1)}, u32[]{:S(2)}, u32[]{:S(2)}) collective-permute-start(bf16[1,4,24,384]{3,2,1,0:T(8,128)(2,1)S(1)} %get-tuple-element.59), channel_id=1, source_target_pairs={{16,24},{17,25},{18,26},{19,27},{20,28},{21,29},{22,30},{23,31}} | collective-permute-start | bytes 221192 | tf_op jit(solution)/shard_map/ppermute | solution.py:33
  78.5 1.3 %collective-permute-start.7 = (bf16[1,4,24,384]{3,2,1,0:T(8,128)(2,1)S(1)}, bf16[1,4,24,384]{3,2,1,0:T(8,128)(2,1)S(1)}, u32[]{:S(2)}, u32[]{:S(2)}) collective-permute-start(bf16[1,4,24,384]{3,2,1,0:T(8,128)(2,1)S(1)} %get-tuple-element.58), channel_id=1, source_target_pairs={{16,8},{17,9},{18,10},{19,11},{20,12},{21,13},{22,14},{23,15}} | collective-permute-start | bytes 221192 | tf_op jit(solution)/shard_map/ppermute | solution.py:33
  79.8 2.4 %collective-permute-done.11 = bf16[4,1,24,384]{3,2,0,1:T(8,128)(2,1)S(1)} collective-permute-done((bf16[4,1,24,384]{3,2,0,1:T(8,128)(2,1)S(1)}, bf16[4,1,24,384]{3,2,0,1:T(8,128)(2,1)S(1)}, u32[]{:S(2)}, u32[]{:S(2)}) %collective-permute-start.11) | collective-permute-done | bytes 73760 | tf_op jit(solution)/shard_map/ppermute | solution.py:33
  82.1 1.5 %collective-permute-start.8 = (bf16[1,4,24,384]{3,2,1,0:T(8,128)(2,1)S(1)}, bf16[1,4,24,384]{3,2,1,0:T(8,128)(2,1)S(1)}, u32[]{:S(2)}, u32[]{:S(2)}) collective-permute-start(bf16[1,4,24,384]{3,2,1,0:T(8,128)(2,1)S(1)} %get-tuple-element.57), channel_id=1, source_target_pairs={{16,0},{17,1},{18,2},{19,3},{20,4},{21,5},{22,6},{23,7}} | collective-permute-start | bytes 221192 | tf_op jit(solution)/shard_map/ppermute | solution.py:33
  84.1 0.6 fusion.42
  84.8 0.8 fusion.49
  85.8 0.2 copy.118
  86.1 2.9 %fusion.52 = bf16[2,4,8,4,384]{4,2,3,1,0:T(8,128)(2,1)S(1)} fusion(bf16[4,6,1,7,2,384]{5,3,4,1,0,2:T(8,128)(2,1)S(1)} %slice.140, bf16[4,6,1,8,4,384]{5,3,4,1,0,2:T(8,128)(2,1)S(1)} %copy.118, pred[8,4]{0,1:T(4,128)(4,1)S(1)} %copy-done.2, bf16[1,3,3,3,384,384]{5,4,3,2,1,0:T(8,128)(2,1)S(1)} %copy-done.1), kind=kOutput, calls=%fused_computation.75 | convolution fusion | flops 2041282560 | bytes 9007136 | tf_op jit(solution)/shard_map/conv_general_dilated | solution.py:22
  89.2 0.7 collective-permute-start.15
  90.0 0.7 collective-permute-start.16
  90.6 0.8 fusion.85
  91.6 0.2 copy.111
  91.8 2.9 %fusion.51 = bf16[2,4,8,4,384]{4,2,3,1,0:T(8,128)(2,1)S(1)} fusion(bf16[4,6,1,7,2,384]{5,3,4,1,0,2:T(8,128)(2,1)S(1)} %slice.135, bf16[4,6,1,8,4,384]{5,3,4,1,0,2:T(8,128)(2,1)S(1)} %copy.111, pred[8,4]{0,1:T(4,128)(4,1)S(1)} %copy-done.2, bf16[1,3,3,3,384,384]{5,4,3,2,1,0:T(8,128)(2,1)S(1)} %copy-done.1), kind=kOutput, calls=%fused_computation.74 | convolution fusion | flops 2041282560 | bytes 9007136 | tf_op jit(solution)/shard_map/conv_general_dilated | solution.py:22
  94.9 1.3 %collective-permute-start.14 = (bf16[1,4,24,384]{3,2,1,0:T(8,128)(2,1)S(1)}, bf16[1,4,24,384]{3,2,1,0:T(8,128)(2,1)S(1)}, u32[]{:S(2)}, u32[]{:S(2)}) collective-permute-start(bf16[1,4,24,384]{3,2,1,0:T(8,128)(2,1)S(1)} %bitcast.113), channel_id=1, source_target_pairs={{24,16},{25,17},{26,18},{27,19},{28,20},{29,21},{30,22},{31,23}} | collective-permute-start | bytes 221192 | tf_op jit(solution)/shard_map/ppermute | solution.py:33
  96.4 5.7 %collective-permute-done.14 = bf16[1,4,24,384]{3,2,1,0:T(8,128)(2,1)S(1)} collective-permute-done((bf16[1,4,24,384]{3,2,1,0:T(8,128)(2,1)S(1)}, bf16[1,4,24,384]{3,2,1,0:T(8,128)(2,1)S(1)}, u32[]{:S(2)}, u32[]{:S(2)}) %collective-permute-start.14) | collective-permute-done | bytes 73760 | tf_op jit(solution)/shard_map/ppermute | solution.py:33
  102.1 0.7 add_convert_fusion
  (83 shorter events, 4.3 us)
Async XLA Ops:
  0.0 9.6 %copy-start = (bf16[4,4,24,384]{3,2,1,0:T(8,128)(2,1)S(1)}, bf16[4,4,24,384]{3,2,1,0:T(8,128)(2,1)}, u32[]{:S(2)}) copy-start(bf16[4,4,24,384]{3,2,1,0:T(8,128)(2,1)} %param.7) | copy-start | bytes 884740
  1.0 16.1 %collective-permute-start.1 = (bf16[4,1,24,384]{3,2,1,0:T(8,128)(2,1)S(1)}, bf16[4,1,24,384]{3,2,1,0:T(8,128)(2,1)S(1)}, u32[]{:S(2)}, u32[]{:S(2)}) collective-permute-start(bf16[4,1,24,384]{3,2,1,0:T(8,128)(2,1)S(1)} %get-tuple-element.61), channel_id=1, source_target_pairs={{1,0},{2,1},{3,2},{4,3},{5,4},{6,5},{7,6},{9,8},{10,9},{11,10},{12... | collective-permute-start | bytes 221192 | tf_op jit(solution)/shard_map/ppermute | solution.py:63
  3.6 13.6 %collective-permute-start = (bf16[4,1,24,384]{3,2,1,0:T(8,128)(2,1)S(1)}, bf16[4,1,24,384]{3,2,1,0:T(8,128)(2,1)S(1)}, u32[]{:S(2)}, u32[]{:S(2)}) collective-permute-start(bf16[4,1,24,384]{3,2,1,0:T(8,128)(2,1)S(1)} %get-tuple-element.60), channel_id=1, source_target_pairs={{0,1},{1,2},{2,3},{3,4},{4,5},{5,6},{6,7},{8,9},{9,10},{10,11},{11... | collective-permute-start | bytes 221192 | tf_op jit(solution)/shard_map/ppermute | solution.py:62
  10.0 0.7 copy-start.2
  17.9 0.7 copy-start.3
  25.9 2.3 %collective-permute-start.3 = (bf16[4,4,24,384]{3,1,2,0:T(4,128)(2,1)S(1)}, bf16[4,4,24,384]{3,1,2,0:T(4,128)(2,1)S(1)}, u32[]{:S(2)}, u32[]{:S(2)}) collective-permute-start(bf16[4,4,24,384]{3,1,2,0:T(4,128)(2,1)S(1)} %pad_maximum_fusion.3), channel_id=1, source_target_pairs={{0,8},{1,9},{2,10},{3,11},{4,12},{5,13},{6,14},{7,15}} | collective-permute-start | bytes 884744 | tf_op jit(solution)/shard_map/ppermute | solution.py:33
  26.5 1.4 %collective-permute-start.2 = (bf16[4,1,24,384]{3,0,2,1:T(4,128)(2,1)S(1)}, bf16[4,1,24,384]{3,0,2,1:T(4,128)(2,1)S(1)}, u32[]{:S(2)}, u32[]{:S(2)}) collective-permute-start(bf16[4,1,24,384]{3,0,2,1:T(4,128)(2,1)S(1)} %get-tuple-element.68), channel_id=1, source_target_pairs={{0,9},{1,10},{2,11},{3,12},{4,13},{5,14},{6,15}} | collective-permute-start | bytes 221192 | tf_op jit(solution)/shard_map/ppermute | solution.py:33
  27.2 0.8 collective-permute-start.4
  29.0 33.6 %collective-permute-start.5 = (bf16[4,4,24,384]{3,2,1,0:T(8,128)(2,1)S(1)}, bf16[4,4,24,384]{3,2,1,0:T(8,128)(2,1)S(1)}, u32[]{:S(2)}, u32[]{:S(2)}) collective-permute-start(bf16[4,4,24,384]{3,2,1,0:T(8,128)(2,1)S(1)} %copy.99), channel_id=1, source_target_pairs={{8,16},{9,17},{10,18},{11,19},{12,20},{13,21},{14,22},{15,23}} | collective-permute-start | bytes 884744 | tf_op jit(solution)/shard_map/ppermute | solution.py:33
  30.3 32.3 %collective-permute-start.10 = (bf16[4,1,24,384]{3,2,1,0:T(8,128)(2,1)S(1)}, bf16[4,1,24,384]{3,2,1,0:T(8,128)(2,1)S(1)}, u32[]{:S(2)}, u32[]{:S(2)}) collective-permute-start(bf16[4,1,24,384]{3,2,1,0:T(8,128)(2,1)S(1)} %get-tuple-element.56), channel_id=1, source_target_pairs={{9,16},{10,17},{11,18},{12,19},{13,20},{14,21},{15,22}} | collective-permute-start | bytes 221192 | tf_op jit(solution)/shard_map/ppermute | solution.py:33
  31.6 31.0 %collective-permute-start.9 = (bf16[4,1,24,384]{3,2,1,0:T(8,128)(2,1)S(1)}, bf16[4,1,24,384]{3,2,1,0:T(8,128)(2,1)S(1)}, u32[]{:S(2)}, u32[]{:S(2)}) collective-permute-start(bf16[4,1,24,384]{3,2,1,0:T(8,128)(2,1)S(1)} %get-tuple-element.55), channel_id=1, source_target_pairs={{8,17},{9,18},{10,19},{11,20},{12,21},{13,22},{14,23}} | collective-permute-start | bytes 221192 | tf_op jit(solution)/shard_map/ppermute | solution.py:33
  63.6 0.7 copy-start.5
  72.6 11.6 %collective-permute-start.12 = (bf16[4,4,24,384]{3,1,2,0:T(4,128)(2,1)S(1)}, bf16[4,4,24,384]{3,1,2,0:T(4,128)(2,1)S(1)}, u32[]{:S(2)}, u32[]{:S(2)}) collective-permute-start(bf16[4,4,24,384]{3,1,2,0:T(4,128)(2,1)S(1)} %get-tuple-element.75), channel_id=1, source_target_pairs={{16,24},{17,25},{18,26},{19,27},{20,28},{21,29},{22,30},{23,31}} | collective-permute-start | bytes 884744 | tf_op jit(solution)/shard_map/ppermute | solution.py:33
  74.1 8.0 %collective-permute-start.11 = (bf16[4,1,24,384]{3,2,0,1:T(8,128)(2,1)S(1)}, bf16[4,1,24,384]{3,2,0,1:T(8,128)(2,1)S(1)}, u32[]{:S(2)}, u32[]{:S(2)}) collective-permute-start(bf16[4,1,24,384]{3,2,0,1:T(8,128)(2,1)S(1)} %copy.127), channel_id=1, source_target_pairs={{16,25},{17,26},{18,27},{19,28},{20,29},{21,30},{22,31}} | collective-permute-start | bytes 221192 | tf_op jit(solution)/shard_map/ppermute | solution.py:33
  75.4 10.7 %copy-start.1 = (bf16[1,3,3,3,384,384]{5,4,3,2,1,0:T(8,128)(2,1)S(1)}, bf16[1,3,3,3,384,384]{5,4,3,2,1,0:T(8,128)(2,1)}, u32[]{:S(2)}) copy-start(bf16[1,3,3,3,384,384]{5,4,3,2,1,0:T(8,128)(2,1)} %param.9) | copy-start | bytes 23887876
  75.4 8.3 %collective-permute-start.13 = (bf16[4,1,24,384]{3,2,0,1:T(8,128)(2,1)S(1)}, bf16[4,1,24,384]{3,2,0,1:T(8,128)(2,1)S(1)}, u32[]{:S(2)}, u32[]{:S(2)}) collective-permute-start(bf16[4,1,24,384]{3,2,0,1:T(8,128)(2,1)S(1)} %copy.128), channel_id=1, source_target_pairs={{17,24},{18,25},{19,26},{20,27},{21,28},{22,29},{23,30}} | collective-permute-start | bytes 221192 | tf_op jit(solution)/shard_map/ppermute | solution.py:33
  77.0 17.9 %collective-permute-start.6 = (bf16[1,4,24,384]{3,2,1,0:T(8,128)(2,1)S(1)}, bf16[1,4,24,384]{3,2,1,0:T(8,128)(2,1)S(1)}, u32[]{:S(2)}, u32[]{:S(2)}) collective-permute-start(bf16[1,4,24,384]{3,2,1,0:T(8,128)(2,1)S(1)} %get-tuple-element.59), channel_id=1, source_target_pairs={{16,24},{17,25},{18,26},{19,27},{20,28},{21,29},{22,30},{23,31}} | collective-permute-start | bytes 221192 | tf_op jit(solution)/shard_map/ppermute | solution.py:33
  78.5 17.9 %collective-permute-start.7 = (bf16[1,4,24,384]{3,2,1,0:T(8,128)(2,1)S(1)}, bf16[1,4,24,384]{3,2,1,0:T(8,128)(2,1)S(1)}, u32[]{:S(2)}, u32[]{:S(2)}) collective-permute-start(bf16[1,4,24,384]{3,2,1,0:T(8,128)(2,1)S(1)} %get-tuple-element.58), channel_id=1, source_target_pairs={{16,8},{17,9},{18,10},{19,11},{20,12},{21,13},{22,14},{23,15}} | collective-permute-start | bytes 221192 | tf_op jit(solution)/shard_map/ppermute | solution.py:33
  82.1 14.2 %collective-permute-start.8 = (bf16[1,4,24,384]{3,2,1,0:T(8,128)(2,1)S(1)}, bf16[1,4,24,384]{3,2,1,0:T(8,128)(2,1)S(1)}, u32[]{:S(2)}, u32[]{:S(2)}) collective-permute-start(bf16[1,4,24,384]{3,2,1,0:T(8,128)(2,1)S(1)} %get-tuple-element.57), channel_id=1, source_target_pairs={{16,0},{17,1},{18,2},{19,3},{20,4},{21,5},{22,6},{23,7}} | collective-permute-start | bytes 221192 | tf_op jit(solution)/shard_map/ppermute | solution.py:33
  89.2 7.2 %collective-permute-start.15 = (bf16[1,4,24,384]{3,2,1,0:T(8,128)(2,1)S(1)}, bf16[1,4,24,384]{3,2,1,0:T(8,128)(2,1)S(1)}, u32[]{:S(2)}, u32[]{:S(2)}) collective-permute-start(bf16[1,4,24,384]{3,2,1,0:T(8,128)(2,1)S(1)} %bitcast.111), channel_id=1, source_target_pairs={{24,8},{25,9},{26,10},{27,11},{28,12},{29,13},{30,14},{31,15}} | collective-permute-start | bytes 221192 | tf_op jit(solution)/shard_map/ppermute | solution.py:33
  90.0 6.4 %collective-permute-start.16 = (bf16[1,4,24,384]{3,2,1,0:T(8,128)(2,1)S(1)}, bf16[1,4,24,384]{3,2,1,0:T(8,128)(2,1)S(1)}, u32[]{:S(2)}, u32[]{:S(2)}) collective-permute-start(bf16[1,4,24,384]{3,2,1,0:T(8,128)(2,1)S(1)} %bitcast.112), channel_id=1, source_target_pairs={{24,0},{25,1},{26,2},{27,3},{28,4},{29,5},{30,6},{31,7}} | collective-permute-start | bytes 221192 | tf_op jit(solution)/shard_map/ppermute | solution.py:33
  94.9 7.2 %collective-permute-start.14 = (bf16[1,4,24,384]{3,2,1,0:T(8,128)(2,1)S(1)}, bf16[1,4,24,384]{3,2,1,0:T(8,128)(2,1)S(1)}, u32[]{:S(2)}, u32[]{:S(2)}) collective-permute-start(bf16[1,4,24,384]{3,2,1,0:T(8,128)(2,1)S(1)} %bitcast.113), channel_id=1, source_target_pairs={{24,16},{25,17},{26,18},{27,19},{28,20},{29,21},{30,22},{31,23}} | collective-permute-start | bytes 221192 | tf_op jit(solution)/shard_map/ppermute | solution.py:33

commit v8 on v6

--- a/solution.py
+++ b/solution.py
@@ -15,15 +15,18 @@
 
 
 def causal_conv(window, kernel, before=2):
-    result = lax.conv_general_dilated(
-        window[None],
+    return batched_conv(window[None], kernel, before)[0]
+
+
+def batched_conv(windows, kernel, before=2):
+    return lax.conv_general_dilated(
+        windows,
         kernel,
         window_strides=(1, 1, 1),
         padding=((before, 0), (0, 0), (1, 1)),
         dimension_numbers=("NDHWC", "DHWIO", "NDHWC"),
         preferred_element_type=jnp.float32,
     )
-    return result[0]
 
 
 def send(value, pairs):
@@ -68,7 +71,12 @@
         final = stage == last_stage
 
         def compute(window, skip, odd=odd, final=final):
-            convolved = causal_conv(activate(window, gain_row), kernel).astype(jnp.bfloat16)
+            activated = jnp.pad(activate(window, gain_row), ((2, 0), (0, 0), (0, 0), (0, 0)))
+            split = frame_count // 2
+            bounds = ((0, split), (split, frame_count)) if split else ((0, frame_count),)
+            halves = jnp.stack([activated[low : high + 2] for low, high in bounds])
+            convolved = batched_conv(halves, kernel, 0).astype(jnp.bfloat16)
+            convolved = convolved.reshape((-1,) + convolved.shape[2:])
             if odd and not final:
                 convolved = (skip.astype(jnp.float32) + convolved).astype(jnp.bfloat16)
             return convolved

time: 95.6 us -> 104 us (1.088)
  waiting for transfers between devices: 48.1 us -> 53.1 us
  matrix products: 13.9 us -> 18.4 us
    ppermute x15, waiting for transfers between devices: 45.1 us -> 50.1 us  [send(): return lax.ppermute(value, BOTH, pairs)]
    conv_general_dilated x3, matrix products: 13.9 us -> 18.4 us  [batched_conv(): lax.conv_general_dilated(windows, kernel, window_strides=(1, 1, 1), paddi...]
where the time goes in v8:
time: 104 us
  waiting for transfers between devices  53.1 us (51%)
  starting transfers between devices  22.2 us (21%)
  matrix products  18.4 us (18%)
  local copies, waits for them, and re-layouts  4.61 us (4%)
  other arithmetic  4.32 us (4%)
    ppermute x15, waiting for transfers between devices, send(): return lax.ppermute(value, BOTH, pairs)  50.1 us
    conv_general_dilated x3, matrix products, batched_conv(): lax.conv_general_dilated(windows, kernel, window_strides=(1, 1, 1), paddi...  18.4 us
    ppermute x15, starting transfers between devices, send(): return lax.ppermute(value, BOTH, pairs)  16.6 us
    ppermute x1, starting transfers between devices, local(): top = lax.ppermute(features[:, height - 1:], 'rows', up)  3.68 us
    ppermute x1, waiting for transfers between devices, local(): bottom = lax.ppermute(features[:, :1], 'rows', down)  3.03 us
  transfers between devices with their start and end apart: 17, of which 4 were waited for; matrix products, arithmetic and copies ran while one was open for 12% of the time, Pallas kernels for 0%

profile of v8, /device:TPU:17, one launch (start us, length us, event | category | flops | bytes accessed | tf_op | source)
XLA Modules:
  0.0 103.6 jit_solution(3660744588294134140)
XLA Ops:
  0.0 0.9 fusion.125
  0.9 3.7 %collective-permute-start = (bf16[4,1,24,384]{3,2,1,0:T(8,128)(2,1)S(1)}, bf16[4,1,24,384]{3,2,1,0:T(8,128)(2,1)S(1)}, u32[]{:S(2)}, u32[]{:S(2)}) collective-permute-start(bf16[4,1,24,384]{3,2,1,0:T(8,128)(2,1)S(1)} %get-tuple-element.59), channel_id=1, source_target_pairs={{0,1},{1,2},{2,3},{3,4},{4,5},{5,6},{6,7},{8,9},{9,10},{10,11},{11... | collective-permute-start | bytes 221192 | tf_op jit(solution)/shard_map/ppermute | solution.py:62
  4.6 1.9 %collective-permute-start.1 = (bf16[4,1,24,384]{3,2,1,0:T(8,128)(2,1)S(1)}, bf16[4,1,24,384]{3,2,1,0:T(8,128)(2,1)S(1)}, u32[]{:S(2)}, u32[]{:S(2)}) collective-permute-start(bf16[4,1,24,384]{3,2,1,0:T(8,128)(2,1)S(1)} %get-tuple-element.60), channel_id=1, source_target_pairs={{1,0},{2,1},{3,2},{4,3},{5,4},{6,5},{7,6},{9,8},{10,9},{11,10},{12... | collective-permute-start | bytes 221192 | tf_op jit(solution)/shard_map/ppermute | solution.py:63
  6.6 0.7 reduce
  7.3 3.0 %collective-permute-done.1 = bf16[4,1,24,384]{3,2,1,0:T(8,128)(2,1)S(1)} collective-permute-done((bf16[4,1,24,384]{3,2,1,0:T(8,128)(2,1)S(1)}, bf16[4,1,24,384]{3,2,1,0:T(8,128)(2,1)S(1)}, u32[]{:S(2)}, u32[]{:S(2)}) %collective-permute-start.1) | collective-permute-done | bytes 73760 | tf_op jit(solution)/shard_map/ppermute | solution.py:63
  10.3 1.0 pad_maximum_fusion
  11.4 0.8 collective-permute-start.3
  12.2 0.7 collective-permute-start.2
  12.9 0.7 collective-permute-start.4
  13.7 0.2 conditional.4
  14.0 1.3 %collective-permute-start.5 = (bf16[4,4,24,384]{3,2,1,0:T(8,128)(2,1)S(1)}, bf16[4,4,24,384]{3,2,1,0:T(8,128)(2,1)S(1)}, u32[]{:S(2)}, u32[]{:S(2)}) collective-permute-start(bf16[4,4,24,384]{3,2,1,0:T(8,128)(2,1)S(1)} %get-tuple-element.66), channel_id=1, source_target_pairs={{8,16},{9,17},{10,18},{11,19},{12,20},{13,21},{14,22},{15,23}} | collective-permute-start | bytes 884744 | tf_op jit(solution)/shard_map/ppermute | solution.py:33
  15.3 1.3 %collective-permute-start.10 = (bf16[4,1,24,384]{3,2,1,0:T(8,128)(2,1)S(1)}, bf16[4,1,24,384]{3,2,1,0:T(8,128)(2,1)S(1)}, u32[]{:S(2)}, u32[]{:S(2)}) collective-permute-start(bf16[4,1,24,384]{3,2,1,0:T(8,128)(2,1)S(1)} %get-tuple-element.53), channel_id=1, source_target_pairs={{9,16},{10,17},{11,18},{12,19},{13,20},{14,21},{15,22}} | collective-permute-start | bytes 221192 | tf_op jit(solution)/shard_map/ppermute | solution.py:33
  16.6 1.3 %collective-permute-start.9 = (bf16[4,1,24,384]{3,2,1,0:T(8,128)(2,1)S(1)}, bf16[4,1,24,384]{3,2,1,0:T(8,128)(2,1)S(1)}, u32[]{:S(2)}, u32[]{:S(2)}) collective-permute-start(bf16[4,1,24,384]{3,2,1,0:T(8,128)(2,1)S(1)} %get-tuple-element.52), channel_id=1, source_target_pairs={{8,17},{9,18},{10,19},{11,20},{12,21},{13,22},{14,23}} | collective-permute-start | bytes 221192 | tf_op jit(solution)/shard_map/ppermute | solution.py:33
  17.9 39.7 %collective-permute-done.10 = bf16[4,1,24,384]{3,2,1,0:T(8,128)(2,1)S(1)} collective-permute-done((bf16[4,1,24,384]{3,2,1,0:T(8,128)(2,1)S(1)}, bf16[4,1,24,384]{3,2,1,0:T(8,128)(2,1)S(1)}, u32[]{:S(2)}, u32[]{:S(2)}) %collective-permute-start.10) | collective-permute-done | bytes 73760 | tf_op jit(solution)/shard_map/ppermute | solution.py:33
  57.7 11.9 %conditional.5 = (bf16[4,4,24,384]{3,2,1,0:T(8,128)(2,1)S(1)}) conditional(s32[]{:T(128)} %convert_element_type.113, () %tuple.27, (bf16[4,6,24,384]{3,2,1,0:T(8,128)(2,1)S(1)}, bf16[384]{0:T(512)(128)(2,1)S(1)}, bf16[3,3,3,384,384]{4,3,2,1,0:T(8,128)(2,1)}) %tuple.48), branch_computations={%region_6.7_spmd, %region_7.9_spmd} | conditional | flops 4087211008 | bytes 24716134 | solution.py:105
  57.7 0.2 fusion.69
  57.9 0.3 fusion.76
  58.3 0.3 fusion.133
  58.7 0.5 pad.18
  59.2 0.3 reshape.137
  59.5 0.2 copy.76
  59.8 0.1 slice.117
  59.9 0.3 copy-done.4
  60.2 8.9 %fusion.66 = bf16[2,4,16,4,384]{4,2,3,1,0:T(8,128)(2,1)S(1)} fusion(bf16[3,3,3,384,384]{4,3,2,1,0:T(8,128)(2,1)} %get-tuple-element.43, bf16[4,6,2,7,2,384]{5,3,2,4,1,0:T(8,128)(2,1)S(1)} %slice.117, bf16[4,6,2,8,4,384]{5,3,2,4,1,0:T(8,128)(2,1)S(1)} %copy.76, pred[16,4]{0,1:T(4,128)(4,1)S(1)} %copy-done.4), kind=kOutput, calls=%fused_computation.69 | convolution fusion | flops 4082565120 | bytes 10051648 | tf_op jit(solution)/shard_map/cond/branch_1_fun/conv_general_dilated | solution.py:22
  69.1 0.3 copy.77
  69.6 1.5 %collective-permute-start.12 = (bf16[4,4,24,384]{3,2,1,0:T(8,128)(2,1)S(1)}, bf16[4,4,24,384]{3,2,1,0:T(8,128)(2,1)S(1)}, u32[]{:S(2)}, u32[]{:S(2)}) collective-permute-start(bf16[4,4,24,384]{3,2,1,0:T(8,128)(2,1)S(1)} %get-tuple-element.67), channel_id=1, source_target_pairs={{16,24},{17,25},{18,26},{19,27},{20,28},{21,29},{22,30},{23,31}} | collective-permute-start | bytes 884744 | tf_op jit(solution)/shard_map/ppermute | solution.py:33
  71.2 1.3 %collective-permute-start.11 = (bf16[4,1,24,384]{3,2,1,0:T(8,128)(2,1)S(1)}, bf16[4,1,24,384]{3,2,1,0:T(8,128)(2,1)S(1)}, u32[]{:S(2)}, u32[]{:S(2)}) collective-permute-start(bf16[4,1,24,384]{3,2,1,0:T(8,128)(2,1)S(1)} %get-tuple-element.50), channel_id=1, source_target_pairs={{16,25},{17,26},{18,27},{19,28},{20,29},{21,30},{22,31}} | collective-permute-start | bytes 221192 | tf_op jit(solution)/shard_map/ppermute | solution.py:33
  72.5 1.3 %collective-permute-start.13 = (bf16[4,1,24,384]{3,2,1,0:T(8,128)(2,1)S(1)}, bf16[4,1,24,384]{3,2,1,0:T(8,128)(2,1)S(1)}, u32[]{:S(2)}, u32[]{:S(2)}) collective-permute-start(bf16[4,1,24,384]{3,2,1,0:T(8,128)(2,1)S(1)} %get-tuple-element.51), channel_id=1, source_target_pairs={{17,24},{18,25},{19,26},{20,27},{21,28},{22,29},{23,30}} | collective-permute-start | bytes 221192 | tf_op jit(solution)/shard_map/ppermute | solution.py:33
  73.8 1.3 %collective-permute-start.6 = (bf16[1,4,24,384]{3,2,1,0:T(8,128)(2,1)S(1)}, bf16[1,4,24,384]{3,2,1,0:T(8,128)(2,1)S(1)}, u32[]{:S(2)}, u32[]{:S(2)}) collective-permute-start(bf16[1,4,24,384]{3,2,1,0:T(8,128)(2,1)S(1)} %get-tuple-element.56), channel_id=1, source_target_pairs={{16,24},{17,25},{18,26},{19,27},{20,28},{21,29},{22,30},{23,31}} | collective-permute-start | bytes 221192 | tf_op jit(solution)/shard_map/ppermute | solution.py:33
  75.1 1.3 %collective-permute-start.7 = (bf16[1,4,24,384]{3,2,1,0:T(8,128)(2,1)S(1)}, bf16[1,4,24,384]{3,2,1,0:T(8,128)(2,1)S(1)}, u32[]{:S(2)}, u32[]{:S(2)}) collective-permute-start(bf16[1,4,24,384]{3,2,1,0:T(8,128)(2,1)S(1)} %get-tuple-element.55), channel_id=1, source_target_pairs={{16,8},{17,9},{18,10},{19,11},{20,12},{21,13},{22,14},{23,15}} | collective-permute-start | bytes 221192 | tf_op jit(solution)/shard_map/ppermute | solution.py:33
  76.4 2.3 %collective-permute-done.11 = bf16[4,1,24,384]{3,2,1,0:T(8,128)(2,1)S(1)} collective-permute-done((bf16[4,1,24,384]{3,2,1,0:T(8,128)(2,1)S(1)}, bf16[4,1,24,384]{3,2,1,0:T(8,128)(2,1)S(1)}, u32[]{:S(2)}, u32[]{:S(2)}) %collective-permute-start.11) | collective-permute-done | bytes 73760 | tf_op jit(solution)/shard_map/ppermute | solution.py:33
  78.7 1.3 %collective-permute-start.8 = (bf16[1,4,24,384]{3,2,1,0:T(8,128)(2,1)S(1)}, bf16[1,4,24,384]{3,2,1,0:T(8,128)(2,1)S(1)}, u32[]{:S(2)}, u32[]{:S(2)}) collective-permute-start(bf16[1,4,24,384]{3,2,1,0:T(8,128)(2,1)S(1)} %get-tuple-element.54), channel_id=1, source_target_pairs={{16,0},{17,1},{18,2},{19,3},{20,4},{21,5},{22,6},{23,7}} | collective-permute-start | bytes 221192 | tf_op jit(solution)/shard_map/ppermute | solution.py:33
  80.0 0.2 fusion.86
  80.2 0.3 fusion.93
  80.6 0.2 copy.100
  80.8 0.2 pad.22.clone
  81.0 0.1 copy.90
  81.3 6.4 %fusion.85 = bf16[2,4,8,4,384]{4,2,3,1,0:T(8,128)(2,1)S(1)} fusion(bf16[4,6,1,7,2,384]{5,3,4,1,0,2:T(8,128)(2,1)S(1)} %slice.134, bf16[4,6,1,8,4,384]{5,3,4,1,0,2:T(8,128)(2,1)S(1)} %copy.90, pred[8,4]{0,1:T(4,128)(4,1)S(1)} %copy-done.1, bf16[1,3,3,3,384,384]{5,4,3,2,1,0:T(8,128)(2,1)} %param.11), kind=kOutput, calls=%fused_computation.95 | convolution fusion | flops 2041282560 | bytes 9007136 | tf_op jit(solution)/shard_map/conv_general_dilated | solution.py:22
  87.9 0.7 collective-permute-start.15
  88.7 0.7 collective-permute-start.16
  89.3 0.3 fusion.107
  89.7 0.2 copy.99
  89.8 0.2 pad.20.clone
  90.1 0.1 copy.83
  90.3 3.0 %fusion.84 = bf16[2,4,8,4,384]{4,2,3,1,0:T(8,128)(2,1)S(1)} fusion(bf16[4,6,1,7,2,384]{5,3,4,1,0,2:T(8,128)(2,1)S(1)} %slice.129, bf16[4,6,1,8,4,384]{5,3,4,1,0,2:T(8,128)(2,1)S(1)} %copy.83, pred[8,4]{0,1:T(4,128)(4,1)S(1)} %copy-done.1, bf16[1,3,3,3,384,384]{5,4,3,2,1,0:T(8,128)(2,1)S(1)} %bitcast.133), kind=kOutput, calls=%fused_computation.94 | convolution fusion | flops 2041282560 | bytes 9007136 | tf_op jit(solution)/shard_map/conv_general_dilated | solution.py:22
  93.5 1.3 %collective-permute-start.14 = (bf16[1,4,24,384]{3,2,1,0:T(8,128)(2,1)S(1)}, bf16[1,4,24,384]{3,2,1,0:T(8,128)(2,1)S(1)}, u32[]{:S(2)}, u32[]{:S(2)}) collective-permute-start(bf16[1,4,24,384]{3,2,1,0:T(8,128)(2,1)S(1)} %bitcast.128), channel_id=1, source_target_pairs={{24,16},{25,17},{26,18},{27,19},{28,20},{29,21},{30,22},{31,23}} | collective-permute-start | bytes 221192 | tf_op jit(solution)/shard_map/ppermute | solution.py:33
  94.9 8.0 %collective-permute-done.14 = bf16[1,4,24,384]{3,2,1,0:T(8,128)(2,1)S(1)} collective-permute-done((bf16[1,4,24,384]{3,2,1,0:T(8,128)(2,1)S(1)}, bf16[1,4,24,384]{3,2,1,0:T(8,128)(2,1)S(1)}, u32[]{:S(2)}, u32[]{:S(2)}) %collective-permute-start.14) | collective-permute-done | bytes 73760 | tf_op jit(solution)/shard_map/ppermute | solution.py:33
  102.9 0.7 add_convert_fusion
  (56 shorter events, 1.3 us)
Async XLA Ops:
  0.9 6.3 %collective-permute-start = (bf16[4,1,24,384]{3,2,1,0:T(8,128)(2,1)S(1)}, bf16[4,1,24,384]{3,2,1,0:T(8,128)(2,1)S(1)}, u32[]{:S(2)}, u32[]{:S(2)}) collective-permute-start(bf16[4,1,24,384]{3,2,1,0:T(8,128)(2,1)S(1)} %get-tuple-element.59), channel_id=1, source_target_pairs={{0,1},{1,2},{2,3},{3,4},{4,5},{5,6},{6,7},{8,9},{9,10},{10,11},{11... | collective-permute-start | bytes 221192 | tf_op jit(solution)/shard_map/ppermute | solution.py:62
  4.6 5.7 %collective-permute-start.1 = (bf16[4,1,24,384]{3,2,1,0:T(8,128)(2,1)S(1)}, bf16[4,1,24,384]{3,2,1,0:T(8,128)(2,1)S(1)}, u32[]{:S(2)}, u32[]{:S(2)}) collective-permute-start(bf16[4,1,24,384]{3,2,1,0:T(8,128)(2,1)S(1)} %get-tuple-element.60), channel_id=1, source_target_pairs={{1,0},{2,1},{3,2},{4,3},{5,4},{6,5},{7,6},{9,8},{10,9},{11,10},{12... | collective-permute-start | bytes 221192 | tf_op jit(solution)/shard_map/ppermute | solution.py:63
  11.3 2.4 %copy-start = (bf16[4,4,24,384]{3,2,1,0:T(8,128)(2,1)S(1)}, bf16[4,4,24,384]{3,2,1,0:T(8,128)(2,1)}, u32[]{:S(2)}) copy-start(bf16[4,4,24,384]{3,2,1,0:T(8,128)(2,1)} %param.9) | copy-start | bytes 884740
  11.4 2.2 %collective-permute-start.3 = (bf16[4,4,24,384]{3,2,1,0:T(8,128)(2,1)S(1)}, bf16[4,4,24,384]{3,2,1,0:T(8,128)(2,1)S(1)}, u32[]{:S(2)}, u32[]{:S(2)}) collective-permute-start(bf16[4,4,24,384]{3,2,1,0:T(8,128)(2,1)S(1)} %get-tuple-element.65), channel_id=1, source_target_pairs={{0,8},{1,9},{2,10},{3,11},{4,12},{5,13},{6,14},{7,15}} | collective-permute-start | bytes 884744 | tf_op jit(solution)/shard_map/ppermute | solution.py:33
  12.2 1.4 %collective-permute-start.2 = (bf16[4,1,24,384]{3,2,1,0:T(8,128)(2,1)S(1)}, bf16[4,1,24,384]{3,2,1,0:T(8,128)(2,1)S(1)}, u32[]{:S(2)}, u32[]{:S(2)}) collective-permute-start(bf16[4,1,24,384]{3,2,1,0:T(8,128)(2,1)S(1)} %get-tuple-element.57), channel_id=1, source_target_pairs={{0,9},{1,10},{2,11},{3,12},{4,13},{5,14},{6,15}} | collective-permute-start | bytes 221192 | tf_op jit(solution)/shard_map/ppermute | solution.py:33
  12.9 0.7 collective-permute-start.4
  14.0 43.7 %collective-permute-start.5 = (bf16[4,4,24,384]{3,2,1,0:T(8,128)(2,1)S(1)}, bf16[4,4,24,384]{3,2,1,0:T(8,128)(2,1)S(1)}, u32[]{:S(2)}, u32[]{:S(2)}) collective-permute-start(bf16[4,4,24,384]{3,2,1,0:T(8,128)(2,1)S(1)} %get-tuple-element.66), channel_id=1, source_target_pairs={{8,16},{9,17},{10,18},{11,19},{12,20},{13,21},{14,22},{15,23}} | collective-permute-start | bytes 884744 | tf_op jit(solution)/shard_map/ppermute | solution.py:33
  15.3 42.3 %collective-permute-start.10 = (bf16[4,1,24,384]{3,2,1,0:T(8,128)(2,1)S(1)}, bf16[4,1,24,384]{3,2,1,0:T(8,128)(2,1)S(1)}, u32[]{:S(2)}, u32[]{:S(2)}) collective-permute-start(bf16[4,1,24,384]{3,2,1,0:T(8,128)(2,1)S(1)} %get-tuple-element.53), channel_id=1, source_target_pairs={{9,16},{10,17},{11,18},{12,19},{13,20},{14,21},{15,22}} | collective-permute-start | bytes 221192 | tf_op jit(solution)/shard_map/ppermute | solution.py:33
  16.6 41.0 %collective-permute-start.9 = (bf16[4,1,24,384]{3,2,1,0:T(8,128)(2,1)S(1)}, bf16[4,1,24,384]{3,2,1,0:T(8,128)(2,1)S(1)}, u32[]{:S(2)}, u32[]{:S(2)}) collective-permute-start(bf16[4,1,24,384]{3,2,1,0:T(8,128)(2,1)S(1)} %get-tuple-element.52), channel_id=1, source_target_pairs={{8,17},{9,18},{10,19},{11,20},{12,21},{13,22},{14,23}} | collective-permute-start | bytes 221192 | tf_op jit(solution)/shard_map/ppermute | solution.py:33
  59.5 0.7 copy-start.4
  69.6 10.5 %collective-permute-start.12 = (bf16[4,4,24,384]{3,2,1,0:T(8,128)(2,1)S(1)}, bf16[4,4,24,384]{3,2,1,0:T(8,128)(2,1)S(1)}, u32[]{:S(2)}, u32[]{:S(2)}) collective-permute-start(bf16[4,4,24,384]{3,2,1,0:T(8,128)(2,1)S(1)} %get-tuple-element.67), channel_id=1, source_target_pairs={{16,24},{17,25},{18,26},{19,27},{20,28},{21,29},{22,30},{23,31}} | collective-permute-start | bytes 884744 | tf_op jit(solution)/shard_map/ppermute | solution.py:33
  71.2 7.6 %collective-permute-start.11 = (bf16[4,1,24,384]{3,2,1,0:T(8,128)(2,1)S(1)}, bf16[4,1,24,384]{3,2,1,0:T(8,128)(2,1)S(1)}, u32[]{:S(2)}, u32[]{:S(2)}) collective-permute-start(bf16[4,1,24,384]{3,2,1,0:T(8,128)(2,1)S(1)} %get-tuple-element.50), channel_id=1, source_target_pairs={{16,25},{17,26},{18,27},{19,28},{20,29},{21,30},{22,31}} | collective-permute-start | bytes 221192 | tf_op jit(solution)/shard_map/ppermute | solution.py:33
  72.5 7.6 %collective-permute-start.13 = (bf16[4,1,24,384]{3,2,1,0:T(8,128)(2,1)S(1)}, bf16[4,1,24,384]{3,2,1,0:T(8,128)(2,1)S(1)}, u32[]{:S(2)}, u32[]{:S(2)}) collective-permute-start(bf16[4,1,24,384]{3,2,1,0:T(8,128)(2,1)S(1)} %get-tuple-element.51), channel_id=1, source_target_pairs={{17,24},{18,25},{19,26},{20,27},{21,28},{22,29},{23,30}} | collective-permute-start | bytes 221192 | tf_op jit(solution)/shard_map/ppermute | solution.py:33
  73.8 19.7 %collective-permute-start.6 = (bf16[1,4,24,384]{3,2,1,0:T(8,128)(2,1)S(1)}, bf16[1,4,24,384]{3,2,1,0:T(8,128)(2,1)S(1)}, u32[]{:S(2)}, u32[]{:S(2)}) collective-permute-start(bf16[1,4,24,384]{3,2,1,0:T(8,128)(2,1)S(1)} %get-tuple-element.56), channel_id=1, source_target_pairs={{16,24},{17,25},{18,26},{19,27},{20,28},{21,29},{22,30},{23,31}} | collective-permute-start | bytes 221192 | tf_op jit(solution)/shard_map/ppermute | solution.py:33
  75.1 19.8 %collective-permute-start.7 = (bf16[1,4,24,384]{3,2,1,0:T(8,128)(2,1)S(1)}, bf16[1,4,24,384]{3,2,1,0:T(8,128)(2,1)S(1)}, u32[]{:S(2)}, u32[]{:S(2)}) collective-permute-start(bf16[1,4,24,384]{3,2,1,0:T(8,128)(2,1)S(1)} %get-tuple-element.55), channel_id=1, source_target_pairs={{16,8},{17,9},{18,10},{19,11},{20,12},{21,13},{22,14},{23,15}} | collective-permute-start | bytes 221192 | tf_op jit(solution)/shard_map/ppermute | solution.py:33
  78.7 16.1 %collective-permute-start.8 = (bf16[1,4,24,384]{3,2,1,0:T(8,128)(2,1)S(1)}, bf16[1,4,24,384]{3,2,1,0:T(8,128)(2,1)S(1)}, u32[]{:S(2)}, u32[]{:S(2)}) collective-permute-start(bf16[1,4,24,384]{3,2,1,0:T(8,128)(2,1)S(1)} %get-tuple-element.54), channel_id=1, source_target_pairs={{16,0},{17,1},{18,2},{19,3},{20,4},{21,5},{22,6},{23,7}} | collective-permute-start | bytes 221192 | tf_op jit(solution)/shard_map/ppermute | solution.py:33
  80.6 0.7 copy-start.1
  80.8 9.5 %slice-start = ((s8[7962624]{0:T(1024)(128)(4,1)}), s8[4194304]{0:T(1024)(128)(4,1)S(1)}, s32[]{:S(2)}) async-start(s8[7962624]{0:T(1024)(128)(4,1)} %bitcast.132), calls=%async_computation | async-start | bytes 8388608
  81.3 9.0 %slice-start.1 = ((s8[7962624]{0:T(1024)(128)(4,1)}), s8[3768320]{0:T(1024)(128)(4,1)S(1)}, s32[]{:S(2)}) async-start(s8[7962624]{0:T(1024)(128)(4,1)} %bitcast.132), calls=%async_computation.1 | async-start | bytes 7536640
  87.9 7.0 %collective-permute-start.15 = (bf16[1,4,24,384]{3,2,1,0:T(8,128)(2,1)S(1)}, bf16[1,4,24,384]{3,2,1,0:T(8,128)(2,1)S(1)}, u32[]{:S(2)}, u32[]{:S(2)}) collective-permute-start(bf16[1,4,24,384]{3,2,1,0:T(8,128)(2,1)S(1)} %bitcast.126), channel_id=1, source_target_pairs={{24,8},{25,9},{26,10},{27,11},{28,12},{29,13},{30,14},{31,15}} | collective-permute-start | bytes 221192 | tf_op jit(solution)/shard_map/ppermute | solution.py:33
  88.7 6.3 %collective-permute-start.16 = (bf16[1,4,24,384]{3,2,1,0:T(8,128)(2,1)S(1)}, bf16[1,4,24,384]{3,2,1,0:T(8,128)(2,1)S(1)}, u32[]{:S(2)}, u32[]{:S(2)}) collective-permute-start(bf16[1,4,24,384]{3,2,1,0:T(8,128)(2,1)S(1)} %bitcast.127), channel_id=1, source_target_pairs={{24,0},{25,1},{26,2},{27,3},{28,4},{29,5},{30,6},{31,7}} | collective-permute-start | bytes 221192 | tf_op jit(solution)/shard_map/ppermute | solution.py:33
  93.5 9.5 %collective-permute-start.14 = (bf16[1,4,24,384]{3,2,1,0:T(8,128)(2,1)S(1)}, bf16[1,4,24,384]{3,2,1,0:T(8,128)(2,1)S(1)}, u32[]{:S(2)}, u32[]{:S(2)}) collective-permute-start(bf16[1,4,24,384]{3,2,1,0:T(8,128)(2,1)S(1)} %bitcast.128), channel_id=1, source_target_pairs={{24,16},{25,17},{26,18},{27,19},{28,20},{29,21},{30,22},{31,23}} | collective-permute-start | bytes 221192 | tf_op jit(solution)/shard_map/ppermute | solution.py:33

commit v9 on v6

--- a/solution.py
+++ b/solution.py
@@ -73,9 +73,6 @@
                 convolved = (skip.astype(jnp.float32) + convolved).astype(jnp.bfloat16)
             return convolved
 
-        def idle(window, skip):
-            return jnp.zeros(skip.shape, jnp.bfloat16)
-
         if final:
             activated = jnp.pad(activate(window, gain_row), ((2, 0), (0, 0), (0, 0), (0, 0)))
             split = (segment_count // 2) * group
@@ -94,7 +91,7 @@
                             segment_index == target, piece, branch
                         )
             break
-        produced = lax.cond(segment_index == stage, compute, idle, window, skip)
+        produced = compute(window, skip)
         if stage == last_stage - 1:
             owned = current[stage * group : (stage + 1) * group]
             for target in range(segment_count):

time: 95.6 us -> 91.9 us (0.961)
  waiting for transfers between devices: 48.1 us -> 31.7 us
  matrix products: 13.9 us -> 25.6 us
    ppermute x15, waiting for transfers between devices: 45.1 us -> 28.7 us  [send(): return lax.ppermute(value, BOTH, pairs)]
    conv_general_dilated x3 -> x5, matrix products: 13.9 us -> 25.6 us  [causal_conv(): lax.conv_general_dilated(window[None], kernel, window_strides=(1, 1, 1),...]
    convert_element_type x2 -> x5, other arithmetic: 1.56 us -> 2.64 us  [activate(): return jax.nn.silu(widened * lax.rsqrt(mean_square + 1e-06) * gain_row.as...]
    unnamed x12 -> x19, local copies, waits for them, and re-layouts: 1.42 us -> 1.96 us
  transfers between devices with their start and end apart: 17 -> 17, of which waited for: 4 -> 4; matrix products, arithmetic and copies ran while one was open for 12% -> 10% of each run, Pallas kernels for 0% -> 0%
where the time goes in v9:
time: 91.9 us; the launch traced here: 91.4 us
  waiting for transfers between devices  31.7 us (34%)
  matrix products  25.6 us (28%)
  starting transfers between devices  22.3 us (24%)
  other arithmetic  5.7 us (6%)
  local copies, waits for them, and re-layouts  5.36 us (6%)
    ppermute x15, waiting for transfers between devices, send(): return lax.ppermute(value, BOTH, pairs)  28.7 us
    conv_general_dilated x5, matrix products, causal_conv(): lax.conv_general_dilated(window[None], kernel, window_strides=(1, 1, 1),...  25.6 us
    ppermute x15, starting transfers between devices, send(): return lax.ppermute(value, BOTH, pairs)  16.7 us
    ppermute x1, starting transfers between devices, local(): top = lax.ppermute(features[:, height - 1:], 'rows', up)  3.68 us
    ppermute x1, waiting for transfers between devices, local(): bottom = lax.ppermute(features[:, :1], 'rows', down)  3.04 us
    convert_element_type x5, other arithmetic, activate(): return jax.nn.silu(widened * lax.rsqrt(mean_square + 1e-06) * gain_row.as...  2.64 us
    unnamed x19, local copies, waits for them, and re-layouts  1.96 us
    ppermute x1, starting transfers between devices, local(): bottom = lax.ppermute(features[:, :1], 'rows', down)  1.92 us
  transfers between devices with their start and end apart: 17, of which 4 were waited for; matrix products, arithmetic and copies ran while one was open for 10% of the time, Pallas kernels for 0%

profile of v9, /device:TPU:17, one launch (start us, length us, event | category | flops | bytes accessed | tf_op | source)
XLA Modules:
  0.0 91.4 jit_solution(17974847673073957362)
XLA Ops:
  0.0 0.9 %slice_bitcast_fusion.1 = (bf16[4,1,24,384]{3,2,0,1:T(8,128)(2,1)S(1)}, bf16[4,1,24,384]{3,2,0,1:T(8,128)(2,1)S(1)}) fusion(bf16[4,4,24,384]{3,2,1,0:T(8,128)(2,1)} %param.3), kind=kLoop, calls=%fused_computation.95 | loop fusion | bytes 294912
  0.9 3.7 %collective-permute-start = (bf16[4,1,24,384]{3,2,0,1:T(8,128)(2,1)S(1)}, bf16[4,1,24,384]{3,2,0,1:T(8,128)(2,1)S(1)}, u32[]{:S(2)}, u32[]{:S(2)}) collective-permute-start(bf16[4,1,24,384]{3,2,0,1:T(8,128)(2,1)S(1)} %get-tuple-element.14), channel_id=1, source_target_pairs={{0,1},{1,2},{2,3},{3,4},{4,5},{5,6},{6,7},{8,9},{9,10},{10,11},{11... | collective-permute-start | bytes 221192 | tf_op jit(solution)/shard_map/ppermute | solution.py:59
  4.6 1.9 %collective-permute-start.1 = (bf16[4,1,24,384]{3,2,0,1:T(8,128)(2,1)S(1)}, bf16[4,1,24,384]{3,2,0,1:T(8,128)(2,1)S(1)}, u32[]{:S(2)}, u32[]{:S(2)}) collective-permute-start(bf16[4,1,24,384]{3,2,0,1:T(8,128)(2,1)S(1)} %get-tuple-element.15), channel_id=1, source_target_pairs={{1,0},{2,1},{3,2},{4,3},{5,4},{6,5},{7,6},{9,8},{10,9},{11,10},{12... | collective-permute-start | bytes 221192 | tf_op jit(solution)/shard_map/ppermute | solution.py:60
  6.6 0.7 convert_reduce_fusion
  7.3 3.0 %collective-permute-done.1 = bf16[4,1,24,384]{3,2,0,1:T(8,128)(2,1)S(1)} collective-permute-done((bf16[4,1,24,384]{3,2,0,1:T(8,128)(2,1)S(1)}, bf16[4,1,24,384]{3,2,0,1:T(8,128)(2,1)S(1)}, u32[]{:S(2)}, u32[]{:S(2)}) %collective-permute-start.1) | collective-permute-done | bytes 73760 | tf_op jit(solution)/shard_map/ppermute | solution.py:60
  10.3 1.1 %multiply_reduce_fusion.2 = f32[4,6,24]{2,1,0:T(8,128)S(1)} fusion(bf16[4,1,24,384]{3,2,1,0:T(8,128)(2,1)S(1)} %bitcast.156, bf16[4,4,24,384]{3,2,1,0:T(8,128)(2,1)} %param.3, bf16[4,1,24,384]{3,2,1,0:T(8,128)(2,1)S(1)} %bitcast.152), kind=kLoop, calls=%fused_computation.67 | loop fusion | flops 1105344 | bytes 444672 | tf_op jit(solution)/shard_map/reduce_sum | solution.py:11
  11.4 1.3 %fusion.85 = bf16[4,6,1,24,384]{4,3,1,0,2:T(8,128)(2,1)S(1)} fusion(bf16[1,4,1,24,384]{4,3,2,1,0:T(8,128)(2,1)S(1)} %bitcast.157, bf16[1,4,4,24,384]{4,3,2,1,0:T(8,128)(2,1)} %bitcast.128, bf16[1,4,1,24,384]{4,3,2,1,0:T(8,128)(2,1)S(1)} %bitcast.153, f32[384]{0:T(512)S(1)} %convert_reduce_fusion, f32[4,6,24]{2,1,0:T(8,128)S(1)} %add_rsqrt_fusion.3), kind=kLoop, calls=%fused_computation.72 | loop fusion | flops 2211840 | bytes 888576 | tf_op jit(solution)/shard_map/convert_element_type | solution.py:14
  12.8 0.2 copy.277
  12.9 0.2 pad.5.clone
  13.4 8.3 %fusion.30 = bf16[4,4,8,4,384]{4,2,3,1,0:T(8,128)(2,1)S(1)} fusion(bf16[1,3,3,3,384,384]{5,4,3,2,1,0:T(8,128)(2,1)} %param.5, bf16[4,6,1,7,2,384]{5,3,4,1,0,2:T(8,128)(2,1)S(1)} %slice.101, bf16[4,6,1,8,4,384]{5,3,4,1,0,2:T(8,128)(2,1)S(1)} %copy.226, pred[8,4]{0,1:T(4,128)(4,1)S(1)} %copy-done.1), kind=kOutput, calls=%fused_computation.21 | convolution fusion | flops 3060695040 | bytes 9203744 | tf_op jit(solution)/shard_map/conv_general_dilated | solution.py:18
  21.7 0.2 copy.227
  22.0 0.7 collective-permute-start.3
  22.8 0.7 collective-permute-start.2
  23.4 0.7 collective-permute-start.4
  24.3 0.3 fusion.86
  24.7 0.2 copy.278
  24.8 0.2 pad.7.clone
  25.3 5.7 %fusion.27 = bf16[4,4,8,4,384]{4,2,3,1,0:T(8,128)(2,1)S(1)} fusion(bf16[1,3,3,3,384,384]{5,4,3,2,1,0:T(8,128)(2,1)S(1)} %bitcast.162, bf16[4,6,1,7,2,384]{5,3,4,1,0,2:T(8,128)(2,1)S(1)} %slice.105, bf16[4,6,1,8,4,384]{5,3,4,1,0,2:T(8,128)(2,1)S(1)} %copy.235, pred[8,4]{0,1:T(4,128)(4,1)S(1)} %copy-done.1), kind=kOutput, calls=%fused_computation.20 | convolution fusion | flops 3060695040 | bytes 9203744 | tf_op jit(solution)/shard_map/conv_general_dilated | solution.py:18
  31.0 0.2 copy.236
  31.4 1.3 %collective-permute-start.5 = (bf16[4,4,24,384]{3,2,1,0:T(8,128)(2,1)S(1)}, bf16[4,4,24,384]{3,2,1,0:T(8,128)(2,1)S(1)}, u32[]{:S(2)}, u32[]{:S(2)}) collective-permute-start(bf16[4,4,24,384]{3,2,1,0:T(8,128)(2,1)S(1)} %fusion.83), channel_id=1, source_target_pairs={{8,16},{9,17},{10,18},{11,19},{12,20},{13,21},{14,22},{15,23}} | collective-permute-start | bytes 884744 | tf_op jit(solution)/shard_map/ppermute | solution.py:30
  32.7 1.3 %collective-permute-start.10 = (bf16[4,1,24,384]{3,2,1,0:T(8,128)(2,1)S(1)}, bf16[4,1,24,384]{3,2,1,0:T(8,128)(2,1)S(1)}, u32[]{:S(2)}, u32[]{:S(2)}) collective-permute-start(bf16[4,1,24,384]{3,2,1,0:T(8,128)(2,1)S(1)} %get-tuple-element.8), channel_id=1, source_target_pairs={{9,16},{10,17},{11,18},{12,19},{13,20},{14,21},{15,22}} | collective-permute-start | bytes 221192 | tf_op jit(solution)/shard_map/ppermute | solution.py:30
  34.0 1.5 %collective-permute-start.9 = (bf16[4,1,24,384]{3,2,1,0:T(8,128)(2,1)S(1)}, bf16[4,1,24,384]{3,2,1,0:T(8,128)(2,1)S(1)}, u32[]{:S(2)}, u32[]{:S(2)}) collective-permute-start(bf16[4,1,24,384]{3,2,1,0:T(8,128)(2,1)S(1)} %get-tuple-element.7), channel_id=1, source_target_pairs={{8,17},{9,18},{10,19},{11,20},{12,21},{13,22},{14,23}} | collective-permute-start | bytes 221192 | tf_op jit(solution)/shard_map/ppermute | solution.py:30
  35.5 18.3 %collective-permute-done.10 = bf16[4,1,24,384]{3,2,1,0:T(8,128)(2,1)S(1)} collective-permute-done((bf16[4,1,24,384]{3,2,1,0:T(8,128)(2,1)S(1)}, bf16[4,1,24,384]{3,2,1,0:T(8,128)(2,1)S(1)}, u32[]{:S(2)}, u32[]{:S(2)}) %collective-permute-start.10) | collective-permute-done | bytes 73760 | tf_op jit(solution)/shard_map/ppermute | solution.py:30
  54.0 0.3 fusion.87
  54.3 0.2 copy.279
  54.5 0.2 pad.9.clone
  54.9 5.7 %fusion.24 = bf16[4,4,8,4,384]{4,2,3,1,0:T(8,128)(2,1)S(1)} fusion(bf16[1,3,3,3,384,384]{5,4,3,2,1,0:T(8,128)(2,1)S(1)} %bitcast.162, bf16[4,6,1,7,2,384]{5,3,4,1,0,2:T(8,128)(2,1)S(1)} %slice.113, bf16[4,6,1,8,4,384]{5,3,4,1,0,2:T(8,128)(2,1)S(1)} %copy.244, pred[8,4]{0,1:T(4,128)(4,1)S(1)} %copy-done.1), kind=kOutput, calls=%fused_computation.19 | convolution fusion | flops 3060695040 | bytes 9203744 | tf_op jit(solution)/shard_map/conv_general_dilated | solution.py:18
  60.6 0.2 copy.245
  61.0 1.3 %collective-permute-start.12 = (bf16[4,4,24,384]{3,2,1,0:T(8,128)(2,1)S(1)}, bf16[4,4,24,384]{3,2,1,0:T(8,128)(2,1)S(1)}, u32[]{:S(2)}, u32[]{:S(2)}) collective-permute-start(bf16[4,4,24,384]{3,2,1,0:T(8,128)(2,1)S(1)} %bitcast.142), channel_id=1, source_target_pairs={{16,24},{17,25},{18,26},{19,27},{20,28},{21,29},{22,30},{23,31}} | collective-permute-start | bytes 884744 | tf_op jit(solution)/shard_map/ppermute | solution.py:30
  62.3 1.3 %collective-permute-start.11 = (bf16[4,1,24,384]{3,2,1,0:T(8,128)(2,1)S(1)}, bf16[4,1,24,384]{3,2,1,0:T(8,128)(2,1)S(1)}, u32[]{:S(2)}, u32[]{:S(2)}) collective-permute-start(bf16[4,1,24,384]{3,2,1,0:T(8,128)(2,1)S(1)} %get-tuple-element.5), channel_id=1, source_target_pairs={{16,25},{17,26},{18,27},{19,28},{20,29},{21,30},{22,31}} | collective-permute-start | bytes 221192 | tf_op jit(solution)/shard_map/ppermute | solution.py:30
  63.6 1.3 %collective-permute-start.13 = (bf16[4,1,24,384]{3,2,1,0:T(8,128)(2,1)S(1)}, bf16[4,1,24,384]{3,2,1,0:T(8,128)(2,1)S(1)}, u32[]{:S(2)}, u32[]{:S(2)}) collective-permute-start(bf16[4,1,24,384]{3,2,1,0:T(8,128)(2,1)S(1)} %get-tuple-element.6), channel_id=1, source_target_pairs={{17,24},{18,25},{19,26},{20,27},{21,28},{22,29},{23,30}} | collective-permute-start | bytes 221192 | tf_op jit(solution)/shard_map/ppermute | solution.py:30
  64.9 1.3 %collective-permute-start.6 = (bf16[1,4,24,384]{3,2,1,0:T(8,128)(2,1)S(1)}, bf16[1,4,24,384]{3,2,1,0:T(8,128)(2,1)S(1)}, u32[]{:S(2)}, u32[]{:S(2)}) collective-permute-start(bf16[1,4,24,384]{3,2,1,0:T(8,128)(2,1)S(1)} %get-tuple-element.11), channel_id=1, source_target_pairs={{16,24},{17,25},{18,26},{19,27},{20,28},{21,29},{22,30},{23,31}} | collective-permute-start | bytes 221192 | tf_op jit(solution)/shard_map/ppermute | solution.py:30
  66.2 1.3 %collective-permute-start.7 = (bf16[1,4,24,384]{3,2,1,0:T(8,128)(2,1)S(1)}, bf16[1,4,24,384]{3,2,1,0:T(8,128)(2,1)S(1)}, u32[]{:S(2)}, u32[]{:S(2)}) collective-permute-start(bf16[1,4,24,384]{3,2,1,0:T(8,128)(2,1)S(1)} %get-tuple-element.10), channel_id=1, source_target_pairs={{16,8},{17,9},{18,10},{19,11},{20,12},{21,13},{22,14},{23,15}} | collective-permute-start | bytes 221192 | tf_op jit(solution)/shard_map/ppermute | solution.py:30
  67.5 2.4 %collective-permute-done.11 = bf16[4,1,24,384]{3,2,1,0:T(8,128)(2,1)S(1)} collective-permute-done((bf16[4,1,24,384]{3,2,1,0:T(8,128)(2,1)S(1)}, bf16[4,1,24,384]{3,2,1,0:T(8,128)(2,1)S(1)}, u32[]{:S(2)}, u32[]{:S(2)}) %collective-permute-start.11) | collective-permute-done | bytes 73760 | tf_op jit(solution)/shard_map/ppermute | solution.py:30
  69.9 1.3 %collective-permute-start.8 = (bf16[1,4,24,384]{3,2,1,0:T(8,128)(2,1)S(1)}, bf16[1,4,24,384]{3,2,1,0:T(8,128)(2,1)S(1)}, u32[]{:S(2)}, u32[]{:S(2)}) collective-permute-start(bf16[1,4,24,384]{3,2,1,0:T(8,128)(2,1)S(1)} %get-tuple-element.9), channel_id=1, source_target_pairs={{16,0},{17,1},{18,2},{19,3},{20,4},{21,5},{22,6},{23,7}} | collective-permute-start | bytes 221192 | tf_op jit(solution)/shard_map/ppermute | solution.py:30
  71.4 0.3 fusion.52
  71.8 0.2 copy.281
  72.0 0.2 pad.13.clone
  72.4 3.0 %fusion.39 = bf16[2,4,8,4,384]{4,2,3,1,0:T(8,128)(2,1)S(1)} fusion(bf16[1,3,3,3,384,384]{5,4,3,2,1,0:T(8,128)(2,1)S(1)} %bitcast.162, bf16[4,6,1,7,2,384]{5,3,4,1,0,2:T(8,128)(2,1)S(1)} %slice.122, bf16[4,6,1,8,4,384]{5,3,4,1,0,2:T(8,128)(2,1)S(1)} %copy.260, pred[8,4]{0,1:T(4,128)(4,1)S(1)} %copy-done.1), kind=kOutput, calls=%fused_computation.24 | convolution fusion | flops 2041282560 | bytes 9007136 | tf_op jit(solution)/shard_map/conv_general_dilated | solution.py:18
  75.6 0.9 collective-permute-start.15
  76.6 0.7 collective-permute-start.16
  77.3 0.3 fusion.88
  77.6 0.2 copy.280
  77.8 0.2 pad.11.clone
  78.2 3.0 %fusion.42 = bf16[2,4,8,4,384]{4,2,3,1,0:T(8,128)(2,1)S(1)} fusion(bf16[1,3,3,3,384,384]{5,4,3,2,1,0:T(8,128)(2,1)S(1)} %bitcast.162, bf16[4,6,1,7,2,384]{5,3,4,1,0,2:T(8,128)(2,1)S(1)} %slice.117, bf16[4,6,1,8,4,384]{5,3,4,1,0,2:T(8,128)(2,1)S(1)} %copy.253, pred[8,4]{0,1:T(4,128)(4,1)S(1)} %copy-done.1), kind=kOutput, calls=%fused_computation.25 | convolution fusion | flops 2041282560 | bytes 9007136 | tf_op jit(solution)/shard_map/conv_general_dilated | solution.py:18
  81.4 1.3 %collective-permute-start.14 = (bf16[1,4,24,384]{3,2,1,0:T(8,128)(2,1)S(1)}, bf16[1,4,24,384]{3,2,1,0:T(8,128)(2,1)S(1)}, u32[]{:S(2)}, u32[]{:S(2)}) collective-permute-start(bf16[1,4,24,384]{3,2,1,0:T(8,128)(2,1)S(1)} %bitcast.160), channel_id=1, source_target_pairs={{24,16},{25,17},{26,18},{27,19},{28,20},{29,21},{30,22},{31,23}} | collective-permute-start | bytes 221192 | tf_op jit(solution)/shard_map/ppermute | solution.py:30
  82.8 7.9 %collective-permute-done.14 = bf16[1,4,24,384]{3,2,1,0:T(8,128)(2,1)S(1)} collective-permute-done((bf16[1,4,24,384]{3,2,1,0:T(8,128)(2,1)S(1)}, bf16[1,4,24,384]{3,2,1,0:T(8,128)(2,1)S(1)}, u32[]{:S(2)}, u32[]{:S(2)}) %collective-permute-start.14) | collective-permute-done | bytes 73760 | tf_op jit(solution)/shard_map/ppermute | solution.py:30
  90.7 0.7 add_convert_fusion
  (63 shorter events, 2.5 us)
Async XLA Ops:
  0.9 6.3 %collective-permute-start = (bf16[4,1,24,384]{3,2,0,1:T(8,128)(2,1)S(1)}, bf16[4,1,24,384]{3,2,0,1:T(8,128)(2,1)S(1)}, u32[]{:S(2)}, u32[]{:S(2)}) collective-permute-start(bf16[4,1,24,384]{3,2,0,1:T(8,128)(2,1)S(1)} %get-tuple-element.14), channel_id=1, source_target_pairs={{0,1},{1,2},{2,3},{3,4},{4,5},{5,6},{6,7},{8,9},{9,10},{10,11},{11... | collective-permute-start | bytes 221192 | tf_op jit(solution)/shard_map/ppermute | solution.py:59
  4.6 5.7 %collective-permute-start.1 = (bf16[4,1,24,384]{3,2,0,1:T(8,128)(2,1)S(1)}, bf16[4,1,24,384]{3,2,0,1:T(8,128)(2,1)S(1)}, u32[]{:S(2)}, u32[]{:S(2)}) collective-permute-start(bf16[4,1,24,384]{3,2,0,1:T(8,128)(2,1)S(1)} %get-tuple-element.15), channel_id=1, source_target_pairs={{1,0},{2,1},{3,2},{4,3},{5,4},{6,5},{7,6},{9,8},{10,9},{11,10},{12... | collective-permute-start | bytes 221192 | tf_op jit(solution)/shard_map/ppermute | solution.py:60
  12.7 0.7 copy-start.1
  13.3 12.0 %slice-start = ((s8[7962624]{0:T(1024)(128)(4,1)}), s8[4194304]{0:T(1024)(128)(4,1)S(1)}, s32[]{:S(2)}) async-start(s8[7962624]{0:T(1024)(128)(4,1)} %bitcast.161), calls=%async_computation | async-start | bytes 8388608
  13.4 11.9 %slice-start.1 = ((s8[7962624]{0:T(1024)(128)(4,1)}), s8[3768320]{0:T(1024)(128)(4,1)S(1)}, s32[]{:S(2)}) async-start(s8[7962624]{0:T(1024)(128)(4,1)} %bitcast.161), calls=%async_computation.1 | async-start | bytes 7536640
  22.0 2.1 %collective-permute-start.3 = (bf16[4,4,24,384]{3,2,1,0:T(8,128)(2,1)S(1)}, bf16[4,4,24,384]{3,2,1,0:T(8,128)(2,1)S(1)}, u32[]{:S(2)}, u32[]{:S(2)}) collective-permute-start(bf16[4,4,24,384]{3,2,1,0:T(8,128)(2,1)S(1)} %bitcast.144), channel_id=1, source_target_pairs={{0,8},{1,9},{2,10},{3,11},{4,12},{5,13},{6,14},{7,15}} | collective-permute-start | bytes 884744 | tf_op jit(solution)/shard_map/ppermute | solution.py:30
  22.8 1.3 %collective-permute-start.2 = (bf16[4,1,24,384]{3,2,1,0:T(8,128)(2,1)S(1)}, bf16[4,1,24,384]{3,2,1,0:T(8,128)(2,1)S(1)}, u32[]{:S(2)}, u32[]{:S(2)}) collective-permute-start(bf16[4,1,24,384]{3,2,1,0:T(8,128)(2,1)S(1)} %get-tuple-element.12), channel_id=1, source_target_pairs={{0,9},{1,10},{2,11},{3,12},{4,13},{5,14},{6,15}} | collective-permute-start | bytes 221192 | tf_op jit(solution)/shard_map/ppermute | solution.py:30
  23.4 0.7 collective-permute-start.4
  25.3 6.0 %copy-start = (bf16[4,4,24,384]{3,2,1,0:T(8,128)(2,1)S(1)}, bf16[4,4,24,384]{3,2,1,0:T(8,128)(2,1)}, u32[]{:S(2)}) copy-start(bf16[4,4,24,384]{3,2,1,0:T(8,128)(2,1)} %param.3) | copy-start | bytes 884740
  31.4 22.4 %collective-permute-start.5 = (bf16[4,4,24,384]{3,2,1,0:T(8,128)(2,1)S(1)}, bf16[4,4,24,384]{3,2,1,0:T(8,128)(2,1)S(1)}, u32[]{:S(2)}, u32[]{:S(2)}) collective-permute-start(bf16[4,4,24,384]{3,2,1,0:T(8,128)(2,1)S(1)} %fusion.83), channel_id=1, source_target_pairs={{8,16},{9,17},{10,18},{11,19},{12,20},{13,21},{14,22},{15,23}} | collective-permute-start | bytes 884744 | tf_op jit(solution)/shard_map/ppermute | solution.py:30
  32.7 21.1 %collective-permute-start.10 = (bf16[4,1,24,384]{3,2,1,0:T(8,128)(2,1)S(1)}, bf16[4,1,24,384]{3,2,1,0:T(8,128)(2,1)S(1)}, u32[]{:S(2)}, u32[]{:S(2)}) collective-permute-start(bf16[4,1,24,384]{3,2,1,0:T(8,128)(2,1)S(1)} %get-tuple-element.8), channel_id=1, source_target_pairs={{9,16},{10,17},{11,18},{12,19},{13,20},{14,21},{15,22}} | collective-permute-start | bytes 221192 | tf_op jit(solution)/shard_map/ppermute | solution.py:30
  34.0 19.8 %collective-permute-start.9 = (bf16[4,1,24,384]{3,2,1,0:T(8,128)(2,1)S(1)}, bf16[4,1,24,384]{3,2,1,0:T(8,128)(2,1)S(1)}, u32[]{:S(2)}, u32[]{:S(2)}) collective-permute-start(bf16[4,1,24,384]{3,2,1,0:T(8,128)(2,1)S(1)} %get-tuple-element.7), channel_id=1, source_target_pairs={{8,17},{9,18},{10,19},{11,20},{12,21},{13,22},{14,23}} | collective-permute-start | bytes 221192 | tf_op jit(solution)/shard_map/ppermute | solution.py:30
  61.0 10.3 %collective-permute-start.12 = (bf16[4,4,24,384]{3,2,1,0:T(8,128)(2,1)S(1)}, bf16[4,4,24,384]{3,2,1,0:T(8,128)(2,1)S(1)}, u32[]{:S(2)}, u32[]{:S(2)}) collective-permute-start(bf16[4,4,24,384]{3,2,1,0:T(8,128)(2,1)S(1)} %bitcast.142), channel_id=1, source_target_pairs={{16,24},{17,25},{18,26},{19,27},{20,28},{21,29},{22,30},{23,31}} | collective-permute-start | bytes 884744 | tf_op jit(solution)/shard_map/ppermute | solution.py:30
  62.3 7.6 %collective-permute-start.11 = (bf16[4,1,24,384]{3,2,1,0:T(8,128)(2,1)S(1)}, bf16[4,1,24,384]{3,2,1,0:T(8,128)(2,1)S(1)}, u32[]{:S(2)}, u32[]{:S(2)}) collective-permute-start(bf16[4,1,24,384]{3,2,1,0:T(8,128)(2,1)S(1)} %get-tuple-element.5), channel_id=1, source_target_pairs={{16,25},{17,26},{18,27},{19,28},{20,29},{21,30},{22,31}} | collective-permute-start | bytes 221192 | tf_op jit(solution)/shard_map/ppermute | solution.py:30
  63.6 7.6 %collective-permute-start.13 = (bf16[4,1,24,384]{3,2,1,0:T(8,128)(2,1)S(1)}, bf16[4,1,24,384]{3,2,1,0:T(8,128)(2,1)S(1)}, u32[]{:S(2)}, u32[]{:S(2)}) collective-permute-start(bf16[4,1,24,384]{3,2,1,0:T(8,128)(2,1)S(1)} %get-tuple-element.6), channel_id=1, source_target_pairs={{17,24},{18,25},{19,26},{20,27},{21,28},{22,29},{23,30}} | collective-permute-start | bytes 221192 | tf_op jit(solution)/shard_map/ppermute | solution.py:30
  64.9 16.4 %collective-permute-start.6 = (bf16[1,4,24,384]{3,2,1,0:T(8,128)(2,1)S(1)}, bf16[1,4,24,384]{3,2,1,0:T(8,128)(2,1)S(1)}, u32[]{:S(2)}, u32[]{:S(2)}) collective-permute-start(bf16[1,4,24,384]{3,2,1,0:T(8,128)(2,1)S(1)} %get-tuple-element.11), channel_id=1, source_target_pairs={{16,24},{17,25},{18,26},{19,27},{20,28},{21,29},{22,30},{23,31}} | collective-permute-start | bytes 221192 | tf_op jit(solution)/shard_map/ppermute | solution.py:30
  66.2 16.5 %collective-permute-start.7 = (bf16[1,4,24,384]{3,2,1,0:T(8,128)(2,1)S(1)}, bf16[1,4,24,384]{3,2,1,0:T(8,128)(2,1)S(1)}, u32[]{:S(2)}, u32[]{:S(2)}) collective-permute-start(bf16[1,4,24,384]{3,2,1,0:T(8,128)(2,1)S(1)} %get-tuple-element.10), channel_id=1, source_target_pairs={{16,8},{17,9},{18,10},{19,11},{20,12},{21,13},{22,14},{23,15}} | collective-permute-start | bytes 221192 | tf_op jit(solution)/shard_map/ppermute | solution.py:30
  69.9 12.8 %collective-permute-start.8 = (bf16[1,4,24,384]{3,2,1,0:T(8,128)(2,1)S(1)}, bf16[1,4,24,384]{3,2,1,0:T(8,128)(2,1)S(1)}, u32[]{:S(2)}, u32[]{:S(2)}) collective-permute-start(bf16[1,4,24,384]{3,2,1,0:T(8,128)(2,1)S(1)} %get-tuple-element.9), channel_id=1, source_target_pairs={{16,0},{17,1},{18,2},{19,3},{20,4},{21,5},{22,6},{23,7}} | collective-permute-start | bytes 221192 | tf_op jit(solution)/shard_map/ppermute | solution.py:30
  75.6 7.2 %collective-permute-start.15 = (bf16[1,4,24,384]{3,2,1,0:T(8,128)(2,1)S(1)}, bf16[1,4,24,384]{3,2,1,0:T(8,128)(2,1)S(1)}, u32[]{:S(2)}, u32[]{:S(2)}) collective-permute-start(bf16[1,4,24,384]{3,2,1,0:T(8,128)(2,1)S(1)} %bitcast.158), channel_id=1, source_target_pairs={{24,8},{25,9},{26,10},{27,11},{28,12},{29,13},{30,14},{31,15}} | collective-permute-start | bytes 221192 | tf_op jit(solution)/shard_map/ppermute | solution.py:30
  76.6 6.2 %collective-permute-start.16 = (bf16[1,4,24,384]{3,2,1,0:T(8,128)(2,1)S(1)}, bf16[1,4,24,384]{3,2,1,0:T(8,128)(2,1)S(1)}, u32[]{:S(2)}, u32[]{:S(2)}) collective-permute-start(bf16[1,4,24,384]{3,2,1,0:T(8,128)(2,1)S(1)} %bitcast.159), channel_id=1, source_target_pairs={{24,0},{25,1},{26,2},{27,3},{28,4},{29,5},{30,6},{31,7}} | collective-permute-start | bytes 221192 | tf_op jit(solution)/shard_map/ppermute | solution.py:30
  81.4 9.4 %collective-permute-start.14 = (bf16[1,4,24,384]{3,2,1,0:T(8,128)(2,1)S(1)}, bf16[1,4,24,384]{3,2,1,0:T(8,128)(2,1)S(1)}, u32[]{:S(2)}, u32[]{:S(2)}) collective-permute-start(bf16[1,4,24,384]{3,2,1,0:T(8,128)(2,1)S(1)} %bitcast.160), channel_id=1, source_target_pairs={{24,16},{25,17},{26,18},{27,19},{28,20},{29,21},{30,22},{31,23}} | collective-permute-start | bytes 221192 | tf_op jit(solution)/shard_map/ppermute | solution.py:30

commit v10 on v4

--- a/solution.py
+++ b/solution.py
@@ -14,12 +14,12 @@
     ).astype(jnp.bfloat16)
 
 
-def causal_conv(window, kernel):
+def causal_conv(window, kernel, before=2):
     result = lax.conv_general_dilated(
         window[None],
         kernel,
         window_strides=(1, 1, 1),
-        padding=((2, 0), (0, 0), (1, 1)),
+        padding=((before, 0), (0, 0), (1, 1)),
         dimension_numbers=("NDHWC", "DHWIO", "NDHWC"),
         preferred_element_type=jnp.float32,
     )
@@ -50,6 +50,12 @@
     group = frame_count // segment_count
     gain_row = gains[0]
     kernel = kernels[0]
+    last_stage = segment_count - 1
+    split = frame_count // 2
+    if frame_count % 2 == 0 and split >= 2:
+        bounds = ((0, split), (split, frame_count))
+    else:
+        bounds = ((0, frame_count),)
 
     def straight(source, target):
         return [(source * row_count + r, target * row_count + r) for r in range(row_count)]
@@ -58,28 +64,17 @@
     down = [(i + 1, i) for i in range(row_count - 1)]
     top = lax.ppermute(features[:, height - 1 :], "rows", up)
     bottom = lax.ppermute(features[:, :1], "rows", down)
-    current = features
-    skip = features
-    last_stage = segment_count - 1
+    parts = [
+        (features[low:high], top[low:high], bottom[low:high]) for low, high in bounds
+    ]
+    skips = [features[low:high] for low, high in bounds]
+    pieces = {}
 
     for stage in range(segment_count):
-        window = jnp.concatenate([top, current, bottom], axis=1)
         odd = stage % 2 == 1
         final = stage == last_stage
-
-        def compute(window, skip, odd=odd, final=final):
-            convolved = causal_conv(activate(window, gain_row), kernel).astype(jnp.bfloat16)
-            if odd and not final:
-                convolved = (skip.astype(jnp.float32) + convolved).astype(jnp.bfloat16)
-            return convolved
-
-        def idle(window, skip):
-            return jnp.zeros(skip.shape, jnp.bfloat16)
-
-        produced = lax.cond(segment_index == stage, compute, idle, window, skip)
-        if final:
-            break
         if stage == last_stage - 1:
+            current = jnp.concatenate([body for body, _, _ in parts], axis=0)
             owned = current[stage * group : (stage + 1) * group]
             for target in range(segment_count):
                 chunk = current[target * group : (target + 1) * group]
@@ -88,18 +83,35 @@
                 elif target != stage:
                     piece = send(chunk, straight(stage, target))
                     owned = jnp.where(segment_index == target, piece, owned)
-        next_skip = current if (not odd and stage > 0 and stage != last_stage - 1) else None
-        current, top, bottom = stage_send(produced, stage, row_count)
-        if next_skip is not None:
-            skip = send(next_skip, straight(stage, stage + 1))
-        elif not odd:
-            skip = features
+        sends_skip = not odd and 0 < stage < last_stage - 1
+        history = None
+        outputs = []
+        for index, ((low, high), (body, above, below)) in enumerate(zip(bounds, parts)):
+            activated = activate(jnp.concatenate([above, body, below], axis=1), gain_row)
+            if history is None:
+                history = jnp.zeros((2,) + activated.shape[1:], activated.dtype)
+            window = jnp.concatenate([history, activated], axis=0)
+            history = window[-2:]
+            convolved = causal_conv(window, kernel, 0).astype(jnp.bfloat16)
+            if final:
+                for target in range(low // group, high // group):
+                    chunk = convolved[target * group - low : (target + 1) * group - low]
+                    if target != last_stage:
+                        chunk = send(chunk, straight(last_stage, target))
+                    pieces[target] = chunk
+                continue
+            if odd:
+                convolved = (skips[index].astype(jnp.float32) + convolved).astype(jnp.bfloat16)
+            outputs.append(stage_send(convolved, stage, row_count))
+            if sends_skip:
+                skips[index] = send(body, straight(stage, stage + 1))
+            elif not odd:
+                skips[index] = features[low:high]
+        parts = outputs
 
-    branch = produced[last_stage * group :]
-    for target in range(last_stage):
-        chunk = produced[target * group : (target + 1) * group]
-        piece = send(chunk, straight(last_stage, target))
-        branch = jnp.where(segment_index == target, piece, branch)
+    branch = pieces[0]
+    for target in range(1, segment_count):
+        branch = jnp.where(segment_index == target, pieces[target], branch)
     return (owned.astype(jnp.float32) + branch.astype(jnp.float32)).astype(jnp.bfloat16)
 
 

time: 98.4 us -> 99.1 us (level)
  the two profiles are of different devices: /device:TPU:1 before, /device:TPU:21 now
where the time goes in v10:
time: 99.1 us; the launch traced here: 98.5 us
  starting transfers between devices  37.6 us (38%)
  matrix products  27.3 us (28%)
  waiting for transfers between devices  20.2 us (20%)
  local copies, waits for them, and re-layouts  8.09 us (8%)
  other arithmetic  4.06 us (4%)
  between operations  1.18 us (1%)
    ppermute x24, starting transfers between devices, send(): return lax.ppermute(value, BOTH, pairs)  32 us
    conv_general_dilated x8, matrix products, causal_conv(): lax.conv_general_dilated(window[None], kernel, window_strides=(1, 1, 1),...  27.3 us
    ppermute x24, waiting for transfers between devices, send(): return lax.ppermute(value, BOTH, pairs)  18.2 us
    ppermute x1, starting transfers between devices, local(): top = lax.ppermute(features[:, height - 1:], 'rows', up)  3.68 us
    ppermute x1, waiting for transfers between devices, local(): bottom = lax.ppermute(features[:, :1], 'rows', down)  2 us
  transfers between devices with their start and end apart: 26, of which 5 were waited for; matrix products, arithmetic and copies ran while one was open for 18% of the time, Pallas kernels for 0%

profile of v10, /device:TPU:21, one launch (start us, length us, event | category | flops | bytes accessed | tf_op | source)
XLA Modules:
  0.0 98.5 jit_solution(15854072703705890823)
XLA Ops:
  0.0 0.9 fusion.222
  0.9 3.7 %collective-permute-start = (bf16[4,1,24,384]{3,2,1,0:T(8,128)(2,1)S(1)}, bf16[4,1,24,384]{3,2,1,0:T(8,128)(2,1)S(1)}, u32[]{:S(2)}, u32[]{:S(2)}) collective-permute-start(bf16[4,1,24,384]{3,2,1,0:T(8,128)(2,1)S(1)} %get-tuple-element.9), channel_id=1, source_target_pairs={{0,1},{1,2},{2,3},{3,4},{4,5},{5,6},{6,7},{8,9},{9,10},{10,11},{11... | collective-permute-start | bytes 221192 | tf_op jit(solution)/shard_map/ppermute | solution.py:65
  4.6 1.9 %collective-permute-start.1 = (bf16[4,1,24,384]{3,2,1,0:T(8,128)(2,1)S(1)}, bf16[4,1,24,384]{3,2,1,0:T(8,128)(2,1)S(1)}, u32[]{:S(2)}, u32[]{:S(2)}) collective-permute-start(bf16[4,1,24,384]{3,2,1,0:T(8,128)(2,1)S(1)} %get-tuple-element.10), channel_id=1, source_target_pairs={{1,0},{2,1},{3,2},{4,3},{5,4},{6,5},{7,6},{9,8},{10,9},{11,10},{12... | collective-permute-start | bytes 221192 | tf_op jit(solution)/shard_map/ppermute | solution.py:66
  6.6 1.0 %fusion.221 = (bf16[2,4,24,384]{3,2,1,0:T(8,128)(2,1)S(1)}, bf16[2,4,24,384]{3,2,1,0:T(8,128)(2,1)S(1)}) fusion(bf16[4,4,24,384]{3,2,1,0:T(8,128)(2,1)} %param.3), kind=kLoop, calls=%fused_computation.237 | loop fusion | bytes 589824 | tf_op jit(solution)/shard_map/slice | solution.py:68
  7.6 0.7 convert_reduce_fusion
  8.3 2.0 %collective-permute-done.1 = bf16[4,1,24,384]{3,2,1,0:T(8,128)(2,1)S(1)} collective-permute-done((bf16[4,1,24,384]{3,2,1,0:T(8,128)(2,1)S(1)}, bf16[4,1,24,384]{3,2,1,0:T(8,128)(2,1)S(1)}, u32[]{:S(2)}, u32[]{:S(2)}) %collective-permute-start.1) | collective-permute-done | bytes 73760 | tf_op jit(solution)/shard_map/ppermute | solution.py:66
  10.5 0.3 fusion.127
  11.6 6.4 %fusion.66 = bf16[2,4,8,4,384]{4,2,3,1,0:T(8,128)(2,1)S(1)} fusion(bf16[1,3,3,3,384,384]{5,4,3,2,1,0:T(8,128)(2,1)} %param.5, bf16[4,6,1,7,2,384]{5,3,4,1,0,2:T(8,128)(2,1)S(1)} %slice.160, bf16[4,6,1,8,4,384]{5,3,4,1,0,2:T(8,128)(2,1)S(1)} %copy.50, pred[8,4]{0,1:T(4,128)(4,1)S(1)} %copy-done.1), kind=kOutput, calls=%fused_computation.39 | convolution fusion | flops 2041282560 | bytes 9007136 | tf_op jit(solution)/shard_map/conv_general_dilated | solution.py:18
  18.2 0.7 collective-permute-start.6
  18.9 0.7 collective-permute-start.5
  19.5 0.7 collective-permute-start.7
  20.8 3.0 %fusion.69 = bf16[2,4,8,4,384]{4,2,3,1,0:T(8,128)(2,1)S(1)} fusion(bf16[1,3,3,3,384,384]{5,4,3,2,1,0:T(8,128)(2,1)S(1)} %bitcast.174, bf16[4,6,1,7,2,384]{5,3,4,1,0,2:T(8,128)(2,1)S(1)} %slice.154, bf16[4,6,1,8,4,384]{5,3,4,1,0,2:T(8,128)(2,1)S(1)} %copy.45, pred[8,4]{0,1:T(4,128)(4,1)S(1)} %copy-done.1), kind=kOutput, calls=%fused_computation.40 | convolution fusion | flops 2041282560 | bytes 9007136 | tf_op jit(solution)/shard_map/conv_general_dilated | solution.py:18
  24.1 0.7 collective-permute-start.3
  24.7 0.7 collective-permute-start.2
  25.4 0.8 collective-permute-start.4
  26.6 0.3 fusion.135
  27.6 3.0 %fusion.63 = bf16[2,4,8,4,384]{4,2,3,1,0:T(8,128)(2,1)S(1)} fusion(bf16[1,3,3,3,384,384]{5,4,3,2,1,0:T(8,128)(2,1)S(1)} %bitcast.174, bf16[4,6,1,7,2,384]{5,3,4,1,0,2:T(8,128)(2,1)S(1)} %slice.164, bf16[4,6,1,8,4,384]{5,3,4,1,0,2:T(8,128)(2,1)S(1)} %copy.55, pred[8,4]{0,1:T(4,128)(4,1)S(1)} %copy-done.1), kind=kOutput, calls=%fused_computation.38 | convolution fusion | flops 2041282560 | bytes 9007136 | tf_op jit(solution)/shard_map/conv_general_dilated | solution.py:18
  31.4 3.0 %fusion.60 = bf16[2,4,8,4,384]{4,2,3,1,0:T(8,128)(2,1)S(1)} fusion(bf16[1,3,3,3,384,384]{5,4,3,2,1,0:T(8,128)(2,1)S(1)} %bitcast.174, bf16[4,6,1,7,2,384]{5,3,4,1,0,2:T(8,128)(2,1)S(1)} %slice.167, bf16[4,6,1,8,4,384]{5,3,4,1,0,2:T(8,128)(2,1)S(1)} %copy.60, pred[8,4]{0,1:T(4,128)(4,1)S(1)} %copy-done.1), kind=kOutput, calls=%fused_computation.37 | convolution fusion | flops 2041282560 | bytes 9007136 | tf_op jit(solution)/shard_map/conv_general_dilated | solution.py:18
  34.7 1.3 %collective-permute-start.8 = (bf16[2,4,24,384]{3,2,1,0:T(8,128)(2,1)S(1)}, bf16[2,4,24,384]{3,2,1,0:T(8,128)(2,1)S(1)}, u32[]{:S(2)}, u32[]{:S(2)}) collective-permute-start(bf16[2,4,24,384]{3,2,1,0:T(8,128)(2,1)S(1)} %get-tuple-element.6), channel_id=1, source_target_pairs={{8,16},{9,17},{10,18},{11,19},{12,20},{13,21},{14,22},{15,23}} | collective-permute-start | bytes 442376 | tf_op jit(solution)/shard_map/ppermute | solution.py:30
  36.0 1.3 %collective-permute-start.18 = (bf16[2,1,24,384]{3,2,1,0:T(8,128)(2,1)S(1)}, bf16[2,1,24,384]{3,2,1,0:T(8,128)(2,1)S(1)}, u32[]{:S(2)}, u32[]{:S(2)}) collective-permute-start(bf16[2,1,24,384]{3,2,1,0:T(8,128)(2,1)S(1)} %get-tuple-element.29), channel_id=1, source_target_pairs={{8,17},{9,18},{10,19},{11,20},{12,21},{13,22},{14,23}} | collective-permute-start | bytes 110600 | tf_op jit(solution)/shard_map/ppermute | solution.py:30
  37.3 1.3 %collective-permute-start.19 = (bf16[2,1,24,384]{3,2,1,0:T(8,128)(2,1)S(1)}, bf16[2,1,24,384]{3,2,1,0:T(8,128)(2,1)S(1)}, u32[]{:S(2)}, u32[]{:S(2)}) collective-permute-start(bf16[2,1,24,384]{3,2,1,0:T(8,128)(2,1)S(1)} %get-tuple-element.30), channel_id=1, source_target_pairs={{9,16},{10,17},{11,18},{12,19},{13,20},{14,21},{15,22}} | collective-permute-start | bytes 110600 | tf_op jit(solution)/shard_map/ppermute | solution.py:30
  38.6 1.3 %collective-permute-start.10 = (bf16[2,4,24,384]{3,2,1,0:T(8,128)(2,1)S(1)}, bf16[2,4,24,384]{3,2,1,0:T(8,128)(2,1)S(1)}, u32[]{:S(2)}, u32[]{:S(2)}) collective-permute-start(bf16[2,4,24,384]{3,2,1,0:T(8,128)(2,1)S(1)} %get-tuple-element.5), channel_id=1, source_target_pairs={{8,16},{9,17},{10,18},{11,19},{12,20},{13,21},{14,22},{15,23}} | collective-permute-start | bytes 442376 | tf_op jit(solution)/shard_map/ppermute | solution.py:30
  39.9 1.3 %collective-permute-start.13 = (bf16[2,1,24,384]{3,2,1,0:T(8,128)(2,1)S(1)}, bf16[2,1,24,384]{3,2,1,0:T(8,128)(2,1)S(1)}, u32[]{:S(2)}, u32[]{:S(2)}) collective-permute-start(bf16[2,1,24,384]{3,2,1,0:T(8,128)(2,1)S(1)} %get-tuple-element.27), channel_id=1, source_target_pairs={{8,17},{9,18},{10,19},{11,20},{12,21},{13,22},{14,23}} | collective-permute-start | bytes 110600 | tf_op jit(solution)/shard_map/ppermute | solution.py:30
  41.2 9.4 %collective-permute-done.18 = bf16[2,1,24,384]{3,2,1,0:T(8,128)(2,1)S(1)} collective-permute-done((bf16[2,1,24,384]{3,2,1,0:T(8,128)(2,1)S(1)}, bf16[2,1,24,384]{3,2,1,0:T(8,128)(2,1)S(1)}, u32[]{:S(2)}, u32[]{:S(2)}) %collective-permute-start.18) | collective-permute-done | bytes 36896 | tf_op jit(solution)/shard_map/ppermute | solution.py:30
  50.6 1.5 %collective-permute-start.14 = (bf16[2,1,24,384]{3,2,1,0:T(8,128)(2,1)S(1)}, bf16[2,1,24,384]{3,2,1,0:T(8,128)(2,1)S(1)}, u32[]{:S(2)}, u32[]{:S(2)}) collective-permute-start(bf16[2,1,24,384]{3,2,1,0:T(8,128)(2,1)S(1)} %get-tuple-element.28), channel_id=1, source_target_pairs={{9,16},{10,17},{11,18},{12,19},{13,20},{14,21},{15,22}} | collective-permute-start | bytes 110600 | tf_op jit(solution)/shard_map/ppermute | solution.py:30
  52.2 2.3 %collective-permute-done.13 = bf16[2,1,24,384]{3,2,1,0:T(8,128)(2,1)S(1)} collective-permute-done((bf16[2,1,24,384]{3,2,1,0:T(8,128)(2,1)S(1)}, bf16[2,1,24,384]{3,2,1,0:T(8,128)(2,1)S(1)}, u32[]{:S(2)}, u32[]{:S(2)}) %collective-permute-start.13) | collective-permute-done | bytes 36896 | tf_op jit(solution)/shard_map/ppermute | solution.py:30
  54.6 2.4 %collective-permute-done.14 = bf16[2,1,24,384]{3,2,1,0:T(8,128)(2,1)S(1)} collective-permute-done((bf16[2,1,24,384]{3,2,1,0:T(8,128)(2,1)S(1)}, bf16[2,1,24,384]{3,2,1,0:T(8,128)(2,1)S(1)}, u32[]{:S(2)}, u32[]{:S(2)}) %collective-permute-start.14) | collective-permute-done | bytes 36896 | tf_op jit(solution)/shard_map/ppermute | solution.py:30
  57.1 0.3 fusion.159
  58.2 3.0 %fusion.54 = bf16[2,4,8,4,384]{4,2,3,1,0:T(8,128)(2,1)S(1)} fusion(bf16[1,3,3,3,384,384]{5,4,3,2,1,0:T(8,128)(2,1)S(1)} %bitcast.174, bf16[4,6,1,7,2,384]{5,3,4,1,0,2:T(8,128)(2,1)S(1)} %slice.180, bf16[4,6,1,8,4,384]{5,3,4,1,0,2:T(8,128)(2,1)S(1)} %copy.70, pred[8,4]{0,1:T(4,128)(4,1)S(1)} %copy-done.1), kind=kOutput, calls=%fused_computation.35 | convolution fusion | flops 2041282560 | bytes 9007136 | tf_op jit(solution)/shard_map/conv_general_dilated | solution.py:18
  61.4 1.3 %collective-permute-start.21 = (bf16[2,4,24,384]{3,2,1,0:T(8,128)(2,1)S(1)}, bf16[2,4,24,384]{3,2,1,0:T(8,128)(2,1)S(1)}, u32[]{:S(2)}, u32[]{:S(2)}) collective-permute-start(bf16[2,4,24,384]{3,2,1,0:T(8,128)(2,1)S(1)} %bitcast.158), channel_id=1, source_target_pairs={{16,24},{17,25},{18,26},{19,27},{20,28},{21,29},{22,30},{23,31}} | collective-permute-start | bytes 442376 | tf_op jit(solution)/shard_map/ppermute | solution.py:30
  62.9 0.2 pad.12.clone
  63.3 3.0 %fusion.57 = bf16[2,4,8,4,384]{4,2,3,1,0:T(8,128)(2,1)S(1)} fusion(bf16[1,3,3,3,384,384]{5,4,3,2,1,0:T(8,128)(2,1)S(1)} %bitcast.174, bf16[4,6,1,7,2,384]{5,3,4,1,0,2:T(8,128)(2,1)S(1)} %slice.174, bf16[4,6,1,8,4,384]{5,3,4,1,0,2:T(8,128)(2,1)S(1)} %copy.65, pred[8,4]{0,1:T(4,128)(4,1)S(1)} %copy-done.1), kind=kOutput, calls=%fused_computation.36 | convolution fusion | flops 2041282560 | bytes 9007136 | tf_op jit(solution)/shard_map/conv_general_dilated | solution.py:18
  66.5 1.3 %collective-permute-start.16 = (bf16[2,4,24,384]{3,2,1,0:T(8,128)(2,1)S(1)}, bf16[2,4,24,384]{3,2,1,0:T(8,128)(2,1)S(1)}, u32[]{:S(2)}, u32[]{:S(2)}) collective-permute-start(bf16[2,4,24,384]{3,2,1,0:T(8,128)(2,1)S(1)} %bitcast.160), channel_id=1, source_target_pairs={{16,24},{17,25},{18,26},{19,27},{20,28},{21,29},{22,30},{23,31}} | collective-permute-start | bytes 442376 | tf_op jit(solution)/shard_map/ppermute | solution.py:30
  67.8 1.3 %collective-permute-start.20 = (bf16[2,1,24,384]{3,2,1,0:T(8,128)(2,1)S(1)}, bf16[2,1,24,384]{3,2,1,0:T(8,128)(2,1)S(1)}, u32[]{:S(2)}, u32[]{:S(2)}) collective-permute-start(bf16[2,1,24,384]{3,2,1,0:T(8,128)(2,1)S(1)} %get-tuple-element.25), channel_id=1, source_target_pairs={{16,25},{17,26},{18,27},{19,28},{20,29},{21,30},{22,31}} | collective-permute-start | bytes 110600 | tf_op jit(solution)/shard_map/ppermute | solution.py:30
  69.1 1.3 %collective-permute-start.22 = (bf16[2,1,24,384]{3,2,1,0:T(8,128)(2,1)S(1)}, bf16[2,1,24,384]{3,2,1,0:T(8,128)(2,1)S(1)}, u32[]{:S(2)}, u32[]{:S(2)}) collective-permute-start(bf16[2,1,24,384]{3,2,1,0:T(8,128)(2,1)S(1)} %get-tuple-element.26), channel_id=1, source_target_pairs={{17,24},{18,25},{19,26},{20,27},{21,28},{22,29},{23,30}} | collective-permute-start | bytes 110600 | tf_op jit(solution)/shard_map/ppermute | solution.py:30
  70.4 1.3 %collective-permute-start.15 = (bf16[2,1,24,384]{3,2,1,0:T(8,128)(2,1)S(1)}, bf16[2,1,24,384]{3,2,1,0:T(8,128)(2,1)S(1)}, u32[]{:S(2)}, u32[]{:S(2)}) collective-permute-start(bf16[2,1,24,384]{3,2,1,0:T(8,128)(2,1)S(1)} %get-tuple-element.23), channel_id=1, source_target_pairs={{16,25},{17,26},{18,27},{19,28},{20,29},{21,30},{22,31}} | collective-permute-start | bytes 110600 | tf_op jit(solution)/shard_map/ppermute | solution.py:30
  71.8 6.7 %collective-permute-start.17 = (bf16[2,1,24,384]{3,2,1,0:T(8,128)(2,1)S(1)}, bf16[2,1,24,384]{3,2,1,0:T(8,128)(2,1)S(1)}, u32[]{:S(2)}, u32[]{:S(2)}) collective-permute-start(bf16[2,1,24,384]{3,2,1,0:T(8,128)(2,1)S(1)} %get-tuple-element.24), channel_id=1, source_target_pairs={{17,24},{18,25},{19,26},{20,27},{21,28},{22,29},{23,30}} | collective-permute-start | bytes 110600 | tf_op jit(solution)/shard_map/ppermute | solution.py:30
  78.5 1.3 %collective-permute-start.11 = (bf16[1,4,24,384]{3,2,1,0:T(8,128)(2,1)S(1)}, bf16[1,4,24,384]{3,2,1,0:T(8,128)(2,1)S(1)}, u32[]{:S(2)}, u32[]{:S(2)}) collective-permute-start(bf16[1,4,24,384]{3,2,1,0:T(8,128)(2,1)S(1)} %get-tuple-element.32), channel_id=1, source_target_pairs={{16,8},{17,9},{18,10},{19,11},{20,12},{21,13},{22,14},{23,15}} | collective-permute-start | bytes 221192 | tf_op jit(solution)/shard_map/ppermute | solution.py:30
  79.8 1.3 %collective-permute-start.12 = (bf16[1,4,24,384]{3,2,1,0:T(8,128)(2,1)S(1)}, bf16[1,4,24,384]{3,2,1,0:T(8,128)(2,1)S(1)}, u32[]{:S(2)}, u32[]{:S(2)}) collective-permute-start(bf16[1,4,24,384]{3,2,1,0:T(8,128)(2,1)S(1)} %get-tuple-element.31), channel_id=1, source_target_pairs={{16,0},{17,1},{18,2},{19,3},{20,4},{21,5},{22,6},{23,7}} | collective-permute-start | bytes 221192 | tf_op jit(solution)/shard_map/ppermute | solution.py:30
  81.2 1.6 %collective-permute-start.9 = (bf16[1,4,24,384]{3,2,1,0:T(8,128)(2,1)S(1)}, bf16[1,4,24,384]{3,2,1,0:T(8,128)(2,1)S(1)}, u32[]{:S(2)}, u32[]{:S(2)}) collective-permute-start(bf16[1,4,24,384]{3,2,1,0:T(8,128)(2,1)S(1)} %slice.166), channel_id=1, source_target_pairs={{16,24},{17,25},{18,26},{19,27},{20,28},{21,29},{22,30},{23,31}} | collective-permute-start | bytes 221192 | tf_op jit(solution)/shard_map/ppermute | solution.py:30
  83.0 0.3 fusion.167
  84.0 3.0 %fusion.48 = bf16[2,4,8,4,384]{4,2,3,1,0:T(8,128)(2,1)S(1)} fusion(bf16[1,3,3,3,384,384]{5,4,3,2,1,0:T(8,128)(2,1)S(1)} %bitcast.174, bf16[4,6,1,7,2,384]{5,3,4,1,0,2:T(8,128)(2,1)S(1)} %slice.189, bf16[4,6,1,8,4,384]{5,3,4,1,0,2:T(8,128)(2,1)S(1)} %copy.82, pred[8,4]{0,1:T(4,128)(4,1)S(1)} %copy-done.1), kind=kOutput, calls=%fused_computation.33 | convolution fusion | flops 2041282560 | bytes 9007136 | tf_op jit(solution)/shard_map/conv_general_dilated | solution.py:18
  87.1 0.7 collective-permute-start.24
  87.9 0.7 collective-permute-start.25
  89.2 3.0 %fusion.51 = bf16[2,4,8,4,384]{4,2,3,1,0:T(8,128)(2,1)S(1)} fusion(bf16[1,3,3,3,384,384]{5,4,3,2,1,0:T(8,128)(2,1)S(1)} %bitcast.174, bf16[4,6,1,7,2,384]{5,3,4,1,0,2:T(8,128)(2,1)S(1)} %slice.184, bf16[4,6,1,8,4,384]{5,3,4,1,0,2:T(8,128)(2,1)S(1)} %copy.75, pred[8,4]{0,1:T(4,128)(4,1)S(1)} %copy-done.1), kind=kOutput, calls=%fused_computation.34 | convolution fusion | flops 2041282560 | bytes 9007136 | tf_op jit(solution)/shard_map/conv_general_dilated | solution.py:18
  92.4 1.3 %collective-permute-start.23 = (bf16[1,4,24,384]{3,2,1,0:T(8,128)(2,1)S(1)}, bf16[1,4,24,384]{3,2,1,0:T(8,128)(2,1)S(1)}, u32[]{:S(2)}, u32[]{:S(2)}) collective-permute-start(bf16[1,4,24,384]{3,2,1,0:T(8,128)(2,1)S(1)} %bitcast.172), channel_id=1, source_target_pairs={{24,16},{25,17},{26,18},{27,19},{28,20},{29,21},{30,22},{31,23}} | collective-permute-start | bytes 221192 | tf_op jit(solution)/shard_map/ppermute | solution.py:30
  93.8 4.0 %collective-permute-done.23 = bf16[1,4,24,384]{3,2,1,0:T(8,128)(2,1)S(1)} collective-permute-done((bf16[1,4,24,384]{3,2,1,0:T(8,128)(2,1)S(1)}, bf16[1,4,24,384]{3,2,1,0:T(8,128)(2,1)S(1)}, u32[]{:S(2)}, u32[]{:S(2)}) %collective-permute-start.23) | collective-permute-done | bytes 73760 | tf_op jit(solution)/shard_map/ppermute | solution.py:30
  97.9 0.7 add_convert_fusion
  (120 shorter events, 7.3 us)
Async XLA Ops:
  0.9 7.3 %collective-permute-start = (bf16[4,1,24,384]{3,2,1,0:T(8,128)(2,1)S(1)}, bf16[4,1,24,384]{3,2,1,0:T(8,128)(2,1)S(1)}, u32[]{:S(2)}, u32[]{:S(2)}) collective-permute-start(bf16[4,1,24,384]{3,2,1,0:T(8,128)(2,1)S(1)} %get-tuple-element.9), channel_id=1, source_target_pairs={{0,1},{1,2},{2,3},{3,4},{4,5},{5,6},{6,7},{8,9},{9,10},{10,11},{11... | collective-permute-start | bytes 221192 | tf_op jit(solution)/shard_map/ppermute | solution.py:65
  4.6 5.7 %collective-permute-start.1 = (bf16[4,1,24,384]{3,2,1,0:T(8,128)(2,1)S(1)}, bf16[4,1,24,384]{3,2,1,0:T(8,128)(2,1)S(1)}, u32[]{:S(2)}, u32[]{:S(2)}) collective-permute-start(bf16[4,1,24,384]{3,2,1,0:T(8,128)(2,1)S(1)} %get-tuple-element.10), channel_id=1, source_target_pairs={{1,0},{2,1},{3,2},{4,3},{5,4},{6,5},{7,6},{9,8},{10,9},{11,10},{12... | collective-permute-start | bytes 221192 | tf_op jit(solution)/shard_map/ppermute | solution.py:66
  10.9 0.7 copy-start.1
  11.5 9.3 %slice-start = ((s8[7962624]{0:T(1024)(128)(4,1)}), s8[4194304]{0:T(1024)(128)(4,1)S(1)}, s32[]{:S(2)}) async-start(s8[7962624]{0:T(1024)(128)(4,1)} %bitcast.173), calls=%async_computation | async-start | bytes 8388608
  11.6 9.2 %slice-start.1 = ((s8[7962624]{0:T(1024)(128)(4,1)}), s8[3768320]{0:T(1024)(128)(4,1)S(1)}, s32[]{:S(2)}) async-start(s8[7962624]{0:T(1024)(128)(4,1)} %bitcast.173), calls=%async_computation.1 | async-start | bytes 7536640
  18.2 8.1 %collective-permute-start.6 = (bf16[2,4,24,384]{3,2,1,0:T(8,128)(2,1)S(1)}, bf16[2,4,24,384]{3,2,1,0:T(8,128)(2,1)S(1)}, u32[]{:S(2)}, u32[]{:S(2)}) collective-permute-start(bf16[2,4,24,384]{3,2,1,0:T(8,128)(2,1)S(1)} %bitcast.163), channel_id=1, source_target_pairs={{0,8},{1,9},{2,10},{3,11},{4,12},{5,13},{6,14},{7,15}} | collective-permute-start | bytes 442376 | tf_op jit(solution)/shard_map/ppermute | solution.py:30
  18.9 6.5 %collective-permute-start.5 = (bf16[2,1,24,384]{3,2,1,0:T(8,128)(2,1)S(1)}, bf16[2,1,24,384]{3,2,1,0:T(8,128)(2,1)S(1)}, u32[]{:S(2)}, u32[]{:S(2)}) collective-permute-start(bf16[2,1,24,384]{3,2,1,0:T(8,128)(2,1)S(1)} %get-tuple-element.35), channel_id=1, source_target_pairs={{0,9},{1,10},{2,11},{3,12},{4,13},{5,14},{6,15}} | collective-permute-start | bytes 110600 | tf_op jit(solution)/shard_map/ppermute | solution.py:30
  19.5 6.7 %collective-permute-start.7 = (bf16[2,1,24,384]{3,2,1,0:T(8,128)(2,1)S(1)}, bf16[2,1,24,384]{3,2,1,0:T(8,128)(2,1)S(1)}, u32[]{:S(2)}, u32[]{:S(2)}) collective-permute-start(bf16[2,1,24,384]{3,2,1,0:T(8,128)(2,1)S(1)} %get-tuple-element.36), channel_id=1, source_target_pairs={{1,8},{2,9},{3,10},{4,11},{5,12},{6,13},{7,14}} | collective-permute-start | bytes 110600 | tf_op jit(solution)/shard_map/ppermute | solution.py:30
  24.1 2.4 %collective-permute-start.3 = (bf16[2,4,24,384]{3,2,1,0:T(8,128)(2,1)S(1)}, bf16[2,4,24,384]{3,2,1,0:T(8,128)(2,1)S(1)}, u32[]{:S(2)}, u32[]{:S(2)}) collective-permute-start(bf16[2,4,24,384]{3,2,1,0:T(8,128)(2,1)S(1)} %bitcast.165), channel_id=1, source_target_pairs={{0,8},{1,9},{2,10},{3,11},{4,12},{5,13},{6,14},{7,15}} | collective-permute-start | bytes 442376 | tf_op jit(solution)/shard_map/ppermute | solution.py:30
  24.7 1.7 %collective-permute-start.2 = (bf16[2,1,24,384]{3,2,1,0:T(8,128)(2,1)S(1)}, bf16[2,1,24,384]{3,2,1,0:T(8,128)(2,1)S(1)}, u32[]{:S(2)}, u32[]{:S(2)}) collective-permute-start(bf16[2,1,24,384]{3,2,1,0:T(8,128)(2,1)S(1)} %get-tuple-element.33), channel_id=1, source_target_pairs={{0,9},{1,10},{2,11},{3,12},{4,13},{5,14},{6,15}} | collective-permute-start | bytes 110600 | tf_op jit(solution)/shard_map/ppermute | solution.py:30
  25.4 1.0 %collective-permute-start.4 = (bf16[2,1,24,384]{3,2,1,0:T(8,128)(2,1)S(1)}, bf16[2,1,24,384]{3,2,1,0:T(8,128)(2,1)S(1)}, u32[]{:S(2)}, u32[]{:S(2)}) collective-permute-start(bf16[2,1,24,384]{3,2,1,0:T(8,128)(2,1)S(1)} %get-tuple-element.34), channel_id=1, source_target_pairs={{1,8},{2,9},{3,10},{4,11},{5,12},{6,13},{7,14}} | collective-permute-start | bytes 110600 | tf_op jit(solution)/shard_map/ppermute | solution.py:30
  31.4 3.2 %copy-start = (bf16[4,4,24,384]{3,2,1,0:T(8,128)(2,1)S(1)}, bf16[4,4,24,384]{3,2,1,0:T(8,128)(2,1)}, u32[]{:S(2)}) copy-start(bf16[4,4,24,384]{3,2,1,0:T(8,128)(2,1)} %param.3) | copy-start | bytes 884740
  34.7 17.4 %collective-permute-start.8 = (bf16[2,4,24,384]{3,2,1,0:T(8,128)(2,1)S(1)}, bf16[2,4,24,384]{3,2,1,0:T(8,128)(2,1)S(1)}, u32[]{:S(2)}, u32[]{:S(2)}) collective-permute-start(bf16[2,4,24,384]{3,2,1,0:T(8,128)(2,1)S(1)} %get-tuple-element.6), channel_id=1, source_target_pairs={{8,16},{9,17},{10,18},{11,19},{12,20},{13,21},{14,22},{15,23}} | collective-permute-start | bytes 442376 | tf_op jit(solution)/shard_map/ppermute | solution.py:30
  36.0 14.6 %collective-permute-start.18 = (bf16[2,1,24,384]{3,2,1,0:T(8,128)(2,1)S(1)}, bf16[2,1,24,384]{3,2,1,0:T(8,128)(2,1)S(1)}, u32[]{:S(2)}, u32[]{:S(2)}) collective-permute-start(bf16[2,1,24,384]{3,2,1,0:T(8,128)(2,1)S(1)} %get-tuple-element.29), channel_id=1, source_target_pairs={{8,17},{9,18},{10,19},{11,20},{12,21},{13,22},{14,23}} | collective-permute-start | bytes 110600 | tf_op jit(solution)/shard_map/ppermute | solution.py:30
  37.3 14.8 %collective-permute-start.19 = (bf16[2,1,24,384]{3,2,1,0:T(8,128)(2,1)S(1)}, bf16[2,1,24,384]{3,2,1,0:T(8,128)(2,1)S(1)}, u32[]{:S(2)}, u32[]{:S(2)}) collective-permute-start(bf16[2,1,24,384]{3,2,1,0:T(8,128)(2,1)S(1)} %get-tuple-element.30), channel_id=1, source_target_pairs={{9,16},{10,17},{11,18},{12,19},{13,20},{14,21},{15,22}} | collective-permute-start | bytes 110600 | tf_op jit(solution)/shard_map/ppermute | solution.py:30
  38.6 18.4 %collective-permute-start.10 = (bf16[2,4,24,384]{3,2,1,0:T(8,128)(2,1)S(1)}, bf16[2,4,24,384]{3,2,1,0:T(8,128)(2,1)S(1)}, u32[]{:S(2)}, u32[]{:S(2)}) collective-permute-start(bf16[2,4,24,384]{3,2,1,0:T(8,128)(2,1)S(1)} %get-tuple-element.5), channel_id=1, source_target_pairs={{8,16},{9,17},{10,18},{11,19},{12,20},{13,21},{14,22},{15,23}} | collective-permute-start | bytes 442376 | tf_op jit(solution)/shard_map/ppermute | solution.py:30
  39.9 14.7 %collective-permute-start.13 = (bf16[2,1,24,384]{3,2,1,0:T(8,128)(2,1)S(1)}, bf16[2,1,24,384]{3,2,1,0:T(8,128)(2,1)S(1)}, u32[]{:S(2)}, u32[]{:S(2)}) collective-permute-start(bf16[2,1,24,384]{3,2,1,0:T(8,128)(2,1)S(1)} %get-tuple-element.27), channel_id=1, source_target_pairs={{8,17},{9,18},{10,19},{11,20},{12,21},{13,22},{14,23}} | collective-permute-start | bytes 110600 | tf_op jit(solution)/shard_map/ppermute | solution.py:30
  50.6 6.4 %collective-permute-start.14 = (bf16[2,1,24,384]{3,2,1,0:T(8,128)(2,1)S(1)}, bf16[2,1,24,384]{3,2,1,0:T(8,128)(2,1)S(1)}, u32[]{:S(2)}, u32[]{:S(2)}) collective-permute-start(bf16[2,1,24,384]{3,2,1,0:T(8,128)(2,1)S(1)} %get-tuple-element.28), channel_id=1, source_target_pairs={{9,16},{10,17},{11,18},{12,19},{13,20},{14,21},{15,22}} | collective-permute-start | bytes 110600 | tf_op jit(solution)/shard_map/ppermute | solution.py:30
  61.4 18.4 %collective-permute-start.21 = (bf16[2,4,24,384]{3,2,1,0:T(8,128)(2,1)S(1)}, bf16[2,4,24,384]{3,2,1,0:T(8,128)(2,1)S(1)}, u32[]{:S(2)}, u32[]{:S(2)}) collective-permute-start(bf16[2,4,24,384]{3,2,1,0:T(8,128)(2,1)S(1)} %bitcast.158), channel_id=1, source_target_pairs={{16,24},{17,25},{18,26},{19,27},{20,28},{21,29},{22,30},{23,31}} | collective-permute-start | bytes 442376 | tf_op jit(solution)/shard_map/ppermute | solution.py:30
  66.5 16.3 %collective-permute-start.16 = (bf16[2,4,24,384]{3,2,1,0:T(8,128)(2,1)S(1)}, bf16[2,4,24,384]{3,2,1,0:T(8,128)(2,1)S(1)}, u32[]{:S(2)}, u32[]{:S(2)}) collective-permute-start(bf16[2,4,24,384]{3,2,1,0:T(8,128)(2,1)S(1)} %bitcast.160), channel_id=1, source_target_pairs={{16,24},{17,25},{18,26},{19,27},{20,28},{21,29},{22,30},{23,31}} | collective-permute-start | bytes 442376 | tf_op jit(solution)/shard_map/ppermute | solution.py:30
  67.8 3.9 %collective-permute-start.20 = (bf16[2,1,24,384]{3,2,1,0:T(8,128)(2,1)S(1)}, bf16[2,1,24,384]{3,2,1,0:T(8,128)(2,1)S(1)}, u32[]{:S(2)}, u32[]{:S(2)}) collective-permute-start(bf16[2,1,24,384]{3,2,1,0:T(8,128)(2,1)S(1)} %get-tuple-element.25), channel_id=1, source_target_pairs={{16,25},{17,26},{18,27},{19,28},{20,29},{21,30},{22,31}} | collective-permute-start | bytes 110600 | tf_op jit(solution)/shard_map/ppermute | solution.py:30
  69.1 9.3 %collective-permute-start.22 = (bf16[2,1,24,384]{3,2,1,0:T(8,128)(2,1)S(1)}, bf16[2,1,24,384]{3,2,1,0:T(8,128)(2,1)S(1)}, u32[]{:S(2)}, u32[]{:S(2)}) collective-permute-start(bf16[2,1,24,384]{3,2,1,0:T(8,128)(2,1)S(1)} %get-tuple-element.26), channel_id=1, source_target_pairs={{17,24},{18,25},{19,26},{20,27},{21,28},{22,29},{23,30}} | collective-permute-start | bytes 110600 | tf_op jit(solution)/shard_map/ppermute | solution.py:30
  70.4 10.8 %collective-permute-start.15 = (bf16[2,1,24,384]{3,2,1,0:T(8,128)(2,1)S(1)}, bf16[2,1,24,384]{3,2,1,0:T(8,128)(2,1)S(1)}, u32[]{:S(2)}, u32[]{:S(2)}) collective-permute-start(bf16[2,1,24,384]{3,2,1,0:T(8,128)(2,1)S(1)} %get-tuple-element.23), channel_id=1, source_target_pairs={{16,25},{17,26},{18,27},{19,28},{20,29},{21,30},{22,31}} | collective-permute-start | bytes 110600 | tf_op jit(solution)/shard_map/ppermute | solution.py:30
  71.8 11.0 %collective-permute-start.17 = (bf16[2,1,24,384]{3,2,1,0:T(8,128)(2,1)S(1)}, bf16[2,1,24,384]{3,2,1,0:T(8,128)(2,1)S(1)}, u32[]{:S(2)}, u32[]{:S(2)}) collective-permute-start(bf16[2,1,24,384]{3,2,1,0:T(8,128)(2,1)S(1)} %get-tuple-element.24), channel_id=1, source_target_pairs={{17,24},{18,25},{19,26},{20,27},{21,28},{22,29},{23,30}} | collective-permute-start | bytes 110600 | tf_op jit(solution)/shard_map/ppermute | solution.py:30
  78.5 13.9 %collective-permute-start.11 = (bf16[1,4,24,384]{3,2,1,0:T(8,128)(2,1)S(1)}, bf16[1,4,24,384]{3,2,1,0:T(8,128)(2,1)S(1)}, u32[]{:S(2)}, u32[]{:S(2)}) collective-permute-start(bf16[1,4,24,384]{3,2,1,0:T(8,128)(2,1)S(1)} %get-tuple-element.32), channel_id=1, source_target_pairs={{16,8},{17,9},{18,10},{19,11},{20,12},{21,13},{22,14},{23,15}} | collective-permute-start | bytes 221192 | tf_op jit(solution)/shard_map/ppermute | solution.py:30
  79.8 14.0 %collective-permute-start.12 = (bf16[1,4,24,384]{3,2,1,0:T(8,128)(2,1)S(1)}, bf16[1,4,24,384]{3,2,1,0:T(8,128)(2,1)S(1)}, u32[]{:S(2)}, u32[]{:S(2)}) collective-permute-start(bf16[1,4,24,384]{3,2,1,0:T(8,128)(2,1)S(1)} %get-tuple-element.31), channel_id=1, source_target_pairs={{16,0},{17,1},{18,2},{19,3},{20,4},{21,5},{22,6},{23,7}} | collective-permute-start | bytes 221192 | tf_op jit(solution)/shard_map/ppermute | solution.py:30
  81.2 12.6 %collective-permute-start.9 = (bf16[1,4,24,384]{3,2,1,0:T(8,128)(2,1)S(1)}, bf16[1,4,24,384]{3,2,1,0:T(8,128)(2,1)S(1)}, u32[]{:S(2)}, u32[]{:S(2)}) collective-permute-start(bf16[1,4,24,384]{3,2,1,0:T(8,128)(2,1)S(1)} %slice.166), channel_id=1, source_target_pairs={{16,24},{17,25},{18,26},{19,27},{20,28},{21,29},{22,30},{23,31}} | collective-permute-start | bytes 221192 | tf_op jit(solution)/shard_map/ppermute | solution.py:30
  87.1 6.7 %collective-permute-start.24 = (bf16[1,4,24,384]{3,2,1,0:T(8,128)(2,1)S(1)}, bf16[1,4,24,384]{3,2,1,0:T(8,128)(2,1)S(1)}, u32[]{:S(2)}, u32[]{:S(2)}) collective-permute-start(bf16[1,4,24,384]{3,2,1,0:T(8,128)(2,1)S(1)} %bitcast.170), channel_id=1, source_target_pairs={{24,8},{25,9},{26,10},{27,11},{28,12},{29,13},{30,14},{31,15}} | collective-permute-start | bytes 221192 | tf_op jit(solution)/shard_map/ppermute | solution.py:30
  87.9 5.9 %collective-permute-start.25 = (bf16[1,4,24,384]{3,2,1,0:T(8,128)(2,1)S(1)}, bf16[1,4,24,384]{3,2,1,0:T(8,128)(2,1)S(1)}, u32[]{:S(2)}, u32[]{:S(2)}) collective-permute-start(bf16[1,4,24,384]{3,2,1,0:T(8,128)(2,1)S(1)} %bitcast.171), channel_id=1, source_target_pairs={{24,0},{25,1},{26,2},{27,3},{28,4},{29,5},{30,6},{31,7}} | collective-permute-start | bytes 221192 | tf_op jit(solution)/shard_map/ppermute | solution.py:30
  92.4 5.5 %collective-permute-start.23 = (bf16[1,4,24,384]{3,2,1,0:T(8,128)(2,1)S(1)}, bf16[1,4,24,384]{3,2,1,0:T(8,128)(2,1)S(1)}, u32[]{:S(2)}, u32[]{:S(2)}) collective-permute-start(bf16[1,4,24,384]{3,2,1,0:T(8,128)(2,1)S(1)} %bitcast.172), channel_id=1, source_target_pairs={{24,16},{25,17},{26,18},{27,19},{28,20},{29,21},{30,22},{31,23}} | collective-permute-start | bytes 221192 | tf_op jit(solution)/shard_map/ppermute | solution.py:30

commit v11 on v9

--- a/solution.py
+++ b/solution.py
@@ -63,18 +63,24 @@
     last_stage = segment_count - 1
 
     for stage in range(segment_count):
-        window = jnp.concatenate([top, current, bottom], axis=1)
+        pieces = [top, current, bottom] if stage else [top, features, bottom]
+        window = jnp.concatenate(
+            [activate(piece, gain_row) for piece in pieces]
+            if stage == 0
+            else [activate(jnp.concatenate(pieces, axis=1), gain_row)],
+            axis=1,
+        )
         odd = stage % 2 == 1
         final = stage == last_stage
 
         def compute(window, skip, odd=odd, final=final):
-            convolved = causal_conv(activate(window, gain_row), kernel).astype(jnp.bfloat16)
+            convolved = causal_conv(window, kernel).astype(jnp.bfloat16)
             if odd and not final:
                 convolved = (skip.astype(jnp.float32) + convolved).astype(jnp.bfloat16)
             return convolved
 
         if final:
-            activated = jnp.pad(activate(window, gain_row), ((2, 0), (0, 0), (0, 0), (0, 0)))
+            activated = jnp.pad(window, ((2, 0), (0, 0), (0, 0), (0, 0)))
             split = (segment_count // 2) * group
             branch = None
             for low, high in ((0, split), (split, frame_count)):
@@ -92,17 +98,20 @@
                         )
             break
         produced = compute(window, skip)
+        next_skip = current if (not odd and stage > 0 and stage != last_stage - 1) else None
+        block_input = current
+        current, top, bottom = stage_send(produced, stage, row_count)
         if stage == last_stage - 1:
-            owned = current[stage * group : (stage + 1) * group]
+            after = current[:1, :1, :1, :1].astype(jnp.float32) * 0
+            owned = block_input[stage * group : (stage + 1) * group]
             for target in range(segment_count):
-                chunk = current[target * group : (target + 1) * group]
+                chunk = block_input[target * group : (target + 1) * group]
                 if stage == 0:
                     owned = jnp.where(segment_index == target, chunk, owned)
                 elif target != stage:
-                    piece = send(chunk, straight(stage, target))
+                    tied = (chunk.astype(jnp.float32) + after).astype(jnp.bfloat16)
+                    piece = send(tied, straight(stage, target))
                     owned = jnp.where(segment_index == target, piece, owned)
-        next_skip = current if (not odd and stage > 0 and stage != last_stage - 1) else None
-        current, top, bottom = stage_send(produced, stage, row_count)
         if next_skip is not None:
             skip = send(next_skip, straight(stage, stage + 1))
         elif not odd:

time: 91.9 us -> 94.2 us (1.025)
  starting transfers between devices: 22.3 us -> 26.9 us
  waiting for transfers between devices: 31.7 us -> 27.3 us
    ppermute x15, starting transfers between devices: 16.7 us -> 21.3 us  [send(): return lax.ppermute(value, BOTH, pairs)]
    ppermute x1, waiting for transfers between devices: 3.04 us -> 0.01 us  [local(): bottom = lax.ppermute(features[:, :1], 'rows', down)]
    slice x1 -> x2, local copies, waits for them, and re-layouts: 0.02 us -> 1.45 us  [the longest x1 0.94 us: local(): top = lax.ppermute(features[:, height - 1:], 'rows', up)]
    ppermute x15, waiting for transfers between devices: 28.7 us -> 27.3 us  [send(): return lax.ppermute(value, BOTH, pairs)]
    unnamed x19 -> x18, local copies, waits for them, and re-layouts: 1.96 us -> 1.02 us
    convert_element_type x5 -> x6, other arithmetic: 2.64 us -> 2.72 us  [activate(): return jax.nn.silu(widened * lax.rsqrt(mean_square + 1e-06) * gain_row.as...]
  transfers between devices with their start and end apart: 17 -> 17, of which waited for: 4 -> 5; matrix products, arithmetic and copies ran while one was open for 10% -> 8% of each run, Pallas kernels for 0% -> 0%
where the time goes in v11:
time: 94.2 us; the launch traced here: 93.2 us
  waiting for transfers between devices  27.3 us (29%)
  starting transfers between devices  26.9 us (29%)
  matrix products  25.6 us (27%)
  other arithmetic  6.08 us (6%)
  local copies, waits for them, and re-layouts  5.84 us (6%)
  between operations  1.45 us (2%)
    ppermute x15, waiting for transfers between devices, send(): return lax.ppermute(value, BOTH, pairs)  27.3 us
    conv_general_dilated x5, matrix products, causal_conv(): lax.conv_general_dilated(window[None], kernel, window_strides=(1, 1, 1),...  25.6 us
    ppermute x15, starting transfers between devices, send(): return lax.ppermute(value, BOTH, pairs)  21.3 us
    ppermute x1, starting transfers between devices, local(): top = lax.ppermute(features[:, height - 1:], 'rows', up)  3.02 us
    convert_element_type x6, other arithmetic, activate(): return jax.nn.silu(widened * lax.rsqrt(mean_square + 1e-06) * gain_row.as...  2.72 us
    ppermute x1, starting transfers between devices, local(): bottom = lax.ppermute(features[:, :1], 'rows', down)  2.58 us
  transfers between devices with their start and end apart: 17, of which 5 were waited for; matrix products, arithmetic and copies ran while one was open for 8% of the time, Pallas kernels for 0%

profile of v11, /device:TPU:17, one launch (start us, length us, event | category | flops | bytes accessed | tf_op | source)
XLA Modules:
  0.0 93.2 jit_solution(11606033047286580798)
XLA Ops:
  0.0 0.9 %fusion.138 = (bf16[4,1,24,384]{3,2,1,0:T(8,128)(2,1)S(1)}, bf16[4,1,24,384]{3,2,1,0:T(8,128)(2,1)S(1)}) fusion(bf16[4,4,24,384]{3,2,1,0:T(8,128)(2,1)} %param.3), kind=kLoop, calls=%fused_computation.150 | loop fusion | bytes 294912 | tf_op jit(solution)/shard_map/slice | solution.py:59
  0.9 2.6 %collective-permute-start.1 = (bf16[4,1,24,384]{3,2,1,0:T(8,128)(2,1)S(1)}, bf16[4,1,24,384]{3,2,1,0:T(8,128)(2,1)S(1)}, u32[]{:S(2)}, u32[]{:S(2)}) collective-permute-start(bf16[4,1,24,384]{3,2,1,0:T(8,128)(2,1)S(1)} %get-tuple-element.15), channel_id=1, source_target_pairs={{1,0},{2,1},{3,2},{4,3},{5,4},{6,5},{7,6},{9,8},{10,9},{11,10},{12... | collective-permute-start | bytes 221192 | tf_op jit(solution)/shard_map/ppermute | solution.py:60
  3.5 3.0 %collective-permute-start = (bf16[4,1,24,384]{3,2,1,0:T(8,128)(2,1)S(1)}, bf16[4,1,24,384]{3,2,1,0:T(8,128)(2,1)S(1)}, u32[]{:S(2)}, u32[]{:S(2)}) collective-permute-start(bf16[4,1,24,384]{3,2,1,0:T(8,128)(2,1)S(1)} %get-tuple-element.14), channel_id=1, source_target_pairs={{0,1},{1,2},{2,3},{3,4},{4,5},{5,6},{6,7},{8,9},{9,10},{10,11},{11... | collective-permute-start | bytes 221192 | tf_op jit(solution)/shard_map/ppermute | solution.py:59
  6.6 1.1 %fusion.83 = f32[4,4,24]{2,1,0:T(4,128)S(1)} fusion(bf16[4,4,24,384]{3,2,1,0:T(8,128)(2,1)} %param.3), kind=kLoop, calls=%fused_computation.70 | loop fusion | flops 441984 | bytes 296448 | tf_op jit(solution)/shard_map/reduce_sum | solution.py:11
  7.7 0.7 convert_reduce_fusion
  8.4 1.2 %fusion.90 = bf16[4,4,24,384]{3,2,1,0:T(8,128)(2,1)S(1)} fusion(bf16[4,4,24,384]{3,2,1,0:T(8,128)(2,1)} %param.3, f32[384]{0:T(512)S(1)} %convert_reduce_fusion, f32[4,4,24]{2,1,0:T(4,128)S(1)} %add_rsqrt_fusion.3), kind=kLoop, calls=%fused_computation.77 | loop fusion | flops 1179648 | bytes 592896 | tf_op jit(solution)/shard_map/convert_element_type | solution.py:14
  10.3 0.2 pad.5.clone
  10.7 8.3 %fusion.30 = bf16[4,4,8,4,384]{4,2,3,1,0:T(8,128)(2,1)S(1)} fusion(bf16[1,3,3,3,384,384]{5,4,3,2,1,0:T(8,128)(2,1)} %param.5, bf16[4,6,1,7,2,384]{5,3,4,1,0,2:T(8,128)(2,1)S(1)} %slice.105, bf16[4,6,1,8,4,384]{5,3,4,1,0,2:T(8,128)(2,1)S(1)} %copy.116, pred[8,4]{0,1:T(4,128)(4,1)S(1)} %copy-done.1), kind=kOutput, calls=%fused_computation.21 | convolution fusion | flops 3060695040 | bytes 9203744 | tf_op jit(solution)/shard_map/conv_general_dilated | solution.py:18
  19.0 0.2 copy.117
  19.4 0.7 collective-permute-start.3
  20.1 0.7 collective-permute-start.2
  20.8 0.7 collective-permute-start.4
  21.6 0.3 fusion.93
  22.0 0.2 copy.157
  22.2 0.2 pad.7.clone
  22.6 5.7 %fusion.27 = bf16[4,4,8,4,384]{4,2,3,1,0:T(8,128)(2,1)S(1)} fusion(bf16[1,3,3,3,384,384]{5,4,3,2,1,0:T(8,128)(2,1)S(1)} %bitcast.145, bf16[4,6,1,7,2,384]{5,3,4,1,0,2:T(8,128)(2,1)S(1)} %slice.109, bf16[4,6,1,8,4,384]{5,3,4,1,0,2:T(8,128)(2,1)S(1)} %copy.123, pred[8,4]{0,1:T(4,128)(4,1)S(1)} %copy-done.1), kind=kOutput, calls=%fused_computation.20 | convolution fusion | flops 3060695040 | bytes 9203744 | tf_op jit(solution)/shard_map/conv_general_dilated | solution.py:18
  28.3 0.2 copy.124
  28.7 1.3 %collective-permute-start.5 = (bf16[4,4,24,384]{3,2,1,0:T(8,128)(2,1)S(1)}, bf16[4,4,24,384]{3,2,1,0:T(8,128)(2,1)S(1)}, u32[]{:S(2)}, u32[]{:S(2)}) collective-permute-start(bf16[4,4,24,384]{3,2,1,0:T(8,128)(2,1)S(1)} %fusion.91), channel_id=1, source_target_pairs={{8,16},{9,17},{10,18},{11,19},{12,20},{13,21},{14,22},{15,23}} | collective-permute-start | bytes 884744 | tf_op jit(solution)/shard_map/ppermute | solution.py:30
  30.0 1.5 %collective-permute-start.6 = (bf16[4,1,24,384]{3,2,1,0:T(8,128)(2,1)S(1)}, bf16[4,1,24,384]{3,2,1,0:T(8,128)(2,1)S(1)}, u32[]{:S(2)}, u32[]{:S(2)}) collective-permute-start(bf16[4,1,24,384]{3,2,1,0:T(8,128)(2,1)S(1)} %get-tuple-element.10), channel_id=1, source_target_pairs={{8,17},{9,18},{10,19},{11,20},{12,21},{13,22},{14,23}} | collective-permute-start | bytes 221192 | tf_op jit(solution)/shard_map/ppermute | solution.py:30
  31.5 1.3 %collective-permute-start.7 = (bf16[4,1,24,384]{3,2,1,0:T(8,128)(2,1)S(1)}, bf16[4,1,24,384]{3,2,1,0:T(8,128)(2,1)S(1)}, u32[]{:S(2)}, u32[]{:S(2)}) collective-permute-start(bf16[4,1,24,384]{3,2,1,0:T(8,128)(2,1)S(1)} %get-tuple-element.11), channel_id=1, source_target_pairs={{9,16},{10,17},{11,18},{12,19},{13,20},{14,21},{15,22}} | collective-permute-start | bytes 221192 | tf_op jit(solution)/shard_map/ppermute | solution.py:30
  32.8 17.8 %collective-permute-done.6 = bf16[4,1,24,384]{3,2,1,0:T(8,128)(2,1)S(1)} collective-permute-done((bf16[4,1,24,384]{3,2,1,0:T(8,128)(2,1)S(1)}, bf16[4,1,24,384]{3,2,1,0:T(8,128)(2,1)S(1)}, u32[]{:S(2)}, u32[]{:S(2)}) %collective-permute-start.6) | collective-permute-done | bytes 73760 | tf_op jit(solution)/shard_map/ppermute | solution.py:30
  50.6 3.3 %collective-permute-done.7 = bf16[4,1,24,384]{3,2,1,0:T(8,128)(2,1)S(1)} collective-permute-done((bf16[4,1,24,384]{3,2,1,0:T(8,128)(2,1)S(1)}, bf16[4,1,24,384]{3,2,1,0:T(8,128)(2,1)S(1)}, u32[]{:S(2)}, u32[]{:S(2)}) %collective-permute-start.7) | collective-permute-done | bytes 73760 | tf_op jit(solution)/shard_map/ppermute | solution.py:30
  54.1 0.3 fusion.94
  54.6 0.2 pad.9.clone
  55.1 5.7 %fusion.24 = bf16[4,4,8,4,384]{4,2,3,1,0:T(8,128)(2,1)S(1)} fusion(bf16[1,3,3,3,384,384]{5,4,3,2,1,0:T(8,128)(2,1)S(1)} %bitcast.145, bf16[4,6,1,7,2,384]{5,3,4,1,0,2:T(8,128)(2,1)S(1)} %slice.114, bf16[4,6,1,8,4,384]{5,3,4,1,0,2:T(8,128)(2,1)S(1)} %copy.130, pred[8,4]{0,1:T(4,128)(4,1)S(1)} %copy-done.1), kind=kOutput, calls=%fused_computation.19 | convolution fusion | flops 3060695040 | bytes 9203744 | tf_op jit(solution)/shard_map/conv_general_dilated | solution.py:18
  60.7 0.2 copy.131
  61.1 1.3 %collective-permute-start.8 = (bf16[4,4,24,384]{3,2,1,0:T(8,128)(2,1)S(1)}, bf16[4,4,24,384]{3,2,1,0:T(8,128)(2,1)S(1)}, u32[]{:S(2)}, u32[]{:S(2)}) collective-permute-start(bf16[4,4,24,384]{3,2,1,0:T(8,128)(2,1)S(1)} %bitcast.131), channel_id=1, source_target_pairs={{16,24},{17,25},{18,26},{19,27},{20,28},{21,29},{22,30},{23,31}} | collective-permute-start | bytes 884744 | tf_op jit(solution)/shard_map/ppermute | solution.py:30
  62.5 1.3 %collective-permute-start.12 = (bf16[4,1,24,384]{3,2,1,0:T(8,128)(2,1)S(1)}, bf16[4,1,24,384]{3,2,1,0:T(8,128)(2,1)S(1)}, u32[]{:S(2)}, u32[]{:S(2)}) collective-permute-start(bf16[4,1,24,384]{3,2,1,0:T(8,128)(2,1)S(1)} %get-tuple-element.5), channel_id=1, source_target_pairs={{16,25},{17,26},{18,27},{19,28},{20,29},{21,30},{22,31}} | collective-permute-start | bytes 221192 | tf_op jit(solution)/shard_map/ppermute | solution.py:30
  63.8 1.3 %collective-permute-start.13 = (bf16[4,1,24,384]{3,2,1,0:T(8,128)(2,1)S(1)}, bf16[4,1,24,384]{3,2,1,0:T(8,128)(2,1)S(1)}, u32[]{:S(2)}, u32[]{:S(2)}) collective-permute-start(bf16[4,1,24,384]{3,2,1,0:T(8,128)(2,1)S(1)} %get-tuple-element.6), channel_id=1, source_target_pairs={{17,24},{18,25},{19,26},{20,27},{21,28},{22,29},{23,30}} | collective-permute-start | bytes 221192 | tf_op jit(solution)/shard_map/ppermute | solution.py:30
  65.1 4.1 %collective-permute-done.12 = bf16[4,1,24,384]{3,2,1,0:T(8,128)(2,1)S(1)} collective-permute-done((bf16[4,1,24,384]{3,2,1,0:T(8,128)(2,1)S(1)}, bf16[4,1,24,384]{3,2,1,0:T(8,128)(2,1)S(1)}, u32[]{:S(2)}, u32[]{:S(2)}) %collective-permute-start.12) | collective-permute-done | bytes 73760 | tf_op jit(solution)/shard_map/ppermute | solution.py:30
  69.2 0.8 collective-permute-done.13
  70.1 0.3 fusion.52
  70.5 0.2 copy.160
  70.7 0.2 pad.13.clone
  71.1 3.0 %fusion.39 = bf16[2,4,8,4,384]{4,2,3,1,0:T(8,128)(2,1)S(1)} fusion(bf16[1,3,3,3,384,384]{5,4,3,2,1,0:T(8,128)(2,1)S(1)} %bitcast.145, bf16[4,6,1,7,2,384]{5,3,4,1,0,2:T(8,128)(2,1)S(1)} %slice.127, bf16[4,6,1,8,4,384]{5,3,4,1,0,2:T(8,128)(2,1)S(1)} %copy.144, pred[8,4]{0,1:T(4,128)(4,1)S(1)} %copy-done.1), kind=kOutput, calls=%fused_computation.24 | convolution fusion | flops 2041282560 | bytes 9007136 | tf_op jit(solution)/shard_map/conv_general_dilated | solution.py:18
  74.3 0.7 collective-permute-start.15
  75.1 0.9 collective-permute-start.16
  76.0 0.3 fusion.95
  76.3 0.2 copy.159
  76.5 0.2 pad.11.clone
  76.9 3.0 %fusion.42 = bf16[2,4,8,4,384]{4,2,3,1,0:T(8,128)(2,1)S(1)} fusion(bf16[1,3,3,3,384,384]{5,4,3,2,1,0:T(8,128)(2,1)S(1)} %bitcast.145, bf16[4,6,1,7,2,384]{5,3,4,1,0,2:T(8,128)(2,1)S(1)} %slice.122, bf16[4,6,1,8,4,384]{5,3,4,1,0,2:T(8,128)(2,1)S(1)} %copy.137, pred[8,4]{0,1:T(4,128)(4,1)S(1)} %copy-done.1), kind=kOutput, calls=%fused_computation.25 | convolution fusion | flops 2041282560 | bytes 9007136 | tf_op jit(solution)/shard_map/conv_general_dilated | solution.py:18
  80.1 1.3 %collective-permute-start.14 = (bf16[1,4,24,384]{3,2,1,0:T(8,128)(2,1)S(1)}, bf16[1,4,24,384]{3,2,1,0:T(8,128)(2,1)S(1)}, u32[]{:S(2)}, u32[]{:S(2)}) collective-permute-start(bf16[1,4,24,384]{3,2,1,0:T(8,128)(2,1)S(1)} %bitcast.143), channel_id=1, source_target_pairs={{24,16},{25,17},{26,18},{27,19},{28,20},{29,21},{30,22},{31,23}} | collective-permute-start | bytes 221192 | tf_op jit(solution)/shard_map/ppermute | solution.py:30
  81.4 0.5 slice.116
  82.6 1.3 %collective-permute-start.10 = (bf16[1,4,24,384]{3,2,1,0:T(8,128)(2,1)S(1)}, bf16[1,4,24,384]{3,2,1,0:T(8,128)(2,1)S(1)}, u32[]{:S(2)}, u32[]{:S(2)}) collective-permute-start(bf16[1,4,24,384]{3,2,1,0:T(8,128)(2,1)S(1)} %get-tuple-element.8), channel_id=1, source_target_pairs={{16,8},{17,9},{18,10},{19,11},{20,12},{21,13},{22,14},{23,15}} | collective-permute-start | bytes 221192 | tf_op jit(solution)/shard_map/ppermute | solution.py:30
  83.9 1.3 %collective-permute-start.11 = (bf16[1,4,24,384]{3,2,1,0:T(8,128)(2,1)S(1)}, bf16[1,4,24,384]{3,2,1,0:T(8,128)(2,1)S(1)}, u32[]{:S(2)}, u32[]{:S(2)}) collective-permute-start(bf16[1,4,24,384]{3,2,1,0:T(8,128)(2,1)S(1)} %get-tuple-element.7), channel_id=1, source_target_pairs={{16,0},{17,1},{18,2},{19,3},{20,4},{21,5},{22,6},{23,7}} | collective-permute-start | bytes 221192 | tf_op jit(solution)/shard_map/ppermute | solution.py:30
  85.2 6.0 %collective-permute-start.9 = (bf16[1,4,24,384]{3,2,1,0:T(8,128)(2,1)S(1)}, bf16[1,4,24,384]{3,2,1,0:T(8,128)(2,1)S(1)}, u32[]{:S(2)}, u32[]{:S(2)}) collective-permute-start(bf16[1,4,24,384]{3,2,1,0:T(8,128)(2,1)S(1)} %get-tuple-element.9), channel_id=1, source_target_pairs={{16,24},{17,25},{18,26},{19,27},{20,28},{21,29},{22,30},{23,31}} | collective-permute-start | bytes 221192 | tf_op jit(solution)/shard_map/ppermute | solution.py:30
  91.3 1.2 %collective-permute-done.9 = bf16[1,4,24,384]{3,2,1,0:T(8,128)(2,1)S(1)} collective-permute-done((bf16[1,4,24,384]{3,2,1,0:T(8,128)(2,1)S(1)}, bf16[1,4,24,384]{3,2,1,0:T(8,128)(2,1)S(1)}, u32[]{:S(2)}, u32[]{:S(2)}) %collective-permute-start.9) | collective-permute-done | bytes 73760 | tf_op jit(solution)/shard_map/ppermute | solution.py:30
  92.5 0.7 add_convert_fusion
  (70 shorter events, 3.3 us)
Async XLA Ops:
  0.9 8.7 %collective-permute-start.1 = (bf16[4,1,24,384]{3,2,1,0:T(8,128)(2,1)S(1)}, bf16[4,1,24,384]{3,2,1,0:T(8,128)(2,1)S(1)}, u32[]{:S(2)}, u32[]{:S(2)}) collective-permute-start(bf16[4,1,24,384]{3,2,1,0:T(8,128)(2,1)S(1)} %get-tuple-element.15), channel_id=1, source_target_pairs={{1,0},{2,1},{3,2},{4,3},{5,4},{6,5},{7,6},{9,8},{10,9},{11,10},{12... | collective-permute-start | bytes 221192 | tf_op jit(solution)/shard_map/ppermute | solution.py:60
  3.5 6.2 %collective-permute-start = (bf16[4,1,24,384]{3,2,1,0:T(8,128)(2,1)S(1)}, bf16[4,1,24,384]{3,2,1,0:T(8,128)(2,1)S(1)}, u32[]{:S(2)}, u32[]{:S(2)}) collective-permute-start(bf16[4,1,24,384]{3,2,1,0:T(8,128)(2,1)S(1)} %get-tuple-element.14), channel_id=1, source_target_pairs={{0,1},{1,2},{2,3},{3,4},{4,5},{5,6},{6,7},{8,9},{9,10},{10,11},{11... | collective-permute-start | bytes 221192 | tf_op jit(solution)/shard_map/ppermute | solution.py:59
  10.1 0.7 copy-start.1
  10.6 12.0 %slice-start = ((s8[7962624]{0:T(1024)(128)(4,1)}), s8[4194304]{0:T(1024)(128)(4,1)S(1)}, s32[]{:S(2)}) async-start(s8[7962624]{0:T(1024)(128)(4,1)} %bitcast.144), calls=%async_computation | async-start | bytes 8388608
  10.7 11.9 %slice-start.1 = ((s8[7962624]{0:T(1024)(128)(4,1)}), s8[3768320]{0:T(1024)(128)(4,1)S(1)}, s32[]{:S(2)}) async-start(s8[7962624]{0:T(1024)(128)(4,1)} %bitcast.144), calls=%async_computation.1 | async-start | bytes 7536640
  19.4 2.1 %collective-permute-start.3 = (bf16[4,4,24,384]{3,2,1,0:T(8,128)(2,1)S(1)}, bf16[4,4,24,384]{3,2,1,0:T(8,128)(2,1)S(1)}, u32[]{:S(2)}, u32[]{:S(2)}) collective-permute-start(bf16[4,4,24,384]{3,2,1,0:T(8,128)(2,1)S(1)} %bitcast.129), channel_id=1, source_target_pairs={{0,8},{1,9},{2,10},{3,11},{4,12},{5,13},{6,14},{7,15}} | collective-permute-start | bytes 884744 | tf_op jit(solution)/shard_map/ppermute | solution.py:30
  20.1 1.3 %collective-permute-start.2 = (bf16[4,1,24,384]{3,2,1,0:T(8,128)(2,1)S(1)}, bf16[4,1,24,384]{3,2,1,0:T(8,128)(2,1)S(1)}, u32[]{:S(2)}, u32[]{:S(2)}) collective-permute-start(bf16[4,1,24,384]{3,2,1,0:T(8,128)(2,1)S(1)} %get-tuple-element.12), channel_id=1, source_target_pairs={{0,9},{1,10},{2,11},{3,12},{4,13},{5,14},{6,15}} | collective-permute-start | bytes 221192 | tf_op jit(solution)/shard_map/ppermute | solution.py:30
  20.8 0.7 collective-permute-start.4
  22.6 6.0 %copy-start = (bf16[4,4,24,384]{3,2,1,0:T(8,128)(2,1)S(1)}, bf16[4,4,24,384]{3,2,1,0:T(8,128)(2,1)}, u32[]{:S(2)}) copy-start(bf16[4,4,24,384]{3,2,1,0:T(8,128)(2,1)} %param.3) | copy-start | bytes 884740
  28.7 25.2 %collective-permute-start.5 = (bf16[4,4,24,384]{3,2,1,0:T(8,128)(2,1)S(1)}, bf16[4,4,24,384]{3,2,1,0:T(8,128)(2,1)S(1)}, u32[]{:S(2)}, u32[]{:S(2)}) collective-permute-start(bf16[4,4,24,384]{3,2,1,0:T(8,128)(2,1)S(1)} %fusion.91), channel_id=1, source_target_pairs={{8,16},{9,17},{10,18},{11,19},{12,20},{13,21},{14,22},{15,23}} | collective-permute-start | bytes 884744 | tf_op jit(solution)/shard_map/ppermute | solution.py:30
  30.0 20.6 %collective-permute-start.6 = (bf16[4,1,24,384]{3,2,1,0:T(8,128)(2,1)S(1)}, bf16[4,1,24,384]{3,2,1,0:T(8,128)(2,1)S(1)}, u32[]{:S(2)}, u32[]{:S(2)}) collective-permute-start(bf16[4,1,24,384]{3,2,1,0:T(8,128)(2,1)S(1)} %get-tuple-element.10), channel_id=1, source_target_pairs={{8,17},{9,18},{10,19},{11,20},{12,21},{13,22},{14,23}} | collective-permute-start | bytes 221192 | tf_op jit(solution)/shard_map/ppermute | solution.py:30
  31.5 22.4 %collective-permute-start.7 = (bf16[4,1,24,384]{3,2,1,0:T(8,128)(2,1)S(1)}, bf16[4,1,24,384]{3,2,1,0:T(8,128)(2,1)S(1)}, u32[]{:S(2)}, u32[]{:S(2)}) collective-permute-start(bf16[4,1,24,384]{3,2,1,0:T(8,128)(2,1)S(1)} %get-tuple-element.11), channel_id=1, source_target_pairs={{9,16},{10,17},{11,18},{12,19},{13,20},{14,21},{15,22}} | collective-permute-start | bytes 221192 | tf_op jit(solution)/shard_map/ppermute | solution.py:30
  61.1 8.9 %collective-permute-start.8 = (bf16[4,4,24,384]{3,2,1,0:T(8,128)(2,1)S(1)}, bf16[4,4,24,384]{3,2,1,0:T(8,128)(2,1)S(1)}, u32[]{:S(2)}, u32[]{:S(2)}) collective-permute-start(bf16[4,4,24,384]{3,2,1,0:T(8,128)(2,1)S(1)} %bitcast.131), channel_id=1, source_target_pairs={{16,24},{17,25},{18,26},{19,27},{20,28},{21,29},{22,30},{23,31}} | collective-permute-start | bytes 884744 | tf_op jit(solution)/shard_map/ppermute | solution.py:30
  62.5 6.7 %collective-permute-start.12 = (bf16[4,1,24,384]{3,2,1,0:T(8,128)(2,1)S(1)}, bf16[4,1,24,384]{3,2,1,0:T(8,128)(2,1)S(1)}, u32[]{:S(2)}, u32[]{:S(2)}) collective-permute-start(bf16[4,1,24,384]{3,2,1,0:T(8,128)(2,1)S(1)} %get-tuple-element.5), channel_id=1, source_target_pairs={{16,25},{17,26},{18,27},{19,28},{20,29},{21,30},{22,31}} | collective-permute-start | bytes 221192 | tf_op jit(solution)/shard_map/ppermute | solution.py:30
  63.8 6.2 %collective-permute-start.13 = (bf16[4,1,24,384]{3,2,1,0:T(8,128)(2,1)S(1)}, bf16[4,1,24,384]{3,2,1,0:T(8,128)(2,1)S(1)}, u32[]{:S(2)}, u32[]{:S(2)}) collective-permute-start(bf16[4,1,24,384]{3,2,1,0:T(8,128)(2,1)S(1)} %get-tuple-element.6), channel_id=1, source_target_pairs={{17,24},{18,25},{19,26},{20,27},{21,28},{22,29},{23,30}} | collective-permute-start | bytes 221192 | tf_op jit(solution)/shard_map/ppermute | solution.py:30
  74.3 10.9 %collective-permute-start.15 = (bf16[1,4,24,384]{3,2,1,0:T(8,128)(2,1)S(1)}, bf16[1,4,24,384]{3,2,1,0:T(8,128)(2,1)S(1)}, u32[]{:S(2)}, u32[]{:S(2)}) collective-permute-start(bf16[1,4,24,384]{3,2,1,0:T(8,128)(2,1)S(1)} %bitcast.142), channel_id=1, source_target_pairs={{24,8},{25,9},{26,10},{27,11},{28,12},{29,13},{30,14},{31,15}} | collective-permute-start | bytes 221192 | tf_op jit(solution)/shard_map/ppermute | solution.py:30
  75.1 16.2 %collective-permute-start.16 = (bf16[1,4,24,384]{3,2,1,0:T(8,128)(2,1)S(1)}, bf16[1,4,24,384]{3,2,1,0:T(8,128)(2,1)S(1)}, u32[]{:S(2)}, u32[]{:S(2)}) collective-permute-start(bf16[1,4,24,384]{3,2,1,0:T(8,128)(2,1)S(1)} %bitcast.141), channel_id=1, source_target_pairs={{24,0},{25,1},{26,2},{27,3},{28,4},{29,5},{30,6},{31,7}} | collective-permute-start | bytes 221192 | tf_op jit(solution)/shard_map/ppermute | solution.py:30
  80.1 11.2 %collective-permute-start.14 = (bf16[1,4,24,384]{3,2,1,0:T(8,128)(2,1)S(1)}, bf16[1,4,24,384]{3,2,1,0:T(8,128)(2,1)S(1)}, u32[]{:S(2)}, u32[]{:S(2)}) collective-permute-start(bf16[1,4,24,384]{3,2,1,0:T(8,128)(2,1)S(1)} %bitcast.143), channel_id=1, source_target_pairs={{24,16},{25,17},{26,18},{27,19},{28,20},{29,21},{30,22},{31,23}} | collective-permute-start | bytes 221192 | tf_op jit(solution)/shard_map/ppermute | solution.py:30
  82.6 8.7 %collective-permute-start.10 = (bf16[1,4,24,384]{3,2,1,0:T(8,128)(2,1)S(1)}, bf16[1,4,24,384]{3,2,1,0:T(8,128)(2,1)S(1)}, u32[]{:S(2)}, u32[]{:S(2)}) collective-permute-start(bf16[1,4,24,384]{3,2,1,0:T(8,128)(2,1)S(1)} %get-tuple-element.8), channel_id=1, source_target_pairs={{16,8},{17,9},{18,10},{19,11},{20,12},{21,13},{22,14},{23,15}} | collective-permute-start | bytes 221192 | tf_op jit(solution)/shard_map/ppermute | solution.py:30
  83.9 7.4 %collective-permute-start.11 = (bf16[1,4,24,384]{3,2,1,0:T(8,128)(2,1)S(1)}, bf16[1,4,24,384]{3,2,1,0:T(8,128)(2,1)S(1)}, u32[]{:S(2)}, u32[]{:S(2)}) collective-permute-start(bf16[1,4,24,384]{3,2,1,0:T(8,128)(2,1)S(1)} %get-tuple-element.7), channel_id=1, source_target_pairs={{16,0},{17,1},{18,2},{19,3},{20,4},{21,5},{22,6},{23,7}} | collective-permute-start | bytes 221192 | tf_op jit(solution)/shard_map/ppermute | solution.py:30
  85.2 7.3 %collective-permute-start.9 = (bf16[1,4,24,384]{3,2,1,0:T(8,128)(2,1)S(1)}, bf16[1,4,24,384]{3,2,1,0:T(8,128)(2,1)S(1)}, u32[]{:S(2)}, u32[]{:S(2)}) collective-permute-start(bf16[1,4,24,384]{3,2,1,0:T(8,128)(2,1)S(1)} %get-tuple-element.9), channel_id=1, source_target_pairs={{16,24},{17,25},{18,26},{19,27},{20,28},{21,29},{22,30},{23,31}} | collective-permute-start | bytes 221192 | tf_op jit(solution)/shard_map/ppermute | solution.py:30

commit v12 on v9

--- a/solution.py
+++ b/solution.py
@@ -63,18 +63,24 @@
     last_stage = segment_count - 1
 
     for stage in range(segment_count):
-        window = jnp.concatenate([top, current, bottom], axis=1)
+        pieces = [top, current, bottom] if stage else [top, features, bottom]
+        window = jnp.concatenate(
+            [activate(piece, gain_row) for piece in pieces]
+            if stage == 0
+            else [activate(jnp.concatenate(pieces, axis=1), gain_row)],
+            axis=1,
+        )
         odd = stage % 2 == 1
         final = stage == last_stage
 
         def compute(window, skip, odd=odd, final=final):
-            convolved = causal_conv(activate(window, gain_row), kernel).astype(jnp.bfloat16)
+            convolved = causal_conv(window, kernel).astype(jnp.bfloat16)
             if odd and not final:
                 convolved = (skip.astype(jnp.float32) + convolved).astype(jnp.bfloat16)
             return convolved
 
         if final:
-            activated = jnp.pad(activate(window, gain_row), ((2, 0), (0, 0), (0, 0), (0, 0)))
+            activated = jnp.pad(window, ((2, 0), (0, 0), (0, 0), (0, 0)))
             split = (segment_count // 2) * group
             branch = None
             for low, high in ((0, split), (split, frame_count)):

time: 91.9 us -> 90.2 us (0.982); the launches traced: 91.4 us -> 88.6 us
  waiting for transfers between devices: 31.7 us -> 28.5 us
    ppermute x1, waiting for transfers between devices: 3.04 us -> 0.01 us  [local(): bottom = lax.ppermute(features[:, :1], 'rows', down)]
    unnamed x19 -> x18, local copies, waits for them, and re-layouts: 1.96 us -> 1.02 us
    slice x0 -> x1, local copies, waits for them, and re-layouts: none -> 0.94 us  [local(): top = lax.ppermute(features[:, height - 1:], 'rows', up)]
    convert_element_type x5 -> x6, other arithmetic: 2.64 us -> 2.72 us  [activate(): return jax.nn.silu(widened * lax.rsqrt(mean_square + 1e-06) * gain_row.as...]
  transfers between devices with their start and end apart: 17 -> 17, of which waited for: 4 -> 3; matrix products, arithmetic and copies ran while one was open for 10% -> 13% of each run, Pallas kernels for 0% -> 0%
where the time goes in v12:
time: 90.2 us; the launch traced here: 88.6 us
  waiting for transfers between devices  28.5 us (32%)
  matrix products  25.6 us (28%)
  starting transfers between devices  22.3 us (25%)
  other arithmetic  6.04 us (7%)
  local copies, waits for them, and re-layouts  5.36 us (6%)
    ppermute x15, waiting for transfers between devices, send(): return lax.ppermute(value, BOTH, pairs)  28.5 us
    conv_general_dilated x5, matrix products, causal_conv(): lax.conv_general_dilated(window[None], kernel, window_strides=(1, 1, 1),...  25.6 us
    ppermute x15, starting transfers between devices, send(): return lax.ppermute(value, BOTH, pairs)  16.7 us
    ppermute x1, starting transfers between devices, local(): top = lax.ppermute(features[:, height - 1:], 'rows', up)  3.02 us
    convert_element_type x6, other arithmetic, activate(): return jax.nn.silu(widened * lax.rsqrt(mean_square + 1e-06) * gain_row.as...  2.72 us
    ppermute x1, starting transfers between devices, local(): bottom = lax.ppermute(features[:, :1], 'rows', down)  2.58 us
  transfers between devices with their start and end apart: 17, of which 3 were waited for; matrix products, arithmetic and copies ran while one was open for 13% of the time, Pallas kernels for 0%

profile of v12, /device:TPU:17, one launch (start us, length us, event | category | flops | bytes accessed | tf_op | source)
XLA Modules:
  0.0 88.6 jit_solution(6072501790947698350)
XLA Ops:
  0.0 0.9 %fusion.139 = (bf16[4,1,24,384]{3,2,1,0:T(8,128)(2,1)S(1)}, bf16[4,1,24,384]{3,2,1,0:T(8,128)(2,1)S(1)}) fusion(bf16[4,4,24,384]{3,2,1,0:T(8,128)(2,1)} %param.3), kind=kLoop, calls=%fused_computation.148 | loop fusion | bytes 294912 | tf_op jit(solution)/shard_map/slice | solution.py:59
  0.9 2.6 %collective-permute-start.1 = (bf16[4,1,24,384]{3,2,1,0:T(8,128)(2,1)S(1)}, bf16[4,1,24,384]{3,2,1,0:T(8,128)(2,1)S(1)}, u32[]{:S(2)}, u32[]{:S(2)}) collective-permute-start(bf16[4,1,24,384]{3,2,1,0:T(8,128)(2,1)S(1)} %get-tuple-element.15), channel_id=1, source_target_pairs={{1,0},{2,1},{3,2},{4,3},{5,4},{6,5},{7,6},{9,8},{10,9},{11,10},{12... | collective-permute-start | bytes 221192 | tf_op jit(solution)/shard_map/ppermute | solution.py:60
  3.5 3.0 %collective-permute-start = (bf16[4,1,24,384]{3,2,1,0:T(8,128)(2,1)S(1)}, bf16[4,1,24,384]{3,2,1,0:T(8,128)(2,1)S(1)}, u32[]{:S(2)}, u32[]{:S(2)}) collective-permute-start(bf16[4,1,24,384]{3,2,1,0:T(8,128)(2,1)S(1)} %get-tuple-element.14), channel_id=1, source_target_pairs={{0,1},{1,2},{2,3},{3,4},{4,5},{5,6},{6,7},{8,9},{9,10},{10,11},{11... | collective-permute-start | bytes 221192 | tf_op jit(solution)/shard_map/ppermute | solution.py:59
  6.6 1.1 %fusion.83 = f32[4,4,24]{2,1,0:T(4,128)S(1)} fusion(bf16[4,4,24,384]{3,2,1,0:T(8,128)(2,1)} %param.3), kind=kLoop, calls=%fused_computation.70 | loop fusion | flops 441984 | bytes 296448 | tf_op jit(solution)/shard_map/reduce_sum | solution.py:11
  7.7 0.7 convert_reduce_fusion
  8.4 1.2 %fusion.90 = bf16[4,4,24,384]{3,2,1,0:T(8,128)(2,1)S(1)} fusion(bf16[4,4,24,384]{3,2,1,0:T(8,128)(2,1)} %param.3, f32[384]{0:T(512)S(1)} %convert_reduce_fusion, f32[4,4,24]{2,1,0:T(4,128)S(1)} %add_rsqrt_fusion.3), kind=kLoop, calls=%fused_computation.77 | loop fusion | flops 1179648 | bytes 592896 | tf_op jit(solution)/shard_map/convert_element_type | solution.py:14
  9.8 0.2 fusion.108
  10.1 0.2 copy.156
  10.3 0.2 pad.5.clone
  10.7 8.3 %fusion.30 = bf16[4,4,8,4,384]{4,2,3,1,0:T(8,128)(2,1)S(1)} fusion(bf16[1,3,3,3,384,384]{5,4,3,2,1,0:T(8,128)(2,1)} %param.5, bf16[4,6,1,7,2,384]{5,3,4,1,0,2:T(8,128)(2,1)S(1)} %slice.101, bf16[4,6,1,8,4,384]{5,3,4,1,0,2:T(8,128)(2,1)S(1)} %copy.116, pred[8,4]{0,1:T(4,128)(4,1)S(1)} %copy-done.1), kind=kOutput, calls=%fused_computation.21 | convolution fusion | flops 3060695040 | bytes 9203744 | tf_op jit(solution)/shard_map/conv_general_dilated | solution.py:18
  19.0 0.2 copy.117
  19.4 0.7 collective-permute-start.3
  20.1 0.7 collective-permute-start.2
  20.8 0.7 collective-permute-start.4
  21.6 0.3 fusion.93
  22.0 0.2 copy.157
  22.2 0.2 pad.7.clone
  22.6 5.7 %fusion.27 = bf16[4,4,8,4,384]{4,2,3,1,0:T(8,128)(2,1)S(1)} fusion(bf16[1,3,3,3,384,384]{5,4,3,2,1,0:T(8,128)(2,1)S(1)} %bitcast.144, bf16[4,6,1,7,2,384]{5,3,4,1,0,2:T(8,128)(2,1)S(1)} %slice.105, bf16[4,6,1,8,4,384]{5,3,4,1,0,2:T(8,128)(2,1)S(1)} %copy.123, pred[8,4]{0,1:T(4,128)(4,1)S(1)} %copy-done.1), kind=kOutput, calls=%fused_computation.20 | convolution fusion | flops 3060695040 | bytes 9203744 | tf_op jit(solution)/shard_map/conv_general_dilated | solution.py:18
  28.3 0.2 copy.124
  28.7 1.3 %collective-permute-start.5 = (bf16[4,4,24,384]{3,2,1,0:T(8,128)(2,1)S(1)}, bf16[4,4,24,384]{3,2,1,0:T(8,128)(2,1)S(1)}, u32[]{:S(2)}, u32[]{:S(2)}) collective-permute-start(bf16[4,4,24,384]{3,2,1,0:T(8,128)(2,1)S(1)} %fusion.91), channel_id=1, source_target_pairs={{8,16},{9,17},{10,18},{11,19},{12,20},{13,21},{14,22},{15,23}} | collective-permute-start | bytes 884744 | tf_op jit(solution)/shard_map/ppermute | solution.py:30
  30.0 1.5 %collective-permute-start.10 = (bf16[4,1,24,384]{3,2,1,0:T(8,128)(2,1)S(1)}, bf16[4,1,24,384]{3,2,1,0:T(8,128)(2,1)S(1)}, u32[]{:S(2)}, u32[]{:S(2)}) collective-permute-start(bf16[4,1,24,384]{3,2,1,0:T(8,128)(2,1)S(1)} %get-tuple-element.8), channel_id=1, source_target_pairs={{9,16},{10,17},{11,18},{12,19},{13,20},{14,21},{15,22}} | collective-permute-start | bytes 221192 | tf_op jit(solution)/shard_map/ppermute | solution.py:30
  31.5 1.3 %collective-permute-start.9 = (bf16[4,1,24,384]{3,2,1,0:T(8,128)(2,1)S(1)}, bf16[4,1,24,384]{3,2,1,0:T(8,128)(2,1)S(1)}, u32[]{:S(2)}, u32[]{:S(2)}) collective-permute-start(bf16[4,1,24,384]{3,2,1,0:T(8,128)(2,1)S(1)} %get-tuple-element.7), channel_id=1, source_target_pairs={{8,17},{9,18},{10,19},{11,20},{12,21},{13,22},{14,23}} | collective-permute-start | bytes 221192 | tf_op jit(solution)/shard_map/ppermute | solution.py:30
  32.8 19.5 %collective-permute-done.10 = bf16[4,1,24,384]{3,2,1,0:T(8,128)(2,1)S(1)} collective-permute-done((bf16[4,1,24,384]{3,2,1,0:T(8,128)(2,1)S(1)}, bf16[4,1,24,384]{3,2,1,0:T(8,128)(2,1)S(1)}, u32[]{:S(2)}, u32[]{:S(2)}) %collective-permute-start.10) | collective-permute-done | bytes 73760 | tf_op jit(solution)/shard_map/ppermute | solution.py:30
  52.5 0.3 fusion.94
  52.9 0.2 copy.158
  53.1 0.2 pad.9.clone
  53.5 5.7 %fusion.24 = bf16[4,4,8,4,384]{4,2,3,1,0:T(8,128)(2,1)S(1)} fusion(bf16[1,3,3,3,384,384]{5,4,3,2,1,0:T(8,128)(2,1)S(1)} %bitcast.144, bf16[4,6,1,7,2,384]{5,3,4,1,0,2:T(8,128)(2,1)S(1)} %slice.113, bf16[4,6,1,8,4,384]{5,3,4,1,0,2:T(8,128)(2,1)S(1)} %copy.130, pred[8,4]{0,1:T(4,128)(4,1)S(1)} %copy-done.1), kind=kOutput, calls=%fused_computation.19 | convolution fusion | flops 3060695040 | bytes 9203744 | tf_op jit(solution)/shard_map/conv_general_dilated | solution.py:18
  59.2 0.2 copy.131
  59.5 1.3 %collective-permute-start.12 = (bf16[4,4,24,384]{3,2,1,0:T(8,128)(2,1)S(1)}, bf16[4,4,24,384]{3,2,1,0:T(8,128)(2,1)S(1)}, u32[]{:S(2)}, u32[]{:S(2)}) collective-permute-start(bf16[4,4,24,384]{3,2,1,0:T(8,128)(2,1)S(1)} %bitcast.128), channel_id=1, source_target_pairs={{16,24},{17,25},{18,26},{19,27},{20,28},{21,29},{22,30},{23,31}} | collective-permute-start | bytes 884744 | tf_op jit(solution)/shard_map/ppermute | solution.py:30
  60.9 1.3 %collective-permute-start.11 = (bf16[4,1,24,384]{3,2,1,0:T(8,128)(2,1)S(1)}, bf16[4,1,24,384]{3,2,1,0:T(8,128)(2,1)S(1)}, u32[]{:S(2)}, u32[]{:S(2)}) collective-permute-start(bf16[4,1,24,384]{3,2,1,0:T(8,128)(2,1)S(1)} %get-tuple-element.5), channel_id=1, source_target_pairs={{16,25},{17,26},{18,27},{19,28},{20,29},{21,30},{22,31}} | collective-permute-start | bytes 221192 | tf_op jit(solution)/shard_map/ppermute | solution.py:30
  62.2 1.3 %collective-permute-start.13 = (bf16[4,1,24,384]{3,2,1,0:T(8,128)(2,1)S(1)}, bf16[4,1,24,384]{3,2,1,0:T(8,128)(2,1)S(1)}, u32[]{:S(2)}, u32[]{:S(2)}) collective-permute-start(bf16[4,1,24,384]{3,2,1,0:T(8,128)(2,1)S(1)} %get-tuple-element.6), channel_id=1, source_target_pairs={{17,24},{18,25},{19,26},{20,27},{21,28},{22,29},{23,30}} | collective-permute-start | bytes 221192 | tf_op jit(solution)/shard_map/ppermute | solution.py:30
  63.5 1.3 %collective-permute-start.6 = (bf16[1,4,24,384]{3,2,1,0:T(8,128)(2,1)S(1)}, bf16[1,4,24,384]{3,2,1,0:T(8,128)(2,1)S(1)}, u32[]{:S(2)}, u32[]{:S(2)}) collective-permute-start(bf16[1,4,24,384]{3,2,1,0:T(8,128)(2,1)S(1)} %get-tuple-element.11), channel_id=1, source_target_pairs={{16,24},{17,25},{18,26},{19,27},{20,28},{21,29},{22,30},{23,31}} | collective-permute-start | bytes 221192 | tf_op jit(solution)/shard_map/ppermute | solution.py:30
  64.8 1.3 %collective-permute-start.7 = (bf16[1,4,24,384]{3,2,1,0:T(8,128)(2,1)S(1)}, bf16[1,4,24,384]{3,2,1,0:T(8,128)(2,1)S(1)}, u32[]{:S(2)}, u32[]{:S(2)}) collective-permute-start(bf16[1,4,24,384]{3,2,1,0:T(8,128)(2,1)S(1)} %get-tuple-element.10), channel_id=1, source_target_pairs={{16,8},{17,9},{18,10},{19,11},{20,12},{21,13},{22,14},{23,15}} | collective-permute-start | bytes 221192 | tf_op jit(solution)/shard_map/ppermute | solution.py:30
  66.1 3.1 %collective-permute-done.11 = bf16[4,1,24,384]{3,2,1,0:T(8,128)(2,1)S(1)} collective-permute-done((bf16[4,1,24,384]{3,2,1,0:T(8,128)(2,1)S(1)}, bf16[4,1,24,384]{3,2,1,0:T(8,128)(2,1)S(1)}, u32[]{:S(2)}, u32[]{:S(2)}) %collective-permute-start.11) | collective-permute-done | bytes 73760 | tf_op jit(solution)/shard_map/ppermute | solution.py:30
  69.2 1.3 %collective-permute-start.8 = (bf16[1,4,24,384]{3,2,1,0:T(8,128)(2,1)S(1)}, bf16[1,4,24,384]{3,2,1,0:T(8,128)(2,1)S(1)}, u32[]{:S(2)}, u32[]{:S(2)}) collective-permute-start(bf16[1,4,24,384]{3,2,1,0:T(8,128)(2,1)S(1)} %get-tuple-element.9), channel_id=1, source_target_pairs={{16,0},{17,1},{18,2},{19,3},{20,4},{21,5},{22,6},{23,7}} | collective-permute-start | bytes 221192 | tf_op jit(solution)/shard_map/ppermute | solution.py:30
  70.7 0.3 fusion.52
  71.1 0.2 copy.160
  71.3 0.2 pad.13.clone
  71.7 3.0 %fusion.39 = bf16[2,4,8,4,384]{4,2,3,1,0:T(8,128)(2,1)S(1)} fusion(bf16[1,3,3,3,384,384]{5,4,3,2,1,0:T(8,128)(2,1)S(1)} %bitcast.144, bf16[4,6,1,7,2,384]{5,3,4,1,0,2:T(8,128)(2,1)S(1)} %slice.122, bf16[4,6,1,8,4,384]{5,3,4,1,0,2:T(8,128)(2,1)S(1)} %copy.144, pred[8,4]{0,1:T(4,128)(4,1)S(1)} %copy-done.1), kind=kOutput, calls=%fused_computation.24 | convolution fusion | flops 2041282560 | bytes 9007136 | tf_op jit(solution)/shard_map/conv_general_dilated | solution.py:18
  74.8 0.9 collective-permute-start.15
  75.8 0.7 collective-permute-start.16
  76.5 0.3 fusion.95
  76.9 0.2 copy.159
  77.0 0.2 pad.11.clone
  77.5 3.0 %fusion.42 = bf16[2,4,8,4,384]{4,2,3,1,0:T(8,128)(2,1)S(1)} fusion(bf16[1,3,3,3,384,384]{5,4,3,2,1,0:T(8,128)(2,1)S(1)} %bitcast.144, bf16[4,6,1,7,2,384]{5,3,4,1,0,2:T(8,128)(2,1)S(1)} %slice.117, bf16[4,6,1,8,4,384]{5,3,4,1,0,2:T(8,128)(2,1)S(1)} %copy.137, pred[8,4]{0,1:T(4,128)(4,1)S(1)} %copy-done.1), kind=kOutput, calls=%fused_computation.25 | convolution fusion | flops 2041282560 | bytes 9007136 | tf_op jit(solution)/shard_map/conv_general_dilated | solution.py:18
  80.6 1.3 %collective-permute-start.14 = (bf16[1,4,24,384]{3,2,1,0:T(8,128)(2,1)S(1)}, bf16[1,4,24,384]{3,2,1,0:T(8,128)(2,1)S(1)}, u32[]{:S(2)}, u32[]{:S(2)}) collective-permute-start(bf16[1,4,24,384]{3,2,1,0:T(8,128)(2,1)S(1)} %bitcast.142), channel_id=1, source_target_pairs={{24,16},{25,17},{26,18},{27,19},{28,20},{29,21},{30,22},{31,23}} | collective-permute-start | bytes 221192 | tf_op jit(solution)/shard_map/ppermute | solution.py:30
  82.1 5.9 %collective-permute-done.14 = bf16[1,4,24,384]{3,2,1,0:T(8,128)(2,1)S(1)} collective-permute-done((bf16[1,4,24,384]{3,2,1,0:T(8,128)(2,1)S(1)}, bf16[1,4,24,384]{3,2,1,0:T(8,128)(2,1)S(1)}, u32[]{:S(2)}, u32[]{:S(2)}) %collective-permute-start.14) | collective-permute-done | bytes 73760 | tf_op jit(solution)/shard_map/ppermute | solution.py:30
  87.9 0.7 add_convert_fusion
  (69 shorter events, 2.8 us)
Async XLA Ops:
  0.9 8.7 %collective-permute-start.1 = (bf16[4,1,24,384]{3,2,1,0:T(8,128)(2,1)S(1)}, bf16[4,1,24,384]{3,2,1,0:T(8,128)(2,1)S(1)}, u32[]{:S(2)}, u32[]{:S(2)}) collective-permute-start(bf16[4,1,24,384]{3,2,1,0:T(8,128)(2,1)S(1)} %get-tuple-element.15), channel_id=1, source_target_pairs={{1,0},{2,1},{3,2},{4,3},{5,4},{6,5},{7,6},{9,8},{10,9},{11,10},{12... | collective-permute-start | bytes 221192 | tf_op jit(solution)/shard_map/ppermute | solution.py:60
  3.5 6.2 %collective-permute-start = (bf16[4,1,24,384]{3,2,1,0:T(8,128)(2,1)S(1)}, bf16[4,1,24,384]{3,2,1,0:T(8,128)(2,1)S(1)}, u32[]{:S(2)}, u32[]{:S(2)}) collective-permute-start(bf16[4,1,24,384]{3,2,1,0:T(8,128)(2,1)S(1)} %get-tuple-element.14), channel_id=1, source_target_pairs={{0,1},{1,2},{2,3},{3,4},{4,5},{5,6},{6,7},{8,9},{9,10},{10,11},{11... | collective-permute-start | bytes 221192 | tf_op jit(solution)/shard_map/ppermute | solution.py:59
  10.1 0.7 copy-start.1
  10.6 12.0 %slice-start = ((s8[7962624]{0:T(1024)(128)(4,1)}), s8[4194304]{0:T(1024)(128)(4,1)S(1)}, s32[]{:S(2)}) async-start(s8[7962624]{0:T(1024)(128)(4,1)} %bitcast.143), calls=%async_computation | async-start | bytes 8388608
  10.7 11.9 %slice-start.1 = ((s8[7962624]{0:T(1024)(128)(4,1)}), s8[3768320]{0:T(1024)(128)(4,1)S(1)}, s32[]{:S(2)}) async-start(s8[7962624]{0:T(1024)(128)(4,1)} %bitcast.143), calls=%async_computation.1 | async-start | bytes 7536640
  19.4 2.1 %collective-permute-start.3 = (bf16[4,4,24,384]{3,2,1,0:T(8,128)(2,1)S(1)}, bf16[4,4,24,384]{3,2,1,0:T(8,128)(2,1)S(1)}, u32[]{:S(2)}, u32[]{:S(2)}) collective-permute-start(bf16[4,4,24,384]{3,2,1,0:T(8,128)(2,1)S(1)} %bitcast.130), channel_id=1, source_target_pairs={{0,8},{1,9},{2,10},{3,11},{4,12},{5,13},{6,14},{7,15}} | collective-permute-start | bytes 884744 | tf_op jit(solution)/shard_map/ppermute | solution.py:30
  20.1 1.3 %collective-permute-start.2 = (bf16[4,1,24,384]{3,2,1,0:T(8,128)(2,1)S(1)}, bf16[4,1,24,384]{3,2,1,0:T(8,128)(2,1)S(1)}, u32[]{:S(2)}, u32[]{:S(2)}) collective-permute-start(bf16[4,1,24,384]{3,2,1,0:T(8,128)(2,1)S(1)} %get-tuple-element.12), channel_id=1, source_target_pairs={{0,9},{1,10},{2,11},{3,12},{4,13},{5,14},{6,15}} | collective-permute-start | bytes 221192 | tf_op jit(solution)/shard_map/ppermute | solution.py:30
  20.8 0.7 collective-permute-start.4
  22.6 6.0 %copy-start = (bf16[4,4,24,384]{3,2,1,0:T(8,128)(2,1)S(1)}, bf16[4,4,24,384]{3,2,1,0:T(8,128)(2,1)}, u32[]{:S(2)}) copy-start(bf16[4,4,24,384]{3,2,1,0:T(8,128)(2,1)} %param.3) | copy-start | bytes 884740
  28.7 23.7 %collective-permute-start.5 = (bf16[4,4,24,384]{3,2,1,0:T(8,128)(2,1)S(1)}, bf16[4,4,24,384]{3,2,1,0:T(8,128)(2,1)S(1)}, u32[]{:S(2)}, u32[]{:S(2)}) collective-permute-start(bf16[4,4,24,384]{3,2,1,0:T(8,128)(2,1)S(1)} %fusion.91), channel_id=1, source_target_pairs={{8,16},{9,17},{10,18},{11,19},{12,20},{13,21},{14,22},{15,23}} | collective-permute-start | bytes 884744 | tf_op jit(solution)/shard_map/ppermute | solution.py:30
  30.0 22.3 %collective-permute-start.10 = (bf16[4,1,24,384]{3,2,1,0:T(8,128)(2,1)S(1)}, bf16[4,1,24,384]{3,2,1,0:T(8,128)(2,1)S(1)}, u32[]{:S(2)}, u32[]{:S(2)}) collective-permute-start(bf16[4,1,24,384]{3,2,1,0:T(8,128)(2,1)S(1)} %get-tuple-element.8), channel_id=1, source_target_pairs={{9,16},{10,17},{11,18},{12,19},{13,20},{14,21},{15,22}} | collective-permute-start | bytes 221192 | tf_op jit(solution)/shard_map/ppermute | solution.py:30
  31.5 20.8 %collective-permute-start.9 = (bf16[4,1,24,384]{3,2,1,0:T(8,128)(2,1)S(1)}, bf16[4,1,24,384]{3,2,1,0:T(8,128)(2,1)S(1)}, u32[]{:S(2)}, u32[]{:S(2)}) collective-permute-start(bf16[4,1,24,384]{3,2,1,0:T(8,128)(2,1)S(1)} %get-tuple-element.7), channel_id=1, source_target_pairs={{8,17},{9,18},{10,19},{11,20},{12,21},{13,22},{14,23}} | collective-permute-start | bytes 221192 | tf_op jit(solution)/shard_map/ppermute | solution.py:30
  59.5 11.0 %collective-permute-start.12 = (bf16[4,4,24,384]{3,2,1,0:T(8,128)(2,1)S(1)}, bf16[4,4,24,384]{3,2,1,0:T(8,128)(2,1)S(1)}, u32[]{:S(2)}, u32[]{:S(2)}) collective-permute-start(bf16[4,4,24,384]{3,2,1,0:T(8,128)(2,1)S(1)} %bitcast.128), channel_id=1, source_target_pairs={{16,24},{17,25},{18,26},{19,27},{20,28},{21,29},{22,30},{23,31}} | collective-permute-start | bytes 884744 | tf_op jit(solution)/shard_map/ppermute | solution.py:30
  60.9 8.3 %collective-permute-start.11 = (bf16[4,1,24,384]{3,2,1,0:T(8,128)(2,1)S(1)}, bf16[4,1,24,384]{3,2,1,0:T(8,128)(2,1)S(1)}, u32[]{:S(2)}, u32[]{:S(2)}) collective-permute-start(bf16[4,1,24,384]{3,2,1,0:T(8,128)(2,1)S(1)} %get-tuple-element.5), channel_id=1, source_target_pairs={{16,25},{17,26},{18,27},{19,28},{20,29},{21,30},{22,31}} | collective-permute-start | bytes 221192 | tf_op jit(solution)/shard_map/ppermute | solution.py:30
  62.2 8.3 %collective-permute-start.13 = (bf16[4,1,24,384]{3,2,1,0:T(8,128)(2,1)S(1)}, bf16[4,1,24,384]{3,2,1,0:T(8,128)(2,1)S(1)}, u32[]{:S(2)}, u32[]{:S(2)}) collective-permute-start(bf16[4,1,24,384]{3,2,1,0:T(8,128)(2,1)S(1)} %get-tuple-element.6), channel_id=1, source_target_pairs={{17,24},{18,25},{19,26},{20,27},{21,28},{22,29},{23,30}} | collective-permute-start | bytes 221192 | tf_op jit(solution)/shard_map/ppermute | solution.py:30
  63.5 17.1 %collective-permute-start.6 = (bf16[1,4,24,384]{3,2,1,0:T(8,128)(2,1)S(1)}, bf16[1,4,24,384]{3,2,1,0:T(8,128)(2,1)S(1)}, u32[]{:S(2)}, u32[]{:S(2)}) collective-permute-start(bf16[1,4,24,384]{3,2,1,0:T(8,128)(2,1)S(1)} %get-tuple-element.11), channel_id=1, source_target_pairs={{16,24},{17,25},{18,26},{19,27},{20,28},{21,29},{22,30},{23,31}} | collective-permute-start | bytes 221192 | tf_op jit(solution)/shard_map/ppermute | solution.py:30
  64.8 17.2 %collective-permute-start.7 = (bf16[1,4,24,384]{3,2,1,0:T(8,128)(2,1)S(1)}, bf16[1,4,24,384]{3,2,1,0:T(8,128)(2,1)S(1)}, u32[]{:S(2)}, u32[]{:S(2)}) collective-permute-start(bf16[1,4,24,384]{3,2,1,0:T(8,128)(2,1)S(1)} %get-tuple-element.10), channel_id=1, source_target_pairs={{16,8},{17,9},{18,10},{19,11},{20,12},{21,13},{22,14},{23,15}} | collective-permute-start | bytes 221192 | tf_op jit(solution)/shard_map/ppermute | solution.py:30
  69.2 12.8 %collective-permute-start.8 = (bf16[1,4,24,384]{3,2,1,0:T(8,128)(2,1)S(1)}, bf16[1,4,24,384]{3,2,1,0:T(8,128)(2,1)S(1)}, u32[]{:S(2)}, u32[]{:S(2)}) collective-permute-start(bf16[1,4,24,384]{3,2,1,0:T(8,128)(2,1)S(1)} %get-tuple-element.9), channel_id=1, source_target_pairs={{16,0},{17,1},{18,2},{19,3},{20,4},{21,5},{22,6},{23,7}} | collective-permute-start | bytes 221192 | tf_op jit(solution)/shard_map/ppermute | solution.py:30
  74.8 7.2 %collective-permute-start.15 = (bf16[1,4,24,384]{3,2,1,0:T(8,128)(2,1)S(1)}, bf16[1,4,24,384]{3,2,1,0:T(8,128)(2,1)S(1)}, u32[]{:S(2)}, u32[]{:S(2)}) collective-permute-start(bf16[1,4,24,384]{3,2,1,0:T(8,128)(2,1)S(1)} %bitcast.140), channel_id=1, source_target_pairs={{24,8},{25,9},{26,10},{27,11},{28,12},{29,13},{30,14},{31,15}} | collective-permute-start | bytes 221192 | tf_op jit(solution)/shard_map/ppermute | solution.py:30
  75.8 6.2 %collective-permute-start.16 = (bf16[1,4,24,384]{3,2,1,0:T(8,128)(2,1)S(1)}, bf16[1,4,24,384]{3,2,1,0:T(8,128)(2,1)S(1)}, u32[]{:S(2)}, u32[]{:S(2)}) collective-permute-start(bf16[1,4,24,384]{3,2,1,0:T(8,128)(2,1)S(1)} %bitcast.141), channel_id=1, source_target_pairs={{24,0},{25,1},{26,2},{27,3},{28,4},{29,5},{30,6},{31,7}} | collective-permute-start | bytes 221192 | tf_op jit(solution)/shard_map/ppermute | solution.py:30
  80.6 7.3 %collective-permute-start.14 = (bf16[1,4,24,384]{3,2,1,0:T(8,128)(2,1)S(1)}, bf16[1,4,24,384]{3,2,1,0:T(8,128)(2,1)S(1)}, u32[]{:S(2)}, u32[]{:S(2)}) collective-permute-start(bf16[1,4,24,384]{3,2,1,0:T(8,128)(2,1)S(1)} %bitcast.142), channel_id=1, source_target_pairs={{24,16},{25,17},{26,18},{27,19},{28,20},{29,21},{30,22},{31,23}} | collective-permute-start | bytes 221192 | tf_op jit(solution)/shard_map/ppermute | solution.py:30

commit v13 on v12

--- a/solution.py
+++ b/solution.py
@@ -81,9 +81,9 @@
 
         if final:
             activated = jnp.pad(window, ((2, 0), (0, 0), (0, 0), (0, 0)))
-            split = (segment_count // 2) * group
+            split = last_stage * group
             branch = None
-            for low, high in ((0, split), (split, frame_count)):
+            for low, high in ((0, split), (split, frame_count)) if split else ((0, frame_count),):
                 part = causal_conv(activated[low : high + 2], kernel, 0).astype(jnp.bfloat16)
                 for target in range(low // group, high // group):
                     chunk = part[target * group - low : (target + 1) * group - low]

time: 90.2 us -> 100 us (1.11)
  the two profiles are of different devices: /device:TPU:17 before, /device:TPU:4 now
where the time goes in v13:
time: 100 us; the launch traced here: 99.7 us
  waiting for transfers between devices  33.2 us (33%)
  matrix products  30.6 us (31%)
  starting transfers between devices  22.9 us (23%)
  other arithmetic  6.65 us (7%)
  local copies, waits for them, and re-layouts  5.48 us (5%)
    ppermute x15, waiting for transfers between devices, send(): return lax.ppermute(value, BOTH, pairs)  33.2 us
    conv_general_dilated x5, matrix products, causal_conv(): lax.conv_general_dilated(window[None], kernel, window_strides=(1, 1, 1),...  30.6 us
    ppermute x15, starting transfers between devices, send(): return lax.ppermute(value, BOTH, pairs)  16.5 us
    ppermute x1, starting transfers between devices, local(): bottom = lax.ppermute(features[:, :1], 'rows', down)  4.54 us
    convert_element_type x5, other arithmetic, activate(): return jax.nn.silu(widened * lax.rsqrt(mean_square + 1e-06) * gain_row.as...  2.83 us
    reduce_sum x6, other arithmetic, activate(): mean_square = jnp.mean(widened * widened, axis=-1, keepdims=True)  2.25 us
  transfers between devices with their start and end apart: 17, of which 4 were waited for; matrix products, arithmetic and copies ran while one was open for 15% of the time, Pallas kernels for 0%

profile of v13, /device:TPU:4, one launch (start us, length us, event | category | flops | bytes accessed | tf_op | source)
XLA Modules:
  0.0 99.7 jit_solution(10306634912511978445)
XLA Ops:
  0.0 0.9 fusion.139
  0.9 1.9 %collective-permute-start = (bf16[4,1,24,384]{3,2,1,0:T(8,128)(2,1)S(1)}, bf16[4,1,24,384]{3,2,1,0:T(8,128)(2,1)S(1)}, u32[]{:S(2)}, u32[]{:S(2)}) collective-permute-start(bf16[4,1,24,384]{3,2,1,0:T(8,128)(2,1)S(1)} %get-tuple-element.17), channel_id=1, source_target_pairs={{0,1},{1,2},{2,3},{3,4},{4,5},{5,6},{6,7},{8,9},{9,10},{10,11},{11... | collective-permute-start | bytes 221192 | tf_op jit(solution)/shard_map/ppermute | solution.py:59
  2.9 4.5 %collective-permute-start.1 = (bf16[4,1,24,384]{3,2,1,0:T(8,128)(2,1)S(1)}, bf16[4,1,24,384]{3,2,1,0:T(8,128)(2,1)S(1)}, u32[]{:S(2)}, u32[]{:S(2)}) collective-permute-start(bf16[4,1,24,384]{3,2,1,0:T(8,128)(2,1)S(1)} %get-tuple-element.18), channel_id=1, source_target_pairs={{1,0},{2,1},{3,2},{4,3},{5,4},{6,5},{7,6},{9,8},{10,9},{11,10},{12... | collective-permute-start | bytes 221192 | tf_op jit(solution)/shard_map/ppermute | solution.py:60
  7.4 1.1 %fusion.84 = f32[4,4,24]{2,1,0:T(4,128)S(1)} fusion(bf16[4,4,24,384]{3,2,1,0:T(8,128)(2,1)} %param.3), kind=kLoop, calls=%fused_computation.72 | loop fusion | flops 441984 | bytes 296448 | tf_op jit(solution)/shard_map/reduce_sum | solution.py:11
  8.5 0.7 convert_reduce_fusion
  9.2 1.2 %fusion.91 = bf16[4,4,24,384]{3,2,1,0:T(8,128)(2,1)S(1)} fusion(bf16[4,4,24,384]{3,2,1,0:T(8,128)(2,1)} %param.3, f32[384]{0:T(512)S(1)} %convert_reduce_fusion, f32[4,4,24]{2,1,0:T(4,128)S(1)} %add_rsqrt_fusion.3), kind=kLoop, calls=%fused_computation.79 | loop fusion | flops 1179648 | bytes 592896 | tf_op jit(solution)/shard_map/convert_element_type | solution.py:14
  10.7 0.2 fusion.107
  11.0 0.2 copy.214
  11.1 0.2 pad.5.clone
  11.6 8.3 %fusion.30 = bf16[4,4,8,4,384]{4,2,3,1,0:T(8,128)(2,1)S(1)} fusion(bf16[1,3,3,3,384,384]{5,4,3,2,1,0:T(8,128)(2,1)} %param.5, bf16[4,6,1,7,2,384]{5,3,4,1,0,2:T(8,128)(2,1)S(1)} %slice.96, bf16[4,6,1,8,4,384]{5,3,4,1,0,2:T(8,128)(2,1)S(1)} %copy.172, pred[8,4]{0,1:T(4,128)(4,1)S(1)} %copy-done.1), kind=kOutput, calls=%fused_computation.25 | convolution fusion | flops 3060695040 | bytes 9203744 | tf_op jit(solution)/shard_map/conv_general_dilated | solution.py:18
  19.9 0.2 copy.173
  20.3 3.5 %collective-permute-start.3 = (bf16[4,4,24,384]{3,2,1,0:T(8,128)(2,1)S(1)}, bf16[4,4,24,384]{3,2,1,0:T(8,128)(2,1)S(1)}, u32[]{:S(2)}, u32[]{:S(2)}) collective-permute-start(bf16[4,4,24,384]{3,2,1,0:T(8,128)(2,1)S(1)} %bitcast.117), channel_id=1, source_target_pairs={{0,8},{1,9},{2,10},{3,11},{4,12},{5,13},{6,14},{7,15}} | collective-permute-start | bytes 884744 | tf_op jit(solution)/shard_map/ppermute | solution.py:30
  23.8 2.2 %collective-permute-start.4 = (bf16[4,1,24,384]{3,2,1,0:T(8,128)(2,1)S(1)}, bf16[4,1,24,384]{3,2,1,0:T(8,128)(2,1)S(1)}, u32[]{:S(2)}, u32[]{:S(2)}) collective-permute-start(bf16[4,1,24,384]{3,2,1,0:T(8,128)(2,1)S(1)} %get-tuple-element.16), channel_id=1, source_target_pairs={{1,8},{2,9},{3,10},{4,11},{5,12},{6,13},{7,14}} | collective-permute-start | bytes 221192 | tf_op jit(solution)/shard_map/ppermute | solution.py:30
  26.0 1.3 %collective-permute-start.2 = (bf16[4,1,24,384]{3,2,1,0:T(8,128)(2,1)S(1)}, bf16[4,1,24,384]{3,2,1,0:T(8,128)(2,1)S(1)}, u32[]{:S(2)}, u32[]{:S(2)}) collective-permute-start(bf16[4,1,24,384]{3,2,1,0:T(8,128)(2,1)S(1)} %get-tuple-element.15), channel_id=1, source_target_pairs={{0,9},{1,10},{2,11},{3,12},{4,13},{5,14},{6,15}} | collective-permute-start | bytes 221192 | tf_op jit(solution)/shard_map/ppermute | solution.py:30
  27.3 4.8 %collective-permute-done.4 = bf16[4,1,24,384]{3,2,1,0:T(8,128)(2,1)S(1)} collective-permute-done((bf16[4,1,24,384]{3,2,1,0:T(8,128)(2,1)S(1)}, bf16[4,1,24,384]{3,2,1,0:T(8,128)(2,1)S(1)}, u32[]{:S(2)}, u32[]{:S(2)}) %collective-permute-start.4) | collective-permute-done | bytes 73760 | tf_op jit(solution)/shard_map/ppermute | solution.py:30
  32.1 0.8 collective-permute-done.2
  33.0 0.3 fusion.94
  33.4 0.2 copy.215
  33.6 0.2 pad.7.clone
  34.0 5.7 %fusion.27 = bf16[4,4,8,4,384]{4,2,3,1,0:T(8,128)(2,1)S(1)} fusion(bf16[1,3,3,3,384,384]{5,4,3,2,1,0:T(8,128)(2,1)S(1)} %bitcast.131, bf16[4,6,1,7,2,384]{5,3,4,1,0,2:T(8,128)(2,1)S(1)} %slice.100, bf16[4,6,1,8,4,384]{5,3,4,1,0,2:T(8,128)(2,1)S(1)} %copy.179, pred[8,4]{0,1:T(4,128)(4,1)S(1)} %copy-done.1), kind=kOutput, calls=%fused_computation.24 | convolution fusion | flops 3060695040 | bytes 9203744 | tf_op jit(solution)/shard_map/conv_general_dilated | solution.py:18
  39.7 0.2 copy.180
  40.1 0.7 collective-permute-start.5
  40.8 0.8 collective-permute-start.10
  41.7 0.7 collective-permute-start.9
  42.4 0.2 multiply_reduce_fusion
  42.6 0.3 fusion.95
  42.9 0.2 copy.216
  43.1 0.2 pad.9.clone
  43.5 7.9 %fusion.24 = bf16[4,4,8,4,384]{4,2,3,1,0:T(8,128)(2,1)S(1)} fusion(bf16[1,3,3,3,384,384]{5,4,3,2,1,0:T(8,128)(2,1)} %param.5, bf16[4,6,1,7,2,384]{5,3,4,1,0,2:T(8,128)(2,1)S(1)} %slice.108, bf16[4,6,1,8,4,384]{5,3,4,1,0,2:T(8,128)(2,1)S(1)} %copy.186, pred[8,4]{0,1:T(4,128)(4,1)S(1)} %copy-done.1), kind=kOutput, calls=%fused_computation.23 | convolution fusion | flops 3060695040 | bytes 9203744 | tf_op jit(solution)/shard_map/conv_general_dilated | solution.py:18
  51.4 0.2 copy.187
  51.8 0.7 collective-permute-start.12
  52.5 0.2 fusion.135
  52.7 0.7 collective-permute-start.13
  53.4 0.7 collective-permute-start.11
  54.1 0.7 collective-permute-start.6
  54.7 0.7 collective-permute-start.7
  55.4 1.3 %collective-permute-start.8 = (bf16[1,4,24,384]{3,2,1,0:T(8,128)(2,1)S(1)}, bf16[1,4,24,384]{3,2,1,0:T(8,128)(2,1)S(1)}, u32[]{:S(2)}, u32[]{:S(2)}) collective-permute-start(bf16[1,4,24,384]{3,2,1,0:T(8,128)(2,1)S(1)} %get-tuple-element.12), channel_id=1, source_target_pairs={{16,0},{17,1},{18,2},{19,3},{20,4},{21,5},{22,6},{23,7}} | collective-permute-start | bytes 221192 | tf_op jit(solution)/shard_map/ppermute | solution.py:30
  56.7 0.6 fusion.39
  57.6 0.8 fusion.46
  58.7 0.3 copy.197
  59.1 7.2 %fusion.36 = bf16[3,4,8,4,384]{4,2,3,1,0:T(8,128)(2,1)S(1)} fusion(bf16[1,3,3,3,384,384]{5,4,3,2,1,0:T(8,128)(2,1)} %param.5, bf16[5,6,1,7,2,384]{5,3,4,1,0,2:T(8,128)(2,1)S(1)} %slice.115, bf16[5,6,1,8,4,384]{5,3,4,1,0,2:T(8,128)(2,1)S(1)} %copy.197, pred[8,4]{0,1:T(4,128)(4,1)S(1)} %copy-done.1), kind=kOutput, calls=%fused_computation.27 | convolution fusion | flops 3061260288 | bytes 9317408 | tf_op jit(solution)/shard_map/conv_general_dilated | solution.py:18
  66.8 0.7 collective-permute-start.14
  67.6 0.7 collective-permute-start.15
  68.4 1.3 %collective-permute-start.16 = (bf16[1,4,24,384]{3,2,1,0:T(8,128)(2,1)S(1)}, bf16[1,4,24,384]{3,2,1,0:T(8,128)(2,1)S(1)}, u32[]{:S(2)}, u32[]{:S(2)}) collective-permute-start(bf16[1,4,24,384]{3,2,1,0:T(8,128)(2,1)S(1)} %bitcast.129), channel_id=1, source_target_pairs={{24,0},{25,1},{26,2},{27,3},{28,4},{29,5},{30,6},{31,7}} | collective-permute-start | bytes 221192 | tf_op jit(solution)/shard_map/ppermute | solution.py:30
  69.7 1.5 %fusion.50 = bf16[1,4,8,4,384]{4,2,3,1,0:T(8,128)(2,1)S(1)} fusion(bf16[1,3,3,3,384,384]{5,4,3,2,1,0:T(8,128)(2,1)S(1)} %bitcast.133, bf16[3,6,1,7,2,384]{5,3,4,1,0,2:T(8,128)(2,1)S(1)} %slice.113, bf16[3,6,1,8,4,384]{5,3,4,1,0,2:T(8,128)(2,1)S(1)} %copy.192, pred[8,4]{0,1:T(4,128)(4,1)S(1)} %copy-done.1), kind=kOutput, calls=%fused_computation.37 | convolution fusion | flops 1021304832 | bytes 8696864 | tf_op jit(solution)/shard_map/conv_general_dilated | solution.py:18
  71.3 10.0 %collective-permute-done.8 = bf16[1,4,24,384]{3,2,1,0:T(8,128)(2,1)S(1)} collective-permute-done((bf16[1,4,24,384]{3,2,1,0:T(8,128)(2,1)S(1)}, bf16[1,4,24,384]{3,2,1,0:T(8,128)(2,1)S(1)}, u32[]{:S(2)}, u32[]{:S(2)}) %collective-permute-start.8) | collective-permute-done | bytes 73760 | tf_op jit(solution)/shard_map/ppermute | solution.py:30
  81.3 17.6 %collective-permute-done.16 = bf16[1,4,24,384]{3,2,1,0:T(8,128)(2,1)S(1)} collective-permute-done((bf16[1,4,24,384]{3,2,1,0:T(8,128)(2,1)S(1)}, bf16[1,4,24,384]{3,2,1,0:T(8,128)(2,1)S(1)}, u32[]{:S(2)}, u32[]{:S(2)}) %collective-permute-start.16) | collective-permute-done | bytes 73760 | tf_op jit(solution)/shard_map/ppermute | solution.py:30
  99.0 0.7 add_convert_fusion
  (72 shorter events, 2.9 us)
Async XLA Ops:
  0.9 9.5 %collective-permute-start = (bf16[4,1,24,384]{3,2,1,0:T(8,128)(2,1)S(1)}, bf16[4,1,24,384]{3,2,1,0:T(8,128)(2,1)S(1)}, u32[]{:S(2)}, u32[]{:S(2)}) collective-permute-start(bf16[4,1,24,384]{3,2,1,0:T(8,128)(2,1)S(1)} %get-tuple-element.17), channel_id=1, source_target_pairs={{0,1},{1,2},{2,3},{3,4},{4,5},{5,6},{6,7},{8,9},{9,10},{10,11},{11... | collective-permute-start | bytes 221192 | tf_op jit(solution)/shard_map/ppermute | solution.py:59
  2.9 7.7 %collective-permute-start.1 = (bf16[4,1,24,384]{3,2,1,0:T(8,128)(2,1)S(1)}, bf16[4,1,24,384]{3,2,1,0:T(8,128)(2,1)S(1)}, u32[]{:S(2)}, u32[]{:S(2)}) collective-permute-start(bf16[4,1,24,384]{3,2,1,0:T(8,128)(2,1)S(1)} %get-tuple-element.18), channel_id=1, source_target_pairs={{1,0},{2,1},{3,2},{4,3},{5,4},{6,5},{7,6},{9,8},{10,9},{11,10},{12... | collective-permute-start | bytes 221192 | tf_op jit(solution)/shard_map/ppermute | solution.py:60
  10.9 0.7 copy-start.1
  11.5 22.5 %slice-start = ((s8[7962624]{0:T(1024)(128)(4,1)}), s8[4194304]{0:T(1024)(128)(4,1)S(1)}, s32[]{:S(2)}) async-start(s8[7962624]{0:T(1024)(128)(4,1)} %bitcast.130), calls=%async_computation | async-start | bytes 8388608
  11.6 22.4 %slice-start.1 = ((s8[7962624]{0:T(1024)(128)(4,1)}), s8[3768320]{0:T(1024)(128)(4,1)S(1)}, s32[]{:S(2)}) async-start(s8[7962624]{0:T(1024)(128)(4,1)} %bitcast.130), calls=%async_computation.1 | async-start | bytes 7536640
  20.3 12.6 %collective-permute-start.3 = (bf16[4,4,24,384]{3,2,1,0:T(8,128)(2,1)S(1)}, bf16[4,4,24,384]{3,2,1,0:T(8,128)(2,1)S(1)}, u32[]{:S(2)}, u32[]{:S(2)}) collective-permute-start(bf16[4,4,24,384]{3,2,1,0:T(8,128)(2,1)S(1)} %bitcast.117), channel_id=1, source_target_pairs={{0,8},{1,9},{2,10},{3,11},{4,12},{5,13},{6,14},{7,15}} | collective-permute-start | bytes 884744 | tf_op jit(solution)/shard_map/ppermute | solution.py:30
  23.8 8.3 %collective-permute-start.4 = (bf16[4,1,24,384]{3,2,1,0:T(8,128)(2,1)S(1)}, bf16[4,1,24,384]{3,2,1,0:T(8,128)(2,1)S(1)}, u32[]{:S(2)}, u32[]{:S(2)}) collective-permute-start(bf16[4,1,24,384]{3,2,1,0:T(8,128)(2,1)S(1)} %get-tuple-element.16), channel_id=1, source_target_pairs={{1,8},{2,9},{3,10},{4,11},{5,12},{6,13},{7,14}} | collective-permute-start | bytes 221192 | tf_op jit(solution)/shard_map/ppermute | solution.py:30
  26.0 6.9 %collective-permute-start.2 = (bf16[4,1,24,384]{3,2,1,0:T(8,128)(2,1)S(1)}, bf16[4,1,24,384]{3,2,1,0:T(8,128)(2,1)S(1)}, u32[]{:S(2)}, u32[]{:S(2)}) collective-permute-start(bf16[4,1,24,384]{3,2,1,0:T(8,128)(2,1)S(1)} %get-tuple-element.15), channel_id=1, source_target_pairs={{0,9},{1,10},{2,11},{3,12},{4,13},{5,14},{6,15}} | collective-permute-start | bytes 221192 | tf_op jit(solution)/shard_map/ppermute | solution.py:30
  34.0 6.0 %copy-start = (bf16[4,4,24,384]{3,2,1,0:T(8,128)(2,1)S(1)}, bf16[4,4,24,384]{3,2,1,0:T(8,128)(2,1)}, u32[]{:S(2)}) copy-start(bf16[4,4,24,384]{3,2,1,0:T(8,128)(2,1)} %param.3) | copy-start | bytes 884740
  40.1 2.3 %collective-permute-start.5 = (bf16[4,4,24,384]{3,2,1,0:T(8,128)(2,1)S(1)}, bf16[4,4,24,384]{3,2,1,0:T(8,128)(2,1)S(1)}, u32[]{:S(2)}, u32[]{:S(2)}) collective-permute-start(bf16[4,4,24,384]{3,2,1,0:T(8,128)(2,1)S(1)} %fusion.92), channel_id=1, source_target_pairs={{8,16},{9,17},{10,18},{11,19},{12,20},{13,21},{14,22},{15,23}} | collective-permute-start | bytes 884744 | tf_op jit(solution)/shard_map/ppermute | solution.py:30
  40.8 1.5 %collective-permute-start.10 = (bf16[4,1,24,384]{3,2,1,0:T(8,128)(2,1)S(1)}, bf16[4,1,24,384]{3,2,1,0:T(8,128)(2,1)S(1)}, u32[]{:S(2)}, u32[]{:S(2)}) collective-permute-start(bf16[4,1,24,384]{3,2,1,0:T(8,128)(2,1)S(1)} %get-tuple-element.11), channel_id=1, source_target_pairs={{9,16},{10,17},{11,18},{12,19},{13,20},{14,21},{15,22}} | collective-permute-start | bytes 221192 | tf_op jit(solution)/shard_map/ppermute | solution.py:30
  41.7 0.7 collective-permute-start.9
  51.8 5.0 %collective-permute-start.12 = (bf16[4,4,24,384]{3,1,2,0:T(4,128)(2,1)S(1)}, bf16[4,4,24,384]{3,1,2,0:T(4,128)(2,1)S(1)}, u32[]{:S(2)}, u32[]{:S(2)}) collective-permute-start(bf16[4,4,24,384]{3,1,2,0:T(4,128)(2,1)S(1)} %slice_bitcast_fusion.1), channel_id=1, source_target_pairs={{16,24},{17,25},{18,26},{19,27},{20,28},{21,29},{22,30},{23,31}} | collective-permute-start | bytes 884744 | tf_op jit(solution)/shard_map/ppermute | solution.py:30
  52.7 2.7 %collective-permute-start.13 = (bf16[4,1,24,384]{3,1,2,0:T(2,128)(2,1)S(1)}, bf16[4,1,24,384]{3,1,2,0:T(2,128)(2,1)S(1)}, u32[]{:S(2)}, u32[]{:S(2)}) collective-permute-start(bf16[4,1,24,384]{3,1,2,0:T(2,128)(2,1)S(1)} %get-tuple-element.9), channel_id=1, source_target_pairs={{17,24},{18,25},{19,26},{20,27},{21,28},{22,29},{23,30}} | collective-permute-start | bytes 221192 | tf_op jit(solution)/shard_map/ppermute | solution.py:30
  53.4 3.4 %collective-permute-start.11 = (bf16[4,1,24,384]{3,1,2,0:T(2,128)(2,1)S(1)}, bf16[4,1,24,384]{3,1,2,0:T(2,128)(2,1)S(1)}, u32[]{:S(2)}, u32[]{:S(2)}) collective-permute-start(bf16[4,1,24,384]{3,1,2,0:T(2,128)(2,1)S(1)} %get-tuple-element.8), channel_id=1, source_target_pairs={{16,25},{17,26},{18,27},{19,28},{20,29},{21,30},{22,31}} | collective-permute-start | bytes 221192 | tf_op jit(solution)/shard_map/ppermute | solution.py:30
  54.1 14.3 %collective-permute-start.6 = (bf16[1,4,24,384]{3,2,1,0:T(8,128)(2,1)S(1)}, bf16[1,4,24,384]{3,2,1,0:T(8,128)(2,1)S(1)}, u32[]{:S(2)}, u32[]{:S(2)}) collective-permute-start(bf16[1,4,24,384]{3,2,1,0:T(8,128)(2,1)S(1)} %get-tuple-element.14), channel_id=1, source_target_pairs={{16,24},{17,25},{18,26},{19,27},{20,28},{21,29},{22,30},{23,31}} | collective-permute-start | bytes 221192 | tf_op jit(solution)/shard_map/ppermute | solution.py:30
  54.7 16.6 %collective-permute-start.7 = (bf16[1,4,24,384]{3,2,1,0:T(8,128)(2,1)S(1)}, bf16[1,4,24,384]{3,2,1,0:T(8,128)(2,1)S(1)}, u32[]{:S(2)}, u32[]{:S(2)}) collective-permute-start(bf16[1,4,24,384]{3,2,1,0:T(8,128)(2,1)S(1)} %get-tuple-element.13), channel_id=1, source_target_pairs={{16,8},{17,9},{18,10},{19,11},{20,12},{21,13},{22,14},{23,15}} | collective-permute-start | bytes 221192 | tf_op jit(solution)/shard_map/ppermute | solution.py:30
  55.4 25.9 %collective-permute-start.8 = (bf16[1,4,24,384]{3,2,1,0:T(8,128)(2,1)S(1)}, bf16[1,4,24,384]{3,2,1,0:T(8,128)(2,1)S(1)}, u32[]{:S(2)}, u32[]{:S(2)}) collective-permute-start(bf16[1,4,24,384]{3,2,1,0:T(8,128)(2,1)S(1)} %get-tuple-element.12), channel_id=1, source_target_pairs={{16,0},{17,1},{18,2},{19,3},{20,4},{21,5},{22,6},{23,7}} | collective-permute-start | bytes 221192 | tf_op jit(solution)/shard_map/ppermute | solution.py:30
  59.0 10.7 %slice-start.2 = ((s8[7962624]{0:T(1024)(128)(4,1)}), s8[4194304]{0:T(1024)(128)(4,1)S(1)}, s32[]{:S(2)}) async-start(s8[7962624]{0:T(1024)(128)(4,1)} %bitcast.132), calls=%async_computation.2 | async-start | bytes 8388608
  59.1 10.6 %slice-start.3 = ((s8[7962624]{0:T(1024)(128)(4,1)}), s8[3768320]{0:T(1024)(128)(4,1)S(1)}, s32[]{:S(2)}) async-start(s8[7962624]{0:T(1024)(128)(4,1)} %bitcast.132), calls=%async_computation.3 | async-start | bytes 7536640
  66.8 14.6 %collective-permute-start.14 = (bf16[1,4,24,384]{3,2,1,0:T(8,128)(2,1)S(1)}, bf16[1,4,24,384]{3,2,1,0:T(8,128)(2,1)S(1)}, u32[]{:S(2)}, u32[]{:S(2)}) collective-permute-start(bf16[1,4,24,384]{3,2,1,0:T(8,128)(2,1)S(1)} %bitcast.127), channel_id=1, source_target_pairs={{24,16},{25,17},{26,18},{27,19},{28,20},{29,21},{30,22},{31,23}} | collective-permute-start | bytes 221192 | tf_op jit(solution)/shard_map/ppermute | solution.py:30
  67.6 13.8 %collective-permute-start.15 = (bf16[1,4,24,384]{3,2,1,0:T(8,128)(2,1)S(1)}, bf16[1,4,24,384]{3,2,1,0:T(8,128)(2,1)S(1)}, u32[]{:S(2)}, u32[]{:S(2)}) collective-permute-start(bf16[1,4,24,384]{3,2,1,0:T(8,128)(2,1)S(1)} %bitcast.128), channel_id=1, source_target_pairs={{24,8},{25,9},{26,10},{27,11},{28,12},{29,13},{30,14},{31,15}} | collective-permute-start | bytes 221192 | tf_op jit(solution)/shard_map/ppermute | solution.py:30
  68.4 30.6 %collective-permute-start.16 = (bf16[1,4,24,384]{3,2,1,0:T(8,128)(2,1)S(1)}, bf16[1,4,24,384]{3,2,1,0:T(8,128)(2,1)S(1)}, u32[]{:S(2)}, u32[]{:S(2)}) collective-permute-start(bf16[1,4,24,384]{3,2,1,0:T(8,128)(2,1)S(1)} %bitcast.129), channel_id=1, source_target_pairs={{24,0},{25,1},{26,2},{27,3},{28,4},{29,5},{30,6},{31,7}} | collective-permute-start | bytes 221192 | tf_op jit(solution)/shard_map/ppermute | solution.py:30

commit v14 on v12

--- a/solution.py
+++ b/solution.py
@@ -83,7 +83,7 @@
             activated = jnp.pad(window, ((2, 0), (0, 0), (0, 0), (0, 0)))
             split = (segment_count // 2) * group
             branch = None
-            for low, high in ((0, split), (split, frame_count)):
+            for low, high in ((split, frame_count), (0, split)):
                 part = causal_conv(activated[low : high + 2], kernel, 0).astype(jnp.bfloat16)
                 for target in range(low // group, high // group):
                     chunk = part[target * group - low : (target + 1) * group - low]

time: 90.2 us -> 92.5 us (1.025)
  the two profiles are of different devices: /device:TPU:17 before, /device:TPU:3 now
where the time goes in v14:
time: 92.5 us; the launch traced here: 92 us
  waiting for transfers between devices  31.1 us (34%)
  matrix products  25.6 us (28%)
  starting transfers between devices  23.1 us (25%)
  other arithmetic  6.04 us (7%)
  local copies, waits for them, and re-layouts  5.36 us (6%)
    ppermute x15, waiting for transfers between devices, send(): return lax.ppermute(value, BOTH, pairs)  31.1 us
    conv_general_dilated x5, matrix products, causal_conv(): lax.conv_general_dilated(window[None], kernel, window_strides=(1, 1, 1),...  25.6 us
    ppermute x15, starting transfers between devices, send(): return lax.ppermute(value, BOTH, pairs)  16.7 us
    ppermute x1, starting transfers between devices, local(): top = lax.ppermute(features[:, height - 1:], 'rows', up)  3.88 us
    convert_element_type x6, other arithmetic, activate(): return jax.nn.silu(widened * lax.rsqrt(mean_square + 1e-06) * gain_row.as...  2.72 us
    ppermute x1, starting transfers between devices, local(): bottom = lax.ppermute(features[:, :1], 'rows', down)  2.58 us
  transfers between devices with their start and end apart: 17, of which 4 were waited for; matrix products, arithmetic and copies ran while one was open for 13% of the time, Pallas kernels for 0%

profile of v14, /device:TPU:3, one launch (start us, length us, event | category | flops | bytes accessed | tf_op | source)
XLA Modules:
  0.0 92.0 jit_solution(1782766233779878949)
XLA Ops:
  0.0 0.9 %fusion.141 = (bf16[4,1,24,384]{3,2,1,0:T(8,128)(2,1)S(1)}, bf16[4,1,24,384]{3,2,1,0:T(8,128)(2,1)S(1)}) fusion(bf16[4,4,24,384]{3,2,1,0:T(8,128)(2,1)} %param.3), kind=kLoop, calls=%fused_computation.150 | loop fusion | bytes 294912 | tf_op jit(solution)/shard_map/slice | solution.py:59
  0.9 2.6 %collective-permute-start.1 = (bf16[4,1,24,384]{3,2,1,0:T(8,128)(2,1)S(1)}, bf16[4,1,24,384]{3,2,1,0:T(8,128)(2,1)S(1)}, u32[]{:S(2)}, u32[]{:S(2)}) collective-permute-start(bf16[4,1,24,384]{3,2,1,0:T(8,128)(2,1)S(1)} %get-tuple-element.15), channel_id=1, source_target_pairs={{1,0},{2,1},{3,2},{4,3},{5,4},{6,5},{7,6},{9,8},{10,9},{11,10},{12... | collective-permute-start | bytes 221192 | tf_op jit(solution)/shard_map/ppermute | solution.py:60
  3.5 3.9 %collective-permute-start = (bf16[4,1,24,384]{3,2,1,0:T(8,128)(2,1)S(1)}, bf16[4,1,24,384]{3,2,1,0:T(8,128)(2,1)S(1)}, u32[]{:S(2)}, u32[]{:S(2)}) collective-permute-start(bf16[4,1,24,384]{3,2,1,0:T(8,128)(2,1)S(1)} %get-tuple-element.14), channel_id=1, source_target_pairs={{0,1},{1,2},{2,3},{3,4},{4,5},{5,6},{6,7},{8,9},{9,10},{10,11},{11... | collective-permute-start | bytes 221192 | tf_op jit(solution)/shard_map/ppermute | solution.py:59
  7.4 1.1 %fusion.83 = f32[4,4,24]{2,1,0:T(4,128)S(1)} fusion(bf16[4,4,24,384]{3,2,1,0:T(8,128)(2,1)} %param.3), kind=kLoop, calls=%fused_computation.70 | loop fusion | flops 441984 | bytes 296448 | tf_op jit(solution)/shard_map/reduce_sum | solution.py:11
  8.5 0.7 convert_reduce_fusion
  9.2 1.2 %fusion.90 = bf16[4,4,24,384]{3,2,1,0:T(8,128)(2,1)S(1)} fusion(bf16[4,4,24,384]{3,2,1,0:T(8,128)(2,1)} %param.3, f32[384]{0:T(512)S(1)} %convert_reduce_fusion, f32[4,4,24]{2,1,0:T(4,128)S(1)} %add_rsqrt_fusion.3), kind=kLoop, calls=%fused_computation.77 | loop fusion | flops 1179648 | bytes 592896 | tf_op jit(solution)/shard_map/convert_element_type | solution.py:14
  11.0 0.2 copy.156
  11.1 0.2 pad.5.clone
  11.6 8.3 %fusion.30 = bf16[4,4,8,4,384]{4,2,3,1,0:T(8,128)(2,1)S(1)} fusion(bf16[1,3,3,3,384,384]{5,4,3,2,1,0:T(8,128)(2,1)} %param.5, bf16[4,6,1,7,2,384]{5,3,4,1,0,2:T(8,128)(2,1)S(1)} %slice.101, bf16[4,6,1,8,4,384]{5,3,4,1,0,2:T(8,128)(2,1)S(1)} %copy.116, pred[8,4]{0,1:T(4,128)(4,1)S(1)} %copy-done.1), kind=kOutput, calls=%fused_computation.21 | convolution fusion | flops 3060695040 | bytes 9203744 | tf_op jit(solution)/shard_map/conv_general_dilated | solution.py:18
  19.9 0.2 copy.117
  20.2 3.2 %collective-permute-start.3 = (bf16[4,4,24,384]{3,2,1,0:T(8,128)(2,1)S(1)}, bf16[4,4,24,384]{3,2,1,0:T(8,128)(2,1)S(1)}, u32[]{:S(2)}, u32[]{:S(2)}) collective-permute-start(bf16[4,4,24,384]{3,2,1,0:T(8,128)(2,1)S(1)} %bitcast.134), channel_id=1, source_target_pairs={{0,8},{1,9},{2,10},{3,11},{4,12},{5,13},{6,14},{7,15}} | collective-permute-start | bytes 884744 | tf_op jit(solution)/shard_map/ppermute | solution.py:30
  23.5 2.5 %collective-permute-start.2 = (bf16[4,1,24,384]{3,2,1,0:T(8,128)(2,1)S(1)}, bf16[4,1,24,384]{3,2,1,0:T(8,128)(2,1)S(1)}, u32[]{:S(2)}, u32[]{:S(2)}) collective-permute-start(bf16[4,1,24,384]{3,2,1,0:T(8,128)(2,1)S(1)} %get-tuple-element.12), channel_id=1, source_target_pairs={{0,9},{1,10},{2,11},{3,12},{4,13},{5,14},{6,15}} | collective-permute-start | bytes 221192 | tf_op jit(solution)/shard_map/ppermute | solution.py:30
  26.0 1.3 %collective-permute-start.4 = (bf16[4,1,24,384]{3,2,1,0:T(8,128)(2,1)S(1)}, bf16[4,1,24,384]{3,2,1,0:T(8,128)(2,1)S(1)}, u32[]{:S(2)}, u32[]{:S(2)}) collective-permute-start(bf16[4,1,24,384]{3,2,1,0:T(8,128)(2,1)S(1)} %get-tuple-element.13), channel_id=1, source_target_pairs={{1,8},{2,9},{3,10},{4,11},{5,12},{6,13},{7,14}} | collective-permute-start | bytes 221192 | tf_op jit(solution)/shard_map/ppermute | solution.py:30
  27.3 4.5 %collective-permute-done.2 = bf16[4,1,24,384]{3,2,1,0:T(8,128)(2,1)S(1)} collective-permute-done((bf16[4,1,24,384]{3,2,1,0:T(8,128)(2,1)S(1)}, bf16[4,1,24,384]{3,2,1,0:T(8,128)(2,1)S(1)}, u32[]{:S(2)}, u32[]{:S(2)}) %collective-permute-start.2) | collective-permute-done | bytes 73760 | tf_op jit(solution)/shard_map/ppermute | solution.py:30
  31.8 0.7 collective-permute-done.4
  32.7 0.3 fusion.93
  33.0 0.2 copy.157
  33.2 0.2 pad.7.clone
  33.7 5.7 %fusion.27 = bf16[4,4,8,4,384]{4,2,3,1,0:T(8,128)(2,1)S(1)} fusion(bf16[1,3,3,3,384,384]{5,4,3,2,1,0:T(8,128)(2,1)S(1)} %bitcast.148, bf16[4,6,1,7,2,384]{5,3,4,1,0,2:T(8,128)(2,1)S(1)} %slice.105, bf16[4,6,1,8,4,384]{5,3,4,1,0,2:T(8,128)(2,1)S(1)} %copy.123, pred[8,4]{0,1:T(4,128)(4,1)S(1)} %copy-done.1), kind=kOutput, calls=%fused_computation.20 | convolution fusion | flops 3060695040 | bytes 9203744 | tf_op jit(solution)/shard_map/conv_general_dilated | solution.py:18
  39.4 0.2 copy.124
  39.8 0.7 collective-permute-start.5
  40.5 0.8 collective-permute-start.10
  41.3 0.7 collective-permute-start.9
  42.2 0.3 fusion.94
  42.5 0.2 copy.158
  42.7 0.2 pad.9.clone
  43.2 5.7 %fusion.24 = bf16[4,4,8,4,384]{4,2,3,1,0:T(8,128)(2,1)S(1)} fusion(bf16[1,3,3,3,384,384]{5,4,3,2,1,0:T(8,128)(2,1)S(1)} %bitcast.148, bf16[4,6,1,7,2,384]{5,3,4,1,0,2:T(8,128)(2,1)S(1)} %slice.113, bf16[4,6,1,8,4,384]{5,3,4,1,0,2:T(8,128)(2,1)S(1)} %copy.130, pred[8,4]{0,1:T(4,128)(4,1)S(1)} %copy-done.1), kind=kOutput, calls=%fused_computation.19 | convolution fusion | flops 3060695040 | bytes 9203744 | tf_op jit(solution)/shard_map/conv_general_dilated | solution.py:18
  48.8 0.2 copy.131
  49.2 0.7 collective-permute-start.12
  49.9 0.7 collective-permute-start.11
  50.6 0.7 collective-permute-start.13
  51.3 0.7 collective-permute-start.6
  52.0 0.7 collective-permute-start.7
  52.6 1.3 %collective-permute-start.8 = (bf16[1,4,24,384]{3,2,1,0:T(8,128)(2,1)S(1)}, bf16[1,4,24,384]{3,2,1,0:T(8,128)(2,1)S(1)}, u32[]{:S(2)}, u32[]{:S(2)}) collective-permute-start(bf16[1,4,24,384]{3,2,1,0:T(8,128)(2,1)S(1)} %get-tuple-element.9), channel_id=1, source_target_pairs={{16,0},{17,1},{18,2},{19,3},{20,4},{21,5},{22,6},{23,7}} | collective-permute-start | bytes 221192 | tf_op jit(solution)/shard_map/ppermute | solution.py:30
  54.1 0.3 fusion.95
  54.5 0.2 copy.160
  54.7 0.2 pad.13.clone
  55.1 3.0 %fusion.39 = bf16[2,4,8,4,384]{4,2,3,1,0:T(8,128)(2,1)S(1)} fusion(bf16[1,3,3,3,384,384]{5,4,3,2,1,0:T(8,128)(2,1)S(1)} %bitcast.148, bf16[4,6,1,7,2,384]{5,3,4,1,0,2:T(8,128)(2,1)S(1)} %slice.122, bf16[4,6,1,8,4,384]{5,3,4,1,0,2:T(8,128)(2,1)S(1)} %copy.144, pred[8,4]{0,1:T(4,128)(4,1)S(1)} %copy-done.1), kind=kOutput, calls=%fused_computation.24 | convolution fusion | flops 2041282560 | bytes 9007136 | tf_op jit(solution)/shard_map/conv_general_dilated | solution.py:18
  58.2 0.9 collective-permute-start.16
  59.1 0.3 fusion.52
  59.5 0.2 copy.159
  59.7 0.2 pad.11.clone
  60.1 3.0 %fusion.42 = bf16[2,4,8,4,384]{4,2,3,1,0:T(8,128)(2,1)S(1)} fusion(bf16[1,3,3,3,384,384]{5,4,3,2,1,0:T(8,128)(2,1)S(1)} %bitcast.148, bf16[4,6,1,7,2,384]{5,3,4,1,0,2:T(8,128)(2,1)S(1)} %slice.117, bf16[4,6,1,8,4,384]{5,3,4,1,0,2:T(8,128)(2,1)S(1)} %copy.135, pred[8,4]{0,1:T(4,128)(4,1)S(1)} %copy-done.1), kind=kOutput, calls=%fused_computation.25 | convolution fusion | flops 2041282560 | bytes 9007136 | tf_op jit(solution)/shard_map/conv_general_dilated | solution.py:18
  63.3 0.7 collective-permute-start.14
  64.1 1.3 %collective-permute-start.15 = (bf16[1,4,24,384]{3,2,1,0:T(8,128)(2,1)S(1)}, bf16[1,4,24,384]{3,2,1,0:T(8,128)(2,1)S(1)}, u32[]{:S(2)}, u32[]{:S(2)}) collective-permute-start(bf16[1,4,24,384]{3,2,1,0:T(8,128)(2,1)S(1)} %bitcast.146), channel_id=1, source_target_pairs={{24,0},{25,1},{26,2},{27,3},{28,4},{29,5},{30,6},{31,7}} | collective-permute-start | bytes 221192 | tf_op jit(solution)/shard_map/ppermute | solution.py:30
  65.5 10.1 %collective-permute-done.8 = bf16[1,4,24,384]{3,2,1,0:T(8,128)(2,1)S(1)} collective-permute-done((bf16[1,4,24,384]{3,2,1,0:T(8,128)(2,1)S(1)}, bf16[1,4,24,384]{3,2,1,0:T(8,128)(2,1)S(1)}, u32[]{:S(2)}, u32[]{:S(2)}) %collective-permute-start.8) | collective-permute-done | bytes 73760 | tf_op jit(solution)/shard_map/ppermute | solution.py:30
  75.6 15.7 %collective-permute-done.15 = bf16[1,4,24,384]{3,2,1,0:T(8,128)(2,1)S(1)} collective-permute-done((bf16[1,4,24,384]{3,2,1,0:T(8,128)(2,1)S(1)}, bf16[1,4,24,384]{3,2,1,0:T(8,128)(2,1)S(1)}, u32[]{:S(2)}, u32[]{:S(2)}) %collective-permute-start.15) | collective-permute-done | bytes 73760 | tf_op jit(solution)/shard_map/ppermute | solution.py:30
  91.3 0.7 add_convert_fusion
  (69 shorter events, 3.0 us)
Async XLA Ops:
  0.9 9.5 %collective-permute-start.1 = (bf16[4,1,24,384]{3,2,1,0:T(8,128)(2,1)S(1)}, bf16[4,1,24,384]{3,2,1,0:T(8,128)(2,1)S(1)}, u32[]{:S(2)}, u32[]{:S(2)}) collective-permute-start(bf16[4,1,24,384]{3,2,1,0:T(8,128)(2,1)S(1)} %get-tuple-element.15), channel_id=1, source_target_pairs={{1,0},{2,1},{3,2},{4,3},{5,4},{6,5},{7,6},{9,8},{10,9},{11,10},{12... | collective-permute-start | bytes 221192 | tf_op jit(solution)/shard_map/ppermute | solution.py:60
  3.5 7.0 %collective-permute-start = (bf16[4,1,24,384]{3,2,1,0:T(8,128)(2,1)S(1)}, bf16[4,1,24,384]{3,2,1,0:T(8,128)(2,1)S(1)}, u32[]{:S(2)}, u32[]{:S(2)}) collective-permute-start(bf16[4,1,24,384]{3,2,1,0:T(8,128)(2,1)S(1)} %get-tuple-element.14), channel_id=1, source_target_pairs={{0,1},{1,2},{2,3},{3,4},{4,5},{5,6},{6,7},{8,9},{9,10},{10,11},{11... | collective-permute-start | bytes 221192 | tf_op jit(solution)/shard_map/ppermute | solution.py:59
  10.9 0.7 copy-start.1
  11.5 22.2 %slice-start = ((s8[7962624]{0:T(1024)(128)(4,1)}), s8[4194304]{0:T(1024)(128)(4,1)S(1)}, s32[]{:S(2)}) async-start(s8[7962624]{0:T(1024)(128)(4,1)} %bitcast.147), calls=%async_computation | async-start | bytes 8388608
  11.6 22.0 %slice-start.1 = ((s8[7962624]{0:T(1024)(128)(4,1)}), s8[3768320]{0:T(1024)(128)(4,1)S(1)}, s32[]{:S(2)}) async-start(s8[7962624]{0:T(1024)(128)(4,1)} %bitcast.147), calls=%async_computation.1 | async-start | bytes 7536640
  20.2 12.3 %collective-permute-start.3 = (bf16[4,4,24,384]{3,2,1,0:T(8,128)(2,1)S(1)}, bf16[4,4,24,384]{3,2,1,0:T(8,128)(2,1)S(1)}, u32[]{:S(2)}, u32[]{:S(2)}) collective-permute-start(bf16[4,4,24,384]{3,2,1,0:T(8,128)(2,1)S(1)} %bitcast.134), channel_id=1, source_target_pairs={{0,8},{1,9},{2,10},{3,11},{4,12},{5,13},{6,14},{7,15}} | collective-permute-start | bytes 884744 | tf_op jit(solution)/shard_map/ppermute | solution.py:30
  23.5 8.3 %collective-permute-start.2 = (bf16[4,1,24,384]{3,2,1,0:T(8,128)(2,1)S(1)}, bf16[4,1,24,384]{3,2,1,0:T(8,128)(2,1)S(1)}, u32[]{:S(2)}, u32[]{:S(2)}) collective-permute-start(bf16[4,1,24,384]{3,2,1,0:T(8,128)(2,1)S(1)} %get-tuple-element.12), channel_id=1, source_target_pairs={{0,9},{1,10},{2,11},{3,12},{4,13},{5,14},{6,15}} | collective-permute-start | bytes 221192 | tf_op jit(solution)/shard_map/ppermute | solution.py:30
  26.0 6.5 %collective-permute-start.4 = (bf16[4,1,24,384]{3,2,1,0:T(8,128)(2,1)S(1)}, bf16[4,1,24,384]{3,2,1,0:T(8,128)(2,1)S(1)}, u32[]{:S(2)}, u32[]{:S(2)}) collective-permute-start(bf16[4,1,24,384]{3,2,1,0:T(8,128)(2,1)S(1)} %get-tuple-element.13), channel_id=1, source_target_pairs={{1,8},{2,9},{3,10},{4,11},{5,12},{6,13},{7,14}} | collective-permute-start | bytes 221192 | tf_op jit(solution)/shard_map/ppermute | solution.py:30
  33.7 6.0 %copy-start = (bf16[4,4,24,384]{3,2,1,0:T(8,128)(2,1)S(1)}, bf16[4,4,24,384]{3,2,1,0:T(8,128)(2,1)}, u32[]{:S(2)}) copy-start(bf16[4,4,24,384]{3,2,1,0:T(8,128)(2,1)} %param.3) | copy-start | bytes 884740
  39.8 2.3 %collective-permute-start.5 = (bf16[4,4,24,384]{3,2,1,0:T(8,128)(2,1)S(1)}, bf16[4,4,24,384]{3,2,1,0:T(8,128)(2,1)S(1)}, u32[]{:S(2)}, u32[]{:S(2)}) collective-permute-start(bf16[4,4,24,384]{3,2,1,0:T(8,128)(2,1)S(1)} %fusion.91), channel_id=1, source_target_pairs={{8,16},{9,17},{10,18},{11,19},{12,20},{13,21},{14,22},{15,23}} | collective-permute-start | bytes 884744 | tf_op jit(solution)/shard_map/ppermute | solution.py:30
  40.5 1.5 %collective-permute-start.10 = (bf16[4,1,24,384]{3,2,1,0:T(8,128)(2,1)S(1)}, bf16[4,1,24,384]{3,2,1,0:T(8,128)(2,1)S(1)}, u32[]{:S(2)}, u32[]{:S(2)}) collective-permute-start(bf16[4,1,24,384]{3,2,1,0:T(8,128)(2,1)S(1)} %get-tuple-element.8), channel_id=1, source_target_pairs={{9,16},{10,17},{11,18},{12,19},{13,20},{14,21},{15,22}} | collective-permute-start | bytes 221192 | tf_op jit(solution)/shard_map/ppermute | solution.py:30
  41.3 0.7 collective-permute-start.9
  49.2 4.8 %collective-permute-start.12 = (bf16[4,4,24,384]{3,2,1,0:T(8,128)(2,1)S(1)}, bf16[4,4,24,384]{3,2,1,0:T(8,128)(2,1)S(1)}, u32[]{:S(2)}, u32[]{:S(2)}) collective-permute-start(bf16[4,4,24,384]{3,2,1,0:T(8,128)(2,1)S(1)} %bitcast.132), channel_id=1, source_target_pairs={{16,24},{17,25},{18,26},{19,27},{20,28},{21,29},{22,30},{23,31}} | collective-permute-start | bytes 884744 | tf_op jit(solution)/shard_map/ppermute | solution.py:30
  49.9 2.7 %collective-permute-start.11 = (bf16[4,1,24,384]{3,2,1,0:T(8,128)(2,1)S(1)}, bf16[4,1,24,384]{3,2,1,0:T(8,128)(2,1)S(1)}, u32[]{:S(2)}, u32[]{:S(2)}) collective-permute-start(bf16[4,1,24,384]{3,2,1,0:T(8,128)(2,1)S(1)} %get-tuple-element.5), channel_id=1, source_target_pairs={{16,25},{17,26},{18,27},{19,28},{20,29},{21,30},{22,31}} | collective-permute-start | bytes 221192 | tf_op jit(solution)/shard_map/ppermute | solution.py:30
  50.6 3.4 %collective-permute-start.13 = (bf16[4,1,24,384]{3,2,1,0:T(8,128)(2,1)S(1)}, bf16[4,1,24,384]{3,2,1,0:T(8,128)(2,1)S(1)}, u32[]{:S(2)}, u32[]{:S(2)}) collective-permute-start(bf16[4,1,24,384]{3,2,1,0:T(8,128)(2,1)S(1)} %get-tuple-element.6), channel_id=1, source_target_pairs={{17,24},{18,25},{19,26},{20,27},{21,28},{22,29},{23,30}} | collective-permute-start | bytes 221192 | tf_op jit(solution)/shard_map/ppermute | solution.py:30
  51.3 12.8 %collective-permute-start.6 = (bf16[1,4,24,384]{3,2,1,0:T(8,128)(2,1)S(1)}, bf16[1,4,24,384]{3,2,1,0:T(8,128)(2,1)S(1)}, u32[]{:S(2)}, u32[]{:S(2)}) collective-permute-start(bf16[1,4,24,384]{3,2,1,0:T(8,128)(2,1)S(1)} %get-tuple-element.11), channel_id=1, source_target_pairs={{16,24},{17,25},{18,26},{19,27},{20,28},{21,29},{22,30},{23,31}} | collective-permute-start | bytes 221192 | tf_op jit(solution)/shard_map/ppermute | solution.py:30
  52.0 13.5 %collective-permute-start.7 = (bf16[1,4,24,384]{3,2,1,0:T(8,128)(2,1)S(1)}, bf16[1,4,24,384]{3,2,1,0:T(8,128)(2,1)S(1)}, u32[]{:S(2)}, u32[]{:S(2)}) collective-permute-start(bf16[1,4,24,384]{3,2,1,0:T(8,128)(2,1)S(1)} %get-tuple-element.10), channel_id=1, source_target_pairs={{16,8},{17,9},{18,10},{19,11},{20,12},{21,13},{22,14},{23,15}} | collective-permute-start | bytes 221192 | tf_op jit(solution)/shard_map/ppermute | solution.py:30
  52.6 23.0 %collective-permute-start.8 = (bf16[1,4,24,384]{3,2,1,0:T(8,128)(2,1)S(1)}, bf16[1,4,24,384]{3,2,1,0:T(8,128)(2,1)S(1)}, u32[]{:S(2)}, u32[]{:S(2)}) collective-permute-start(bf16[1,4,24,384]{3,2,1,0:T(8,128)(2,1)S(1)} %get-tuple-element.9), channel_id=1, source_target_pairs={{16,0},{17,1},{18,2},{19,3},{20,4},{21,5},{22,6},{23,7}} | collective-permute-start | bytes 221192 | tf_op jit(solution)/shard_map/ppermute | solution.py:30
  58.2 17.4 %collective-permute-start.16 = (bf16[1,4,24,384]{3,2,1,0:T(8,128)(2,1)S(1)}, bf16[1,4,24,384]{3,2,1,0:T(8,128)(2,1)S(1)}, u32[]{:S(2)}, u32[]{:S(2)}) collective-permute-start(bf16[1,4,24,384]{3,2,1,0:T(8,128)(2,1)S(1)} %bitcast.144), channel_id=1, source_target_pairs={{24,16},{25,17},{26,18},{27,19},{28,20},{29,21},{30,22},{31,23}} | collective-permute-start | bytes 221192 | tf_op jit(solution)/shard_map/ppermute | solution.py:30
  63.3 12.3 %collective-permute-start.14 = (bf16[1,4,24,384]{3,2,1,0:T(8,128)(2,1)S(1)}, bf16[1,4,24,384]{3,2,1,0:T(8,128)(2,1)S(1)}, u32[]{:S(2)}, u32[]{:S(2)}) collective-permute-start(bf16[1,4,24,384]{3,2,1,0:T(8,128)(2,1)S(1)} %bitcast.145), channel_id=1, source_target_pairs={{24,8},{25,9},{26,10},{27,11},{28,12},{29,13},{30,14},{31,15}} | collective-permute-start | bytes 221192 | tf_op jit(solution)/shard_map/ppermute | solution.py:30
  64.1 27.3 %collective-permute-start.15 = (bf16[1,4,24,384]{3,2,1,0:T(8,128)(2,1)S(1)}, bf16[1,4,24,384]{3,2,1,0:T(8,128)(2,1)S(1)}, u32[]{:S(2)}, u32[]{:S(2)}) collective-permute-start(bf16[1,4,24,384]{3,2,1,0:T(8,128)(2,1)S(1)} %bitcast.146), channel_id=1, source_target_pairs={{24,0},{25,1},{26,2},{27,3},{28,4},{29,5},{30,6},{31,7}} | collective-permute-start | bytes 221192 | tf_op jit(solution)/shard_map/ppermute | solution.py:30

commit v15 on v12

--- a/solution.py
+++ b/solution.py
@@ -15,25 +15,31 @@
 
 
 def causal_conv(window, kernel, before=2):
-    result = lax.conv_general_dilated(
-        window[None],
+    return batched_conv(window[None], kernel, before)[0]
+
+
+def batched_conv(windows, kernel, before=2):
+    return lax.conv_general_dilated(
+        windows,
         kernel,
         window_strides=(1, 1, 1),
         padding=((before, 0), (0, 0), (1, 1)),
         dimension_numbers=("NDHWC", "DHWIO", "NDHWC"),
         preferred_element_type=jnp.float32,
     )
-    return result[0]
 
 
 def send(value, pairs):
     return lax.ppermute(value, BOTH, pairs)
 
 
-def stage_send(value, stage, row_count):
+def stage_send(value, stage, row_count, edges_after=False):
     base, nxt = stage * row_count, (stage + 1) * row_count
     height = value.shape[1]
     body = send(value, [(base + r, nxt + r) for r in range(row_count)])
+    if edges_after:
+        tie = body[:1, :1, :1, :1].astype(jnp.float32) * 0
+        value = (value.astype(jnp.float32) + tie).astype(jnp.bfloat16)
     top = send(
         value[:, height - 1 :],
         [(base + r, nxt + r + 1) for r in range(row_count - 1)],
@@ -61,6 +67,7 @@
     current = features
     skip = features
     last_stage = segment_count - 1
+    split_rows = True
 
     for stage in range(segment_count):
         pieces = [top, current, bottom] if stage else [top, features, bottom]
@@ -97,7 +104,22 @@
                             segment_index == target, piece, branch
                         )
             break
-        produced = compute(window, skip)
+        if 0 < stage < last_stage and height >= 3 and split_rows:
+            inner = activate(current, gain_row)
+            middle = causal_conv(inner, kernel)
+            edges = jnp.stack(
+                [
+                    jnp.concatenate([activate(top, gain_row), inner[:, :2]], axis=1),
+                    jnp.concatenate([inner[:, height - 2 :], activate(bottom, gain_row)], axis=1),
+                ]
+            )
+            rims = batched_conv(edges, kernel)
+            convolved = jnp.concatenate([rims[0], middle, rims[1]], axis=1).astype(jnp.bfloat16)
+            if odd:
+                convolved = (skip.astype(jnp.float32) + convolved).astype(jnp.bfloat16)
+            produced = convolved
+        else:
+            produced = compute(window, skip)
         if stage == last_stage - 1:
             owned = current[stage * group : (stage + 1) * group]
             for target in range(segment_count):
@@ -108,7 +130,9 @@
                     piece = send(chunk, straight(stage, target))
                     owned = jnp.where(segment_index == target, piece, owned)
         next_skip = current if (not odd and stage > 0 and stage != last_stage - 1) else None
-        current, top, bottom = stage_send(produced, stage, row_count)
+        current, top, bottom = stage_send(
+            produced, stage, row_count, split_rows and height >= 3 and stage + 1 < last_stage
+        )
         if next_skip is not None:
             skip = send(next_skip, straight(stage, stage + 1))
         elif not odd:

time: 90.2 us -> 118 us (1.31)
  matrix products: 25.6 us -> 36 us
  waiting for transfers between devices: 28.5 us -> 36.1 us
  other arithmetic: 6.04 us -> 10.6 us
  local copies, waits for them, and re-layouts: 5.36 us -> 8.65 us
  between operations: 0.81 us -> 2.4 us
    conv_general_dilated x5 -> x7, matrix products: 25.6 us -> 36 us  [batched_conv(): lax.conv_general_dilated(windows, kernel, window_strides=(1, 1, 1), paddi...]
    ppermute x15, waiting for transfers between devices: 28.5 us -> 36.1 us  [send(): return lax.ppermute(value, BOTH, pairs)]
    conv_general_dilated x0 -> x2, other arithmetic: none -> 1.29 us  [batched_conv(): lax.conv_general_dilated(windows, kernel, window_strides=(1, 1, 1), paddi...]
    convert_element_type x6 -> x8, other arithmetic: 2.72 us -> 3.77 us  [activate(): return jax.nn.silu(widened * lax.rsqrt(mean_square + 1e-06) * gain_row.as...]
    reduce_sum x6 -> x10, other arithmetic: 1.76 us -> 2.59 us  [activate(): mean_square = jnp.mean(widened * widened, axis=-1, keepdims=True)]
  transfers between devices with their start and end apart: 17 -> 17, of which waited for: 3 -> 5; matrix products, arithmetic and copies ran while one was open for 13% -> 12% of each run, Pallas kernels for 0% -> 0%
where the time goes in v15:
time: 118 us; the launch traced here: 117 us
  waiting for transfers between devices  36.1 us (31%)
  matrix products  36 us (31%)
  starting transfers between devices  22.7 us (19%)
  other arithmetic  10.6 us (9%)
  local copies, waits for them, and re-layouts  8.65 us (7%)
  between operations  2.4 us (2%)
    ppermute x15, waiting for transfers between devices, send(): return lax.ppermute(value, BOTH, pairs)  36.1 us
    conv_general_dilated x7, matrix products, batched_conv(): lax.conv_general_dilated(windows, kernel, window_strides=(1, 1, 1), paddi...  36 us
    ppermute x15, starting transfers between devices, send(): return lax.ppermute(value, BOTH, pairs)  17.1 us
    convert_element_type x8, other arithmetic, activate(): return jax.nn.silu(widened * lax.rsqrt(mean_square + 1e-06) * gain_row.as...  3.77 us
    ppermute x1, starting transfers between devices, local(): top = lax.ppermute(features[:, height - 1:], 'rows', up)  3.02 us
    reduce_sum x10, other arithmetic, activate(): mean_square = jnp.mean(widened * widened, axis=-1, keepdims=True)  2.59 us
    ppermute x1, starting transfers between devices, local(): bottom = lax.ppermute(features[:, :1], 'rows', down)  2.58 us
  transfers between devices with their start and end apart: 17, of which 5 were waited for; matrix products, arithmetic and copies ran while one was open for 12% of the time, Pallas kernels for 0%

profile of v15, /device:TPU:17, one launch (start us, length us, event | category | flops | bytes accessed | tf_op | source)
XLA Modules:
  0.0 116.5 jit_solution(13020344646407433566)
XLA Ops:
  0.0 0.9 fusion.210
  0.9 2.6 %collective-permute-start.1 = (bf16[4,1,24,384]{3,2,1,0:T(8,128)(2,1)S(1)}, bf16[4,1,24,384]{3,2,1,0:T(8,128)(2,1)S(1)}, u32[]{:S(2)}, u32[]{:S(2)}) collective-permute-start(bf16[4,1,24,384]{3,2,1,0:T(8,128)(2,1)S(1)} %get-tuple-element.17), channel_id=1, source_target_pairs={{1,0},{2,1},{3,2},{4,3},{5,4},{6,5},{7,6},{9,8},{10,9},{11,10},{12... | collective-permute-start | bytes 221192 | tf_op jit(solution)/shard_map/ppermute | solution.py:66
  3.5 3.0 %collective-permute-start = (bf16[4,1,24,384]{3,2,1,0:T(8,128)(2,1)S(1)}, bf16[4,1,24,384]{3,2,1,0:T(8,128)(2,1)S(1)}, u32[]{:S(2)}, u32[]{:S(2)}) collective-permute-start(bf16[4,1,24,384]{3,2,1,0:T(8,128)(2,1)S(1)} %get-tuple-element.16), channel_id=1, source_target_pairs={{0,1},{1,2},{2,3},{3,4},{4,5},{5,6},{6,7},{8,9},{9,10},{10,11},{11... | collective-permute-start | bytes 221192 | tf_op jit(solution)/shard_map/ppermute | solution.py:65
  6.6 1.1 fusion.111
  7.7 0.7 convert_reduce_fusion
  8.4 1.2 %fusion.118 = bf16[4,4,24,384]{3,2,1,0:T(8,128)(2,1)S(1)} fusion(bf16[4,4,24,384]{3,2,1,0:T(8,128)(2,1)} %param.3, f32[384]{0:T(512)S(1)} %convert_reduce_fusion, f32[4,4,24]{2,1,0:T(4,128)S(1)} %add_rsqrt_fusion.3), kind=kLoop, calls=%fused_computation.101 | loop fusion | flops 1179648 | bytes 592896 | tf_op jit(solution)/shard_map/convert_element_type | solution.py:14
  10.7 0.2 copy-done.1
  10.9 8.3 %fusion.22 = bf16[4,4,8,4,384]{4,2,3,1,0:T(8,128)(2,1)S(1)} fusion(bf16[1,3,3,3,384,384]{5,4,3,2,1,0:T(8,128)(2,1)} %param.5, bf16[4,6,1,7,2,384]{5,3,4,1,0,2:T(8,128)(2,1)S(1)} %slice.143, bf16[4,6,1,8,4,384]{5,3,4,1,0,2:T(8,128)(2,1)S(1)} %copy.133, pred[8,4]{0,1:T(4,128)(4,1)S(1)} %copy-done.1), kind=kOutput, calls=%fused_computation.24 | convolution fusion | flops 3060695040 | bytes 9203744 | tf_op jit(solution)/shard_map/conv_general_dilated | solution.py:22
  19.6 0.7 collective-permute-start.2
  20.4 0.3 fusion.214
  21.1 3.0 %fusion.70 = bf16[4,2,8,4,384]{4,2,3,1,0:T(8,128)(2,1)S(1)} fusion(bf16[1,3,3,3,384,384]{5,4,3,2,1,0:T(8,128)(2,1)S(1)} %bitcast.173, bf16[4,4,1,7,2,384]{5,3,4,1,0,2:T(8,128)(2,1)S(1)} %slice.153, bf16[4,4,1,8,4,384]{5,3,4,1,0,2:T(8,128)(2,1)S(1)} %copy.141, pred[8,4]{0,1:T(4,128)(4,1)S(1)} %copy-done.1), kind=kOutput, calls=%fused_computation.50 | convolution fusion | flops 1530789888 | bytes 8724512 | tf_op jit(solution)/shard_map/conv_general_dilated | solution.py:22
  24.1 0.5 slice.145
  25.4 0.7 collective-permute-start.4
  26.0 0.2 fusion.102
  26.6 0.8 collective-permute-start.3
  28.5 0.6 fusion.51
  29.2 6.2 %fusion.58 = bf16[4,1,16,4,384]{4,2,3,1,0:T(8,128)(2,1)S(1)} fusion(bf16[1,3,3,3,384,384]{5,4,3,2,1,0:T(8,128)(2,1)} %param.5, bf16[4,3,2,8,6,384]{5,4,3,1,0,2:T(8,128)(2,1)S(1)} %fusion.51, pred[16,4]{0,1:T(4,128)(4,1)S(1)} %copy-done.2), kind=kOutput, calls=%fused_computation.46 | convolution fusion | flops 1529020416 | bytes 9044032 | tf_op jit(solution)/shard_map/conv_general_dilated | solution.py:22
  35.7 0.6 copy-done
  36.4 1.3 %collective-permute-start.5 = (bf16[4,4,24,384]{3,2,1,0:T(8,128)(2,1)S(1)}, bf16[4,4,24,384]{3,2,1,0:T(8,128)(2,1)S(1)}, u32[]{:S(2)}, u32[]{:S(2)}) collective-permute-start(bf16[4,4,24,384]{3,2,1,0:T(8,128)(2,1)S(1)} %fusion.119), channel_id=1, source_target_pairs={{8,16},{9,17},{10,18},{11,19},{12,20},{13,21},{14,22},{15,23}} | collective-permute-start | bytes 884744 | tf_op jit(solution)/shard_map/ppermute | solution.py:33
  37.7 21.5 %collective-permute-done.5 = bf16[4,4,24,384]{3,2,1,0:T(8,128)(2,1)S(1)} collective-permute-done((bf16[4,4,24,384]{3,2,1,0:T(8,128)(2,1)S(1)}, bf16[4,4,24,384]{3,2,1,0:T(8,128)(2,1)S(1)}, u32[]{:S(2)}, u32[]{:S(2)}) %collective-permute-start.5) | collective-permute-done | bytes 294944 | tf_op jit(solution)/shard_map/ppermute | solution.py:33
  59.4 0.3 fusion.213
  60.0 6.2 %fusion.67 = bf16[4,2,8,4,384]{4,2,3,1,0:T(8,128)(2,1)S(1)} fusion(bf16[1,3,3,3,384,384]{5,4,3,2,1,0:T(8,128)(2,1)} %param.5, bf16[4,4,1,7,2,384]{5,3,4,1,0,2:T(8,128)(2,1)S(1)} %slice.169, bf16[4,4,1,8,4,384]{5,3,4,1,0,2:T(8,128)(2,1)S(1)} %copy.151, pred[8,4]{0,1:T(4,128)(4,1)S(1)} %copy-done.1), kind=kOutput, calls=%fused_computation.49 | convolution fusion | flops 1530789888 | bytes 8724512 | tf_op jit(solution)/shard_map/conv_general_dilated | solution.py:22
  66.4 0.2 fusion.110
  66.7 0.5 slice.160
  68.0 1.3 %collective-permute-start.10 = (bf16[4,1,24,384]{3,2,1,0:T(8,128)(2,1)S(1)}, bf16[4,1,24,384]{3,2,1,0:T(8,128)(2,1)S(1)}, u32[]{:S(2)}, u32[]{:S(2)}) collective-permute-start(bf16[4,1,24,384]{3,2,1,0:T(8,128)(2,1)S(1)} %get-tuple-element.6), channel_id=1, source_target_pairs={{9,16},{10,17},{11,18},{12,19},{13,20},{14,21},{15,22}} | collective-permute-start | bytes 221192 | tf_op jit(solution)/shard_map/ppermute | solution.py:33
  69.4 1.5 %collective-permute-start.9 = (bf16[4,1,24,384]{3,2,1,0:T(8,128)(2,1)S(1)}, bf16[4,1,24,384]{3,2,1,0:T(8,128)(2,1)S(1)}, u32[]{:S(2)}, u32[]{:S(2)}) collective-permute-start(bf16[4,1,24,384]{3,2,1,0:T(8,128)(2,1)S(1)} %get-tuple-element.5), channel_id=1, source_target_pairs={{8,17},{9,18},{10,19},{11,20},{12,21},{13,22},{14,23}} | collective-permute-start | bytes 221192 | tf_op jit(solution)/shard_map/ppermute | solution.py:33
  70.9 3.6 %collective-permute-done.10 = bf16[4,1,24,384]{3,2,1,0:T(8,128)(2,1)S(1)} collective-permute-done((bf16[4,1,24,384]{3,2,1,0:T(8,128)(2,1)S(1)}, bf16[4,1,24,384]{3,2,1,0:T(8,128)(2,1)S(1)}, u32[]{:S(2)}, u32[]{:S(2)}) %collective-permute-start.10) | collective-permute-done | bytes 73760 | tf_op jit(solution)/shard_map/ppermute | solution.py:33
  74.6 0.4 collective-permute-done.9
  76.0 0.6 fusion.52
  76.6 6.5 %fusion.55 = bf16[4,1,16,4,384]{4,2,3,1,0:T(8,128)(2,1)S(1)} fusion(bf16[1,3,3,3,384,384]{5,4,3,2,1,0:T(8,128)(2,1)} %param.5, bf16[4,3,2,8,6,384]{5,4,3,1,0,2:T(8,128)(2,1)S(1)} %fusion.52, pred[16,4]{0,1:T(4,128)(4,1)S(1)} %copy-done.2), kind=kOutput, calls=%fused_computation.45 | convolution fusion | flops 1529020416 | bytes 9044032 | tf_op jit(solution)/shard_map/conv_general_dilated | solution.py:22
  83.7 0.5 pad_maximum_fusion.1
  84.2 1.3 %collective-permute-start.12 = (bf16[4,4,24,384]{3,1,2,0:T(4,128)(2,1)S(1)}, bf16[4,4,24,384]{3,1,2,0:T(4,128)(2,1)S(1)}, u32[]{:S(2)}, u32[]{:S(2)}) collective-permute-start(bf16[4,4,24,384]{3,1,2,0:T(4,128)(2,1)S(1)} %pad_maximum_fusion.1), channel_id=1, source_target_pairs={{16,24},{17,25},{18,26},{19,27},{20,28},{21,29},{22,30},{23,31}} | collective-permute-start | bytes 884744 | tf_op jit(solution)/shard_map/ppermute | solution.py:33
  85.5 1.3 %collective-permute-start.11 = (bf16[4,1,24,384]{3,0,2,1:T(4,128)(2,1)S(1)}, bf16[4,1,24,384]{3,0,2,1:T(4,128)(2,1)S(1)}, u32[]{:S(2)}, u32[]{:S(2)}) collective-permute-start(bf16[4,1,24,384]{3,0,2,1:T(4,128)(2,1)S(1)} %get-tuple-element.22), channel_id=1, source_target_pairs={{16,25},{17,26},{18,27},{19,28},{20,29},{21,30},{22,31}} | collective-permute-start | bytes 221192 | tf_op jit(solution)/shard_map/ppermute | solution.py:33
  86.8 1.3 %collective-permute-start.13 = (bf16[4,1,24,384]{3,0,2,1:T(4,128)(2,1)S(1)}, bf16[4,1,24,384]{3,0,2,1:T(4,128)(2,1)S(1)}, u32[]{:S(2)}, u32[]{:S(2)}) collective-permute-start(bf16[4,1,24,384]{3,0,2,1:T(4,128)(2,1)S(1)} %get-tuple-element.23), channel_id=1, source_target_pairs={{17,24},{18,25},{19,26},{20,27},{21,28},{22,29},{23,30}} | collective-permute-start | bytes 221192 | tf_op jit(solution)/shard_map/ppermute | solution.py:33
  88.2 1.3 %collective-permute-start.6 = (bf16[1,4,24,384]{3,2,1,0:T(8,128)(2,1)S(1)}, bf16[1,4,24,384]{3,2,1,0:T(8,128)(2,1)S(1)}, u32[]{:S(2)}, u32[]{:S(2)}) collective-permute-start(bf16[1,4,24,384]{3,2,1,0:T(8,128)(2,1)S(1)} %get-tuple-element.11), channel_id=1, source_target_pairs={{16,24},{17,25},{18,26},{19,27},{20,28},{21,29},{22,30},{23,31}} | collective-permute-start | bytes 221192 | tf_op jit(solution)/shard_map/ppermute | solution.py:33
  89.5 1.5 %collective-permute-start.7 = (bf16[1,4,24,384]{3,2,1,0:T(8,128)(2,1)S(1)}, bf16[1,4,24,384]{3,2,1,0:T(8,128)(2,1)S(1)}, u32[]{:S(2)}, u32[]{:S(2)}) collective-permute-start(bf16[1,4,24,384]{3,2,1,0:T(8,128)(2,1)S(1)} %get-tuple-element.10), channel_id=1, source_target_pairs={{16,8},{17,9},{18,10},{19,11},{20,12},{21,13},{22,14},{23,15}} | collective-permute-start | bytes 221192 | tf_op jit(solution)/shard_map/ppermute | solution.py:33
  90.9 1.3 %collective-permute-done.11 = bf16[4,1,24,384]{3,0,2,1:T(4,128)(2,1)S(1)} collective-permute-done((bf16[4,1,24,384]{3,0,2,1:T(4,128)(2,1)S(1)}, bf16[4,1,24,384]{3,0,2,1:T(4,128)(2,1)S(1)}, u32[]{:S(2)}, u32[]{:S(2)}) %collective-permute-start.11) | collective-permute-done | bytes 73760 | tf_op jit(solution)/shard_map/ppermute | solution.py:33
  92.2 1.3 %collective-permute-start.8 = (bf16[1,4,24,384]{3,2,1,0:T(8,128)(2,1)S(1)}, bf16[1,4,24,384]{3,2,1,0:T(8,128)(2,1)S(1)}, u32[]{:S(2)}, u32[]{:S(2)}) collective-permute-start(bf16[1,4,24,384]{3,2,1,0:T(8,128)(2,1)S(1)} %get-tuple-element.9), channel_id=1, source_target_pairs={{16,0},{17,1},{18,2},{19,3},{20,4},{21,5},{22,6},{23,7}} | collective-permute-start | bytes 221192 | tf_op jit(solution)/shard_map/ppermute | solution.py:33
  94.0 0.6 fusion.43
  94.7 0.8 fusion.50
  96.0 2.9 %fusion.61 = bf16[2,4,8,4,384]{4,2,3,1,0:T(8,128)(2,1)S(1)} fusion(bf16[1,3,3,3,384,384]{5,4,3,2,1,0:T(8,128)(2,1)S(1)} %bitcast.175, bf16[4,6,1,7,2,384]{5,3,4,1,0,2:T(8,128)(2,1)S(1)} %slice.176, bf16[4,6,1,8,4,384]{5,3,4,1,0,2:T(8,128)(2,1)S(1)} %copy.168, pred[8,4]{0,1:T(4,128)(4,1)S(1)} %copy-done.1), kind=kOutput, calls=%fused_computation.47 | convolution fusion | flops 2041282560 | bytes 9007136 | tf_op jit(solution)/shard_map/conv_general_dilated | solution.py:22
  99.1 0.7 collective-permute-start.15
  99.9 0.9 collective-permute-start.16
  100.8 0.8 fusion.121
  102.0 2.9 %fusion.64 = bf16[2,4,8,4,384]{4,2,3,1,0:T(8,128)(2,1)S(1)} fusion(bf16[1,3,3,3,384,384]{5,4,3,2,1,0:T(8,128)(2,1)S(1)} %bitcast.175, bf16[4,6,1,7,2,384]{5,3,4,1,0,2:T(8,128)(2,1)S(1)} %slice.171, bf16[4,6,1,8,4,384]{5,3,4,1,0,2:T(8,128)(2,1)S(1)} %copy.161, pred[8,4]{0,1:T(4,128)(4,1)S(1)} %copy-done.1), kind=kOutput, calls=%fused_computation.48 | convolution fusion | flops 2041282560 | bytes 9007136 | tf_op jit(solution)/shard_map/conv_general_dilated | solution.py:22
  105.1 1.3 %collective-permute-start.14 = (bf16[1,4,24,384]{3,2,1,0:T(8,128)(2,1)S(1)}, bf16[1,4,24,384]{3,2,1,0:T(8,128)(2,1)S(1)}, u32[]{:S(2)}, u32[]{:S(2)}) collective-permute-start(bf16[1,4,24,384]{3,2,1,0:T(8,128)(2,1)S(1)} %bitcast.171), channel_id=1, source_target_pairs={{24,16},{25,17},{26,18},{27,19},{28,20},{29,21},{30,22},{31,23}} | collective-permute-start | bytes 221192 | tf_op jit(solution)/shard_map/ppermute | solution.py:33
  106.6 9.3 %collective-permute-done.14 = bf16[1,4,24,384]{3,2,1,0:T(8,128)(2,1)S(1)} collective-permute-done((bf16[1,4,24,384]{3,2,1,0:T(8,128)(2,1)S(1)}, bf16[1,4,24,384]{3,2,1,0:T(8,128)(2,1)S(1)}, u32[]{:S(2)}, u32[]{:S(2)}) %collective-permute-start.14) | collective-permute-done | bytes 73760 | tf_op jit(solution)/shard_map/ppermute | solution.py:33
  115.8 0.7 add_convert_fusion.2
  (121 shorter events, 7.8 us)
Async XLA Ops:
  0.9 8.7 %collective-permute-start.1 = (bf16[4,1,24,384]{3,2,1,0:T(8,128)(2,1)S(1)}, bf16[4,1,24,384]{3,2,1,0:T(8,128)(2,1)S(1)}, u32[]{:S(2)}, u32[]{:S(2)}) collective-permute-start(bf16[4,1,24,384]{3,2,1,0:T(8,128)(2,1)S(1)} %get-tuple-element.17), channel_id=1, source_target_pairs={{1,0},{2,1},{3,2},{4,3},{5,4},{6,5},{7,6},{9,8},{10,9},{11,10},{12... | collective-permute-start | bytes 221192 | tf_op jit(solution)/shard_map/ppermute | solution.py:66
  3.5 6.2 %collective-permute-start = (bf16[4,1,24,384]{3,2,1,0:T(8,128)(2,1)S(1)}, bf16[4,1,24,384]{3,2,1,0:T(8,128)(2,1)S(1)}, u32[]{:S(2)}, u32[]{:S(2)}) collective-permute-start(bf16[4,1,24,384]{3,2,1,0:T(8,128)(2,1)S(1)} %get-tuple-element.16), channel_id=1, source_target_pairs={{0,1},{1,2},{2,3},{3,4},{4,5},{5,6},{6,7},{8,9},{9,10},{10,11},{11... | collective-permute-start | bytes 221192 | tf_op jit(solution)/shard_map/ppermute | solution.py:65
  10.3 0.7 copy-start.1
  10.6 10.5 %slice-start = ((s8[7962624]{0:T(1024)(128)(4,1)}), s8[4194304]{0:T(1024)(128)(4,1)S(1)}, s32[]{:S(2)}) async-start(s8[7962624]{0:T(1024)(128)(4,1)} %bitcast.172), calls=%async_computation | async-start | bytes 8388608
  10.9 10.2 %slice-start.1 = ((s8[7962624]{0:T(1024)(128)(4,1)}), s8[3768320]{0:T(1024)(128)(4,1)S(1)}, s32[]{:S(2)}) async-start(s8[7962624]{0:T(1024)(128)(4,1)} %bitcast.172), calls=%async_computation.1 | async-start | bytes 7536640
  19.6 0.7 collective-permute-start.2
  25.4 2.1 %collective-permute-start.4 = (bf16[4,1,24,384]{3,2,1,0:T(8,128)(2,1)S(1)}, bf16[4,1,24,384]{3,2,1,0:T(8,128)(2,1)S(1)}, u32[]{:S(2)}, u32[]{:S(2)}) collective-permute-start(bf16[4,1,24,384]{3,2,1,0:T(8,128)(2,1)S(1)} %get-tuple-element.13), channel_id=1, source_target_pairs={{1,8},{2,9},{3,10},{4,11},{5,12},{6,13},{7,14}} | collective-permute-start | bytes 221192 | tf_op jit(solution)/shard_map/ppermute | solution.py:33
  26.6 1.0 collective-permute-start.3
  28.3 0.9 copy-start.2
  35.4 1.0 copy-start
  36.4 22.8 %collective-permute-start.5 = (bf16[4,4,24,384]{3,2,1,0:T(8,128)(2,1)S(1)}, bf16[4,4,24,384]{3,2,1,0:T(8,128)(2,1)S(1)}, u32[]{:S(2)}, u32[]{:S(2)}) collective-permute-start(bf16[4,4,24,384]{3,2,1,0:T(8,128)(2,1)S(1)} %fusion.119), channel_id=1, source_target_pairs={{8,16},{9,17},{10,18},{11,19},{12,20},{13,21},{14,22},{15,23}} | collective-permute-start | bytes 884744 | tf_op jit(solution)/shard_map/ppermute | solution.py:33
  68.0 6.6 %collective-permute-start.10 = (bf16[4,1,24,384]{3,2,1,0:T(8,128)(2,1)S(1)}, bf16[4,1,24,384]{3,2,1,0:T(8,128)(2,1)S(1)}, u32[]{:S(2)}, u32[]{:S(2)}) collective-permute-start(bf16[4,1,24,384]{3,2,1,0:T(8,128)(2,1)S(1)} %get-tuple-element.6), channel_id=1, source_target_pairs={{9,16},{10,17},{11,18},{12,19},{13,20},{14,21},{15,22}} | collective-permute-start | bytes 221192 | tf_op jit(solution)/shard_map/ppermute | solution.py:33
  69.4 5.7 %collective-permute-start.9 = (bf16[4,1,24,384]{3,2,1,0:T(8,128)(2,1)S(1)}, bf16[4,1,24,384]{3,2,1,0:T(8,128)(2,1)S(1)}, u32[]{:S(2)}, u32[]{:S(2)}) collective-permute-start(bf16[4,1,24,384]{3,2,1,0:T(8,128)(2,1)S(1)} %get-tuple-element.5), channel_id=1, source_target_pairs={{8,17},{9,18},{10,19},{11,20},{12,21},{13,22},{14,23}} | collective-permute-start | bytes 221192 | tf_op jit(solution)/shard_map/ppermute | solution.py:33
  76.0 20.0 %slice-start.2 = ((s8[7962624]{0:T(1024)(128)(4,1)}), s8[4194304]{0:T(1024)(128)(4,1)S(1)}, s32[]{:S(2)}) async-start(s8[7962624]{0:T(1024)(128)(4,1)} %bitcast.174), calls=%async_computation.2 | async-start | bytes 8388608
  76.6 19.4 %slice-start.3 = ((s8[7962624]{0:T(1024)(128)(4,1)}), s8[3768320]{0:T(1024)(128)(4,1)S(1)}, s32[]{:S(2)}) async-start(s8[7962624]{0:T(1024)(128)(4,1)} %bitcast.174), calls=%async_computation.3 | async-start | bytes 7536640
  84.2 9.8 %collective-permute-start.12 = (bf16[4,4,24,384]{3,1,2,0:T(4,128)(2,1)S(1)}, bf16[4,4,24,384]{3,1,2,0:T(4,128)(2,1)S(1)}, u32[]{:S(2)}, u32[]{:S(2)}) collective-permute-start(bf16[4,4,24,384]{3,1,2,0:T(4,128)(2,1)S(1)} %pad_maximum_fusion.1), channel_id=1, source_target_pairs={{16,24},{17,25},{18,26},{19,27},{20,28},{21,29},{22,30},{23,31}} | collective-permute-start | bytes 884744 | tf_op jit(solution)/shard_map/ppermute | solution.py:33
  85.5 6.7 %collective-permute-start.11 = (bf16[4,1,24,384]{3,0,2,1:T(4,128)(2,1)S(1)}, bf16[4,1,24,384]{3,0,2,1:T(4,128)(2,1)S(1)}, u32[]{:S(2)}, u32[]{:S(2)}) collective-permute-start(bf16[4,1,24,384]{3,0,2,1:T(4,128)(2,1)S(1)} %get-tuple-element.22), channel_id=1, source_target_pairs={{16,25},{17,26},{18,27},{19,28},{20,29},{21,30},{22,31}} | collective-permute-start | bytes 221192 | tf_op jit(solution)/shard_map/ppermute | solution.py:33
  86.8 6.8 %collective-permute-start.13 = (bf16[4,1,24,384]{3,0,2,1:T(4,128)(2,1)S(1)}, bf16[4,1,24,384]{3,0,2,1:T(4,128)(2,1)S(1)}, u32[]{:S(2)}, u32[]{:S(2)}) collective-permute-start(bf16[4,1,24,384]{3,0,2,1:T(4,128)(2,1)S(1)} %get-tuple-element.23), channel_id=1, source_target_pairs={{17,24},{18,25},{19,26},{20,27},{21,28},{22,29},{23,30}} | collective-permute-start | bytes 221192 | tf_op jit(solution)/shard_map/ppermute | solution.py:33
  88.2 16.9 %collective-permute-start.6 = (bf16[1,4,24,384]{3,2,1,0:T(8,128)(2,1)S(1)}, bf16[1,4,24,384]{3,2,1,0:T(8,128)(2,1)S(1)}, u32[]{:S(2)}, u32[]{:S(2)}) collective-permute-start(bf16[1,4,24,384]{3,2,1,0:T(8,128)(2,1)S(1)} %get-tuple-element.11), channel_id=1, source_target_pairs={{16,24},{17,25},{18,26},{19,27},{20,28},{21,29},{22,30},{23,31}} | collective-permute-start | bytes 221192 | tf_op jit(solution)/shard_map/ppermute | solution.py:33
  89.5 17.1 %collective-permute-start.7 = (bf16[1,4,24,384]{3,2,1,0:T(8,128)(2,1)S(1)}, bf16[1,4,24,384]{3,2,1,0:T(8,128)(2,1)S(1)}, u32[]{:S(2)}, u32[]{:S(2)}) collective-permute-start(bf16[1,4,24,384]{3,2,1,0:T(8,128)(2,1)S(1)} %get-tuple-element.10), channel_id=1, source_target_pairs={{16,8},{17,9},{18,10},{19,11},{20,12},{21,13},{22,14},{23,15}} | collective-permute-start | bytes 221192 | tf_op jit(solution)/shard_map/ppermute | solution.py:33
  92.2 14.3 %collective-permute-start.8 = (bf16[1,4,24,384]{3,2,1,0:T(8,128)(2,1)S(1)}, bf16[1,4,24,384]{3,2,1,0:T(8,128)(2,1)S(1)}, u32[]{:S(2)}, u32[]{:S(2)}) collective-permute-start(bf16[1,4,24,384]{3,2,1,0:T(8,128)(2,1)S(1)} %get-tuple-element.9), channel_id=1, source_target_pairs={{16,0},{17,1},{18,2},{19,3},{20,4},{21,5},{22,6},{23,7}} | collective-permute-start | bytes 221192 | tf_op jit(solution)/shard_map/ppermute | solution.py:33
  99.1 7.5 %collective-permute-start.15 = (bf16[1,4,24,384]{3,2,1,0:T(8,128)(2,1)S(1)}, bf16[1,4,24,384]{3,2,1,0:T(8,128)(2,1)S(1)}, u32[]{:S(2)}, u32[]{:S(2)}) collective-permute-start(bf16[1,4,24,384]{3,2,1,0:T(8,128)(2,1)S(1)} %bitcast.169), channel_id=1, source_target_pairs={{24,8},{25,9},{26,10},{27,11},{28,12},{29,13},{30,14},{31,15}} | collective-permute-start | bytes 221192 | tf_op jit(solution)/shard_map/ppermute | solution.py:33
  99.9 6.7 %collective-permute-start.16 = (bf16[1,4,24,384]{3,2,1,0:T(8,128)(2,1)S(1)}, bf16[1,4,24,384]{3,2,1,0:T(8,128)(2,1)S(1)}, u32[]{:S(2)}, u32[]{:S(2)}) collective-permute-start(bf16[1,4,24,384]{3,2,1,0:T(8,128)(2,1)S(1)} %bitcast.170), channel_id=1, source_target_pairs={{24,0},{25,1},{26,2},{27,3},{28,4},{29,5},{30,6},{31,7}} | collective-permute-start | bytes 221192 | tf_op jit(solution)/shard_map/ppermute | solution.py:33
  105.1 10.7 %collective-permute-start.14 = (bf16[1,4,24,384]{3,2,1,0:T(8,128)(2,1)S(1)}, bf16[1,4,24,384]{3,2,1,0:T(8,128)(2,1)S(1)}, u32[]{:S(2)}, u32[]{:S(2)}) collective-permute-start(bf16[1,4,24,384]{3,2,1,0:T(8,128)(2,1)S(1)} %bitcast.171), channel_id=1, source_target_pairs={{24,16},{25,17},{26,18},{27,19},{28,20},{29,21},{30,22},{31,23}} | collective-permute-start | bytes 221192 | tf_op jit(solution)/shard_map/ppermute | solution.py:33

commit v16 on v12

--- a/solution.py
+++ b/solution.py
@@ -61,6 +61,7 @@
     current = features
     skip = features
     last_stage = segment_count - 1
+    early = {}
 
     for stage in range(segment_count):
         pieces = [top, current, bottom] if stage else [top, features, bottom]
@@ -98,12 +99,19 @@
                         )
             break
         produced = compute(window, skip)
+        if stage == last_stage - 2:
+            early = {}
+            for target in range(stage + 1):
+                chunk = produced[target * group : (target + 1) * group]
+                early[target] = chunk if target == stage else send(chunk, straight(stage, target))
         if stage == last_stage - 1:
             owned = current[stage * group : (stage + 1) * group]
             for target in range(segment_count):
                 chunk = current[target * group : (target + 1) * group]
                 if stage == 0:
                     owned = jnp.where(segment_index == target, chunk, owned)
+                elif target in early:
+                    owned = jnp.where(segment_index == target, early[target], owned)
                 elif target != stage:
                     piece = send(chunk, straight(stage, target))
                     owned = jnp.where(segment_index == target, piece, owned)

time: 90.2 us -> 90.3 us (level); the launches traced: 88.6 us -> 89.9 us
  waiting for transfers between devices: 28.5 us -> 31.7 us
  starting transfers between devices: 22.3 us -> 20.4 us
    ppermute x15 -> x14, waiting for transfers between devices: 28.5 us -> 31.7 us  [send(): return lax.ppermute(value, BOTH, pairs)]
    ppermute x15 -> x14, starting transfers between devices: 16.7 us -> 14.8 us  [send(): return lax.ppermute(value, BOTH, pairs)]
  transfers between devices with their start and end apart: 17 -> 16, of which waited for: 3 -> 5; matrix products, arithmetic and copies ran while one was open for 13% -> 13% of each run, Pallas kernels for 0% -> 0%
where the time goes in v16:
time: 90.3 us; the launch traced here: 89.9 us
  waiting for transfers between devices  31.7 us (35%)
  matrix products  25.6 us (28%)
  starting transfers between devices  20.4 us (23%)
  other arithmetic  6.04 us (7%)
  local copies, waits for them, and re-layouts  5.35 us (6%)
    ppermute x14, waiting for transfers between devices, send(): return lax.ppermute(value, BOTH, pairs)  31.7 us
    conv_general_dilated x5, matrix products, causal_conv(): lax.conv_general_dilated(window[None], kernel, window_strides=(1, 1, 1),...  25.6 us
    ppermute x14, starting transfers between devices, send(): return lax.ppermute(value, BOTH, pairs)  14.8 us
    ppermute x1, starting transfers between devices, local(): top = lax.ppermute(features[:, height - 1:], 'rows', up)  3.02 us
    convert_element_type x6, other arithmetic, activate(): return jax.nn.silu(widened * lax.rsqrt(mean_square + 1e-06) * gain_row.as...  2.72 us
    ppermute x1, starting transfers between devices, local(): bottom = lax.ppermute(features[:, :1], 'rows', down)  2.58 us
  transfers between devices with their start and end apart: 16, of which 5 were waited for; matrix products, arithmetic and copies ran while one was open for 13% of the time, Pallas kernels for 0%

profile of v16, /device:TPU:17, one launch (start us, length us, event | category | flops | bytes accessed | tf_op | source)
XLA Modules:
  0.0 89.9 jit_solution(4859541667117603135)
XLA Ops:
  0.0 0.9 %fusion.138 = (bf16[4,1,24,384]{3,2,1,0:T(8,128)(2,1)S(1)}, bf16[4,1,24,384]{3,2,1,0:T(8,128)(2,1)S(1)}) fusion(bf16[4,4,24,384]{3,2,1,0:T(8,128)(2,1)} %param.3), kind=kLoop, calls=%fused_computation.147 | loop fusion | bytes 294912 | tf_op jit(solution)/shard_map/slice | solution.py:59
  0.9 2.6 %collective-permute-start.1 = (bf16[4,1,24,384]{3,2,1,0:T(8,128)(2,1)S(1)}, bf16[4,1,24,384]{3,2,1,0:T(8,128)(2,1)S(1)}, u32[]{:S(2)}, u32[]{:S(2)}) collective-permute-start(bf16[4,1,24,384]{3,2,1,0:T(8,128)(2,1)S(1)} %get-tuple-element.12), channel_id=1, source_target_pairs={{1,0},{2,1},{3,2},{4,3},{5,4},{6,5},{7,6},{9,8},{10,9},{11,10},{12... | collective-permute-start | bytes 221192 | tf_op jit(solution)/shard_map/ppermute | solution.py:60
  3.5 3.0 %collective-permute-start = (bf16[4,1,24,384]{3,2,1,0:T(8,128)(2,1)S(1)}, bf16[4,1,24,384]{3,2,1,0:T(8,128)(2,1)S(1)}, u32[]{:S(2)}, u32[]{:S(2)}) collective-permute-start(bf16[4,1,24,384]{3,2,1,0:T(8,128)(2,1)S(1)} %get-tuple-element.11), channel_id=1, source_target_pairs={{0,1},{1,2},{2,3},{3,4},{4,5},{5,6},{6,7},{8,9},{9,10},{10,11},{11... | collective-permute-start | bytes 221192 | tf_op jit(solution)/shard_map/ppermute | solution.py:59
  6.6 1.1 %fusion.83 = f32[4,4,24]{2,1,0:T(4,128)S(1)} fusion(bf16[4,4,24,384]{3,2,1,0:T(8,128)(2,1)} %param.3), kind=kLoop, calls=%fused_computation.70 | loop fusion | flops 441984 | bytes 296448 | tf_op jit(solution)/shard_map/reduce_sum | solution.py:11
  7.7 0.7 convert_reduce_fusion
  8.4 1.2 %fusion.90 = bf16[4,4,24,384]{3,2,1,0:T(8,128)(2,1)S(1)} fusion(bf16[4,4,24,384]{3,2,1,0:T(8,128)(2,1)} %param.3, f32[384]{0:T(512)S(1)} %convert_reduce_fusion, f32[4,4,24]{2,1,0:T(4,128)S(1)} %add_rsqrt_fusion.3), kind=kLoop, calls=%fused_computation.77 | loop fusion | flops 1179648 | bytes 592896 | tf_op jit(solution)/shard_map/convert_element_type | solution.py:14
  10.1 0.2 copy.156
  10.3 0.2 pad.5.clone
  10.7 8.3 %fusion.30 = bf16[4,4,8,4,384]{4,2,3,1,0:T(8,128)(2,1)S(1)} fusion(bf16[1,3,3,3,384,384]{5,4,3,2,1,0:T(8,128)(2,1)} %param.5, bf16[4,6,1,7,2,384]{5,3,4,1,0,2:T(8,128)(2,1)S(1)} %slice.101, bf16[4,6,1,8,4,384]{5,3,4,1,0,2:T(8,128)(2,1)S(1)} %copy.116, pred[8,4]{0,1:T(4,128)(4,1)S(1)} %copy-done.1), kind=kOutput, calls=%fused_computation.21 | convolution fusion | flops 3060695040 | bytes 9203744 | tf_op jit(solution)/shard_map/conv_general_dilated | solution.py:18
  19.0 0.2 copy.117
  19.4 0.7 collective-permute-start.3
  20.1 0.7 collective-permute-start.2
  20.8 0.7 collective-permute-start.4
  21.6 0.3 fusion.93
  22.0 0.2 copy.157
  22.2 0.2 pad.7.clone
  22.6 5.7 %fusion.27 = bf16[4,4,8,4,384]{4,2,3,1,0:T(8,128)(2,1)S(1)} fusion(bf16[1,3,3,3,384,384]{5,4,3,2,1,0:T(8,128)(2,1)S(1)} %bitcast.144, bf16[4,6,1,7,2,384]{5,3,4,1,0,2:T(8,128)(2,1)S(1)} %slice.105, bf16[4,6,1,8,4,384]{5,3,4,1,0,2:T(8,128)(2,1)S(1)} %copy.123, pred[8,4]{0,1:T(4,128)(4,1)S(1)} %copy-done.1), kind=kOutput, calls=%fused_computation.20 | convolution fusion | flops 3060695040 | bytes 9203744 | tf_op jit(solution)/shard_map/conv_general_dilated | solution.py:18
  28.3 0.2 copy.124
  28.7 1.3 %collective-permute-start.5 = (bf16[4,4,24,384]{3,2,1,0:T(8,128)(2,1)S(1)}, bf16[4,4,24,384]{3,2,1,0:T(8,128)(2,1)S(1)}, u32[]{:S(2)}, u32[]{:S(2)}) collective-permute-start(bf16[4,4,24,384]{3,2,1,0:T(8,128)(2,1)S(1)} %fusion.91), channel_id=1, source_target_pairs={{8,16},{9,17},{10,18},{11,19},{12,20},{13,21},{14,22},{15,23}} | collective-permute-start | bytes 884744 | tf_op jit(solution)/shard_map/ppermute | solution.py:30
  30.0 1.5 %collective-permute-start.8 = (bf16[4,1,24,384]{3,2,1,0:T(8,128)(2,1)S(1)}, bf16[4,1,24,384]{3,2,1,0:T(8,128)(2,1)S(1)}, u32[]{:S(2)}, u32[]{:S(2)}) collective-permute-start(bf16[4,1,24,384]{3,2,1,0:T(8,128)(2,1)S(1)} %get-tuple-element.7), channel_id=1, source_target_pairs={{8,17},{9,18},{10,19},{11,20},{12,21},{13,22},{14,23}} | collective-permute-start | bytes 221192 | tf_op jit(solution)/shard_map/ppermute | solution.py:30
  31.5 1.3 %collective-permute-start.9 = (bf16[4,1,24,384]{3,2,1,0:T(8,128)(2,1)S(1)}, bf16[4,1,24,384]{3,2,1,0:T(8,128)(2,1)S(1)}, u32[]{:S(2)}, u32[]{:S(2)}) collective-permute-start(bf16[4,1,24,384]{3,2,1,0:T(8,128)(2,1)S(1)} %get-tuple-element.8), channel_id=1, source_target_pairs={{9,16},{10,17},{11,18},{12,19},{13,20},{14,21},{15,22}} | collective-permute-start | bytes 221192 | tf_op jit(solution)/shard_map/ppermute | solution.py:30
  32.8 17.8 %collective-permute-done.8 = bf16[4,1,24,384]{3,2,1,0:T(8,128)(2,1)S(1)} collective-permute-done((bf16[4,1,24,384]{3,2,1,0:T(8,128)(2,1)S(1)}, bf16[4,1,24,384]{3,2,1,0:T(8,128)(2,1)S(1)}, u32[]{:S(2)}, u32[]{:S(2)}) %collective-permute-start.8) | collective-permute-done | bytes 73760 | tf_op jit(solution)/shard_map/ppermute | solution.py:30
  50.6 3.3 %collective-permute-done.9 = bf16[4,1,24,384]{3,2,1,0:T(8,128)(2,1)S(1)} collective-permute-done((bf16[4,1,24,384]{3,2,1,0:T(8,128)(2,1)S(1)}, bf16[4,1,24,384]{3,2,1,0:T(8,128)(2,1)S(1)}, u32[]{:S(2)}, u32[]{:S(2)}) %collective-permute-start.9) | collective-permute-done | bytes 73760 | tf_op jit(solution)/shard_map/ppermute | solution.py:30
  54.1 0.3 fusion.94
  54.5 0.2 copy.158
  54.6 0.2 pad.9.clone
  55.1 5.7 %fusion.24 = bf16[4,4,8,4,384]{4,2,3,1,0:T(8,128)(2,1)S(1)} fusion(bf16[1,3,3,3,384,384]{5,4,3,2,1,0:T(8,128)(2,1)S(1)} %bitcast.144, bf16[4,6,1,7,2,384]{5,3,4,1,0,2:T(8,128)(2,1)S(1)} %slice.113, bf16[4,6,1,8,4,384]{5,3,4,1,0,2:T(8,128)(2,1)S(1)} %copy.130, pred[8,4]{0,1:T(4,128)(4,1)S(1)} %copy-done.1), kind=kOutput, calls=%fused_computation.19 | convolution fusion | flops 3060695040 | bytes 9203744 | tf_op jit(solution)/shard_map/conv_general_dilated | solution.py:18
  60.7 0.2 copy.131
  61.1 1.3 %collective-permute-start.11 = (bf16[4,4,24,384]{3,2,1,0:T(8,128)(2,1)S(1)}, bf16[4,4,24,384]{3,2,1,0:T(8,128)(2,1)S(1)}, u32[]{:S(2)}, u32[]{:S(2)}) collective-permute-start(bf16[4,4,24,384]{3,2,1,0:T(8,128)(2,1)S(1)} %bitcast.128), channel_id=1, source_target_pairs={{16,24},{17,25},{18,26},{19,27},{20,28},{21,29},{22,30},{23,31}} | collective-permute-start | bytes 884744 | tf_op jit(solution)/shard_map/ppermute | solution.py:30
  62.5 1.3 %collective-permute-start.10 = (bf16[4,1,24,384]{3,2,1,0:T(8,128)(2,1)S(1)}, bf16[4,1,24,384]{3,2,1,0:T(8,128)(2,1)S(1)}, u32[]{:S(2)}, u32[]{:S(2)}) collective-permute-start(bf16[4,1,24,384]{3,2,1,0:T(8,128)(2,1)S(1)} %get-tuple-element.5), channel_id=1, source_target_pairs={{16,25},{17,26},{18,27},{19,28},{20,29},{21,30},{22,31}} | collective-permute-start | bytes 221192 | tf_op jit(solution)/shard_map/ppermute | solution.py:30
  63.8 1.3 %collective-permute-start.12 = (bf16[4,1,24,384]{3,2,1,0:T(8,128)(2,1)S(1)}, bf16[4,1,24,384]{3,2,1,0:T(8,128)(2,1)S(1)}, u32[]{:S(2)}, u32[]{:S(2)}) collective-permute-start(bf16[4,1,24,384]{3,2,1,0:T(8,128)(2,1)S(1)} %get-tuple-element.6), channel_id=1, source_target_pairs={{17,24},{18,25},{19,26},{20,27},{21,28},{22,29},{23,30}} | collective-permute-start | bytes 221192 | tf_op jit(solution)/shard_map/ppermute | solution.py:30
  65.1 0.7 collective-permute-start.7
  65.8 1.3 %collective-permute-start.6 = (bf16[1,4,24,384]{3,2,1,0:T(8,128)(2,1)S(1)}, bf16[1,4,24,384]{3,2,1,0:T(8,128)(2,1)S(1)}, u32[]{:S(2)}, u32[]{:S(2)}) collective-permute-start(bf16[1,4,24,384]{3,2,1,0:T(8,128)(2,1)S(1)} %slice.107), channel_id=1, source_target_pairs={{16,24},{17,25},{18,26},{19,27},{20,28},{21,29},{22,30},{23,31}} | collective-permute-start | bytes 221192 | tf_op jit(solution)/shard_map/ppermute | solution.py:30
  67.1 2.9 %collective-permute-done.10 = bf16[4,1,24,384]{3,2,1,0:T(8,128)(2,1)S(1)} collective-permute-done((bf16[4,1,24,384]{3,2,1,0:T(8,128)(2,1)S(1)}, bf16[4,1,24,384]{3,2,1,0:T(8,128)(2,1)S(1)}, u32[]{:S(2)}, u32[]{:S(2)}) %collective-permute-start.10) | collective-permute-done | bytes 73760 | tf_op jit(solution)/shard_map/ppermute | solution.py:30
  70.0 0.8 collective-permute-done.12
  70.9 0.3 fusion.52
  71.3 0.2 copy.160
  71.5 0.2 pad.13.clone
  71.9 3.0 %fusion.39 = bf16[2,4,8,4,384]{4,2,3,1,0:T(8,128)(2,1)S(1)} fusion(bf16[1,3,3,3,384,384]{5,4,3,2,1,0:T(8,128)(2,1)S(1)} %bitcast.144, bf16[4,6,1,7,2,384]{5,3,4,1,0,2:T(8,128)(2,1)S(1)} %slice.122, bf16[4,6,1,8,4,384]{5,3,4,1,0,2:T(8,128)(2,1)S(1)} %copy.144, pred[8,4]{0,1:T(4,128)(4,1)S(1)} %copy-done.1), kind=kOutput, calls=%fused_computation.24 | convolution fusion | flops 2041282560 | bytes 9007136 | tf_op jit(solution)/shard_map/conv_general_dilated | solution.py:18
  75.1 0.9 collective-permute-start.14
  76.1 0.7 collective-permute-start.15
  76.7 0.3 fusion.95
  77.1 0.2 copy.159
  77.3 0.2 pad.11.clone
  77.7 3.0 %fusion.42 = bf16[2,4,8,4,384]{4,2,3,1,0:T(8,128)(2,1)S(1)} fusion(bf16[1,3,3,3,384,384]{5,4,3,2,1,0:T(8,128)(2,1)S(1)} %bitcast.144, bf16[4,6,1,7,2,384]{5,3,4,1,0,2:T(8,128)(2,1)S(1)} %slice.117, bf16[4,6,1,8,4,384]{5,3,4,1,0,2:T(8,128)(2,1)S(1)} %copy.137, pred[8,4]{0,1:T(4,128)(4,1)S(1)} %copy-done.1), kind=kOutput, calls=%fused_computation.25 | convolution fusion | flops 2041282560 | bytes 9007136 | tf_op jit(solution)/shard_map/conv_general_dilated | solution.py:18
  80.8 1.3 %collective-permute-start.13 = (bf16[1,4,24,384]{3,2,1,0:T(8,128)(2,1)S(1)}, bf16[1,4,24,384]{3,2,1,0:T(8,128)(2,1)S(1)}, u32[]{:S(2)}, u32[]{:S(2)}) collective-permute-start(bf16[1,4,24,384]{3,2,1,0:T(8,128)(2,1)S(1)} %bitcast.142), channel_id=1, source_target_pairs={{24,16},{25,17},{26,18},{27,19},{28,20},{29,21},{30,22},{31,23}} | collective-permute-start | bytes 221192 | tf_op jit(solution)/shard_map/ppermute | solution.py:30
  82.3 6.9 %collective-permute-done.13 = bf16[1,4,24,384]{3,2,1,0:T(8,128)(2,1)S(1)} collective-permute-done((bf16[1,4,24,384]{3,2,1,0:T(8,128)(2,1)S(1)}, bf16[1,4,24,384]{3,2,1,0:T(8,128)(2,1)S(1)}, u32[]{:S(2)}, u32[]{:S(2)}) %collective-permute-start.13) | collective-permute-done | bytes 73760 | tf_op jit(solution)/shard_map/ppermute | solution.py:30
  89.2 0.7 add_convert_fusion
  (68 shorter events, 3.0 us)
Async XLA Ops:
  0.9 8.7 %collective-permute-start.1 = (bf16[4,1,24,384]{3,2,1,0:T(8,128)(2,1)S(1)}, bf16[4,1,24,384]{3,2,1,0:T(8,128)(2,1)S(1)}, u32[]{:S(2)}, u32[]{:S(2)}) collective-permute-start(bf16[4,1,24,384]{3,2,1,0:T(8,128)(2,1)S(1)} %get-tuple-element.12), channel_id=1, source_target_pairs={{1,0},{2,1},{3,2},{4,3},{5,4},{6,5},{7,6},{9,8},{10,9},{11,10},{12... | collective-permute-start | bytes 221192 | tf_op jit(solution)/shard_map/ppermute | solution.py:60
  3.5 6.2 %collective-permute-start = (bf16[4,1,24,384]{3,2,1,0:T(8,128)(2,1)S(1)}, bf16[4,1,24,384]{3,2,1,0:T(8,128)(2,1)S(1)}, u32[]{:S(2)}, u32[]{:S(2)}) collective-permute-start(bf16[4,1,24,384]{3,2,1,0:T(8,128)(2,1)S(1)} %get-tuple-element.11), channel_id=1, source_target_pairs={{0,1},{1,2},{2,3},{3,4},{4,5},{5,6},{6,7},{8,9},{9,10},{10,11},{11... | collective-permute-start | bytes 221192 | tf_op jit(solution)/shard_map/ppermute | solution.py:59
  10.1 0.7 copy-start.1
  10.6 12.0 %slice-start = ((s8[7962624]{0:T(1024)(128)(4,1)}), s8[4194304]{0:T(1024)(128)(4,1)S(1)}, s32[]{:S(2)}) async-start(s8[7962624]{0:T(1024)(128)(4,1)} %bitcast.143), calls=%async_computation | async-start | bytes 8388608
  10.7 11.9 %slice-start.1 = ((s8[7962624]{0:T(1024)(128)(4,1)}), s8[3768320]{0:T(1024)(128)(4,1)S(1)}, s32[]{:S(2)}) async-start(s8[7962624]{0:T(1024)(128)(4,1)} %bitcast.143), calls=%async_computation.1 | async-start | bytes 7536640
  19.4 2.1 %collective-permute-start.3 = (bf16[4,4,24,384]{3,2,1,0:T(8,128)(2,1)S(1)}, bf16[4,4,24,384]{3,2,1,0:T(8,128)(2,1)S(1)}, u32[]{:S(2)}, u32[]{:S(2)}) collective-permute-start(bf16[4,4,24,384]{3,2,1,0:T(8,128)(2,1)S(1)} %bitcast.130), channel_id=1, source_target_pairs={{0,8},{1,9},{2,10},{3,11},{4,12},{5,13},{6,14},{7,15}} | collective-permute-start | bytes 884744 | tf_op jit(solution)/shard_map/ppermute | solution.py:30
  20.1 1.3 %collective-permute-start.2 = (bf16[4,1,24,384]{3,2,1,0:T(8,128)(2,1)S(1)}, bf16[4,1,24,384]{3,2,1,0:T(8,128)(2,1)S(1)}, u32[]{:S(2)}, u32[]{:S(2)}) collective-permute-start(bf16[4,1,24,384]{3,2,1,0:T(8,128)(2,1)S(1)} %get-tuple-element.9), channel_id=1, source_target_pairs={{0,9},{1,10},{2,11},{3,12},{4,13},{5,14},{6,15}} | collective-permute-start | bytes 221192 | tf_op jit(solution)/shard_map/ppermute | solution.py:30
  20.8 0.7 collective-permute-start.4
  22.6 6.0 %copy-start = (bf16[4,4,24,384]{3,2,1,0:T(8,128)(2,1)S(1)}, bf16[4,4,24,384]{3,2,1,0:T(8,128)(2,1)}, u32[]{:S(2)}) copy-start(bf16[4,4,24,384]{3,2,1,0:T(8,128)(2,1)} %param.3) | copy-start | bytes 884740
  28.7 25.2 %collective-permute-start.5 = (bf16[4,4,24,384]{3,2,1,0:T(8,128)(2,1)S(1)}, bf16[4,4,24,384]{3,2,1,0:T(8,128)(2,1)S(1)}, u32[]{:S(2)}, u32[]{:S(2)}) collective-permute-start(bf16[4,4,24,384]{3,2,1,0:T(8,128)(2,1)S(1)} %fusion.91), channel_id=1, source_target_pairs={{8,16},{9,17},{10,18},{11,19},{12,20},{13,21},{14,22},{15,23}} | collective-permute-start | bytes 884744 | tf_op jit(solution)/shard_map/ppermute | solution.py:30
  30.0 20.6 %collective-permute-start.8 = (bf16[4,1,24,384]{3,2,1,0:T(8,128)(2,1)S(1)}, bf16[4,1,24,384]{3,2,1,0:T(8,128)(2,1)S(1)}, u32[]{:S(2)}, u32[]{:S(2)}) collective-permute-start(bf16[4,1,24,384]{3,2,1,0:T(8,128)(2,1)S(1)} %get-tuple-element.7), channel_id=1, source_target_pairs={{8,17},{9,18},{10,19},{11,20},{12,21},{13,22},{14,23}} | collective-permute-start | bytes 221192 | tf_op jit(solution)/shard_map/ppermute | solution.py:30
  31.5 22.4 %collective-permute-start.9 = (bf16[4,1,24,384]{3,2,1,0:T(8,128)(2,1)S(1)}, bf16[4,1,24,384]{3,2,1,0:T(8,128)(2,1)S(1)}, u32[]{:S(2)}, u32[]{:S(2)}) collective-permute-start(bf16[4,1,24,384]{3,2,1,0:T(8,128)(2,1)S(1)} %get-tuple-element.8), channel_id=1, source_target_pairs={{9,16},{10,17},{11,18},{12,19},{13,20},{14,21},{15,22}} | collective-permute-start | bytes 221192 | tf_op jit(solution)/shard_map/ppermute | solution.py:30
  61.1 9.6 %collective-permute-start.11 = (bf16[4,4,24,384]{3,2,1,0:T(8,128)(2,1)S(1)}, bf16[4,4,24,384]{3,2,1,0:T(8,128)(2,1)S(1)}, u32[]{:S(2)}, u32[]{:S(2)}) collective-permute-start(bf16[4,4,24,384]{3,2,1,0:T(8,128)(2,1)S(1)} %bitcast.128), channel_id=1, source_target_pairs={{16,24},{17,25},{18,26},{19,27},{20,28},{21,29},{22,30},{23,31}} | collective-permute-start | bytes 884744 | tf_op jit(solution)/shard_map/ppermute | solution.py:30
  62.5 7.5 %collective-permute-start.10 = (bf16[4,1,24,384]{3,2,1,0:T(8,128)(2,1)S(1)}, bf16[4,1,24,384]{3,2,1,0:T(8,128)(2,1)S(1)}, u32[]{:S(2)}, u32[]{:S(2)}) collective-permute-start(bf16[4,1,24,384]{3,2,1,0:T(8,128)(2,1)S(1)} %get-tuple-element.5), channel_id=1, source_target_pairs={{16,25},{17,26},{18,27},{19,28},{20,29},{21,30},{22,31}} | collective-permute-start | bytes 221192 | tf_op jit(solution)/shard_map/ppermute | solution.py:30
  63.8 7.0 %collective-permute-start.12 = (bf16[4,1,24,384]{3,2,1,0:T(8,128)(2,1)S(1)}, bf16[4,1,24,384]{3,2,1,0:T(8,128)(2,1)S(1)}, u32[]{:S(2)}, u32[]{:S(2)}) collective-permute-start(bf16[4,1,24,384]{3,2,1,0:T(8,128)(2,1)S(1)} %get-tuple-element.6), channel_id=1, source_target_pairs={{17,24},{18,25},{19,26},{20,27},{21,28},{22,29},{23,30}} | collective-permute-start | bytes 221192 | tf_op jit(solution)/shard_map/ppermute | solution.py:30
  65.1 17.2 %collective-permute-start.7 = (bf16[1,4,24,384]{3,2,1,0:T(8,128)(2,1)S(1)}, bf16[1,4,24,384]{3,2,1,0:T(8,128)(2,1)S(1)}, u32[]{:S(2)}, u32[]{:S(2)}) collective-permute-start(bf16[1,4,24,384]{3,2,1,0:T(8,128)(2,1)S(1)} %slice.109), channel_id=1, source_target_pairs={{8,0},{9,1},{10,2},{11,3},{12,4},{13,5},{14,6},{15,7}} | collective-permute-start | bytes 221192 | tf_op jit(solution)/shard_map/ppermute | solution.py:30
  65.8 16.5 %collective-permute-start.6 = (bf16[1,4,24,384]{3,2,1,0:T(8,128)(2,1)S(1)}, bf16[1,4,24,384]{3,2,1,0:T(8,128)(2,1)S(1)}, u32[]{:S(2)}, u32[]{:S(2)}) collective-permute-start(bf16[1,4,24,384]{3,2,1,0:T(8,128)(2,1)S(1)} %slice.107), channel_id=1, source_target_pairs={{16,24},{17,25},{18,26},{19,27},{20,28},{21,29},{22,30},{23,31}} | collective-permute-start | bytes 221192 | tf_op jit(solution)/shard_map/ppermute | solution.py:30
  75.1 7.2 %collective-permute-start.14 = (bf16[1,4,24,384]{3,2,1,0:T(8,128)(2,1)S(1)}, bf16[1,4,24,384]{3,2,1,0:T(8,128)(2,1)S(1)}, u32[]{:S(2)}, u32[]{:S(2)}) collective-permute-start(bf16[1,4,24,384]{3,2,1,0:T(8,128)(2,1)S(1)} %bitcast.140), channel_id=1, source_target_pairs={{24,8},{25,9},{26,10},{27,11},{28,12},{29,13},{30,14},{31,15}} | collective-permute-start | bytes 221192 | tf_op jit(solution)/shard_map/ppermute | solution.py:30
  76.1 6.2 %collective-permute-start.15 = (bf16[1,4,24,384]{3,2,1,0:T(8,128)(2,1)S(1)}, bf16[1,4,24,384]{3,2,1,0:T(8,128)(2,1)S(1)}, u32[]{:S(2)}, u32[]{:S(2)}) collective-permute-start(bf16[1,4,24,384]{3,2,1,0:T(8,128)(2,1)S(1)} %bitcast.141), channel_id=1, source_target_pairs={{24,0},{25,1},{26,2},{27,3},{28,4},{29,5},{30,6},{31,7}} | collective-permute-start | bytes 221192 | tf_op jit(solution)/shard_map/ppermute | solution.py:30
  80.8 8.3 %collective-permute-start.13 = (bf16[1,4,24,384]{3,2,1,0:T(8,128)(2,1)S(1)}, bf16[1,4,24,384]{3,2,1,0:T(8,128)(2,1)S(1)}, u32[]{:S(2)}, u32[]{:S(2)}) collective-permute-start(bf16[1,4,24,384]{3,2,1,0:T(8,128)(2,1)S(1)} %bitcast.142), channel_id=1, source_target_pairs={{24,16},{25,17},{26,18},{27,19},{28,20},{29,21},{30,22},{31,23}} | collective-permute-start | bytes 221192 | tf_op jit(solution)/shard_map/ppermute | solution.py:30

commit v17 on v12

--- a/solution.py
+++ b/solution.py
@@ -56,8 +56,8 @@
 
     up = [(i, i + 1) for i in range(row_count - 1)]
     down = [(i + 1, i) for i in range(row_count - 1)]
-    top = lax.ppermute(features[:, height - 1 :], "rows", up)
-    bottom = lax.ppermute(features[:, :1], "rows", down)
+    top = send(features[:, height - 1 :], up)
+    bottom = send(features[:, :1], down)
     current = features
     skip = features
     last_stage = segment_count - 1

time: 90.2 us -> 88.3 us (0.979)
  starting transfers between devices: 22.3 us -> 18 us
  waiting for transfers between devices: 28.5 us -> 30.9 us
    ppermute x2 -> x0, starting transfers between devices: 5.6 us -> none  [the longest x1 3.02 us: local(): top = lax.ppermute(features[:, height - 1:], 'rows', up)]
    ppermute x15 -> x17, waiting for transfers between devices: 28.5 us -> 30.9 us  [send(): return lax.ppermute(value, BOTH, pairs)]
    ppermute x15 -> x17, starting transfers between devices: 16.7 us -> 18 us  [send(): return lax.ppermute(value, BOTH, pairs)]
where the time goes in v17:
time: 88.3 us; the launch traced here: 86.7 us
  waiting for transfers between devices  30.9 us (35%)
  matrix products  25.6 us (29%)
  starting transfers between devices  18 us (20%)
  other arithmetic  6.04 us (7%)
  local copies, waits for them, and re-layouts  5.36 us (6%)
    ppermute x17, waiting for transfers between devices, send(): return lax.ppermute(value, BOTH, pairs)  30.9 us
    conv_general_dilated x5, matrix products, causal_conv(): lax.conv_general_dilated(window[None], kernel, window_strides=(1, 1, 1),...  25.6 us
    ppermute x17, starting transfers between devices, send(): return lax.ppermute(value, BOTH, pairs)  18 us
    convert_element_type x6, other arithmetic, activate(): return jax.nn.silu(widened * lax.rsqrt(mean_square + 1e-06) * gain_row.as...  2.72 us
  transfers between devices with their start and end apart: 17, of which 3 were waited for; matrix products, arithmetic and copies ran while one was open for 13% of the time, Pallas kernels for 0%

profile of v17, /device:TPU:17, one launch (start us, length us, event | category | flops | bytes accessed | tf_op | source)
XLA Modules:
  0.0 86.7 jit_solution(6850096812672254999)
XLA Ops:
  0.0 0.9 %fusion.139 = (bf16[4,1,24,384]{3,2,1,0:T(8,128)(2,1)S(1)}, bf16[4,1,24,384]{3,2,1,0:T(8,128)(2,1)S(1)}) fusion(bf16[4,4,24,384]{3,2,1,0:T(8,128)(2,1)} %param.3), kind=kLoop, calls=%fused_computation.148 | loop fusion | bytes 294912 | tf_op jit(solution)/shard_map/slice | solution.py:59
  0.9 0.7 collective-permute-start.1
  1.6 0.7 collective-permute-start
  2.3 1.1 %fusion.83 = f32[4,4,24]{2,1,0:T(4,128)S(1)} fusion(bf16[4,4,24,384]{3,2,1,0:T(8,128)(2,1)} %param.3), kind=kLoop, calls=%fused_computation.70 | loop fusion | flops 441984 | bytes 296448 | tf_op jit(solution)/shard_map/reduce_sum | solution.py:11
  3.4 0.7 convert_reduce_fusion
  4.1 1.2 %fusion.90 = bf16[4,4,24,384]{3,2,1,0:T(8,128)(2,1)S(1)} fusion(bf16[4,4,24,384]{3,2,1,0:T(8,128)(2,1)} %param.3, f32[384]{0:T(512)S(1)} %convert_reduce_fusion, f32[4,4,24]{2,1,0:T(4,128)S(1)} %add_rsqrt_fusion.3), kind=kLoop, calls=%fused_computation.77 | loop fusion | flops 1179648 | bytes 592896 | tf_op jit(solution)/shard_map/convert_element_type | solution.py:14
  5.6 0.2 fusion.108
  5.8 0.2 copy.156
  6.0 0.2 pad.5.clone
  6.5 8.3 %fusion.30 = bf16[4,4,8,4,384]{4,2,3,1,0:T(8,128)(2,1)S(1)} fusion(bf16[1,3,3,3,384,384]{5,4,3,2,1,0:T(8,128)(2,1)} %param.5, bf16[4,6,1,7,2,384]{5,3,4,1,0,2:T(8,128)(2,1)S(1)} %slice.101, bf16[4,6,1,8,4,384]{5,3,4,1,0,2:T(8,128)(2,1)S(1)} %copy.116, pred[8,4]{0,1:T(4,128)(4,1)S(1)} %copy-done.1), kind=kOutput, calls=%fused_computation.21 | convolution fusion | flops 3060695040 | bytes 9203744 | tf_op jit(solution)/shard_map/conv_general_dilated | solution.py:18
  14.7 0.2 copy.117
  15.1 0.7 collective-permute-start.3
  15.8 0.7 collective-permute-start.2
  16.5 0.7 collective-permute-start.4
  17.4 0.3 fusion.93
  17.7 0.2 copy.157
  17.9 0.2 pad.7.clone
  18.4 5.7 %fusion.27 = bf16[4,4,8,4,384]{4,2,3,1,0:T(8,128)(2,1)S(1)} fusion(bf16[1,3,3,3,384,384]{5,4,3,2,1,0:T(8,128)(2,1)S(1)} %bitcast.144, bf16[4,6,1,7,2,384]{5,3,4,1,0,2:T(8,128)(2,1)S(1)} %slice.105, bf16[4,6,1,8,4,384]{5,3,4,1,0,2:T(8,128)(2,1)S(1)} %copy.123, pred[8,4]{0,1:T(4,128)(4,1)S(1)} %copy-done.1), kind=kOutput, calls=%fused_computation.20 | convolution fusion | flops 3060695040 | bytes 9203744 | tf_op jit(solution)/shard_map/conv_general_dilated | solution.py:18
  24.0 0.2 copy.124
  24.4 1.3 %collective-permute-start.5 = (bf16[4,4,24,384]{3,2,1,0:T(8,128)(2,1)S(1)}, bf16[4,4,24,384]{3,2,1,0:T(8,128)(2,1)S(1)}, u32[]{:S(2)}, u32[]{:S(2)}) collective-permute-start(bf16[4,4,24,384]{3,2,1,0:T(8,128)(2,1)S(1)} %fusion.91), channel_id=1, source_target_pairs={{8,16},{9,17},{10,18},{11,19},{12,20},{13,21},{14,22},{15,23}} | collective-permute-start | bytes 884744 | tf_op jit(solution)/shard_map/ppermute | solution.py:30
  25.8 1.5 %collective-permute-start.10 = (bf16[4,1,24,384]{3,2,1,0:T(8,128)(2,1)S(1)}, bf16[4,1,24,384]{3,2,1,0:T(8,128)(2,1)S(1)}, u32[]{:S(2)}, u32[]{:S(2)}) collective-permute-start(bf16[4,1,24,384]{3,2,1,0:T(8,128)(2,1)S(1)} %get-tuple-element.8), channel_id=1, source_target_pairs={{9,16},{10,17},{11,18},{12,19},{13,20},{14,21},{15,22}} | collective-permute-start | bytes 221192 | tf_op jit(solution)/shard_map/ppermute | solution.py:30
  27.2 1.3 %collective-permute-start.9 = (bf16[4,1,24,384]{3,2,1,0:T(8,128)(2,1)S(1)}, bf16[4,1,24,384]{3,2,1,0:T(8,128)(2,1)S(1)}, u32[]{:S(2)}, u32[]{:S(2)}) collective-permute-start(bf16[4,1,24,384]{3,2,1,0:T(8,128)(2,1)S(1)} %get-tuple-element.7), channel_id=1, source_target_pairs={{8,17},{9,18},{10,19},{11,20},{12,21},{13,22},{14,23}} | collective-permute-start | bytes 221192 | tf_op jit(solution)/shard_map/ppermute | solution.py:30
  28.5 21.4 %collective-permute-done.10 = bf16[4,1,24,384]{3,2,1,0:T(8,128)(2,1)S(1)} collective-permute-done((bf16[4,1,24,384]{3,2,1,0:T(8,128)(2,1)S(1)}, bf16[4,1,24,384]{3,2,1,0:T(8,128)(2,1)S(1)}, u32[]{:S(2)}, u32[]{:S(2)}) %collective-permute-start.10) | collective-permute-done | bytes 73760 | tf_op jit(solution)/shard_map/ppermute | solution.py:30
  50.2 0.3 fusion.94
  50.5 0.2 copy.158
  50.7 0.2 pad.9.clone
  51.1 5.7 %fusion.24 = bf16[4,4,8,4,384]{4,2,3,1,0:T(8,128)(2,1)S(1)} fusion(bf16[1,3,3,3,384,384]{5,4,3,2,1,0:T(8,128)(2,1)S(1)} %bitcast.144, bf16[4,6,1,7,2,384]{5,3,4,1,0,2:T(8,128)(2,1)S(1)} %slice.113, bf16[4,6,1,8,4,384]{5,3,4,1,0,2:T(8,128)(2,1)S(1)} %copy.130, pred[8,4]{0,1:T(4,128)(4,1)S(1)} %copy-done.1), kind=kOutput, calls=%fused_computation.19 | convolution fusion | flops 3060695040 | bytes 9203744 | tf_op jit(solution)/shard_map/conv_general_dilated | solution.py:18
  56.8 0.2 copy.131
  57.1 1.3 %collective-permute-start.12 = (bf16[4,4,24,384]{3,2,1,0:T(8,128)(2,1)S(1)}, bf16[4,4,24,384]{3,2,1,0:T(8,128)(2,1)S(1)}, u32[]{:S(2)}, u32[]{:S(2)}) collective-permute-start(bf16[4,4,24,384]{3,2,1,0:T(8,128)(2,1)S(1)} %bitcast.128), channel_id=1, source_target_pairs={{16,24},{17,25},{18,26},{19,27},{20,28},{21,29},{22,30},{23,31}} | collective-permute-start | bytes 884744 | tf_op jit(solution)/shard_map/ppermute | solution.py:30
  58.5 1.3 %collective-permute-start.11 = (bf16[4,1,24,384]{3,2,1,0:T(8,128)(2,1)S(1)}, bf16[4,1,24,384]{3,2,1,0:T(8,128)(2,1)S(1)}, u32[]{:S(2)}, u32[]{:S(2)}) collective-permute-start(bf16[4,1,24,384]{3,2,1,0:T(8,128)(2,1)S(1)} %get-tuple-element.5), channel_id=1, source_target_pairs={{16,25},{17,26},{18,27},{19,28},{20,29},{21,30},{22,31}} | collective-permute-start | bytes 221192 | tf_op jit(solution)/shard_map/ppermute | solution.py:30
  59.8 1.3 %collective-permute-start.13 = (bf16[4,1,24,384]{3,2,1,0:T(8,128)(2,1)S(1)}, bf16[4,1,24,384]{3,2,1,0:T(8,128)(2,1)S(1)}, u32[]{:S(2)}, u32[]{:S(2)}) collective-permute-start(bf16[4,1,24,384]{3,2,1,0:T(8,128)(2,1)S(1)} %get-tuple-element.6), channel_id=1, source_target_pairs={{17,24},{18,25},{19,26},{20,27},{21,28},{22,29},{23,30}} | collective-permute-start | bytes 221192 | tf_op jit(solution)/shard_map/ppermute | solution.py:30
  61.1 1.3 %collective-permute-start.6 = (bf16[1,4,24,384]{3,2,1,0:T(8,128)(2,1)S(1)}, bf16[1,4,24,384]{3,2,1,0:T(8,128)(2,1)S(1)}, u32[]{:S(2)}, u32[]{:S(2)}) collective-permute-start(bf16[1,4,24,384]{3,2,1,0:T(8,128)(2,1)S(1)} %get-tuple-element.11), channel_id=1, source_target_pairs={{16,24},{17,25},{18,26},{19,27},{20,28},{21,29},{22,30},{23,31}} | collective-permute-start | bytes 221192 | tf_op jit(solution)/shard_map/ppermute | solution.py:30
  62.4 1.3 %collective-permute-start.7 = (bf16[1,4,24,384]{3,2,1,0:T(8,128)(2,1)S(1)}, bf16[1,4,24,384]{3,2,1,0:T(8,128)(2,1)S(1)}, u32[]{:S(2)}, u32[]{:S(2)}) collective-permute-start(bf16[1,4,24,384]{3,2,1,0:T(8,128)(2,1)S(1)} %get-tuple-element.10), channel_id=1, source_target_pairs={{16,8},{17,9},{18,10},{19,11},{20,12},{21,13},{22,14},{23,15}} | collective-permute-start | bytes 221192 | tf_op jit(solution)/shard_map/ppermute | solution.py:30
  63.7 2.4 %collective-permute-done.11 = bf16[4,1,24,384]{3,2,1,0:T(8,128)(2,1)S(1)} collective-permute-done((bf16[4,1,24,384]{3,2,1,0:T(8,128)(2,1)S(1)}, bf16[4,1,24,384]{3,2,1,0:T(8,128)(2,1)S(1)}, u32[]{:S(2)}, u32[]{:S(2)}) %collective-permute-start.11) | collective-permute-done | bytes 73760 | tf_op jit(solution)/shard_map/ppermute | solution.py:30
  66.2 1.3 %collective-permute-start.8 = (bf16[1,4,24,384]{3,2,1,0:T(8,128)(2,1)S(1)}, bf16[1,4,24,384]{3,2,1,0:T(8,128)(2,1)S(1)}, u32[]{:S(2)}, u32[]{:S(2)}) collective-permute-start(bf16[1,4,24,384]{3,2,1,0:T(8,128)(2,1)S(1)} %get-tuple-element.9), channel_id=1, source_target_pairs={{16,0},{17,1},{18,2},{19,3},{20,4},{21,5},{22,6},{23,7}} | collective-permute-start | bytes 221192 | tf_op jit(solution)/shard_map/ppermute | solution.py:30
  67.7 0.3 fusion.52
  68.1 0.2 copy.160
  68.2 0.2 pad.13.clone
  68.7 3.0 %fusion.39 = bf16[2,4,8,4,384]{4,2,3,1,0:T(8,128)(2,1)S(1)} fusion(bf16[1,3,3,3,384,384]{5,4,3,2,1,0:T(8,128)(2,1)S(1)} %bitcast.144, bf16[4,6,1,7,2,384]{5,3,4,1,0,2:T(8,128)(2,1)S(1)} %slice.122, bf16[4,6,1,8,4,384]{5,3,4,1,0,2:T(8,128)(2,1)S(1)} %copy.144, pred[8,4]{0,1:T(4,128)(4,1)S(1)} %copy-done.1), kind=kOutput, calls=%fused_computation.24 | convolution fusion | flops 2041282560 | bytes 9007136 | tf_op jit(solution)/shard_map/conv_general_dilated | solution.py:18
  71.8 0.9 %collective-permute-start.15 = (bf16[1,4,24,384]{3,2,1,0:T(8,128)(2,1)S(1)}, bf16[1,4,24,384]{3,2,1,0:T(8,128)(2,1)S(1)}, u32[]{:S(2)}, u32[]{:S(2)}) collective-permute-start(bf16[1,4,24,384]{3,2,1,0:T(8,128)(2,1)S(1)} %bitcast.140), channel_id=1, source_target_pairs={{24,8},{25,9},{26,10},{27,11},{28,12},{29,13},{30,14},{31,15}} | collective-permute-start | bytes 221192 | tf_op jit(solution)/shard_map/ppermute | solution.py:30
  72.8 0.7 collective-permute-start.16
  73.5 0.3 fusion.95
  73.8 0.2 copy.159
  74.0 0.2 pad.11.clone
  74.4 3.0 %fusion.42 = bf16[2,4,8,4,384]{4,2,3,1,0:T(8,128)(2,1)S(1)} fusion(bf16[1,3,3,3,384,384]{5,4,3,2,1,0:T(8,128)(2,1)S(1)} %bitcast.144, bf16[4,6,1,7,2,384]{5,3,4,1,0,2:T(8,128)(2,1)S(1)} %slice.117, bf16[4,6,1,8,4,384]{5,3,4,1,0,2:T(8,128)(2,1)S(1)} %copy.137, pred[8,4]{0,1:T(4,128)(4,1)S(1)} %copy-done.1), kind=kOutput, calls=%fused_computation.25 | convolution fusion | flops 2041282560 | bytes 9007136 | tf_op jit(solution)/shard_map/conv_general_dilated | solution.py:18
  77.6 1.3 %collective-permute-start.14 = (bf16[1,4,24,384]{3,2,1,0:T(8,128)(2,1)S(1)}, bf16[1,4,24,384]{3,2,1,0:T(8,128)(2,1)S(1)}, u32[]{:S(2)}, u32[]{:S(2)}) collective-permute-start(bf16[1,4,24,384]{3,2,1,0:T(8,128)(2,1)S(1)} %bitcast.142), channel_id=1, source_target_pairs={{24,16},{25,17},{26,18},{27,19},{28,20},{29,21},{30,22},{31,23}} | collective-permute-start | bytes 221192 | tf_op jit(solution)/shard_map/ppermute | solution.py:30
  79.0 7.0 %collective-permute-done.14 = bf16[1,4,24,384]{3,2,1,0:T(8,128)(2,1)S(1)} collective-permute-done((bf16[1,4,24,384]{3,2,1,0:T(8,128)(2,1)S(1)}, bf16[1,4,24,384]{3,2,1,0:T(8,128)(2,1)S(1)}, u32[]{:S(2)}, u32[]{:S(2)}) %collective-permute-start.14) | collective-permute-done | bytes 73760 | tf_op jit(solution)/shard_map/ppermute | solution.py:30
  86.0 0.7 add_convert_fusion
  (69 shorter events, 2.8 us)
Async XLA Ops:
  0.9 4.4 %collective-permute-start.1 = (bf16[4,1,24,384]{3,2,1,0:T(8,128)(2,1)S(1)}, bf16[4,1,24,384]{3,2,1,0:T(8,128)(2,1)S(1)}, u32[]{:S(2)}, u32[]{:S(2)}) collective-permute-start(bf16[4,1,24,384]{3,2,1,0:T(8,128)(2,1)S(1)} %get-tuple-element.15), channel_id=1, source_target_pairs={{1,0},{2,1},{3,2},{4,3},{5,4},{6,5},{7,6}} | collective-permute-start | bytes 221192 | tf_op jit(solution)/shard_map/ppermute | solution.py:30
  1.6 3.8 %collective-permute-start = (bf16[4,1,24,384]{3,2,1,0:T(8,128)(2,1)S(1)}, bf16[4,1,24,384]{3,2,1,0:T(8,128)(2,1)S(1)}, u32[]{:S(2)}, u32[]{:S(2)}) collective-permute-start(bf16[4,1,24,384]{3,2,1,0:T(8,128)(2,1)S(1)} %get-tuple-element.14), channel_id=1, source_target_pairs={{0,1},{1,2},{2,3},{3,4},{4,5},{5,6},{6,7}} | collective-permute-start | bytes 221192 | tf_op jit(solution)/shard_map/ppermute | solution.py:30
  5.8 0.7 copy-start.1
  6.3 12.0 %slice-start = ((s8[7962624]{0:T(1024)(128)(4,1)}), s8[4194304]{0:T(1024)(128)(4,1)S(1)}, s32[]{:S(2)}) async-start(s8[7962624]{0:T(1024)(128)(4,1)} %bitcast.143), calls=%async_computation | async-start | bytes 8388608
  6.5 11.9 %slice-start.1 = ((s8[7962624]{0:T(1024)(128)(4,1)}), s8[3768320]{0:T(1024)(128)(4,1)S(1)}, s32[]{:S(2)}) async-start(s8[7962624]{0:T(1024)(128)(4,1)} %bitcast.143), calls=%async_computation.1 | async-start | bytes 7536640
  15.1 2.1 %collective-permute-start.3 = (bf16[4,4,24,384]{3,2,1,0:T(8,128)(2,1)S(1)}, bf16[4,4,24,384]{3,2,1,0:T(8,128)(2,1)S(1)}, u32[]{:S(2)}, u32[]{:S(2)}) collective-permute-start(bf16[4,4,24,384]{3,2,1,0:T(8,128)(2,1)S(1)} %bitcast.130), channel_id=1, source_target_pairs={{0,8},{1,9},{2,10},{3,11},{4,12},{5,13},{6,14},{7,15}} | collective-permute-start | bytes 884744 | tf_op jit(solution)/shard_map/ppermute | solution.py:30
  15.8 1.3 %collective-permute-start.2 = (bf16[4,1,24,384]{3,2,1,0:T(8,128)(2,1)S(1)}, bf16[4,1,24,384]{3,2,1,0:T(8,128)(2,1)S(1)}, u32[]{:S(2)}, u32[]{:S(2)}) collective-permute-start(bf16[4,1,24,384]{3,2,1,0:T(8,128)(2,1)S(1)} %get-tuple-element.12), channel_id=1, source_target_pairs={{0,9},{1,10},{2,11},{3,12},{4,13},{5,14},{6,15}} | collective-permute-start | bytes 221192 | tf_op jit(solution)/shard_map/ppermute | solution.py:30
  16.5 0.7 collective-permute-start.4
  18.3 6.0 %copy-start = (bf16[4,4,24,384]{3,2,1,0:T(8,128)(2,1)S(1)}, bf16[4,4,24,384]{3,2,1,0:T(8,128)(2,1)}, u32[]{:S(2)}) copy-start(bf16[4,4,24,384]{3,2,1,0:T(8,128)(2,1)} %param.3) | copy-start | bytes 884740
  24.4 25.5 %collective-permute-start.5 = (bf16[4,4,24,384]{3,2,1,0:T(8,128)(2,1)S(1)}, bf16[4,4,24,384]{3,2,1,0:T(8,128)(2,1)S(1)}, u32[]{:S(2)}, u32[]{:S(2)}) collective-permute-start(bf16[4,4,24,384]{3,2,1,0:T(8,128)(2,1)S(1)} %fusion.91), channel_id=1, source_target_pairs={{8,16},{9,17},{10,18},{11,19},{12,20},{13,21},{14,22},{15,23}} | collective-permute-start | bytes 884744 | tf_op jit(solution)/shard_map/ppermute | solution.py:30
  25.8 24.2 %collective-permute-start.10 = (bf16[4,1,24,384]{3,2,1,0:T(8,128)(2,1)S(1)}, bf16[4,1,24,384]{3,2,1,0:T(8,128)(2,1)S(1)}, u32[]{:S(2)}, u32[]{:S(2)}) collective-permute-start(bf16[4,1,24,384]{3,2,1,0:T(8,128)(2,1)S(1)} %get-tuple-element.8), channel_id=1, source_target_pairs={{9,16},{10,17},{11,18},{12,19},{13,20},{14,21},{15,22}} | collective-permute-start | bytes 221192 | tf_op jit(solution)/shard_map/ppermute | solution.py:30
  27.2 22.7 %collective-permute-start.9 = (bf16[4,1,24,384]{3,2,1,0:T(8,128)(2,1)S(1)}, bf16[4,1,24,384]{3,2,1,0:T(8,128)(2,1)S(1)}, u32[]{:S(2)}, u32[]{:S(2)}) collective-permute-start(bf16[4,1,24,384]{3,2,1,0:T(8,128)(2,1)S(1)} %get-tuple-element.7), channel_id=1, source_target_pairs={{8,17},{9,18},{10,19},{11,20},{12,21},{13,22},{14,23}} | collective-permute-start | bytes 221192 | tf_op jit(solution)/shard_map/ppermute | solution.py:30
  57.1 10.3 %collective-permute-start.12 = (bf16[4,4,24,384]{3,2,1,0:T(8,128)(2,1)S(1)}, bf16[4,4,24,384]{3,2,1,0:T(8,128)(2,1)S(1)}, u32[]{:S(2)}, u32[]{:S(2)}) collective-permute-start(bf16[4,4,24,384]{3,2,1,0:T(8,128)(2,1)S(1)} %bitcast.128), channel_id=1, source_target_pairs={{16,24},{17,25},{18,26},{19,27},{20,28},{21,29},{22,30},{23,31}} | collective-permute-start | bytes 884744 | tf_op jit(solution)/shard_map/ppermute | solution.py:30
  58.5 7.7 %collective-permute-start.11 = (bf16[4,1,24,384]{3,2,1,0:T(8,128)(2,1)S(1)}, bf16[4,1,24,384]{3,2,1,0:T(8,128)(2,1)S(1)}, u32[]{:S(2)}, u32[]{:S(2)}) collective-permute-start(bf16[4,1,24,384]{3,2,1,0:T(8,128)(2,1)S(1)} %get-tuple-element.5), channel_id=1, source_target_pairs={{16,25},{17,26},{18,27},{19,28},{20,29},{21,30},{22,31}} | collective-permute-start | bytes 221192 | tf_op jit(solution)/shard_map/ppermute | solution.py:30
  59.8 7.7 %collective-permute-start.13 = (bf16[4,1,24,384]{3,2,1,0:T(8,128)(2,1)S(1)}, bf16[4,1,24,384]{3,2,1,0:T(8,128)(2,1)S(1)}, u32[]{:S(2)}, u32[]{:S(2)}) collective-permute-start(bf16[4,1,24,384]{3,2,1,0:T(8,128)(2,1)S(1)} %get-tuple-element.6), channel_id=1, source_target_pairs={{17,24},{18,25},{19,26},{20,27},{21,28},{22,29},{23,30}} | collective-permute-start | bytes 221192 | tf_op jit(solution)/shard_map/ppermute | solution.py:30
  61.1 16.5 %collective-permute-start.6 = (bf16[1,4,24,384]{3,2,1,0:T(8,128)(2,1)S(1)}, bf16[1,4,24,384]{3,2,1,0:T(8,128)(2,1)S(1)}, u32[]{:S(2)}, u32[]{:S(2)}) collective-permute-start(bf16[1,4,24,384]{3,2,1,0:T(8,128)(2,1)S(1)} %get-tuple-element.11), channel_id=1, source_target_pairs={{16,24},{17,25},{18,26},{19,27},{20,28},{21,29},{22,30},{23,31}} | collective-permute-start | bytes 221192 | tf_op jit(solution)/shard_map/ppermute | solution.py:30
  62.4 16.6 %collective-permute-start.7 = (bf16[1,4,24,384]{3,2,1,0:T(8,128)(2,1)S(1)}, bf16[1,4,24,384]{3,2,1,0:T(8,128)(2,1)S(1)}, u32[]{:S(2)}, u32[]{:S(2)}) collective-permute-start(bf16[1,4,24,384]{3,2,1,0:T(8,128)(2,1)S(1)} %get-tuple-element.10), channel_id=1, source_target_pairs={{16,8},{17,9},{18,10},{19,11},{20,12},{21,13},{22,14},{23,15}} | collective-permute-start | bytes 221192 | tf_op jit(solution)/shard_map/ppermute | solution.py:30
  66.2 12.8 %collective-permute-start.8 = (bf16[1,4,24,384]{3,2,1,0:T(8,128)(2,1)S(1)}, bf16[1,4,24,384]{3,2,1,0:T(8,128)(2,1)S(1)}, u32[]{:S(2)}, u32[]{:S(2)}) collective-permute-start(bf16[1,4,24,384]{3,2,1,0:T(8,128)(2,1)S(1)} %get-tuple-element.9), channel_id=1, source_target_pairs={{16,0},{17,1},{18,2},{19,3},{20,4},{21,5},{22,6},{23,7}} | collective-permute-start | bytes 221192 | tf_op jit(solution)/shard_map/ppermute | solution.py:30
  71.8 7.2 %collective-permute-start.15 = (bf16[1,4,24,384]{3,2,1,0:T(8,128)(2,1)S(1)}, bf16[1,4,24,384]{3,2,1,0:T(8,128)(2,1)S(1)}, u32[]{:S(2)}, u32[]{:S(2)}) collective-permute-start(bf16[1,4,24,384]{3,2,1,0:T(8,128)(2,1)S(1)} %bitcast.140), channel_id=1, source_target_pairs={{24,8},{25,9},{26,10},{27,11},{28,12},{29,13},{30,14},{31,15}} | collective-permute-start | bytes 221192 | tf_op jit(solution)/shard_map/ppermute | solution.py:30
  72.8 6.2 %collective-permute-start.16 = (bf16[1,4,24,384]{3,2,1,0:T(8,128)(2,1)S(1)}, bf16[1,4,24,384]{3,2,1,0:T(8,128)(2,1)S(1)}, u32[]{:S(2)}, u32[]{:S(2)}) collective-permute-start(bf16[1,4,24,384]{3,2,1,0:T(8,128)(2,1)S(1)} %bitcast.141), channel_id=1, source_target_pairs={{24,0},{25,1},{26,2},{27,3},{28,4},{29,5},{30,6},{31,7}} | collective-permute-start | bytes 221192 | tf_op jit(solution)/shard_map/ppermute | solution.py:30
  77.6 8.4 %collective-permute-start.14 = (bf16[1,4,24,384]{3,2,1,0:T(8,128)(2,1)S(1)}, bf16[1,4,24,384]{3,2,1,0:T(8,128)(2,1)S(1)}, u32[]{:S(2)}, u32[]{:S(2)}) collective-permute-start(bf16[1,4,24,384]{3,2,1,0:T(8,128)(2,1)S(1)} %bitcast.142), channel_id=1, source_target_pairs={{24,16},{25,17},{26,18},{27,19},{28,20},{29,21},{30,22},{31,23}} | collective-permute-start | bytes 221192 | tf_op jit(solution)/shard_map/ppermute | solution.py:30

commit v18 on v17

--- a/solution.py
+++ b/solution.py
@@ -83,7 +83,9 @@
             activated = jnp.pad(window, ((2, 0), (0, 0), (0, 0), (0, 0)))
             split = (segment_count // 2) * group
             branch = None
-            for low, high in ((0, split), (split, frame_count)):
+            own_start = frame_count - group
+            bounds = [(0, split), (split, own_start), (own_start, frame_count)]
+            for low, high in [(a, b) for a, b in bounds if b > a]:
                 part = causal_conv(activated[low : high + 2], kernel, 0).astype(jnp.bfloat16)
                 for target in range(low // group, high // group):
                     chunk = part[target * group - low : (target + 1) * group - low]

time: 88.3 us -> 96.1 us (1.088)
  matrix products: 25.6 us -> 31.3 us
  waiting for transfers between devices: 30.9 us -> 32.3 us
    conv_general_dilated x5 -> x6, matrix products: 25.6 us -> 31.3 us  [causal_conv(): lax.conv_general_dilated(window[None], kernel, window_strides=(1, 1, 1),...]
    ppermute x17, waiting for transfers between devices: 30.9 us -> 32.3 us  [send(): return lax.ppermute(value, BOTH, pairs)]
    convert_element_type x6 -> x5, other arithmetic: 2.72 us -> 2.83 us  [activate(): return jax.nn.silu(widened * lax.rsqrt(mean_square + 1e-06) * gain_row.as...]
  transfers between devices with their start and end apart: 17 -> 17, of which waited for: 3 -> 4; matrix products, arithmetic and copies ran while one was open for 13% -> 17% of each run, Pallas kernels for 0% -> 0%
where the time goes in v18:
time: 96.1 us; the launch traced here: 94.5 us
  waiting for transfers between devices  32.3 us (34%)
  matrix products  31.3 us (33%)
  starting transfers between devices  17.8 us (19%)
  other arithmetic  6.64 us (7%)
  local copies, waits for them, and re-layouts  5.66 us (6%)
    ppermute x17, waiting for transfers between devices, send(): return lax.ppermute(value, BOTH, pairs)  32.3 us
    conv_general_dilated x6, matrix products, causal_conv(): lax.conv_general_dilated(window[None], kernel, window_strides=(1, 1, 1),...  31.3 us
    ppermute x17, starting transfers between devices, send(): return lax.ppermute(value, BOTH, pairs)  17.8 us
    convert_element_type x5, other arithmetic, activate(): return jax.nn.silu(widened * lax.rsqrt(mean_square + 1e-06) * gain_row.as...  2.83 us
    reduce_sum x6, other arithmetic, activate(): mean_square = jnp.mean(widened * widened, axis=-1, keepdims=True)  2.25 us
  transfers between devices with their start and end apart: 17, of which 4 were waited for; matrix products, arithmetic and copies ran while one was open for 17% of the time, Pallas kernels for 0%

profile of v18, /device:TPU:17, one launch (start us, length us, event | category | flops | bytes accessed | tf_op | source)
XLA Modules:
  0.0 94.5 jit_solution(11585123403756267135)
XLA Ops:
  0.0 0.9 fusion.157
  0.9 0.7 collective-permute-start.1
  1.6 0.7 collective-permute-start
  2.3 1.1 %fusion.98 = f32[4,4,24]{2,1,0:T(4,128)S(1)} fusion(bf16[4,4,24,384]{3,2,1,0:T(8,128)(2,1)} %param.3), kind=kLoop, calls=%fused_computation.80 | loop fusion | flops 441984 | bytes 296448 | tf_op jit(solution)/shard_map/reduce_sum | solution.py:11
  3.4 0.7 convert_reduce_fusion
  4.1 1.2 %fusion.105 = bf16[4,4,24,384]{3,2,1,0:T(8,128)(2,1)S(1)} fusion(bf16[4,4,24,384]{3,2,1,0:T(8,128)(2,1)} %param.3, f32[384]{0:T(512)S(1)} %convert_reduce_fusion, f32[4,4,24]{2,1,0:T(4,128)S(1)} %add_rsqrt_fusion.3), kind=kLoop, calls=%fused_computation.87 | loop fusion | flops 1179648 | bytes 592896 | tf_op jit(solution)/shard_map/convert_element_type | solution.py:14
  5.6 0.2 fusion.123
  5.8 0.2 copy.234
  6.0 0.2 pad.5.clone
  6.5 8.3 %fusion.33 = bf16[4,4,8,4,384]{4,2,3,1,0:T(8,128)(2,1)S(1)} fusion(bf16[1,3,3,3,384,384]{5,4,3,2,1,0:T(8,128)(2,1)} %param.5, bf16[4,6,1,7,2,384]{5,3,4,1,0,2:T(8,128)(2,1)S(1)} %slice.93, bf16[4,6,1,8,4,384]{5,3,4,1,0,2:T(8,128)(2,1)S(1)} %copy.187, pred[8,4]{0,1:T(4,128)(4,1)S(1)} %copy-done.1), kind=kOutput, calls=%fused_computation.27 | convolution fusion | flops 3060695040 | bytes 9203744 | tf_op jit(solution)/shard_map/conv_general_dilated | solution.py:18
  14.7 0.2 copy.188
  15.1 0.7 collective-permute-start.3
  15.8 0.7 collective-permute-start.2
  16.5 0.7 collective-permute-start.4
  17.4 0.3 fusion.108
  17.7 0.2 copy.235
  17.9 0.2 pad.7.clone
  18.4 5.6 %fusion.30 = bf16[4,4,8,4,384]{4,2,3,1,0:T(8,128)(2,1)S(1)} fusion(bf16[1,3,3,3,384,384]{5,4,3,2,1,0:T(8,128)(2,1)S(1)} %bitcast.144, bf16[4,6,1,7,2,384]{5,3,4,1,0,2:T(8,128)(2,1)S(1)} %slice.97, bf16[4,6,1,8,4,384]{5,3,4,1,0,2:T(8,128)(2,1)S(1)} %copy.194, pred[8,4]{0,1:T(4,128)(4,1)S(1)} %copy-done.1), kind=kOutput, calls=%fused_computation.26 | convolution fusion | flops 3060695040 | bytes 9203744 | tf_op jit(solution)/shard_map/conv_general_dilated | solution.py:18
  24.0 0.2 copy.195
  24.4 1.3 %collective-permute-start.5 = (bf16[4,4,24,384]{3,2,1,0:T(8,128)(2,1)S(1)}, bf16[4,4,24,384]{3,2,1,0:T(8,128)(2,1)S(1)}, u32[]{:S(2)}, u32[]{:S(2)}) collective-permute-start(bf16[4,4,24,384]{3,2,1,0:T(8,128)(2,1)S(1)} %fusion.106), channel_id=1, source_target_pairs={{8,16},{9,17},{10,18},{11,19},{12,20},{13,21},{14,22},{15,23}} | collective-permute-start | bytes 884744 | tf_op jit(solution)/shard_map/ppermute | solution.py:30
  25.7 1.5 %collective-permute-start.10 = (bf16[4,1,24,384]{3,2,1,0:T(8,128)(2,1)S(1)}, bf16[4,1,24,384]{3,2,1,0:T(8,128)(2,1)S(1)}, u32[]{:S(2)}, u32[]{:S(2)}) collective-permute-start(bf16[4,1,24,384]{3,2,1,0:T(8,128)(2,1)S(1)} %get-tuple-element.10), channel_id=1, source_target_pairs={{9,16},{10,17},{11,18},{12,19},{13,20},{14,21},{15,22}} | collective-permute-start | bytes 221192 | tf_op jit(solution)/shard_map/ppermute | solution.py:30
  27.2 1.3 %collective-permute-start.9 = (bf16[4,1,24,384]{3,2,1,0:T(8,128)(2,1)S(1)}, bf16[4,1,24,384]{3,2,1,0:T(8,128)(2,1)S(1)}, u32[]{:S(2)}, u32[]{:S(2)}) collective-permute-start(bf16[4,1,24,384]{3,2,1,0:T(8,128)(2,1)S(1)} %get-tuple-element.9), channel_id=1, source_target_pairs={{8,17},{9,18},{10,19},{11,20},{12,21},{13,22},{14,23}} | collective-permute-start | bytes 221192 | tf_op jit(solution)/shard_map/ppermute | solution.py:30
  28.5 21.4 %collective-permute-done.10 = bf16[4,1,24,384]{3,2,1,0:T(8,128)(2,1)S(1)} collective-permute-done((bf16[4,1,24,384]{3,2,1,0:T(8,128)(2,1)S(1)}, bf16[4,1,24,384]{3,2,1,0:T(8,128)(2,1)S(1)}, u32[]{:S(2)}, u32[]{:S(2)}) %collective-permute-start.10) | collective-permute-done | bytes 73760 | tf_op jit(solution)/shard_map/ppermute | solution.py:30
  50.1 0.3 fusion.109
  50.5 0.2 copy.236
  50.6 0.2 pad.9.clone
  51.1 7.9 %fusion.27 = bf16[4,4,8,4,384]{4,2,3,1,0:T(8,128)(2,1)S(1)} fusion(bf16[1,3,3,3,384,384]{5,4,3,2,1,0:T(8,128)(2,1)} %param.5, bf16[4,6,1,7,2,384]{5,3,4,1,0,2:T(8,128)(2,1)S(1)} %slice.105, bf16[4,6,1,8,4,384]{5,3,4,1,0,2:T(8,128)(2,1)S(1)} %copy.201, pred[8,4]{0,1:T(4,128)(4,1)S(1)} %copy-done.1), kind=kOutput, calls=%fused_computation.25 | convolution fusion | flops 3060695040 | bytes 9203744 | tf_op jit(solution)/shard_map/conv_general_dilated | solution.py:18
  59.0 0.2 copy.202
  59.3 1.3 %collective-permute-start.12 = (bf16[4,4,24,384]{3,1,2,0:T(4,128)(2,1)S(1)}, bf16[4,4,24,384]{3,1,2,0:T(4,128)(2,1)S(1)}, u32[]{:S(2)}, u32[]{:S(2)}) collective-permute-start(bf16[4,4,24,384]{3,1,2,0:T(4,128)(2,1)S(1)} %slice_bitcast_fusion.2), channel_id=1, source_target_pairs={{16,24},{17,25},{18,26},{19,27},{20,28},{21,29},{22,30},{23,31}} | collective-permute-start | bytes 884744 | tf_op jit(solution)/shard_map/ppermute | solution.py:30
  60.6 0.2 fusion.153
  60.8 1.3 %collective-permute-start.11 = (bf16[4,1,24,384]{3,1,2,0:T(2,128)(2,1)S(1)}, bf16[4,1,24,384]{3,1,2,0:T(2,128)(2,1)S(1)}, u32[]{:S(2)}, u32[]{:S(2)}) collective-permute-start(bf16[4,1,24,384]{3,1,2,0:T(2,128)(2,1)S(1)} %get-tuple-element.7), channel_id=1, source_target_pairs={{16,25},{17,26},{18,27},{19,28},{20,29},{21,30},{22,31}} | collective-permute-start | bytes 221192 | tf_op jit(solution)/shard_map/ppermute | solution.py:30
  62.1 1.3 %collective-permute-start.13 = (bf16[4,1,24,384]{3,1,2,0:T(2,128)(2,1)S(1)}, bf16[4,1,24,384]{3,1,2,0:T(2,128)(2,1)S(1)}, u32[]{:S(2)}, u32[]{:S(2)}) collective-permute-start(bf16[4,1,24,384]{3,1,2,0:T(2,128)(2,1)S(1)} %get-tuple-element.8), channel_id=1, source_target_pairs={{17,24},{18,25},{19,26},{20,27},{21,28},{22,29},{23,30}} | collective-permute-start | bytes 221192 | tf_op jit(solution)/shard_map/ppermute | solution.py:30
  63.5 1.3 %collective-permute-start.6 = (bf16[1,4,24,384]{3,2,1,0:T(8,128)(2,1)S(1)}, bf16[1,4,24,384]{3,2,1,0:T(8,128)(2,1)S(1)}, u32[]{:S(2)}, u32[]{:S(2)}) collective-permute-start(bf16[1,4,24,384]{3,2,1,0:T(8,128)(2,1)S(1)} %get-tuple-element.13), channel_id=1, source_target_pairs={{16,24},{17,25},{18,26},{19,27},{20,28},{21,29},{22,30},{23,31}} | collective-permute-start | bytes 221192 | tf_op jit(solution)/shard_map/ppermute | solution.py:30
  64.8 1.3 %collective-permute-start.7 = (bf16[1,4,24,384]{3,2,1,0:T(8,128)(2,1)S(1)}, bf16[1,4,24,384]{3,2,1,0:T(8,128)(2,1)S(1)}, u32[]{:S(2)}, u32[]{:S(2)}) collective-permute-start(bf16[1,4,24,384]{3,2,1,0:T(8,128)(2,1)S(1)} %get-tuple-element.12), channel_id=1, source_target_pairs={{16,8},{17,9},{18,10},{19,11},{20,12},{21,13},{22,14},{23,15}} | collective-permute-start | bytes 221192 | tf_op jit(solution)/shard_map/ppermute | solution.py:30
  66.1 3.8 %collective-permute-done.11 = bf16[4,1,24,384]{3,1,2,0:T(2,128)(2,1)S(1)} collective-permute-done((bf16[4,1,24,384]{3,1,2,0:T(2,128)(2,1)S(1)}, bf16[4,1,24,384]{3,1,2,0:T(2,128)(2,1)S(1)}, u32[]{:S(2)}, u32[]{:S(2)}) %collective-permute-start.11) | collective-permute-done | bytes 73760 | tf_op jit(solution)/shard_map/ppermute | solution.py:30
  69.9 1.3 %collective-permute-start.8 = (bf16[1,4,24,384]{3,2,1,0:T(8,128)(2,1)S(1)}, bf16[1,4,24,384]{3,2,1,0:T(8,128)(2,1)S(1)}, u32[]{:S(2)}, u32[]{:S(2)}) collective-permute-start(bf16[1,4,24,384]{3,2,1,0:T(8,128)(2,1)S(1)} %get-tuple-element.11), channel_id=1, source_target_pairs={{16,0},{17,1},{18,2},{19,3},{20,4},{21,5},{22,6},{23,7}} | collective-permute-start | bytes 221192 | tf_op jit(solution)/shard_map/ppermute | solution.py:30
  71.2 0.3 collective-permute-done.13
  71.5 0.6 fusion.39
  72.3 0.8 fusion.46
  73.4 0.2 copy.217
  73.7 6.4 %fusion.47 = bf16[2,4,8,4,384]{4,2,3,1,0:T(8,128)(2,1)S(1)} fusion(bf16[1,3,3,3,384,384]{5,4,3,2,1,0:T(8,128)(2,1)} %param.5, bf16[4,6,1,7,2,384]{5,3,4,1,0,2:T(8,128)(2,1)S(1)} %slice.115, bf16[4,6,1,8,4,384]{5,3,4,1,0,2:T(8,128)(2,1)S(1)} %copy.217, pred[8,4]{0,1:T(4,128)(4,1)S(1)} %copy-done.1), kind=kOutput, calls=%fused_computation.37 | convolution fusion | flops 2041282560 | bytes 9007136 | tf_op jit(solution)/shard_map/conv_general_dilated | solution.py:18
  80.3 0.7 collective-permute-start.15
  81.0 0.7 collective-permute-start.16
  82.1 1.5 %fusion.56 = bf16[1,4,8,4,384]{4,2,3,1,0:T(8,128)(2,1)S(1)} fusion(bf16[1,3,3,3,384,384]{5,4,3,2,1,0:T(8,128)(2,1)S(1)} %bitcast.146, bf16[3,6,1,7,2,384]{5,3,4,1,0,2:T(8,128)(2,1)S(1)} %slice.113, bf16[3,6,1,8,4,384]{5,3,4,1,0,2:T(8,128)(2,1)S(1)} %copy.212, pred[8,4]{0,1:T(4,128)(4,1)S(1)} %copy-done.1), kind=kOutput, calls=%fused_computation.40 | convolution fusion | flops 1021304832 | bytes 8696864 | tf_op jit(solution)/shard_map/conv_general_dilated | solution.py:18
  84.1 1.3 %collective-permute-start.14 = (bf16[1,4,24,384]{3,2,1,0:T(8,128)(2,1)S(1)}, bf16[1,4,24,384]{3,2,1,0:T(8,128)(2,1)S(1)}, u32[]{:S(2)}, u32[]{:S(2)}) collective-permute-start(bf16[1,4,24,384]{3,2,1,0:T(8,128)(2,1)S(1)} %bitcast.142), channel_id=1, source_target_pairs={{24,16},{25,17},{26,18},{27,19},{28,20},{29,21},{30,22},{31,23}} | collective-permute-start | bytes 221192 | tf_op jit(solution)/shard_map/ppermute | solution.py:30
  85.4 1.6 %fusion.59 = bf16[1,4,8,4,384]{4,2,3,1,0:T(8,128)(2,1)S(1)} fusion(bf16[1,3,3,3,384,384]{5,4,3,2,1,0:T(8,128)(2,1)S(1)} %bitcast.146, bf16[3,6,1,7,2,384]{5,3,4,1,0,2:T(8,128)(2,1)S(1)} %slice.110, bf16[3,6,1,8,4,384]{5,3,4,1,0,2:T(8,128)(2,1)S(1)} %copy.207, pred[8,4]{0,1:T(4,128)(4,1)S(1)} %copy-done.1), kind=kOutput, calls=%fused_computation.41 | convolution fusion | flops 1021304832 | bytes 8696864 | tf_op jit(solution)/shard_map/conv_general_dilated | solution.py:18
  87.1 6.8 %collective-permute-done.14 = bf16[1,4,24,384]{3,2,1,0:T(8,128)(2,1)S(1)} collective-permute-done((bf16[1,4,24,384]{3,2,1,0:T(8,128)(2,1)S(1)}, bf16[1,4,24,384]{3,2,1,0:T(8,128)(2,1)S(1)}, u32[]{:S(2)}, u32[]{:S(2)}) %collective-permute-start.14) | collective-permute-done | bytes 73760 | tf_op jit(solution)/shard_map/ppermute | solution.py:30
  93.8 0.7 add_convert_fusion
  (76 shorter events, 3.3 us)
Async XLA Ops:
  0.9 4.4 %collective-permute-start.1 = (bf16[4,1,24,384]{3,2,1,0:T(8,128)(2,1)S(1)}, bf16[4,1,24,384]{3,2,1,0:T(8,128)(2,1)S(1)}, u32[]{:S(2)}, u32[]{:S(2)}) collective-permute-start(bf16[4,1,24,384]{3,2,1,0:T(8,128)(2,1)S(1)} %get-tuple-element.17), channel_id=1, source_target_pairs={{1,0},{2,1},{3,2},{4,3},{5,4},{6,5},{7,6}} | collective-permute-start | bytes 221192 | tf_op jit(solution)/shard_map/ppermute | solution.py:30
  1.6 3.8 %collective-permute-start = (bf16[4,1,24,384]{3,2,1,0:T(8,128)(2,1)S(1)}, bf16[4,1,24,384]{3,2,1,0:T(8,128)(2,1)S(1)}, u32[]{:S(2)}, u32[]{:S(2)}) collective-permute-start(bf16[4,1,24,384]{3,2,1,0:T(8,128)(2,1)S(1)} %get-tuple-element.16), channel_id=1, source_target_pairs={{0,1},{1,2},{2,3},{3,4},{4,5},{5,6},{6,7}} | collective-permute-start | bytes 221192 | tf_op jit(solution)/shard_map/ppermute | solution.py:30
  5.8 0.7 copy-start.1
  6.3 12.0 %slice-start = ((s8[7962624]{0:T(1024)(128)(4,1)}), s8[4194304]{0:T(1024)(128)(4,1)S(1)}, s32[]{:S(2)}) async-start(s8[7962624]{0:T(1024)(128)(4,1)} %bitcast.143), calls=%async_computation | async-start | bytes 8388608
  6.5 11.9 %slice-start.1 = ((s8[7962624]{0:T(1024)(128)(4,1)}), s8[3768320]{0:T(1024)(128)(4,1)S(1)}, s32[]{:S(2)}) async-start(s8[7962624]{0:T(1024)(128)(4,1)} %bitcast.143), calls=%async_computation.1 | async-start | bytes 7536640
  15.1 2.1 %collective-permute-start.3 = (bf16[4,4,24,384]{3,2,1,0:T(8,128)(2,1)S(1)}, bf16[4,4,24,384]{3,2,1,0:T(8,128)(2,1)S(1)}, u32[]{:S(2)}, u32[]{:S(2)}) collective-permute-start(bf16[4,4,24,384]{3,2,1,0:T(8,128)(2,1)S(1)} %bitcast.130), channel_id=1, source_target_pairs={{0,8},{1,9},{2,10},{3,11},{4,12},{5,13},{6,14},{7,15}} | collective-permute-start | bytes 884744 | tf_op jit(solution)/shard_map/ppermute | solution.py:30
  15.8 1.3 %collective-permute-start.2 = (bf16[4,1,24,384]{3,2,1,0:T(8,128)(2,1)S(1)}, bf16[4,1,24,384]{3,2,1,0:T(8,128)(2,1)S(1)}, u32[]{:S(2)}, u32[]{:S(2)}) collective-permute-start(bf16[4,1,24,384]{3,2,1,0:T(8,128)(2,1)S(1)} %get-tuple-element.14), channel_id=1, source_target_pairs={{0,9},{1,10},{2,11},{3,12},{4,13},{5,14},{6,15}} | collective-permute-start | bytes 221192 | tf_op jit(solution)/shard_map/ppermute | solution.py:30
  16.5 0.7 collective-permute-start.4
  18.3 6.0 %copy-start = (bf16[4,4,24,384]{3,2,1,0:T(8,128)(2,1)S(1)}, bf16[4,4,24,384]{3,2,1,0:T(8,128)(2,1)}, u32[]{:S(2)}) copy-start(bf16[4,4,24,384]{3,2,1,0:T(8,128)(2,1)} %param.3) | copy-start | bytes 884740
  24.4 25.5 %collective-permute-start.5 = (bf16[4,4,24,384]{3,2,1,0:T(8,128)(2,1)S(1)}, bf16[4,4,24,384]{3,2,1,0:T(8,128)(2,1)S(1)}, u32[]{:S(2)}, u32[]{:S(2)}) collective-permute-start(bf16[4,4,24,384]{3,2,1,0:T(8,128)(2,1)S(1)} %fusion.106), channel_id=1, source_target_pairs={{8,16},{9,17},{10,18},{11,19},{12,20},{13,21},{14,22},{15,23}} | collective-permute-start | bytes 884744 | tf_op jit(solution)/shard_map/ppermute | solution.py:30
  25.7 24.2 %collective-permute-start.10 = (bf16[4,1,24,384]{3,2,1,0:T(8,128)(2,1)S(1)}, bf16[4,1,24,384]{3,2,1,0:T(8,128)(2,1)S(1)}, u32[]{:S(2)}, u32[]{:S(2)}) collective-permute-start(bf16[4,1,24,384]{3,2,1,0:T(8,128)(2,1)S(1)} %get-tuple-element.10), channel_id=1, source_target_pairs={{9,16},{10,17},{11,18},{12,19},{13,20},{14,21},{15,22}} | collective-permute-start | bytes 221192 | tf_op jit(solution)/shard_map/ppermute | solution.py:30
  27.2 22.7 %collective-permute-start.9 = (bf16[4,1,24,384]{3,2,1,0:T(8,128)(2,1)S(1)}, bf16[4,1,24,384]{3,2,1,0:T(8,128)(2,1)S(1)}, u32[]{:S(2)}, u32[]{:S(2)}) collective-permute-start(bf16[4,1,24,384]{3,2,1,0:T(8,128)(2,1)S(1)} %get-tuple-element.9), channel_id=1, source_target_pairs={{8,17},{9,18},{10,19},{11,20},{12,21},{13,22},{14,23}} | collective-permute-start | bytes 221192 | tf_op jit(solution)/shard_map/ppermute | solution.py:30
  59.3 12.2 %collective-permute-start.12 = (bf16[4,4,24,384]{3,1,2,0:T(4,128)(2,1)S(1)}, bf16[4,4,24,384]{3,1,2,0:T(4,128)(2,1)S(1)}, u32[]{:S(2)}, u32[]{:S(2)}) collective-permute-start(bf16[4,4,24,384]{3,1,2,0:T(4,128)(2,1)S(1)} %slice_bitcast_fusion.2), channel_id=1, source_target_pairs={{16,24},{17,25},{18,26},{19,27},{20,28},{21,29},{22,30},{23,31}} | collective-permute-start | bytes 884744 | tf_op jit(solution)/shard_map/ppermute | solution.py:30
  60.8 9.1 %collective-permute-start.11 = (bf16[4,1,24,384]{3,1,2,0:T(2,128)(2,1)S(1)}, bf16[4,1,24,384]{3,1,2,0:T(2,128)(2,1)S(1)}, u32[]{:S(2)}, u32[]{:S(2)}) collective-permute-start(bf16[4,1,24,384]{3,1,2,0:T(2,128)(2,1)S(1)} %get-tuple-element.7), channel_id=1, source_target_pairs={{16,25},{17,26},{18,27},{19,28},{20,29},{21,30},{22,31}} | collective-permute-start | bytes 221192 | tf_op jit(solution)/shard_map/ppermute | solution.py:30
  62.1 9.3 %collective-permute-start.13 = (bf16[4,1,24,384]{3,1,2,0:T(2,128)(2,1)S(1)}, bf16[4,1,24,384]{3,1,2,0:T(2,128)(2,1)S(1)}, u32[]{:S(2)}, u32[]{:S(2)}) collective-permute-start(bf16[4,1,24,384]{3,1,2,0:T(2,128)(2,1)S(1)} %get-tuple-element.8), channel_id=1, source_target_pairs={{17,24},{18,25},{19,26},{20,27},{21,28},{22,29},{23,30}} | collective-permute-start | bytes 221192 | tf_op jit(solution)/shard_map/ppermute | solution.py:30
  63.5 20.6 %collective-permute-start.6 = (bf16[1,4,24,384]{3,2,1,0:T(8,128)(2,1)S(1)}, bf16[1,4,24,384]{3,2,1,0:T(8,128)(2,1)S(1)}, u32[]{:S(2)}, u32[]{:S(2)}) collective-permute-start(bf16[1,4,24,384]{3,2,1,0:T(8,128)(2,1)S(1)} %get-tuple-element.13), channel_id=1, source_target_pairs={{16,24},{17,25},{18,26},{19,27},{20,28},{21,29},{22,30},{23,31}} | collective-permute-start | bytes 221192 | tf_op jit(solution)/shard_map/ppermute | solution.py:30
  64.8 22.2 %collective-permute-start.7 = (bf16[1,4,24,384]{3,2,1,0:T(8,128)(2,1)S(1)}, bf16[1,4,24,384]{3,2,1,0:T(8,128)(2,1)S(1)}, u32[]{:S(2)}, u32[]{:S(2)}) collective-permute-start(bf16[1,4,24,384]{3,2,1,0:T(8,128)(2,1)S(1)} %get-tuple-element.12), channel_id=1, source_target_pairs={{16,8},{17,9},{18,10},{19,11},{20,12},{21,13},{22,14},{23,15}} | collective-permute-start | bytes 221192 | tf_op jit(solution)/shard_map/ppermute | solution.py:30
  69.9 17.1 %collective-permute-start.8 = (bf16[1,4,24,384]{3,2,1,0:T(8,128)(2,1)S(1)}, bf16[1,4,24,384]{3,2,1,0:T(8,128)(2,1)S(1)}, u32[]{:S(2)}, u32[]{:S(2)}) collective-permute-start(bf16[1,4,24,384]{3,2,1,0:T(8,128)(2,1)S(1)} %get-tuple-element.11), channel_id=1, source_target_pairs={{16,0},{17,1},{18,2},{19,3},{20,4},{21,5},{22,6},{23,7}} | collective-permute-start | bytes 221192 | tf_op jit(solution)/shard_map/ppermute | solution.py:30
  73.6 8.4 %slice-start.2 = ((s8[7962624]{0:T(1024)(128)(4,1)}), s8[4194304]{0:T(1024)(128)(4,1)S(1)}, s32[]{:S(2)}) async-start(s8[7962624]{0:T(1024)(128)(4,1)} %bitcast.145), calls=%async_computation.2 | async-start | bytes 8388608
  73.7 8.3 %slice-start.3 = ((s8[7962624]{0:T(1024)(128)(4,1)}), s8[3768320]{0:T(1024)(128)(4,1)S(1)}, s32[]{:S(2)}) async-start(s8[7962624]{0:T(1024)(128)(4,1)} %bitcast.145), calls=%async_computation.3 | async-start | bytes 7536640
  80.3 6.8 %collective-permute-start.15 = (bf16[1,4,24,384]{3,2,1,0:T(8,128)(2,1)S(1)}, bf16[1,4,24,384]{3,2,1,0:T(8,128)(2,1)S(1)}, u32[]{:S(2)}, u32[]{:S(2)}) collective-permute-start(bf16[1,4,24,384]{3,2,1,0:T(8,128)(2,1)S(1)} %bitcast.140), channel_id=1, source_target_pairs={{24,8},{25,9},{26,10},{27,11},{28,12},{29,13},{30,14},{31,15}} | collective-permute-start | bytes 221192 | tf_op jit(solution)/shard_map/ppermute | solution.py:30
  81.0 6.0 %collective-permute-start.16 = (bf16[1,4,24,384]{3,2,1,0:T(8,128)(2,1)S(1)}, bf16[1,4,24,384]{3,2,1,0:T(8,128)(2,1)S(1)}, u32[]{:S(2)}, u32[]{:S(2)}) collective-permute-start(bf16[1,4,24,384]{3,2,1,0:T(8,128)(2,1)S(1)} %bitcast.141), channel_id=1, source_target_pairs={{24,0},{25,1},{26,2},{27,3},{28,4},{29,5},{30,6},{31,7}} | collective-permute-start | bytes 221192 | tf_op jit(solution)/shard_map/ppermute | solution.py:30
  84.1 9.8 %collective-permute-start.14 = (bf16[1,4,24,384]{3,2,1,0:T(8,128)(2,1)S(1)}, bf16[1,4,24,384]{3,2,1,0:T(8,128)(2,1)S(1)}, u32[]{:S(2)}, u32[]{:S(2)}) collective-permute-start(bf16[1,4,24,384]{3,2,1,0:T(8,128)(2,1)S(1)} %bitcast.142), channel_id=1, source_target_pairs={{24,16},{25,17},{26,18},{27,19},{28,20},{29,21},{30,22},{31,23}} | collective-permute-start | bytes 221192 | tf_op jit(solution)/shard_map/ppermute | solution.py:30

commit v19 on v16

--- a/solution.py
+++ b/solution.py
@@ -56,8 +56,8 @@
 
     up = [(i, i + 1) for i in range(row_count - 1)]
     down = [(i + 1, i) for i in range(row_count - 1)]
-    top = lax.ppermute(features[:, height - 1 :], "rows", up)
-    bottom = lax.ppermute(features[:, :1], "rows", down)
+    top = send(features[:, height - 1 :], up)
+    bottom = send(features[:, :1], down)
     current = features
     skip = features
     last_stage = segment_count - 1

time: 90.3 us -> 88.4 us (0.979)
  starting transfers between devices: 20.4 us -> 16.1 us
  waiting for transfers between devices: 31.7 us -> 34.1 us
    ppermute x2 -> x0, starting transfers between devices: 5.6 us -> none  [the longest x1 3.02 us: local(): top = lax.ppermute(features[:, height - 1:], 'rows', up)]
    ppermute x14 -> x16, waiting for transfers between devices: 31.7 us -> 34.1 us  [send(): return lax.ppermute(value, BOTH, pairs)]
    ppermute x14 -> x16, starting transfers between devices: 14.8 us -> 16.1 us  [send(): return lax.ppermute(value, BOTH, pairs)]
where the time goes in v19:
time: 88.4 us; the launch traced here: 87.9 us
  waiting for transfers between devices  34.1 us (39%)
  matrix products  25.6 us (29%)
  starting transfers between devices  16.1 us (18%)
  other arithmetic  6.04 us (7%)
  local copies, waits for them, and re-layouts  5.35 us (6%)
    ppermute x16, waiting for transfers between devices, send(): return lax.ppermute(value, BOTH, pairs)  34.1 us
    conv_general_dilated x5, matrix products, causal_conv(): lax.conv_general_dilated(window[None], kernel, window_strides=(1, 1, 1),...  25.6 us
    ppermute x16, starting transfers between devices, send(): return lax.ppermute(value, BOTH, pairs)  16.1 us
    convert_element_type x6, other arithmetic, activate(): return jax.nn.silu(widened * lax.rsqrt(mean_square + 1e-06) * gain_row.as...  2.72 us
  transfers between devices with their start and end apart: 16, of which 5 were waited for; matrix products, arithmetic and copies ran while one was open for 13% of the time, Pallas kernels for 0%

profile of v19, /device:TPU:17, one launch (start us, length us, event | category | flops | bytes accessed | tf_op | source)
XLA Modules:
  0.0 87.9 jit_solution(3181381328009466695)
XLA Ops:
  0.0 0.9 %fusion.138 = (bf16[4,1,24,384]{3,2,1,0:T(8,128)(2,1)S(1)}, bf16[4,1,24,384]{3,2,1,0:T(8,128)(2,1)S(1)}) fusion(bf16[4,4,24,384]{3,2,1,0:T(8,128)(2,1)} %param.3), kind=kLoop, calls=%fused_computation.147 | loop fusion | bytes 294912 | tf_op jit(solution)/shard_map/slice | solution.py:59
  0.9 0.7 collective-permute-start.1
  1.6 0.7 collective-permute-start
  2.3 1.1 %fusion.83 = f32[4,4,24]{2,1,0:T(4,128)S(1)} fusion(bf16[4,4,24,384]{3,2,1,0:T(8,128)(2,1)} %param.3), kind=kLoop, calls=%fused_computation.70 | loop fusion | flops 441984 | bytes 296448 | tf_op jit(solution)/shard_map/reduce_sum | solution.py:11
  3.4 0.7 convert_reduce_fusion
  4.1 1.2 %fusion.90 = bf16[4,4,24,384]{3,2,1,0:T(8,128)(2,1)S(1)} fusion(bf16[4,4,24,384]{3,2,1,0:T(8,128)(2,1)} %param.3, f32[384]{0:T(512)S(1)} %convert_reduce_fusion, f32[4,4,24]{2,1,0:T(4,128)S(1)} %add_rsqrt_fusion.3), kind=kLoop, calls=%fused_computation.77 | loop fusion | flops 1179648 | bytes 592896 | tf_op jit(solution)/shard_map/convert_element_type | solution.py:14
  5.8 0.2 copy.156
  6.0 0.2 pad.5.clone
  6.5 8.3 %fusion.30 = bf16[4,4,8,4,384]{4,2,3,1,0:T(8,128)(2,1)S(1)} fusion(bf16[1,3,3,3,384,384]{5,4,3,2,1,0:T(8,128)(2,1)} %param.5, bf16[4,6,1,7,2,384]{5,3,4,1,0,2:T(8,128)(2,1)S(1)} %slice.101, bf16[4,6,1,8,4,384]{5,3,4,1,0,2:T(8,128)(2,1)S(1)} %copy.116, pred[8,4]{0,1:T(4,128)(4,1)S(1)} %copy-done.1), kind=kOutput, calls=%fused_computation.21 | convolution fusion | flops 3060695040 | bytes 9203744 | tf_op jit(solution)/shard_map/conv_general_dilated | solution.py:18
  14.7 0.2 copy.117
  15.1 0.7 collective-permute-start.3
  15.8 0.7 collective-permute-start.2
  16.5 0.7 collective-permute-start.4
  17.4 0.3 fusion.93
  17.7 0.2 copy.157
  17.9 0.2 pad.7.clone
  18.4 5.7 %fusion.27 = bf16[4,4,8,4,384]{4,2,3,1,0:T(8,128)(2,1)S(1)} fusion(bf16[1,3,3,3,384,384]{5,4,3,2,1,0:T(8,128)(2,1)S(1)} %bitcast.144, bf16[4,6,1,7,2,384]{5,3,4,1,0,2:T(8,128)(2,1)S(1)} %slice.105, bf16[4,6,1,8,4,384]{5,3,4,1,0,2:T(8,128)(2,1)S(1)} %copy.123, pred[8,4]{0,1:T(4,128)(4,1)S(1)} %copy-done.1), kind=kOutput, calls=%fused_computation.20 | convolution fusion | flops 3060695040 | bytes 9203744 | tf_op jit(solution)/shard_map/conv_general_dilated | solution.py:18
  24.0 0.2 copy.124
  24.4 1.3 %collective-permute-start.5 = (bf16[4,4,24,384]{3,2,1,0:T(8,128)(2,1)S(1)}, bf16[4,4,24,384]{3,2,1,0:T(8,128)(2,1)S(1)}, u32[]{:S(2)}, u32[]{:S(2)}) collective-permute-start(bf16[4,4,24,384]{3,2,1,0:T(8,128)(2,1)S(1)} %fusion.91), channel_id=1, source_target_pairs={{8,16},{9,17},{10,18},{11,19},{12,20},{13,21},{14,22},{15,23}} | collective-permute-start | bytes 884744 | tf_op jit(solution)/shard_map/ppermute | solution.py:30
  25.8 1.5 %collective-permute-start.8 = (bf16[4,1,24,384]{3,2,1,0:T(8,128)(2,1)S(1)}, bf16[4,1,24,384]{3,2,1,0:T(8,128)(2,1)S(1)}, u32[]{:S(2)}, u32[]{:S(2)}) collective-permute-start(bf16[4,1,24,384]{3,2,1,0:T(8,128)(2,1)S(1)} %get-tuple-element.7), channel_id=1, source_target_pairs={{8,17},{9,18},{10,19},{11,20},{12,21},{13,22},{14,23}} | collective-permute-start | bytes 221192 | tf_op jit(solution)/shard_map/ppermute | solution.py:30
  27.2 1.3 %collective-permute-start.9 = (bf16[4,1,24,384]{3,2,1,0:T(8,128)(2,1)S(1)}, bf16[4,1,24,384]{3,2,1,0:T(8,128)(2,1)S(1)}, u32[]{:S(2)}, u32[]{:S(2)}) collective-permute-start(bf16[4,1,24,384]{3,2,1,0:T(8,128)(2,1)S(1)} %get-tuple-element.8), channel_id=1, source_target_pairs={{9,16},{10,17},{11,18},{12,19},{13,20},{14,21},{15,22}} | collective-permute-start | bytes 221192 | tf_op jit(solution)/shard_map/ppermute | solution.py:30
  28.5 18.6 %collective-permute-done.8 = bf16[4,1,24,384]{3,2,1,0:T(8,128)(2,1)S(1)} collective-permute-done((bf16[4,1,24,384]{3,2,1,0:T(8,128)(2,1)S(1)}, bf16[4,1,24,384]{3,2,1,0:T(8,128)(2,1)S(1)}, u32[]{:S(2)}, u32[]{:S(2)}) %collective-permute-start.8) | collective-permute-done | bytes 73760 | tf_op jit(solution)/shard_map/ppermute | solution.py:30
  47.2 4.4 %collective-permute-done.9 = bf16[4,1,24,384]{3,2,1,0:T(8,128)(2,1)S(1)} collective-permute-done((bf16[4,1,24,384]{3,2,1,0:T(8,128)(2,1)S(1)}, bf16[4,1,24,384]{3,2,1,0:T(8,128)(2,1)S(1)}, u32[]{:S(2)}, u32[]{:S(2)}) %collective-permute-start.9) | collective-permute-done | bytes 73760 | tf_op jit(solution)/shard_map/ppermute | solution.py:30
  51.7 0.3 fusion.94
  52.1 0.2 copy.158
  52.3 0.2 pad.9.clone
  52.7 5.7 %fusion.24 = bf16[4,4,8,4,384]{4,2,3,1,0:T(8,128)(2,1)S(1)} fusion(bf16[1,3,3,3,384,384]{5,4,3,2,1,0:T(8,128)(2,1)S(1)} %bitcast.144, bf16[4,6,1,7,2,384]{5,3,4,1,0,2:T(8,128)(2,1)S(1)} %slice.113, bf16[4,6,1,8,4,384]{5,3,4,1,0,2:T(8,128)(2,1)S(1)} %copy.130, pred[8,4]{0,1:T(4,128)(4,1)S(1)} %copy-done.1), kind=kOutput, calls=%fused_computation.19 | convolution fusion | flops 3060695040 | bytes 9203744 | tf_op jit(solution)/shard_map/conv_general_dilated | solution.py:18
  58.4 0.2 copy.131
  58.7 1.3 %collective-permute-start.11 = (bf16[4,4,24,384]{3,2,1,0:T(8,128)(2,1)S(1)}, bf16[4,4,24,384]{3,2,1,0:T(8,128)(2,1)S(1)}, u32[]{:S(2)}, u32[]{:S(2)}) collective-permute-start(bf16[4,4,24,384]{3,2,1,0:T(8,128)(2,1)S(1)} %bitcast.128), channel_id=1, source_target_pairs={{16,24},{17,25},{18,26},{19,27},{20,28},{21,29},{22,30},{23,31}} | collective-permute-start | bytes 884744 | tf_op jit(solution)/shard_map/ppermute | solution.py:30
  60.1 1.3 %collective-permute-start.10 = (bf16[4,1,24,384]{3,2,1,0:T(8,128)(2,1)S(1)}, bf16[4,1,24,384]{3,2,1,0:T(8,128)(2,1)S(1)}, u32[]{:S(2)}, u32[]{:S(2)}) collective-permute-start(bf16[4,1,24,384]{3,2,1,0:T(8,128)(2,1)S(1)} %get-tuple-element.5), channel_id=1, source_target_pairs={{16,25},{17,26},{18,27},{19,28},{20,29},{21,30},{22,31}} | collective-permute-start | bytes 221192 | tf_op jit(solution)/shard_map/ppermute | solution.py:30
  61.4 1.3 %collective-permute-start.12 = (bf16[4,1,24,384]{3,2,1,0:T(8,128)(2,1)S(1)}, bf16[4,1,24,384]{3,2,1,0:T(8,128)(2,1)S(1)}, u32[]{:S(2)}, u32[]{:S(2)}) collective-permute-start(bf16[4,1,24,384]{3,2,1,0:T(8,128)(2,1)S(1)} %get-tuple-element.6), channel_id=1, source_target_pairs={{17,24},{18,25},{19,26},{20,27},{21,28},{22,29},{23,30}} | collective-permute-start | bytes 221192 | tf_op jit(solution)/shard_map/ppermute | solution.py:30
  62.7 0.7 collective-permute-start.7
  63.4 1.3 %collective-permute-start.6 = (bf16[1,4,24,384]{3,2,1,0:T(8,128)(2,1)S(1)}, bf16[1,4,24,384]{3,2,1,0:T(8,128)(2,1)S(1)}, u32[]{:S(2)}, u32[]{:S(2)}) collective-permute-start(bf16[1,4,24,384]{3,2,1,0:T(8,128)(2,1)S(1)} %slice.107), channel_id=1, source_target_pairs={{16,24},{17,25},{18,26},{19,27},{20,28},{21,29},{22,30},{23,31}} | collective-permute-start | bytes 221192 | tf_op jit(solution)/shard_map/ppermute | solution.py:30
  64.7 2.3 %collective-permute-done.10 = bf16[4,1,24,384]{3,2,1,0:T(8,128)(2,1)S(1)} collective-permute-done((bf16[4,1,24,384]{3,2,1,0:T(8,128)(2,1)S(1)}, bf16[4,1,24,384]{3,2,1,0:T(8,128)(2,1)S(1)}, u32[]{:S(2)}, u32[]{:S(2)}) %collective-permute-start.10) | collective-permute-done | bytes 73760 | tf_op jit(solution)/shard_map/ppermute | solution.py:30
  67.0 0.8 collective-permute-done.12
  67.9 0.3 fusion.52
  68.3 0.2 copy.160
  68.5 0.2 pad.13.clone
  68.9 3.0 %fusion.39 = bf16[2,4,8,4,384]{4,2,3,1,0:T(8,128)(2,1)S(1)} fusion(bf16[1,3,3,3,384,384]{5,4,3,2,1,0:T(8,128)(2,1)S(1)} %bitcast.144, bf16[4,6,1,7,2,384]{5,3,4,1,0,2:T(8,128)(2,1)S(1)} %slice.122, bf16[4,6,1,8,4,384]{5,3,4,1,0,2:T(8,128)(2,1)S(1)} %copy.144, pred[8,4]{0,1:T(4,128)(4,1)S(1)} %copy-done.1), kind=kOutput, calls=%fused_computation.24 | convolution fusion | flops 2041282560 | bytes 9007136 | tf_op jit(solution)/shard_map/conv_general_dilated | solution.py:18
  72.1 0.9 %collective-permute-start.14 = (bf16[1,4,24,384]{3,2,1,0:T(8,128)(2,1)S(1)}, bf16[1,4,24,384]{3,2,1,0:T(8,128)(2,1)S(1)}, u32[]{:S(2)}, u32[]{:S(2)}) collective-permute-start(bf16[1,4,24,384]{3,2,1,0:T(8,128)(2,1)S(1)} %bitcast.140), channel_id=1, source_target_pairs={{24,8},{25,9},{26,10},{27,11},{28,12},{29,13},{30,14},{31,15}} | collective-permute-start | bytes 221192 | tf_op jit(solution)/shard_map/ppermute | solution.py:30
  73.1 0.7 collective-permute-start.15
  73.8 0.3 fusion.95
  74.1 0.2 copy.159
  74.3 0.2 pad.11.clone
  74.7 3.0 %fusion.42 = bf16[2,4,8,4,384]{4,2,3,1,0:T(8,128)(2,1)S(1)} fusion(bf16[1,3,3,3,384,384]{5,4,3,2,1,0:T(8,128)(2,1)S(1)} %bitcast.144, bf16[4,6,1,7,2,384]{5,3,4,1,0,2:T(8,128)(2,1)S(1)} %slice.117, bf16[4,6,1,8,4,384]{5,3,4,1,0,2:T(8,128)(2,1)S(1)} %copy.137, pred[8,4]{0,1:T(4,128)(4,1)S(1)} %copy-done.1), kind=kOutput, calls=%fused_computation.25 | convolution fusion | flops 2041282560 | bytes 9007136 | tf_op jit(solution)/shard_map/conv_general_dilated | solution.py:18
  77.8 1.3 %collective-permute-start.13 = (bf16[1,4,24,384]{3,2,1,0:T(8,128)(2,1)S(1)}, bf16[1,4,24,384]{3,2,1,0:T(8,128)(2,1)S(1)}, u32[]{:S(2)}, u32[]{:S(2)}) collective-permute-start(bf16[1,4,24,384]{3,2,1,0:T(8,128)(2,1)S(1)} %bitcast.142), channel_id=1, source_target_pairs={{24,16},{25,17},{26,18},{27,19},{28,20},{29,21},{30,22},{31,23}} | collective-permute-start | bytes 221192 | tf_op jit(solution)/shard_map/ppermute | solution.py:30
  79.3 8.0 %collective-permute-done.13 = bf16[1,4,24,384]{3,2,1,0:T(8,128)(2,1)S(1)} collective-permute-done((bf16[1,4,24,384]{3,2,1,0:T(8,128)(2,1)S(1)}, bf16[1,4,24,384]{3,2,1,0:T(8,128)(2,1)S(1)}, u32[]{:S(2)}, u32[]{:S(2)}) %collective-permute-start.13) | collective-permute-done | bytes 73760 | tf_op jit(solution)/shard_map/ppermute | solution.py:30
  87.3 0.7 add_convert_fusion
  (68 shorter events, 3.0 us)
Async XLA Ops:
  0.9 4.4 %collective-permute-start.1 = (bf16[4,1,24,384]{3,2,1,0:T(8,128)(2,1)S(1)}, bf16[4,1,24,384]{3,2,1,0:T(8,128)(2,1)S(1)}, u32[]{:S(2)}, u32[]{:S(2)}) collective-permute-start(bf16[4,1,24,384]{3,2,1,0:T(8,128)(2,1)S(1)} %get-tuple-element.12), channel_id=1, source_target_pairs={{1,0},{2,1},{3,2},{4,3},{5,4},{6,5},{7,6}} | collective-permute-start | bytes 221192 | tf_op jit(solution)/shard_map/ppermute | solution.py:30
  1.6 3.8 %collective-permute-start = (bf16[4,1,24,384]{3,2,1,0:T(8,128)(2,1)S(1)}, bf16[4,1,24,384]{3,2,1,0:T(8,128)(2,1)S(1)}, u32[]{:S(2)}, u32[]{:S(2)}) collective-permute-start(bf16[4,1,24,384]{3,2,1,0:T(8,128)(2,1)S(1)} %get-tuple-element.11), channel_id=1, source_target_pairs={{0,1},{1,2},{2,3},{3,4},{4,5},{5,6},{6,7}} | collective-permute-start | bytes 221192 | tf_op jit(solution)/shard_map/ppermute | solution.py:30
  5.8 0.7 copy-start.1
  6.3 12.0 %slice-start = ((s8[7962624]{0:T(1024)(128)(4,1)}), s8[4194304]{0:T(1024)(128)(4,1)S(1)}, s32[]{:S(2)}) async-start(s8[7962624]{0:T(1024)(128)(4,1)} %bitcast.143), calls=%async_computation | async-start | bytes 8388608
  6.5 11.9 %slice-start.1 = ((s8[7962624]{0:T(1024)(128)(4,1)}), s8[3768320]{0:T(1024)(128)(4,1)S(1)}, s32[]{:S(2)}) async-start(s8[7962624]{0:T(1024)(128)(4,1)} %bitcast.143), calls=%async_computation.1 | async-start | bytes 7536640
  15.1 2.1 %collective-permute-start.3 = (bf16[4,4,24,384]{3,2,1,0:T(8,128)(2,1)S(1)}, bf16[4,4,24,384]{3,2,1,0:T(8,128)(2,1)S(1)}, u32[]{:S(2)}, u32[]{:S(2)}) collective-permute-start(bf16[4,4,24,384]{3,2,1,0:T(8,128)(2,1)S(1)} %bitcast.130), channel_id=1, source_target_pairs={{0,8},{1,9},{2,10},{3,11},{4,12},{5,13},{6,14},{7,15}} | collective-permute-start | bytes 884744 | tf_op jit(solution)/shard_map/ppermute | solution.py:30
  15.8 1.3 %collective-permute-start.2 = (bf16[4,1,24,384]{3,2,1,0:T(8,128)(2,1)S(1)}, bf16[4,1,24,384]{3,2,1,0:T(8,128)(2,1)S(1)}, u32[]{:S(2)}, u32[]{:S(2)}) collective-permute-start(bf16[4,1,24,384]{3,2,1,0:T(8,128)(2,1)S(1)} %get-tuple-element.9), channel_id=1, source_target_pairs={{0,9},{1,10},{2,11},{3,12},{4,13},{5,14},{6,15}} | collective-permute-start | bytes 221192 | tf_op jit(solution)/shard_map/ppermute | solution.py:30
  16.5 0.7 collective-permute-start.4
  18.3 6.0 %copy-start = (bf16[4,4,24,384]{3,2,1,0:T(8,128)(2,1)S(1)}, bf16[4,4,24,384]{3,2,1,0:T(8,128)(2,1)}, u32[]{:S(2)}) copy-start(bf16[4,4,24,384]{3,2,1,0:T(8,128)(2,1)} %param.3) | copy-start | bytes 884740
  24.4 27.1 %collective-permute-start.5 = (bf16[4,4,24,384]{3,2,1,0:T(8,128)(2,1)S(1)}, bf16[4,4,24,384]{3,2,1,0:T(8,128)(2,1)S(1)}, u32[]{:S(2)}, u32[]{:S(2)}) collective-permute-start(bf16[4,4,24,384]{3,2,1,0:T(8,128)(2,1)S(1)} %fusion.91), channel_id=1, source_target_pairs={{8,16},{9,17},{10,18},{11,19},{12,20},{13,21},{14,22},{15,23}} | collective-permute-start | bytes 884744 | tf_op jit(solution)/shard_map/ppermute | solution.py:30
  25.8 21.4 %collective-permute-start.8 = (bf16[4,1,24,384]{3,2,1,0:T(8,128)(2,1)S(1)}, bf16[4,1,24,384]{3,2,1,0:T(8,128)(2,1)S(1)}, u32[]{:S(2)}, u32[]{:S(2)}) collective-permute-start(bf16[4,1,24,384]{3,2,1,0:T(8,128)(2,1)S(1)} %get-tuple-element.7), channel_id=1, source_target_pairs={{8,17},{9,18},{10,19},{11,20},{12,21},{13,22},{14,23}} | collective-permute-start | bytes 221192 | tf_op jit(solution)/shard_map/ppermute | solution.py:30
  27.2 24.3 %collective-permute-start.9 = (bf16[4,1,24,384]{3,2,1,0:T(8,128)(2,1)S(1)}, bf16[4,1,24,384]{3,2,1,0:T(8,128)(2,1)S(1)}, u32[]{:S(2)}, u32[]{:S(2)}) collective-permute-start(bf16[4,1,24,384]{3,2,1,0:T(8,128)(2,1)S(1)} %get-tuple-element.8), channel_id=1, source_target_pairs={{9,16},{10,17},{11,18},{12,19},{13,20},{14,21},{15,22}} | collective-permute-start | bytes 221192 | tf_op jit(solution)/shard_map/ppermute | solution.py:30
  58.7 9.0 %collective-permute-start.11 = (bf16[4,4,24,384]{3,2,1,0:T(8,128)(2,1)S(1)}, bf16[4,4,24,384]{3,2,1,0:T(8,128)(2,1)S(1)}, u32[]{:S(2)}, u32[]{:S(2)}) collective-permute-start(bf16[4,4,24,384]{3,2,1,0:T(8,128)(2,1)S(1)} %bitcast.128), channel_id=1, source_target_pairs={{16,24},{17,25},{18,26},{19,27},{20,28},{21,29},{22,30},{23,31}} | collective-permute-start | bytes 884744 | tf_op jit(solution)/shard_map/ppermute | solution.py:30
  60.1 6.9 %collective-permute-start.10 = (bf16[4,1,24,384]{3,2,1,0:T(8,128)(2,1)S(1)}, bf16[4,1,24,384]{3,2,1,0:T(8,128)(2,1)S(1)}, u32[]{:S(2)}, u32[]{:S(2)}) collective-permute-start(bf16[4,1,24,384]{3,2,1,0:T(8,128)(2,1)S(1)} %get-tuple-element.5), channel_id=1, source_target_pairs={{16,25},{17,26},{18,27},{19,28},{20,29},{21,30},{22,31}} | collective-permute-start | bytes 221192 | tf_op jit(solution)/shard_map/ppermute | solution.py:30
  61.4 6.4 %collective-permute-start.12 = (bf16[4,1,24,384]{3,2,1,0:T(8,128)(2,1)S(1)}, bf16[4,1,24,384]{3,2,1,0:T(8,128)(2,1)S(1)}, u32[]{:S(2)}, u32[]{:S(2)}) collective-permute-start(bf16[4,1,24,384]{3,2,1,0:T(8,128)(2,1)S(1)} %get-tuple-element.6), channel_id=1, source_target_pairs={{17,24},{18,25},{19,26},{20,27},{21,28},{22,29},{23,30}} | collective-permute-start | bytes 221192 | tf_op jit(solution)/shard_map/ppermute | solution.py:30
  62.7 16.6 %collective-permute-start.7 = (bf16[1,4,24,384]{3,2,1,0:T(8,128)(2,1)S(1)}, bf16[1,4,24,384]{3,2,1,0:T(8,128)(2,1)S(1)}, u32[]{:S(2)}, u32[]{:S(2)}) collective-permute-start(bf16[1,4,24,384]{3,2,1,0:T(8,128)(2,1)S(1)} %slice.109), channel_id=1, source_target_pairs={{8,0},{9,1},{10,2},{11,3},{12,4},{13,5},{14,6},{15,7}} | collective-permute-start | bytes 221192 | tf_op jit(solution)/shard_map/ppermute | solution.py:30
  63.4 15.9 %collective-permute-start.6 = (bf16[1,4,24,384]{3,2,1,0:T(8,128)(2,1)S(1)}, bf16[1,4,24,384]{3,2,1,0:T(8,128)(2,1)S(1)}, u32[]{:S(2)}, u32[]{:S(2)}) collective-permute-start(bf16[1,4,24,384]{3,2,1,0:T(8,128)(2,1)S(1)} %slice.107), channel_id=1, source_target_pairs={{16,24},{17,25},{18,26},{19,27},{20,28},{21,29},{22,30},{23,31}} | collective-permute-start | bytes 221192 | tf_op jit(solution)/shard_map/ppermute | solution.py:30
  72.1 7.2 %collective-permute-start.14 = (bf16[1,4,24,384]{3,2,1,0:T(8,128)(2,1)S(1)}, bf16[1,4,24,384]{3,2,1,0:T(8,128)(2,1)S(1)}, u32[]{:S(2)}, u32[]{:S(2)}) collective-permute-start(bf16[1,4,24,384]{3,2,1,0:T(8,128)(2,1)S(1)} %bitcast.140), channel_id=1, source_target_pairs={{24,8},{25,9},{26,10},{27,11},{28,12},{29,13},{30,14},{31,15}} | collective-permute-start | bytes 221192 | tf_op jit(solution)/shard_map/ppermute | solution.py:30
  73.1 6.2 %collective-permute-start.15 = (bf16[1,4,24,384]{3,2,1,0:T(8,128)(2,1)S(1)}, bf16[1,4,24,384]{3,2,1,0:T(8,128)(2,1)S(1)}, u32[]{:S(2)}, u32[]{:S(2)}) collective-permute-start(bf16[1,4,24,384]{3,2,1,0:T(8,128)(2,1)S(1)} %bitcast.141), channel_id=1, source_target_pairs={{24,0},{25,1},{26,2},{27,3},{28,4},{29,5},{30,6},{31,7}} | collective-permute-start | bytes 221192 | tf_op jit(solution)/shard_map/ppermute | solution.py:30
  77.8 9.4 %collective-permute-start.13 = (bf16[1,4,24,384]{3,2,1,0:T(8,128)(2,1)S(1)}, bf16[1,4,24,384]{3,2,1,0:T(8,128)(2,1)S(1)}, u32[]{:S(2)}, u32[]{:S(2)}) collective-permute-start(bf16[1,4,24,384]{3,2,1,0:T(8,128)(2,1)S(1)} %bitcast.142), channel_id=1, source_target_pairs={{24,16},{25,17},{26,18},{27,19},{28,20},{29,21},{30,22},{31,23}} | collective-permute-start | bytes 221192 | tf_op jit(solution)/shard_map/ppermute | solution.py:30

commit v20 on v17

--- a/solution.py
+++ b/solution.py
@@ -64,12 +64,7 @@
 
     for stage in range(segment_count):
         pieces = [top, current, bottom] if stage else [top, features, bottom]
-        window = jnp.concatenate(
-            [activate(piece, gain_row) for piece in pieces]
-            if stage == 0
-            else [activate(jnp.concatenate(pieces, axis=1), gain_row)],
-            axis=1,
-        )
+        window = jnp.concatenate([activate(piece, gain_row) for piece in pieces], axis=1)
         odd = stage % 2 == 1
         final = stage == last_stage
 

time: 88.3 us -> 88.4 us (level)
  the two profiles are of different devices: /device:TPU:17 before, /device:TPU:22 now
where the time goes in v20:
time: 88.4 us; the launch traced here: 88 us
  waiting for transfers between devices  31.1 us (35%)
  matrix products  25.6 us (29%)
  starting transfers between devices  18.3 us (21%)
  other arithmetic  6.76 us (8%)
  local copies, waits for them, and re-layouts  5.36 us (6%)
    ppermute x17, waiting for transfers between devices, send(): return lax.ppermute(value, BOTH, pairs)  31.1 us
    conv_general_dilated x5, matrix products, causal_conv(): lax.conv_general_dilated(window[None], kernel, window_strides=(1, 1, 1),...  25.6 us
    ppermute x17, starting transfers between devices, send(): return lax.ppermute(value, BOTH, pairs)  18.3 us
    convert_element_type x8, other arithmetic, activate(): return jax.nn.silu(widened * lax.rsqrt(mean_square + 1e-06) * gain_row.as...  2.64 us
    reduce_sum x12, other arithmetic, activate(): mean_square = jnp.mean(widened * widened, axis=-1, keepdims=True)  2.28 us
  transfers between devices with their start and end apart: 17, of which 4 were waited for; matrix products, arithmetic and copies ran while one was open for 14% of the time, Pallas kernels for 0%

profile of v20, /device:TPU:22, one launch (start us, length us, event | category | flops | bytes accessed | tf_op | source)
XLA Modules:
  0.0 88.0 jit_solution(8551683404943271430)
XLA Ops:
  0.0 0.9 %fusion.201 = (bf16[4,1,24,384]{3,2,1,0:T(8,128)(2,1)S(1)}, bf16[4,1,24,384]{3,2,1,0:T(8,128)(2,1)S(1)}) fusion(bf16[4,4,24,384]{3,2,1,0:T(8,128)(2,1)} %param.3), kind=kLoop, calls=%fused_computation.229 | loop fusion | bytes 294912 | tf_op jit(solution)/shard_map/slice | solution.py:59
  0.9 0.7 collective-permute-start.1
  1.6 0.7 collective-permute-start
  2.3 1.1 %fusion.99 = f32[4,4,24]{2,1,0:T(4,128)S(1)} fusion(bf16[4,4,24,384]{3,2,1,0:T(8,128)(2,1)} %param.3), kind=kLoop, calls=%fused_computation.85 | loop fusion | flops 441984 | bytes 296448 | tf_op jit(solution)/shard_map/reduce_sum | solution.py:11
  3.4 0.7 convert_reduce_fusion
  4.1 1.2 %fusion.106 = bf16[4,4,24,384]{3,2,1,0:T(8,128)(2,1)S(1)} fusion(bf16[4,4,24,384]{3,2,1,0:T(8,128)(2,1)} %param.3, f32[384]{0:T(512)S(1)} %convert_reduce_fusion, f32[4,4,24]{2,1,0:T(4,128)S(1)} %add_rsqrt_fusion.3), kind=kLoop, calls=%fused_computation.92 | loop fusion | flops 1179648 | bytes 592896 | tf_op jit(solution)/shard_map/convert_element_type | solution.py:14
  5.8 0.2 copy.66
  6.0 0.2 pad.5.clone
  6.5 8.3 %fusion.30 = bf16[4,4,8,4,384]{4,2,3,1,0:T(8,128)(2,1)S(1)} fusion(bf16[1,3,3,3,384,384]{5,4,3,2,1,0:T(8,128)(2,1)} %param.5, bf16[4,6,1,7,2,384]{5,3,4,1,0,2:T(8,128)(2,1)S(1)} %slice.101, bf16[4,6,1,8,4,384]{5,3,4,1,0,2:T(8,128)(2,1)S(1)} %copy.32, pred[8,4]{0,1:T(4,128)(4,1)S(1)} %copy-done.1), kind=kOutput, calls=%fused_computation.21 | convolution fusion | flops 3060695040 | bytes 9203744 | tf_op jit(solution)/shard_map/conv_general_dilated | solution.py:18
  14.7 0.2 copy.33
  15.1 0.7 collective-permute-start.4
  15.8 0.7 collective-permute-start.3
  16.5 0.8 collective-permute-start.2
  17.9 0.3 fusion.82
  18.3 0.2 copy.67
  18.4 0.2 pad.7.clone
  18.9 5.7 %fusion.27 = bf16[4,4,8,4,384]{4,2,3,1,0:T(8,128)(2,1)S(1)} fusion(bf16[1,3,3,3,384,384]{5,4,3,2,1,0:T(8,128)(2,1)S(1)} %bitcast.114, bf16[4,6,1,7,2,384]{5,3,4,1,0,2:T(8,128)(2,1)S(1)} %slice.105, bf16[4,6,1,8,4,384]{5,3,4,1,0,2:T(8,128)(2,1)S(1)} %copy.37, pred[8,4]{0,1:T(4,128)(4,1)S(1)} %copy-done.1), kind=kOutput, calls=%fused_computation.20 | convolution fusion | flops 3060695040 | bytes 9203744 | tf_op jit(solution)/shard_map/conv_general_dilated | solution.py:18
  24.6 0.2 copy.38
  25.0 1.3 %collective-permute-start.10 = (bf16[4,1,24,384]{3,2,1,0:T(8,128)(2,1)S(1)}, bf16[4,1,24,384]{3,2,1,0:T(8,128)(2,1)S(1)}, u32[]{:S(2)}, u32[]{:S(2)}) collective-permute-start(bf16[4,1,24,384]{3,2,1,0:T(8,128)(2,1)S(1)} %get-tuple-element.10), channel_id=1, source_target_pairs={{9,16},{10,17},{11,18},{12,19},{13,20},{14,21},{15,22}} | collective-permute-start | bytes 221192 | tf_op jit(solution)/shard_map/ppermute | solution.py:30
  26.3 1.3 %collective-permute-start.5 = (bf16[4,4,24,384]{3,2,1,0:T(8,128)(2,1)S(1)}, bf16[4,4,24,384]{3,2,1,0:T(8,128)(2,1)S(1)}, u32[]{:S(2)}, u32[]{:S(2)}) collective-permute-start(bf16[4,4,24,384]{3,2,1,0:T(8,128)(2,1)S(1)} %fusion.107), channel_id=1, source_target_pairs={{8,16},{9,17},{10,18},{11,19},{12,20},{13,21},{14,22},{15,23}} | collective-permute-start | bytes 884744 | tf_op jit(solution)/shard_map/ppermute | solution.py:30
  27.6 1.5 %collective-permute-start.9 = (bf16[4,1,24,384]{3,2,1,0:T(8,128)(2,1)S(1)}, bf16[4,1,24,384]{3,2,1,0:T(8,128)(2,1)S(1)}, u32[]{:S(2)}, u32[]{:S(2)}) collective-permute-start(bf16[4,1,24,384]{3,2,1,0:T(8,128)(2,1)S(1)} %get-tuple-element.9), channel_id=1, source_target_pairs={{8,17},{9,18},{10,19},{11,20},{12,21},{13,22},{14,23}} | collective-permute-start | bytes 221192 | tf_op jit(solution)/shard_map/ppermute | solution.py:30
  29.1 11.2 %collective-permute-done.10 = bf16[4,1,24,384]{3,2,1,0:T(8,128)(2,1)S(1)} collective-permute-done((bf16[4,1,24,384]{3,2,1,0:T(8,128)(2,1)S(1)}, bf16[4,1,24,384]{3,2,1,0:T(8,128)(2,1)S(1)}, u32[]{:S(2)}, u32[]{:S(2)}) %collective-permute-start.10) | collective-permute-done | bytes 73760 | tf_op jit(solution)/shard_map/ppermute | solution.py:30
  40.4 10.8 %collective-permute-done.9 = bf16[4,1,24,384]{3,2,1,0:T(8,128)(2,1)S(1)} collective-permute-done((bf16[4,1,24,384]{3,2,1,0:T(8,128)(2,1)S(1)}, bf16[4,1,24,384]{3,2,1,0:T(8,128)(2,1)S(1)}, u32[]{:S(2)}, u32[]{:S(2)}) %collective-permute-start.9) | collective-permute-done | bytes 73760 | tf_op jit(solution)/shard_map/ppermute | solution.py:30
  51.6 0.3 fusion.90
  52.0 0.2 copy.68
  52.1 0.2 pad.9.clone
  52.6 5.7 %fusion.24 = bf16[4,4,8,4,384]{4,2,3,1,0:T(8,128)(2,1)S(1)} fusion(bf16[1,3,3,3,384,384]{5,4,3,2,1,0:T(8,128)(2,1)S(1)} %bitcast.114, bf16[4,6,1,7,2,384]{5,3,4,1,0,2:T(8,128)(2,1)S(1)} %slice.113, bf16[4,6,1,8,4,384]{5,3,4,1,0,2:T(8,128)(2,1)S(1)} %copy.42, pred[8,4]{0,1:T(4,128)(4,1)S(1)} %copy-done.1), kind=kOutput, calls=%fused_computation.19 | convolution fusion | flops 3060695040 | bytes 9203744 | tf_op jit(solution)/shard_map/conv_general_dilated | solution.py:18
  58.3 0.2 copy.43
  58.6 1.3 %collective-permute-start.12 = (bf16[4,4,24,384]{3,2,1,0:T(8,128)(2,1)S(1)}, bf16[4,4,24,384]{3,2,1,0:T(8,128)(2,1)S(1)}, u32[]{:S(2)}, u32[]{:S(2)}) collective-permute-start(bf16[4,4,24,384]{3,2,1,0:T(8,128)(2,1)S(1)} %bitcast.102), channel_id=1, source_target_pairs={{16,24},{17,25},{18,26},{19,27},{20,28},{21,29},{22,30},{23,31}} | collective-permute-start | bytes 884744 | tf_op jit(solution)/shard_map/ppermute | solution.py:30
  60.0 1.3 %collective-permute-start.13 = (bf16[4,1,24,384]{3,2,1,0:T(8,128)(2,1)S(1)}, bf16[4,1,24,384]{3,2,1,0:T(8,128)(2,1)S(1)}, u32[]{:S(2)}, u32[]{:S(2)}) collective-permute-start(bf16[4,1,24,384]{3,2,1,0:T(8,128)(2,1)S(1)} %get-tuple-element.8), channel_id=1, source_target_pairs={{17,24},{18,25},{19,26},{20,27},{21,28},{22,29},{23,30}} | collective-permute-start | bytes 221192 | tf_op jit(solution)/shard_map/ppermute | solution.py:30
  61.3 1.3 %collective-permute-start.11 = (bf16[4,1,24,384]{3,2,1,0:T(8,128)(2,1)S(1)}, bf16[4,1,24,384]{3,2,1,0:T(8,128)(2,1)S(1)}, u32[]{:S(2)}, u32[]{:S(2)}) collective-permute-start(bf16[4,1,24,384]{3,2,1,0:T(8,128)(2,1)S(1)} %get-tuple-element.7), channel_id=1, source_target_pairs={{16,25},{17,26},{18,27},{19,28},{20,29},{21,30},{22,31}} | collective-permute-start | bytes 221192 | tf_op jit(solution)/shard_map/ppermute | solution.py:30
  62.6 1.3 %collective-permute-start.6 = (bf16[1,4,24,384]{3,2,1,0:T(8,128)(2,1)S(1)}, bf16[1,4,24,384]{3,2,1,0:T(8,128)(2,1)S(1)}, u32[]{:S(2)}, u32[]{:S(2)}) collective-permute-start(bf16[1,4,24,384]{3,2,1,0:T(8,128)(2,1)S(1)} %get-tuple-element.13), channel_id=1, source_target_pairs={{16,24},{17,25},{18,26},{19,27},{20,28},{21,29},{22,30},{23,31}} | collective-permute-start | bytes 221192 | tf_op jit(solution)/shard_map/ppermute | solution.py:30
  63.9 1.3 %collective-permute-start.7 = (bf16[1,4,24,384]{3,2,1,0:T(8,128)(2,1)S(1)}, bf16[1,4,24,384]{3,2,1,0:T(8,128)(2,1)S(1)}, u32[]{:S(2)}, u32[]{:S(2)}) collective-permute-start(bf16[1,4,24,384]{3,2,1,0:T(8,128)(2,1)S(1)} %get-tuple-element.12), channel_id=1, source_target_pairs={{16,8},{17,9},{18,10},{19,11},{20,12},{21,13},{22,14},{23,15}} | collective-permute-start | bytes 221192 | tf_op jit(solution)/shard_map/ppermute | solution.py:30
  65.2 1.1 %collective-permute-done.13 = bf16[4,1,24,384]{3,2,1,0:T(8,128)(2,1)S(1)} collective-permute-done((bf16[4,1,24,384]{3,2,1,0:T(8,128)(2,1)S(1)}, bf16[4,1,24,384]{3,2,1,0:T(8,128)(2,1)S(1)}, u32[]{:S(2)}, u32[]{:S(2)}) %collective-permute-start.13) | collective-permute-done | bytes 73760 | tf_op jit(solution)/shard_map/ppermute | solution.py:30
  66.3 1.5 %collective-permute-start.8 = (bf16[1,4,24,384]{3,2,1,0:T(8,128)(2,1)S(1)}, bf16[1,4,24,384]{3,2,1,0:T(8,128)(2,1)S(1)}, u32[]{:S(2)}, u32[]{:S(2)}) collective-permute-start(bf16[1,4,24,384]{3,2,1,0:T(8,128)(2,1)S(1)} %get-tuple-element.11), channel_id=1, source_target_pairs={{16,0},{17,1},{18,2},{19,3},{20,4},{21,5},{22,6},{23,7}} | collective-permute-start | bytes 221192 | tf_op jit(solution)/shard_map/ppermute | solution.py:30
  68.1 0.2 fusion.169
  68.5 0.3 fusion.98
  68.9 0.2 copy.70
  69.0 0.2 pad.13.clone
  69.5 3.0 %fusion.39 = bf16[2,4,8,4,384]{4,2,3,1,0:T(8,128)(2,1)S(1)} fusion(bf16[1,3,3,3,384,384]{5,4,3,2,1,0:T(8,128)(2,1)S(1)} %bitcast.114, bf16[4,6,1,7,2,384]{5,3,4,1,0,2:T(8,128)(2,1)S(1)} %slice.122, bf16[4,6,1,8,4,384]{5,3,4,1,0,2:T(8,128)(2,1)S(1)} %copy.54, pred[8,4]{0,1:T(4,128)(4,1)S(1)} %copy-done.1), kind=kOutput, calls=%fused_computation.24 | convolution fusion | flops 2041282560 | bytes 9007136 | tf_op jit(solution)/shard_map/conv_general_dilated | solution.py:18
  72.6 0.7 collective-permute-start.15
  73.4 0.7 collective-permute-start.16
  74.1 0.2 copy.69
  74.3 0.2 pad.11.clone
  74.7 3.0 %fusion.42 = bf16[2,4,8,4,384]{4,2,3,1,0:T(8,128)(2,1)S(1)} fusion(bf16[1,3,3,3,384,384]{5,4,3,2,1,0:T(8,128)(2,1)S(1)} %bitcast.114, bf16[4,6,1,7,2,384]{5,3,4,1,0,2:T(8,128)(2,1)S(1)} %slice.117, bf16[4,6,1,8,4,384]{5,3,4,1,0,2:T(8,128)(2,1)S(1)} %copy.47, pred[8,4]{0,1:T(4,128)(4,1)S(1)} %copy-done.1), kind=kOutput, calls=%fused_computation.25 | convolution fusion | flops 2041282560 | bytes 9007136 | tf_op jit(solution)/shard_map/conv_general_dilated | solution.py:18
  77.8 1.3 %collective-permute-start.14 = (bf16[1,4,24,384]{3,2,1,0:T(8,128)(2,1)S(1)}, bf16[1,4,24,384]{3,2,1,0:T(8,128)(2,1)S(1)}, u32[]{:S(2)}, u32[]{:S(2)}) collective-permute-start(bf16[1,4,24,384]{3,2,1,0:T(8,128)(2,1)S(1)} %bitcast.112), channel_id=1, source_target_pairs={{24,16},{25,17},{26,18},{27,19},{28,20},{29,21},{30,22},{31,23}} | collective-permute-start | bytes 221192 | tf_op jit(solution)/shard_map/ppermute | solution.py:30
  79.3 8.0 %collective-permute-done.14 = bf16[1,4,24,384]{3,2,1,0:T(8,128)(2,1)S(1)} collective-permute-done((bf16[1,4,24,384]{3,2,1,0:T(8,128)(2,1)S(1)}, bf16[1,4,24,384]{3,2,1,0:T(8,128)(2,1)S(1)}, u32[]{:S(2)}, u32[]{:S(2)}) %collective-permute-start.14) | collective-permute-done | bytes 73760 | tf_op jit(solution)/shard_map/ppermute | solution.py:30
  87.3 0.7 add_convert_fusion
  (86 shorter events, 4.1 us)
Async XLA Ops:
  0.9 4.4 %collective-permute-start.1 = (bf16[4,1,24,384]{3,2,1,0:T(8,128)(2,1)S(1)}, bf16[4,1,24,384]{3,2,1,0:T(8,128)(2,1)S(1)}, u32[]{:S(2)}, u32[]{:S(2)}) collective-permute-start(bf16[4,1,24,384]{3,2,1,0:T(8,128)(2,1)S(1)} %get-tuple-element.17), channel_id=1, source_target_pairs={{1,0},{2,1},{3,2},{4,3},{5,4},{6,5},{7,6}} | collective-permute-start | bytes 221192 | tf_op jit(solution)/shard_map/ppermute | solution.py:30
  1.6 3.8 %collective-permute-start = (bf16[4,1,24,384]{3,2,1,0:T(8,128)(2,1)S(1)}, bf16[4,1,24,384]{3,2,1,0:T(8,128)(2,1)S(1)}, u32[]{:S(2)}, u32[]{:S(2)}) collective-permute-start(bf16[4,1,24,384]{3,2,1,0:T(8,128)(2,1)S(1)} %get-tuple-element.16), channel_id=1, source_target_pairs={{0,1},{1,2},{2,3},{3,4},{4,5},{5,6},{6,7}} | collective-permute-start | bytes 221192 | tf_op jit(solution)/shard_map/ppermute | solution.py:30
  5.8 0.7 copy-start.1
  6.3 12.5 %slice-start = ((s8[7962624]{0:T(1024)(128)(4,1)}), s8[4194304]{0:T(1024)(128)(4,1)S(1)}, s32[]{:S(2)}) async-start(s8[7962624]{0:T(1024)(128)(4,1)} %bitcast.113), calls=%async_computation | async-start | bytes 8388608
  6.5 12.4 %slice-start.1 = ((s8[7962624]{0:T(1024)(128)(4,1)}), s8[3768320]{0:T(1024)(128)(4,1)S(1)}, s32[]{:S(2)}) async-start(s8[7962624]{0:T(1024)(128)(4,1)} %bitcast.113), calls=%async_computation.1 | async-start | bytes 7536640
  15.1 2.2 %collective-permute-start.4 = (bf16[4,1,24,384]{3,2,1,0:T(8,128)(2,1)S(1)}, bf16[4,1,24,384]{3,2,1,0:T(8,128)(2,1)S(1)}, u32[]{:S(2)}, u32[]{:S(2)}) collective-permute-start(bf16[4,1,24,384]{3,2,1,0:T(8,128)(2,1)S(1)} %get-tuple-element.15), channel_id=1, source_target_pairs={{1,8},{2,9},{3,10},{4,11},{5,12},{6,13},{7,14}} | collective-permute-start | bytes 221192 | tf_op jit(solution)/shard_map/ppermute | solution.py:30
  15.8 2.0 %collective-permute-start.3 = (bf16[4,4,24,384]{3,2,1,0:T(8,128)(2,1)S(1)}, bf16[4,4,24,384]{3,2,1,0:T(8,128)(2,1)S(1)}, u32[]{:S(2)}, u32[]{:S(2)}) collective-permute-start(bf16[4,4,24,384]{3,2,1,0:T(8,128)(2,1)S(1)} %bitcast.105), channel_id=1, source_target_pairs={{0,8},{1,9},{2,10},{3,11},{4,12},{5,13},{6,14},{7,15}} | collective-permute-start | bytes 884744 | tf_op jit(solution)/shard_map/ppermute | solution.py:30
  16.5 1.0 %collective-permute-start.2 = (bf16[4,1,24,384]{3,2,1,0:T(8,128)(2,1)S(1)}, bf16[4,1,24,384]{3,2,1,0:T(8,128)(2,1)S(1)}, u32[]{:S(2)}, u32[]{:S(2)}) collective-permute-start(bf16[4,1,24,384]{3,2,1,0:T(8,128)(2,1)S(1)} %get-tuple-element.14), channel_id=1, source_target_pairs={{0,9},{1,10},{2,11},{3,12},{4,13},{5,14},{6,15}} | collective-permute-start | bytes 221192 | tf_op jit(solution)/shard_map/ppermute | solution.py:30
  18.9 6.0 %copy-start = (bf16[4,4,24,384]{3,2,1,0:T(8,128)(2,1)S(1)}, bf16[4,4,24,384]{3,2,1,0:T(8,128)(2,1)}, u32[]{:S(2)}) copy-start(bf16[4,4,24,384]{3,2,1,0:T(8,128)(2,1)} %param.3) | copy-start | bytes 884740
  25.0 15.3 %collective-permute-start.10 = (bf16[4,1,24,384]{3,2,1,0:T(8,128)(2,1)S(1)}, bf16[4,1,24,384]{3,2,1,0:T(8,128)(2,1)S(1)}, u32[]{:S(2)}, u32[]{:S(2)}) collective-permute-start(bf16[4,1,24,384]{3,2,1,0:T(8,128)(2,1)S(1)} %get-tuple-element.10), channel_id=1, source_target_pairs={{9,16},{10,17},{11,18},{12,19},{13,20},{14,21},{15,22}} | collective-permute-start | bytes 221192 | tf_op jit(solution)/shard_map/ppermute | solution.py:30
  26.3 25.2 %collective-permute-start.5 = (bf16[4,4,24,384]{3,2,1,0:T(8,128)(2,1)S(1)}, bf16[4,4,24,384]{3,2,1,0:T(8,128)(2,1)S(1)}, u32[]{:S(2)}, u32[]{:S(2)}) collective-permute-start(bf16[4,4,24,384]{3,2,1,0:T(8,128)(2,1)S(1)} %fusion.107), channel_id=1, source_target_pairs={{8,16},{9,17},{10,18},{11,19},{12,20},{13,21},{14,22},{15,23}} | collective-permute-start | bytes 884744 | tf_op jit(solution)/shard_map/ppermute | solution.py:30
  27.6 23.6 %collective-permute-start.9 = (bf16[4,1,24,384]{3,2,1,0:T(8,128)(2,1)S(1)}, bf16[4,1,24,384]{3,2,1,0:T(8,128)(2,1)S(1)}, u32[]{:S(2)}, u32[]{:S(2)}) collective-permute-start(bf16[4,1,24,384]{3,2,1,0:T(8,128)(2,1)S(1)} %get-tuple-element.9), channel_id=1, source_target_pairs={{8,17},{9,18},{10,19},{11,20},{12,21},{13,22},{14,23}} | collective-permute-start | bytes 221192 | tf_op jit(solution)/shard_map/ppermute | solution.py:30
  58.6 9.7 %collective-permute-start.12 = (bf16[4,4,24,384]{3,2,1,0:T(8,128)(2,1)S(1)}, bf16[4,4,24,384]{3,2,1,0:T(8,128)(2,1)S(1)}, u32[]{:S(2)}, u32[]{:S(2)}) collective-permute-start(bf16[4,4,24,384]{3,2,1,0:T(8,128)(2,1)S(1)} %bitcast.102), channel_id=1, source_target_pairs={{16,24},{17,25},{18,26},{19,27},{20,28},{21,29},{22,30},{23,31}} | collective-permute-start | bytes 884744 | tf_op jit(solution)/shard_map/ppermute | solution.py:30
  60.0 6.4 %collective-permute-start.13 = (bf16[4,1,24,384]{3,2,1,0:T(8,128)(2,1)S(1)}, bf16[4,1,24,384]{3,2,1,0:T(8,128)(2,1)S(1)}, u32[]{:S(2)}, u32[]{:S(2)}) collective-permute-start(bf16[4,1,24,384]{3,2,1,0:T(8,128)(2,1)S(1)} %get-tuple-element.8), channel_id=1, source_target_pairs={{17,24},{18,25},{19,26},{20,27},{21,28},{22,29},{23,30}} | collective-permute-start | bytes 221192 | tf_op jit(solution)/shard_map/ppermute | solution.py:30
  61.3 6.7 %collective-permute-start.11 = (bf16[4,1,24,384]{3,2,1,0:T(8,128)(2,1)S(1)}, bf16[4,1,24,384]{3,2,1,0:T(8,128)(2,1)S(1)}, u32[]{:S(2)}, u32[]{:S(2)}) collective-permute-start(bf16[4,1,24,384]{3,2,1,0:T(8,128)(2,1)S(1)} %get-tuple-element.7), channel_id=1, source_target_pairs={{16,25},{17,26},{18,27},{19,28},{20,29},{21,30},{22,31}} | collective-permute-start | bytes 221192 | tf_op jit(solution)/shard_map/ppermute | solution.py:30
  62.6 15.2 %collective-permute-start.6 = (bf16[1,4,24,384]{3,2,1,0:T(8,128)(2,1)S(1)}, bf16[1,4,24,384]{3,2,1,0:T(8,128)(2,1)S(1)}, u32[]{:S(2)}, u32[]{:S(2)}) collective-permute-start(bf16[1,4,24,384]{3,2,1,0:T(8,128)(2,1)S(1)} %get-tuple-element.13), channel_id=1, source_target_pairs={{16,24},{17,25},{18,26},{19,27},{20,28},{21,29},{22,30},{23,31}} | collective-permute-start | bytes 221192 | tf_op jit(solution)/shard_map/ppermute | solution.py:30
  63.9 15.3 %collective-permute-start.7 = (bf16[1,4,24,384]{3,2,1,0:T(8,128)(2,1)S(1)}, bf16[1,4,24,384]{3,2,1,0:T(8,128)(2,1)S(1)}, u32[]{:S(2)}, u32[]{:S(2)}) collective-permute-start(bf16[1,4,24,384]{3,2,1,0:T(8,128)(2,1)S(1)} %get-tuple-element.12), channel_id=1, source_target_pairs={{16,8},{17,9},{18,10},{19,11},{20,12},{21,13},{22,14},{23,15}} | collective-permute-start | bytes 221192 | tf_op jit(solution)/shard_map/ppermute | solution.py:30
  66.3 12.9 %collective-permute-start.8 = (bf16[1,4,24,384]{3,2,1,0:T(8,128)(2,1)S(1)}, bf16[1,4,24,384]{3,2,1,0:T(8,128)(2,1)S(1)}, u32[]{:S(2)}, u32[]{:S(2)}) collective-permute-start(bf16[1,4,24,384]{3,2,1,0:T(8,128)(2,1)S(1)} %get-tuple-element.11), channel_id=1, source_target_pairs={{16,0},{17,1},{18,2},{19,3},{20,4},{21,5},{22,6},{23,7}} | collective-permute-start | bytes 221192 | tf_op jit(solution)/shard_map/ppermute | solution.py:30
  72.6 6.7 %collective-permute-start.15 = (bf16[1,4,24,384]{3,2,1,0:T(8,128)(2,1)S(1)}, bf16[1,4,24,384]{3,2,1,0:T(8,128)(2,1)S(1)}, u32[]{:S(2)}, u32[]{:S(2)}) collective-permute-start(bf16[1,4,24,384]{3,2,1,0:T(8,128)(2,1)S(1)} %bitcast.110), channel_id=1, source_target_pairs={{24,8},{25,9},{26,10},{27,11},{28,12},{29,13},{30,14},{31,15}} | collective-permute-start | bytes 221192 | tf_op jit(solution)/shard_map/ppermute | solution.py:30
  73.4 5.9 %collective-permute-start.16 = (bf16[1,4,24,384]{3,2,1,0:T(8,128)(2,1)S(1)}, bf16[1,4,24,384]{3,2,1,0:T(8,128)(2,1)S(1)}, u32[]{:S(2)}, u32[]{:S(2)}) collective-permute-start(bf16[1,4,24,384]{3,2,1,0:T(8,128)(2,1)S(1)} %bitcast.111), channel_id=1, source_target_pairs={{24,0},{25,1},{26,2},{27,3},{28,4},{29,5},{30,6},{31,7}} | collective-permute-start | bytes 221192 | tf_op jit(solution)/shard_map/ppermute | solution.py:30
  77.8 9.5 %collective-permute-start.14 = (bf16[1,4,24,384]{3,2,1,0:T(8,128)(2,1)S(1)}, bf16[1,4,24,384]{3,2,1,0:T(8,128)(2,1)S(1)}, u32[]{:S(2)}, u32[]{:S(2)}) collective-permute-start(bf16[1,4,24,384]{3,2,1,0:T(8,128)(2,1)S(1)} %bitcast.112), channel_id=1, source_target_pairs={{24,16},{25,17},{26,18},{27,19},{28,20},{29,21},{30,22},{31,23}} | collective-permute-start | bytes 221192 | tf_op jit(solution)/shard_map/ppermute | solution.py:30
